TPU v7x, 256 devices: a whole 4x4x8 slice. The times are simulated.
256 devices in a mesh: tm: 32 (over z, x_hi, core), chan: 8 (over y, x_lo).
Axes of the slice: x: 4 (x_hi: 2, x_lo: 2; x = x_hi * 2 + x_lo), y: 4, z: 8, core: 2. Of those that a mesh axis runs over, the one named last changes fastest.
Arguments:
- states: bfloat16 [2, 8192, 2048], P(None, 'tm'), may hold values from -6 to 6
- upstream: bfloat16 [2, 8192, 2048], P(None, 'tm'), may hold values from -6 to 6
- w_in: bfloat16 [2, 2, 2048, 2048], P(None, None, None, 'chan'), may hold values from -0.09375 to 0.09375
- w_out: bfloat16 [2048, 2048], P('chan'), may hold values from -0.125 to 0.125
- lengths: int32 [2], replicated, may hold values from 2048 to 8192, as said below
Outputs:
- grad_states: bfloat16 [2, 8192, 2048], P(None, 'tm', 'chan')
- grad_in: float32 [2, 2, 2048, 2048], P(None, None, 'tm', 'chan')
- grad_out: float32 [2048, 2048], P('chan', 'tm')
Inputs may be any that keep to these rules, and one draw needn't show every extreme that they name: `lengths`: one trajectory has all 8192 steps valid, the other at least a quarter of them.
All inputs are finite; a program needn't handle non-finite values.
Results may differ from a plain program's by a relative error of at most 0.0029.
Values may be sent and summed in bfloat16 or wider, within the bound.
No kernel may reach another device: no remote copies, remote signals or barrier semaphores. Data moves between devices by JAX's collectives and lax.ppermute only.
A program may use at most 128 MiB of HBM per device.

v0:
```python
import jax
import jax.numpy as jnp
from jax import lax
from jax.sharding import PartitionSpec as P

DILATION_STEPS = 1024


def shifted(x, axis, by):
    peers = lax.axis_size(axis)
    pairs = [(i, i + by) for i in range(peers) if 0 <= i + by < peers]
    return lax.ppermute(x, axis, pairs)


def contract_rows(left, right):
    return lax.dot_general(
        left, right, (((0,), (0,)), ((), ())), preferred_element_type=jnp.float32
    )


def local_grads(present_step, previous_step, grad_rows, w_in, w_out):
    filt = jnp.dot(present_step, w_in[0, 0], preferred_element_type=jnp.float32) + jnp.dot(
        previous_step, w_in[1, 0], preferred_element_type=jnp.float32
    )
    gate = jnp.dot(present_step, w_in[0, 1], preferred_element_type=jnp.float32) + jnp.dot(
        previous_step, w_in[1, 1], preferred_element_type=jnp.float32
    )
    tangent = jnp.tanh(filt)
    sigma = jax.nn.sigmoid(gate)
    mixed = (tangent * sigma).astype(jnp.bfloat16)
    dmix = lax.dot_general(
        grad_rows, w_out, (((1,), (1,)), ((), ())), preferred_element_type=jnp.float32
    )
    filter_gradient = (dmix * (1.0 - tangent * tangent) * sigma).astype(jnp.bfloat16)
    gate_gradient = (dmix * tangent * sigma * (1.0 - sigma)).astype(jnp.bfloat16)
    terms = jnp.stack(
        [
            jnp.stack(
                [
                    contract_rows(present_step, filter_gradient),
                    contract_rows(present_step, gate_gradient),
                ]
            ),
            jnp.stack(
                [
                    contract_rows(previous_step, filter_gradient),
                    contract_rows(previous_step, gate_gradient),
                ]
            ),
        ]
    )
    out_term = contract_rows(mixed, grad_rows)
    return (jnp.stack([filter_gradient, gate_gradient], axis=1), terms, out_term)


def local(states, upstream, w_in, w_out, lengths):
    traj, window_extent, width = states.shape
    blocks = w_in.shape[3]
    receptive_extent = DILATION_STEPS // window_extent
    previous_step = shifted(states, "tm", receptive_extent)
    first = lax.axis_index("tm") * window_extent
    positions = first + jnp.arange(window_extent, dtype=jnp.int32)
    valid = positions[None, :] < lengths[:, None]
    grad_rows = jnp.where(valid[:, :, None], upstream, jnp.zeros_like(upstream))
    flat, terms, out_term = local_grads(
        states.reshape(traj * window_extent, width),
        previous_step.reshape(traj * window_extent, width),
        grad_rows.reshape(traj * window_extent, width),
        w_in,
        w_out,
    )
    branch_grads = flat.reshape(traj, window_extent, 2, blocks)
    scale = lax.rsqrt(jnp.sum(lengths.astype(jnp.float32)))
    later = shifted(branch_grads, "tm", -receptive_extent)
    share = width // lax.axis_size("chan")
    own_rows = lax.dynamic_slice_in_dim(grad_rows, lax.axis_index("chan") * share, share, 2)
    partial_value = jnp.einsum(
        "btfc,frc->btr", branch_grads, w_in[0], preferred_element_type=jnp.float32
    )
    partial_value = partial_value + jnp.einsum(
        "btfc,frc->btr", later, w_in[1], preferred_element_type=jnp.float32
    )
    summed = lax.psum_scatter(partial_value, "chan", scatter_dimension=2, tiled=True)
    grad_states = (own_rows.astype(jnp.float32) + summed).astype(jnp.bfloat16)
    in_summed, out_summed = (
        lax.psum_scatter(terms, "tm", scatter_dimension=2, tiled=True),
        lax.psum_scatter(out_term, "tm", scatter_dimension=1, tiled=True),
    )
    return (grad_states, in_summed * scale, out_summed * scale)


def solution(mesh):
    placed = (
        P(None, "tm", None),
        P(None, "tm", None),
        P(None, None, None, "chan"),
        P("chan", None),
        P(),
    )
    return jax.shard_map(
        local,
        mesh=mesh,
        in_specs=placed,
        out_specs=(P(None, "tm", "chan"), P(None, None, "tm", "chan"), P("chan", "tm")),
        check_vma=False,
    )
```

profile of v0, /device:TPU:98, one launch (start us, length us, event | category | flops | bytes accessed | tf_op | source)
XLA Modules:
  0.0 586.3 jit_solution(2051890219245385128)
XLA Ops:
  7.2 0.0 copy-start
  7.2 0.0 reduce-scatter.5.cloned.1.call-start
  7.2 5.2 collective-permute-start
  12.4 0.7 broadcast_compare_fusion
  13.2 2.7 fusion.11
  15.9 0.0 copy-done.2
  15.9 0.0 copy-start.6
  15.9 2.1 fusion.14
  18.0 0.0 copy-done.6
  18.0 0.2 broadcast_select_fusion
  18.2 0.0 copy-done
  18.2 0.0 copy-start.4
  18.2 0.7 fusion.21
  19.0 38.6 %collective-permute-done = bf16[2,256,2048]{2,1,0:T(8,128)(2,1)} collective-permute-done((bf16[2,256,2048]{2,1,0:T(8,128)(2,1)}, bf16[2,256,2048]{2,1,0:T(8,128)(2,1)}, u32[]{:S(2)}, u32[]{:S(2)}) %collective-permute-start) | collective-permute-done | bytes 2097184 | tf_op jit(solution)/shard_map/ppermute | solution.py:12
  57.6 2.3 fusion.9
  59.9 2.4 multiply_convert_fusion.2
  62.4 2.3 fusion.20
  64.6 0.0 reduce-scatter.5.cloned.1.call-update
  64.7 0.0 all-reduce.3.cloned.1.call-start
  64.7 0.0 copy-start.3
  64.7 2.5 convolution_bitcast_fusion.1
  67.2 0.7 convolution_bitcast_fusion.3
  67.9 2.3 convolution_bitcast_fusion
  70.3 0.7 convolution_bitcast_fusion.2
  71.0 1.1 maximum_bitcast_fusion
  72.1 3.8 pad_maximum_fusion
  75.9 13.3 %copy.13 = f32[2,2,2048,256]{3,1,0,2:T(2,128)} copy(f32[2,2,2048,256]{2,3,1,0:T(8,128)} %pad_maximum_fusion) | data formatting | bytes 16777216 | tf_op jit(solution)/shard_map/stack | solution.py:36
  89.3 0.0 all-reduce.3.cloned.1.call-update
  89.3 0.0 reduce-scatter.3.cloned.1.call-start
  89.3 0.1 pad_maximum_fusion.1
  89.4 0.0 copy-start.5
  89.4 2.2 collective-permute-start.1
  91.6 2.9 fusion.1
  94.5 11.8 %collective-permute-done.1 = bf16[2,256,2,256]{3,1,2,0:T(8,128)(2,1)S(1)} collective-permute-done((bf16[2,256,2,256]{3,1,2,0:T(8,128)(2,1)S(1)}, bf16[2,256,2,256]{3,1,2,0:T(8,128)(2,1)S(1)}, u32[]{:S(2)}, u32[]{:S(2)}) %collective-permute-start.1) | collective-permute-done | bytes 524320 | tf_op jit(solution)/shard_map/ppermute | solution.py:12
  106.3 0.0 copy-done.5
  106.3 3.2 bitcast_add_fusion
  109.6 0.0 reduce-scatter.3.cloned.1.call-update
  109.6 0.0 copy-start.1
  109.6 0.6 copy-done.7
  110.2 0.6 convert_reduce_fusion
  111.5 0.6 dynamic-slice
  112.8 72.5 %reduce-scatter.5.cloned.1.call-done = f32[256,64]{0,1:T(8,128)} async-done(((f32[256,2048]{0,1:T(8,128)}), f32[256,64]{0,1:T(8,128)}) %reduce-scatter.5.cloned.1.call-update) | async-done | bytes 65552 | tf_op jit(solution)/shard_map/reduce_scatter | solution.py:87
  185.2 1.5 broadcast_multiply_fusion
  186.7 291.3 %all-reduce.3.cloned.1.call-done = f32[2,2,2048,256]{3,1,0,2:T(2,128)} async-done(((f32[2,2,2048,256]{3,1,0,2:T(2,128)}), f32[2,2,2048,256]{3,1,0,2:T(2,128)}) %all-reduce.3.cloned.1.call-update) | async-done | bytes 8388624
  478.0 1.0 dynamic-slice_multiply_fusion
  479.0 0.8 copy.14
  479.8 98.1 %reduce-scatter.3.cloned.1.call-done = f32[2,256,256]{2,1,0:T(8,128)} async-done(((f32[2,256,2048]{2,1,0:T(8,128)}), f32[2,256,256]{2,1,0:T(8,128)}) %reduce-scatter.3.cloned.1.call-update) | async-done | bytes 524304 | tf_op jit(solution)/shard_map/reduce_scatter | solution.py:83
  577.9 1.8 add_convert_fusion
  (8 shorter events, 0.0 us)
Async XLA Ops:
  7.2 11.1 %copy-start = (bf16[256,2048]{1,0:T(8,128)(2,1)S(1)}, bf16[256,2048]{1,0:T(8,128)(2,1)}, u32[]{:S(2)}) copy-start(bf16[256,2048]{1,0:T(8,128)(2,1)} %param.8) | copy-start | bytes 3145732
  7.2 178.1 %reduce-scatter.5.cloned.1.call-start = ((), (), s32[]{:S(2)}) async-start(), calls=%async_computation.3 | async-start | bytes 2162688 | tf_op jit(solution)/shard_map/reduce_scatter | solution.py:87
  7.2 50.4 %collective-permute-start = (bf16[2,256,2048]{2,1,0:T(8,128)(2,1)}, bf16[2,256,2048]{2,1,0:T(8,128)(2,1)}, u32[]{:S(2)}, u32[]{:S(2)}) collective-permute-start(bf16[2,256,2048]{2,1,0:T(8,128)(2,1)} %param.5), channel_id=1, source_target_pairs={{0,32},{8,40},{16,48},{24,56},{32,64},{40,72},{48,80},{56,88},{64,... | collective-permute-start | bytes 6291464 | tf_op jit(solution)/shard_map/ppermute | solution.py:12
  13.2 2.7 copy-start.2
  15.9 2.1 copy-start.6
  18.2 39.4 %copy-start.4 = (bf16[2,2,2048,256]{3,2,1,0:T(8,128)(2,1)S(1)}, bf16[2,2,2048,256]{3,2,1,0:T(8,128)(2,1)}, u32[]{:S(2)}) copy-start(bf16[2,2,2048,256]{3,2,1,0:T(8,128)(2,1)} %param.7) | copy-start | bytes 12582916
  64.7 413.3 %all-reduce.3.cloned.1.call-start = ((), (), s32[]{:S(2)}) async-start(), calls=%async_computation.4 | async-start | bytes 16777216
  64.7 2.5 copy-start.3
  89.3 488.6 %reduce-scatter.3.cloned.1.call-start = ((), (), s32[]{:S(2)}) async-start(), calls=%async_computation.2 | async-start | bytes 4718592 | tf_op jit(solution)/shard_map/reduce_scatter | solution.py:83
  89.4 16.9 %copy-start.5 = (bf16[2,2,2048,256]{3,2,1,0:T(8,128)(2,1)S(1)}, bf16[2,2,2048,256]{3,2,1,0:T(8,128)(2,1)}, u32[]{:S(2)}) copy-start(bf16[2,2,2048,256]{3,2,1,0:T(8,128)(2,1)} %param.7) | copy-start | bytes 12582916
  89.4 16.9 %collective-permute-start.1 = (bf16[2,256,2,256]{3,1,2,0:T(8,128)(2,1)S(1)}, bf16[2,256,2,256]{3,1,2,0:T(8,128)(2,1)S(1)}, u32[]{:S(2)}, u32[]{:S(2)}) collective-permute-start(bf16[2,256,2,256]{3,1,2,0:T(8,128)(2,1)S(1)} %pad_maximum_fusion.1), channel_id=1, source_target_pairs={{32,0},{40,8},{48,16},{56,24},{64,32},{72,40},{80,48},{88,56},{96,... | collective-permute-start | bytes 1572872 | tf_op jit(solution)/shard_map/ppermute | solution.py:12
  109.6 0.7 copy-start.7
  109.6 2.0 copy-start.8
  109.6 470.1 %copy-start.1 = (bf16[256,2048]{1,0:T(8,128)(2,1)S(1)}, bf16[256,2048]{1,0:T(8,128)(2,1)}, u32[]{:S(2)}) copy-start(bf16[256,2048]{1,0:T(8,128)(2,1)} %param.8) | copy-start | bytes 3145732
Sparse Core Ops, SparseCore 0:
  64.8 120.4 reduce-scatter.4
  187.9 290.0 all-reduce.2
  480.5 97.3 reduce-scatter.2
where the time goes:
time: 590 us; the launch traced here: 586 us
  waiting for transfers between devices  512 us (87%)
  matrix products  25 us (4%)
  local copies, waits for them, and re-layouts  15.3 us (3%)
  between operations  15.3 us (3%)
  other arithmetic  10.9 us (2%)
  starting transfers between devices  7.47 us (1%)
    unnamed x4, waiting for transfers between devices  291 us
    reduce_scatter x1, waiting for transfers between devices, local(): lax.psum_scatter(partial_value, 'chan', scatter_dimension=2, tiled=True)  98.1 us
    reduce_scatter x1, waiting for transfers between devices, local(): lax.psum_scatter(out_term, 'tm', scatter_dimension=1, tiled=True)  72.5 us
    ppermute x2, waiting for transfers between devices, shifted(): return lax.ppermute(x, axis, pairs)  50.4 us
    another operation x1, local copies, waits for them, and re-layouts, local_grads(): jnp.stack([jnp.stack([contract_rows(present_step, filter_gradient), contr...  13.3 us
  transfers between devices with their start and end apart: 5, of which 5 were waited for; matrix products, arithmetic and copies ran while one was open for 7% of the time, Pallas kernels for 0%

commit v1 on v0

v1 whole, which is shorter than its diff:
```python
import jax
import jax.numpy as jnp
from jax import lax
from jax.sharding import PartitionSpec as P

DILATION_STEPS = 1024


def shifted(x, axis, by):
    peers = lax.axis_size(axis)
    pairs = [(i, i + by) for i in range(peers) if 0 <= i + by < peers]
    return lax.ppermute(x, axis, pairs)


def contract_rows(left, right):
    return lax.dot_general(
        left, right, (((0,), (0,)), ((), ())), preferred_element_type=jnp.float32
    )


def contract_cols(left, right):
    return lax.dot_general(
        left, right, (((1,), (1,)), ((), ())), preferred_element_type=jnp.float32
    )


def local(states, upstream, w_in, w_out, lengths):
    traj, window_extent, width = states.shape
    blocks = w_in.shape[3]
    rows_n = traj * window_extent
    receptive_extent = DILATION_STEPS // window_extent
    rows = states.reshape(rows_n, width)
    w_now = jnp.concatenate([w_in[0, 0], w_in[0, 1]], axis=1)
    w_dil = jnp.concatenate([w_in[1, 0], w_in[1, 1]], axis=1)
    dilated = jnp.dot(rows, w_dil, preferred_element_type=jnp.float32)
    dilated_prior = shifted(
        dilated.reshape(traj, window_extent, 2 * blocks), "tm", receptive_extent
    ).reshape(rows_n, 2 * blocks)
    pre = jnp.dot(rows, w_now, preferred_element_type=jnp.float32) + dilated_prior
    filt = pre[:, :blocks]
    gate = pre[:, blocks:]
    first = lax.axis_index("tm") * window_extent
    positions = first + jnp.arange(window_extent, dtype=jnp.int32)
    valid = positions[None, :] < lengths[:, None]
    grad_rows = jnp.where(valid[:, :, None], upstream, jnp.zeros_like(upstream))
    grad_flat = grad_rows.reshape(rows_n, width)
    tangent = jnp.tanh(filt)
    sigma = jax.nn.sigmoid(gate)
    mixed = (tangent * sigma).astype(jnp.bfloat16)
    dmix = contract_cols(grad_flat, w_out)
    filter_gradient = (dmix * (1.0 - tangent * tangent) * sigma).astype(jnp.bfloat16)
    gate_gradient = (dmix * tangent * sigma * (1.0 - sigma)).astype(jnp.bfloat16)
    branch_grads = jnp.concatenate([filter_gradient, gate_gradient], axis=1)
    later = shifted(
        branch_grads.reshape(traj, window_extent, 2 * blocks), "tm", -receptive_extent
    ).reshape(rows_n, 2 * blocks)
    partial_value = contract_cols(w_now, branch_grads) + contract_cols(w_dil, later)
    summed = lax.psum_scatter(partial_value, "chan", scatter_dimension=0, tiled=True)
    share = width // lax.axis_size("chan")
    own_rows = lax.dynamic_slice_in_dim(grad_rows, lax.axis_index("chan") * share, share, 2)
    summed = summed.reshape(share, traj, window_extent).transpose(1, 2, 0)
    grad_states = (own_rows.astype(jnp.float32) + summed).astype(jnp.bfloat16)
    weight_terms = jnp.concatenate(
        [
            contract_rows(rows, branch_grads),
            contract_rows(rows, later),
            contract_rows(grad_flat, mixed),
        ],
        axis=1,
    )
    reduced = lax.psum_scatter(weight_terms, "tm", scatter_dimension=0, tiled=True)
    scale = lax.rsqrt(jnp.sum(lengths.astype(jnp.float32)))
    part = reduced.shape[0]
    in_summed = reduced[:, : 4 * blocks].reshape(part, 2, 2, blocks).transpose(1, 2, 0, 3)
    out_summed = reduced[:, 4 * blocks :].T
    return (grad_states, in_summed * scale, out_summed * scale)


def solution(mesh):
    placed = (
        P(None, "tm", None),
        P(None, "tm", None),
        P(None, None, None, "chan"),
        P("chan", None),
        P(),
    )
    return jax.shard_map(
        local,
        mesh=mesh,
        in_specs=placed,
        out_specs=(P(None, "tm", "chan"), P(None, None, "tm", "chan"), P("chan", "tm")),
        check_vma=False,
    )
```

time: 590 us -> 346 us (0.59)
  waiting for transfers between devices: 512 us -> 263 us
  local copies, waits for them, and re-layouts: 15.3 us -> 27.5 us
    unnamed x4 -> x3, waiting for transfers between devices: 291 us -> 163 us
    reduce_scatter x2 -> x1, waiting for transfers between devices: 171 us -> 69 us  [local(): lax.psum_scatter(partial_value, 'chan', scatter_dimension=0, tiled=True)]
    ppermute x2, waiting for transfers between devices: 50.4 us -> 31 us  [shifted(): return lax.ppermute(x, axis, pairs)]
    unnamed x20 -> x31, local copies, waits for them, and re-layouts: 1.99 us -> 16.1 us
    another operation x1 -> x0, local copies, waits for them, and re-layouts: 13.3 us -> none  [local_grads(): jnp.stack([jnp.stack([contract_rows(present_step, filter_gradient), contr...]
    dot_general x7 -> x5, matrix products: 16.4 us -> 15.3 us  [the longest x3 10.1 us: contract_cols(): lax.dot_general(left, right, (((1,), (1,)), ((), ())), preferred_element_...]
  transfers between devices with their start and end apart: 5 -> 4, of which waited for: 5 -> 4; matrix products, arithmetic and copies ran while one was open for 7% -> 9% of each run, Pallas kernels for 0% -> 0%
where the time goes in v1:
time: 346 us; the launch traced here: 342 us
  waiting for transfers between devices  263 us (76%)
  local copies, waits for them, and re-layouts  27.5 us (8%)
  matrix products  21.3 us (6%)
  between operations  15 us (4%)
  other arithmetic  7.5 us (2%)
  starting transfers between devices  7.16 us (2%)
    unnamed x3, waiting for transfers between devices  163 us
    reduce_scatter x1, waiting for transfers between devices, local(): lax.psum_scatter(partial_value, 'chan', scatter_dimension=0, tiled=True)  69 us
    ppermute x2, waiting for transfers between devices, shifted(): return lax.ppermute(x, axis, pairs)  31 us
    unnamed x31, local copies, waits for them, and re-layouts  16.1 us
    dot_general x3, matrix products, contract_cols(): lax.dot_general(left, right, (((1,), (1,)), ((), ())), preferred_element_...  10.1 us
    ppermute x2, starting transfers between devices, shifted(): return lax.ppermute(x, axis, pairs)  7.08 us
  transfers between devices with their start and end apart: 4, of which 4 were waited for; matrix products, arithmetic and copies ran while one was open for 9% of the time, Pallas kernels for 0%

profile of v1, /device:TPU:98, one launch (start us, length us, event | category | flops | bytes accessed | tf_op | source)
XLA Modules:
  0.0 341.8 jit_solution(3470800208933979490)
XLA Ops:
  7.2 0.0 copy-start
  7.2 0.0 reduce-scatter.5.cloned.1.call-start
  7.2 3.9 %slice_bitcast_fusion.1 = (bf16[2048,256]{1,0:T(8,128)(2,1)S(1)}, bf16[2048,256]{1,0:T(8,128)(2,1)}, bf16[2048,256]{1,0:T(8,128)(2,1)}, bf16[2048,256]{1,0:T(8,128)(2,1)S(1)}) fusion(bf16[2,2,2048,256]{3,2,1,0:T(8,128)(2,1)} %param.7), kind=kLoop, calls=%fused_computation.11 | loop fusion | bytes 8388608 | tf_op jit(solution)/shard_map/squeeze | solution.py:34
  11.1 0.0 copy-done
  11.1 2.2 fusion
  13.4 0.0 copy-done.2
  13.4 2.3 copy.19
  15.7 5.0 %collective-permute-start = (f32[2,256,512]{1,0,2:T(2,128)}, f32[2,256,512]{1,0,2:T(2,128)}, u32[]{:S(2)}, u32[]{:S(2)}) collective-permute-start(f32[2,256,512]{1,0,2:T(2,128)} %copy.19), channel_id=1, source_target_pairs={{0,32},{8,40},{16,48},{24,56},{32,64},{40,72},{48,80},{56,88},{64,... | collective-permute-start | bytes 3145736 | tf_op jit(solution)/shard_map/ppermute | solution.py:12
  20.7 0.0 copy-done.11
  20.7 0.1 broadcast_compare_fusion
  20.8 3.0 convolution_bitcast_fusion.2
  23.8 0.0 copy-done.4
  23.8 0.2 broadcast_select_fusion
  24.0 19.4 %collective-permute-done = f32[2,256,512]{1,0,2:T(2,128)} collective-permute-done((f32[2,256,512]{1,0,2:T(2,128)}, f32[2,256,512]{1,0,2:T(2,128)}, u32[]{:S(2)}, u32[]{:S(2)}) %collective-permute-start) | collective-permute-done | bytes 1048608 | tf_op jit(solution)/shard_map/ppermute | solution.py:12
  43.4 1.3 copy.31
  44.7 0.0 copy-start.12
  44.7 0.2 add.32
  44.9 1.2 copy-done.12
  46.1 0.9 multiply_convert_fusion.2
  47.0 0.0 copy-start.9
  47.0 0.0 copy-start.7
  47.0 0.0 copy-start.8
  47.1 2.1 collective-permute-start.1
  49.2 3.2 fusion.1
  52.5 0.0 copy-done.9
  52.5 11.6 %collective-permute-done.1 = bf16[2,256,512]{1,2,0:T(8,128)(2,1)} collective-permute-done((bf16[2,256,512]{1,2,0:T(8,128)(2,1)S(1)}, bf16[2,256,512]{1,2,0:T(8,128)(2,1)}, u32[]{:S(2)}, u32[]{:S(2)}) %collective-permute-start.1) | collective-permute-done | bytes 524320 | tf_op jit(solution)/shard_map/ppermute | solution.py:12
  64.0 2.1 copy.21
  66.1 5.9 %convolution_add_fusion = f32[2048,512]{1,0:T(8,128)} fusion(f32[2048,512]{1,0:T(8,128)} %fusion.1, bf16[512,512]{1,0:T(8,128)(2,1)} %bitcast.56, bf16[2048,256]{1,0:T(8,128)(2,1)} %copy-done.2, bf16[2048,256]{1,0:T(8,128)(2,1)S(1)} %get-tuple-element.12), kind=kOutput, calls=%fused_computation.3 | convolution fusion | flops 1078984704 | bytes 11010048 | tf_op jit(solution)/shard_map/dot_general | solution.py:22
  72.1 0.0 reduce-scatter.5.cloned.1.call-update
  72.1 0.0 reduce-scatter.7.cloned.1.call-start
  72.1 1.1 copy-done.6
  73.3 2.4 fusion.5
  75.7 1.3 convolution_bitcast_fusion.1
  77.0 2.3 convolution_bitcast_fusion
  79.3 4.5 %pad_maximum_fusion = f32[2048,1280]{0,1:T(8,128)} fusion(f32[2048,256]{0,1:T(8,128)S(1)} %fusion.5, f32[2048,512]{0,1:T(8,128)S(1)} %convolution_bitcast_fusion, f32[2048,512]{0,1:T(8,128)S(1)} %convolution_bitcast_fusion.1), kind=kLoop, calls=%fused_computation | loop fusion | flops 5242880 | bytes 20971520 | tf_op jit(solution)/shard_map/concatenate | solution.py:63
  83.8 11.4 %copy.26 = f32[2048,1280]{1,0:T(8,128)} copy(f32[2048,1280]{0,1:T(8,128)} %pad_maximum_fusion) | data formatting | bytes 20971520
  95.2 0.0 reduce-scatter.7.cloned.1.call-update
  95.2 0.6 convert_reduce_fusion
  96.5 69.0 %reduce-scatter.5.cloned.1.call-done = f32[256,512]{1,0:T(8,128)} async-done(((f32[2048,512]{1,0:T(8,128)}), f32[256,512]{1,0:T(8,128)}) %reduce-scatter.5.cloned.1.call-update) | async-done | bytes 524304 | tf_op jit(solution)/shard_map/reduce_scatter | solution.py:58
  165.5 1.2 copy.25
  166.8 0.0 copy-start.1
  166.8 1.9 add_convert_fusion
  168.6 163.3 %reduce-scatter.7.cloned.1.call-done = f32[64,1280]{1,0:T(8,128)} async-done(((f32[2048,1280]{1,0:T(8,128)}), f32[64,1280]{1,0:T(8,128)}) %reduce-scatter.7.cloned.1.call-update) | async-done | bytes 327696
  332.0 1.0 slice.34
  333.0 0.2 copy.28
  333.2 0.9 copy.23
  334.1 0.1 copy.29
  334.2 0.7 copy.24
  (20 shorter events, 0.2 us)
Async XLA Ops:
  7.2 4.0 %copy-start = (bf16[2,256,2048]{2,1,0:T(8,128)(2,1)S(1)}, bf16[2,256,2048]{2,1,0:T(8,128)(2,1)}, u32[]{:S(2)}) copy-start(bf16[2,256,2048]{2,1,0:T(8,128)(2,1)} %param.5) | copy-start | bytes 6291460
  7.2 158.3 %reduce-scatter.5.cloned.1.call-start = ((), (), s32[]{:S(2)}) async-start(), calls=%async_computation.2 | async-start | bytes 4718592 | tf_op jit(solution)/shard_map/reduce_scatter | solution.py:58
  11.1 2.2 copy-start.2
  13.4 7.3 %copy-start.11 = (s32[2]{0:T(128)S(1)}, s32[2]{0:T(128)}, u32[]{:S(2)}) copy-start(s32[2]{0:T(128)} %param.9) | copy-start | bytes 28
  15.7 27.7 %collective-permute-start = (f32[2,256,512]{1,0,2:T(2,128)}, f32[2,256,512]{1,0,2:T(2,128)}, u32[]{:S(2)}, u32[]{:S(2)}) collective-permute-start(f32[2,256,512]{1,0,2:T(2,128)} %copy.19), channel_id=1, source_target_pairs={{0,32},{8,40},{16,48},{24,56},{32,64},{40,72},{48,80},{56,88},{64,... | collective-permute-start | bytes 3145736 | tf_op jit(solution)/shard_map/ppermute | solution.py:12
  20.8 3.0 copy-start.4
  24.0 20.9 %copy-start.3 = (bf16[2,256,2048]{2,1,0:T(8,128)(2,1)}, bf16[2,256,2048]{2,1,0:T(8,128)(2,1)S(1)}, u32[]{:S(2)}) copy-start(bf16[2,256,2048]{2,1,0:T(8,128)(2,1)S(1)} %broadcast_select_fusion) | copy-start | bytes 6291460
  44.7 1.4 copy-start.12
  44.9 2.1 copy-start.5
  47.0 5.4 %copy-start.9 = (bf16[512,256]{0,1:T(8,128)(2,1)}, bf16[512,256]{0,1:T(8,128)(2,1)S(1)}, u32[]{:S(2)}) copy-start(bf16[512,256]{0,1:T(8,128)(2,1)S(1)} %get-tuple-element.17) | copy-start | bytes 786436
  47.0 2.2 copy-start.7
  47.0 2.2 copy-start.8
  47.1 16.9 %collective-permute-start.1 = (bf16[2,256,512]{1,2,0:T(8,128)(2,1)S(1)}, bf16[2,256,512]{1,2,0:T(8,128)(2,1)}, u32[]{:S(2)}, u32[]{:S(2)}) collective-permute-start(bf16[2,256,512]{1,2,0:T(8,128)(2,1)S(1)} %bitcast.58), channel_id=1, source_target_pairs={{32,0},{40,8},{48,16},{56,24},{64,32},{72,40},{80,48},{88,56},{96,... | collective-permute-start | bytes 1572872 | tf_op jit(solution)/shard_map/ppermute | solution.py:12
  72.1 1.2 copy-start.6
  72.1 259.9 %reduce-scatter.7.cloned.1.call-start = ((), (), s32[]{:S(2)}) async-start(), calls=%async_computation.3 | async-start | bytes 10813440
  73.3 2.4 copy-start.10
  166.8 168.2 %copy-start.1 = (bf16[2,256,2048]{2,1,0:T(8,128)(2,1)S(1)}, bf16[2,256,2048]{2,1,0:T(8,128)(2,1)}, u32[]{:S(2)}) copy-start(bf16[2,256,2048]{2,1,0:T(8,128)(2,1)} %param.5) | copy-start | bytes 6291460
  332.0 2.1 slice-start
Sparse Core Ops, SparseCore 0:
  72.2 93.2 reduce-scatter.4
  170.0 161.9 reduce-scatter.6

commit v2 on v1

--- a/solution.py
+++ b/solution.py
@@ -6,8 +6,11 @@
 DILATION_STEPS = 1024
 
 
+TIME = ("outer", "core")
+
+
 def shifted(x, axis, by):
-    peers = lax.axis_size(axis)
+    peers = lax.axis_size(axis[0]) * lax.axis_size(axis[1])
     pairs = [(i, i + by) for i in range(peers) if 0 <= i + by < peers]
     return lax.ppermute(x, axis, pairs)
 
@@ -34,12 +37,12 @@
     w_dil = jnp.concatenate([w_in[1, 0], w_in[1, 1]], axis=1)
     dilated = jnp.dot(rows, w_dil, preferred_element_type=jnp.float32)
     dilated_prior = shifted(
-        dilated.reshape(traj, window_extent, 2 * blocks), "tm", receptive_extent
+        dilated.reshape(traj, window_extent, 2 * blocks), TIME, receptive_extent
     ).reshape(rows_n, 2 * blocks)
     pre = jnp.dot(rows, w_now, preferred_element_type=jnp.float32) + dilated_prior
     filt = pre[:, :blocks]
     gate = pre[:, blocks:]
-    first = lax.axis_index("tm") * window_extent
+    first = lax.axis_index(TIME) * window_extent
     positions = first + jnp.arange(window_extent, dtype=jnp.int32)
     valid = positions[None, :] < lengths[:, None]
     grad_rows = jnp.where(valid[:, :, None], upstream, jnp.zeros_like(upstream))
@@ -52,10 +55,12 @@
     gate_gradient = (dmix * tangent * sigma * (1.0 - sigma)).astype(jnp.bfloat16)
     branch_grads = jnp.concatenate([filter_gradient, gate_gradient], axis=1)
     later = shifted(
-        branch_grads.reshape(traj, window_extent, 2 * blocks), "tm", -receptive_extent
+        branch_grads.reshape(traj, window_extent, 2 * blocks), TIME, -receptive_extent
     ).reshape(rows_n, 2 * blocks)
     partial_value = contract_cols(w_now, branch_grads) + contract_cols(w_dil, later)
-    summed = lax.psum_scatter(partial_value, "chan", scatter_dimension=0, tiled=True)
+    summed = lax.psum_scatter(
+        partial_value.astype(jnp.bfloat16), "chan", scatter_dimension=0, tiled=True
+    ).astype(jnp.float32)
     share = width // lax.axis_size("chan")
     own_rows = lax.dynamic_slice_in_dim(grad_rows, lax.axis_index("chan") * share, share, 2)
     summed = summed.reshape(share, traj, window_extent).transpose(1, 2, 0)
@@ -68,7 +73,14 @@
         ],
         axis=1,
     )
-    reduced = lax.psum_scatter(weight_terms, "tm", scatter_dimension=0, tiled=True)
+    pair = lax.axis_index("core")
+    halves = weight_terms.reshape(lax.axis_size("outer"), 2, -1, weight_terms.shape[1])
+    keep = lax.dynamic_index_in_dim(halves, pair, axis=1, keepdims=False)
+    give = lax.dynamic_index_in_dim(halves, 1 - pair, axis=1, keepdims=False)
+    paired = keep + lax.ppermute(give, "core", [(0, 1), (1, 0)])
+    reduced = lax.psum_scatter(
+        paired.reshape(-1, weight_terms.shape[1]), "outer", scatter_dimension=0, tiled=True
+    )
     scale = lax.rsqrt(jnp.sum(lengths.astype(jnp.float32)))
     part = reduced.shape[0]
     in_summed = reduced[:, : 4 * blocks].reshape(part, 2, 2, blocks).transpose(1, 2, 0, 3)
@@ -77,9 +89,13 @@
 
 
 def solution(mesh):
+    tm, chan = mesh.shape["tm"], mesh.shape["chan"]
+    mesh = jax.sharding.Mesh(
+        mesh.devices.reshape(tm // 2, 2, chan), ("outer", "core", "chan")
+    )
     placed = (
-        P(None, "tm", None),
-        P(None, "tm", None),
+        P(None, TIME, None),
+        P(None, TIME, None),
         P(None, None, None, "chan"),
         P("chan", None),
         P(),
@@ -88,6 +104,6 @@
         local,
         mesh=mesh,
         in_specs=placed,
-        out_specs=(P(None, "tm", "chan"), P(None, None, "tm", "chan"), P("chan", "tm")),
+        out_specs=(P(None, TIME, "chan"), P(None, None, TIME, "chan"), P("chan", TIME)),
         check_vma=False,
     )

time: 346 us -> 385 us (1.11)
  waiting for transfers between devices: 263 us -> 296 us
  other arithmetic: 7.5 us -> 16.8 us
    reduce_scatter x1 -> x2, waiting for transfers between devices: 69 us -> 263 us  [the longest x1 218 us: local(): lax.psum_scatter(paired.reshape(-1, weight_terms.shape[1]), 'outer', scat...]
    unnamed x3 -> x2, waiting for transfers between devices: 163 us -> 0.03 us
    unnamed x31 -> x29, local copies, waits for them, and re-layouts: 16.1 us -> 3.17 us
    concatenate x0 -> x1, local copies, waits for them, and re-layouts: none -> 11.3 us  [local(): jnp.concatenate([contract_rows(rows, branch_grads), contract_rows(rows, l...]
    add x0 -> x1, other arithmetic: none -> 7.08 us  [local(): paired = keep + lax.ppermute(give, 'core', [(0, 1), (1, 0)])]
    squeeze x0 -> x1, local copies, waits for them, and re-layouts: none -> 5.43 us  [local(): give = lax.dynamic_index_in_dim(halves, 1 - pair, axis=1, keepdims=False)]
  transfers between devices with their start and end apart: 4 -> 5, of which waited for: 4 -> 5; matrix products, arithmetic and copies ran while one was open for 9% -> 6% of each run, Pallas kernels for 0% -> 0%
where the time goes in v2:
time: 385 us; the launch traced here: 381 us
  waiting for transfers between devices  296 us (77%)
  local copies, waits for them, and re-layouts  28.4 us (7%)
  matrix products  17.5 us (5%)
  other arithmetic  16.8 us (4%)
  between operations  15 us (4%)
  starting transfers between devices  7.03 us (2%)
    reduce_scatter x1, waiting for transfers between devices, local(): lax.psum_scatter(paired.reshape(-1, weight_terms.shape[1]), 'outer', scat...  218 us
    reduce_scatter x1, waiting for transfers between devices, local(): lax.psum_scatter(partial_value.astype(jnp.bfloat16), 'chan', scatter_dime...  45 us
    ppermute x2, waiting for transfers between devices, shifted(): return lax.ppermute(x, axis, pairs)  32 us
    concatenate x1, local copies, waits for them, and re-layouts, local(): jnp.concatenate([contract_rows(rows, branch_grads), contract_rows(rows, l...  11.3 us
    dot_general x3, matrix products, contract_cols(): lax.dot_general(left, right, (((1,), (1,)), ((), ())), preferred_element_...  8.94 us
  transfers between devices with their start and end apart: 5, of which 5 were waited for; matrix products, arithmetic and copies ran while one was open for 6% of the time, Pallas kernels for 0%

profile of v2, /device:TPU:98, one launch (start us, length us, event | category | flops | bytes accessed | tf_op | source)
XLA Modules:
  0.0 380.9 jit_solution(6323677097728439232)
XLA Ops:
  7.2 0.0 copy-start
  7.2 0.0 reduce-scatter.3.cloned.1.call-start
  7.2 3.9 %slice_bitcast_fusion.1 = (bf16[2048,256]{1,0:T(8,128)(2,1)S(1)}, bf16[2048,256]{1,0:T(8,128)(2,1)}, bf16[2048,256]{1,0:T(8,128)(2,1)}, bf16[2048,256]{1,0:T(8,128)(2,1)S(1)}) fusion(bf16[2,2,2048,256]{3,2,1,0:T(8,128)(2,1)} %param.7), kind=kLoop, calls=%fused_computation.13 | loop fusion | bytes 8388608 | tf_op jit(solution)/shard_map/squeeze | solution.py:37
  11.2 0.0 copy-done
  11.2 2.3 fusion
  13.5 2.3 copy.12
  15.7 5.0 %collective-permute-start = (f32[2,256,512]{1,0,2:T(2,128)}, f32[2,256,512]{1,0,2:T(2,128)}, u32[]{:S(2)}, u32[]{:S(2)}) collective-permute-start(f32[2,256,512]{1,0,2:T(2,128)} %copy.12), channel_id=1, source_target_pairs={{0,32},{8,40},{16,48},{24,56},{32,64},{40,72},{48,80},{56,88},{64,... | collective-permute-start | bytes 3145736 | tf_op jit(solution)/shard_map/ppermute | solution.py:15
  20.8 0.1 broadcast_compare_fusion
  20.9 3.0 convolution_bitcast_fusion.2
  23.9 0.2 broadcast_select_fusion
  24.1 19.4 %collective-permute-done = f32[2,256,512]{1,0,2:T(2,128)} collective-permute-done((f32[2,256,512]{1,0,2:T(2,128)}, f32[2,256,512]{1,0,2:T(2,128)}, u32[]{:S(2)}, u32[]{:S(2)}) %collective-permute-start) | collective-permute-done | bytes 1048608 | tf_op jit(solution)/shard_map/ppermute | solution.py:15
  43.5 1.3 copy.20
  44.8 0.0 copy-start.13
  44.8 0.2 add.47
  45.0 1.0 copy-done.13
  46.0 0.9 multiply_convert_fusion.2
  46.9 0.0 copy-start.10
  47.0 1.9 collective-permute-start.1
  48.9 0.0 copy-done.4
  48.9 0.8 fusion.5
  49.7 0.0 copy-done.10
  49.8 1.3 convolution_bitcast_fusion.1
  51.0 12.6 %collective-permute-done.1 = bf16[2,256,512]{1,2,0:T(8,128)(2,1)S(1)} collective-permute-done((bf16[2,256,512]{1,2,0:T(8,128)(2,1)S(1)}, bf16[2,256,512]{1,2,0:T(8,128)(2,1)S(1)}, u32[]{:S(2)}, u32[]{:S(2)}) %collective-permute-start.1) | collective-permute-done | bytes 524320 | tf_op jit(solution)/shard_map/ppermute | solution.py:15
  63.7 0.8 copy-done.6
  64.5 1.3 convolution_bitcast_fusion
  65.8 4.4 %pad_maximum_fusion = f32[2048,1280]{0,1:T(8,128)} fusion(f32[2048,256]{0,1:T(8,128)S(1)} %fusion.5, f32[2048,512]{0,1:T(8,128)S(1)} %convolution_bitcast_fusion, f32[2048,512]{0,1:T(8,128)S(1)} %convolution_bitcast_fusion.1), kind=kLoop, calls=%fused_computation | loop fusion | flops 5242880 | bytes 20971520 | tf_op jit(solution)/shard_map/concatenate | solution.py:68
  70.2 11.3 %copy.16 = f32[2048,1280]{1,0:T(8,128)} copy(f32[2048,1280]{0,1:T(8,128)} %pad_maximum_fusion) | data formatting | bytes 20971520 | tf_op jit(solution)/shard_map/concatenate | solution.py:68
  81.5 5.4 %dynamic-slice_bitcast_fusion = f32[16,64,1280]{2,1,0:T(8,128)} fusion(f32[16,2,64,1280]{3,2,1,0:T(8,128)} %bitcast.56, s32[]{:T(128)S(6)} %select_n.17), kind=kLoop, calls=%fused_computation.2 | loop fusion | bytes 10485764 | tf_op jit(solution)/shard_map/jit(dynamic_index_in_dim)/squeeze | solution.py:79
  86.9 0.0 collective-permute-start.2
  87.0 3.2 fusion.1
  90.2 0.2 copy.14
  90.4 4.8 %add_convert_fusion = bf16[2048,512]{1,0:T(8,128)(2,1)} fusion(f32[2048,512]{1,0:T(8,128)} %fusion.1, bf16[512,512]{1,0:T(8,128)(2,1)S(1)} %bitcast.62, bf16[2048,256]{1,0:T(8,128)(2,1)S(1)} %copy-done.3, bf16[2048,256]{1,0:T(8,128)(2,1)S(1)} %get-tuple-element.3), kind=kOutput, calls=%fused_computation.3 | convolution fusion | flops 1080033280 | bytes 8912896 | tf_op jit(solution)/shard_map/dot_general | solution.py:25
  95.2 0.0 reduce-scatter.3.cloned.1.call-update
  95.3 0.0 reduce-scatter.5.cloned.1.call-start
  95.3 0.6 collective-permute-done.2
  95.9 7.1 %bitcast_add_fusion = f32[16,64,1280]{2,1,0:T(8,128)} fusion(f32[16,64,1280]{2,1,0:T(8,128)} %collective-permute-done.2, f32[16,2,64,1280]{3,2,1,0:T(8,128)} %bitcast.57, s32[]{:T(128)S(6)} %select_n.16), kind=kLoop, calls=%fused_computation.1 | loop fusion | flops 1310720 | bytes 15728644 | tf_op jit(solution)/shard_map/add | solution.py:80
  103.0 0.0 reduce-scatter.5.cloned.1.call-update
  103.0 0.0 copy-start.1
  103.1 0.6 convert_reduce_fusion
  104.4 45.0 %reduce-scatter.3.cloned.1.call-done = bf16[256,512]{1,0:T(8,128)(2,1)} async-done(((bf16[2048,512]{1,0:T(8,128)(2,1)}), bf16[256,512]{1,0:T(8,128)(2,1)}) %reduce-scatter.3.cloned.1.call-update) | async-done | bytes 262160 | tf_op jit(solution)/shard_map/reduce_scatter | solution.py:61
  149.4 1.1 copy.18
  150.5 1.7 add_convert_fusion.1
  152.2 218.5 %reduce-scatter.5.cloned.1.call-done = f32[64,1280]{1,0:T(8,128)} async-done(((f32[1024,1280]{1,0:T(8,128)}), f32[64,1280]{1,0:T(8,128)}) %reduce-scatter.5.cloned.1.call-update) | async-done | bytes 327696 | tf_op jit(solution)/shard_map/reduce_scatter | solution.py:81
  370.6 1.0 slice_multiply_fusion
  371.6 0.2 mul.63
  371.8 0.8 copy.24
  372.6 1.5 fusion.6
  374.0 0.0 copy-done.1
  (21 shorter events, 0.1 us)
Async XLA Ops:
  7.2 4.0 %copy-start = (bf16[2,256,2048]{2,1,0:T(8,128)(2,1)S(1)}, bf16[2,256,2048]{2,1,0:T(8,128)(2,1)}, u32[]{:S(2)}) copy-start(bf16[2,256,2048]{2,1,0:T(8,128)(2,1)} %param.5) | copy-start | bytes 6291460
  7.2 142.2 %reduce-scatter.3.cloned.1.call-start = ((), (), s32[]{:S(2)}) async-start(), calls=%async_computation.2 | async-start | bytes 2359296 | tf_op jit(solution)/shard_map/reduce_scatter | solution.py:61
  11.2 2.3 copy-start.2
  13.5 7.3 %copy-start.12 = (s32[2]{0:T(128)S(1)}, s32[2]{0:T(128)}, u32[]{:S(2)}) copy-start(s32[2]{0:T(128)} %param.9) | copy-start | bytes 28
  15.7 27.7 %collective-permute-start = (f32[2,256,512]{1,0,2:T(2,128)}, f32[2,256,512]{1,0,2:T(2,128)}, u32[]{:S(2)}, u32[]{:S(2)}) collective-permute-start(f32[2,256,512]{1,0,2:T(2,128)} %copy.12), channel_id=1, source_target_pairs={{0,32},{8,40},{16,48},{24,56},{32,64},{40,72},{48,80},{56,88},{64,... | collective-permute-start | bytes 3145736 | tf_op jit(solution)/shard_map/ppermute | solution.py:15
  20.9 3.0 copy-start.5
  24.1 24.9 %copy-start.4 = (bf16[2,256,2048]{2,1,0:T(8,128)(2,1)}, bf16[2,256,2048]{2,1,0:T(8,128)(2,1)S(1)}, u32[]{:S(2)}) copy-start(bf16[2,256,2048]{2,1,0:T(8,128)(2,1)S(1)} %broadcast_select_fusion) | copy-start | bytes 6291460
  44.8 1.2 copy-start.13
  46.9 2.8 copy-start.10
  47.0 16.7 %collective-permute-start.1 = (bf16[2,256,512]{1,2,0:T(8,128)(2,1)S(1)}, bf16[2,256,512]{1,2,0:T(8,128)(2,1)S(1)}, u32[]{:S(2)}, u32[]{:S(2)}) collective-permute-start(bf16[2,256,512]{1,2,0:T(8,128)(2,1)S(1)} %bitcast.66), channel_id=1, source_target_pairs={{32,0},{40,8},{48,16},{56,24},{64,32},{72,40},{80,48},{88,56},{96,... | collective-permute-start | bytes 1572872 | tf_op jit(solution)/shard_map/ppermute | solution.py:15
  63.7 0.8 copy-start.6
  81.5 5.5 %copy-start.8 = (bf16[2048,256]{1,0:T(8,128)(2,1)S(1)}, bf16[2048,256]{1,0:T(8,128)(2,1)}, u32[]{:S(2)}) copy-start(bf16[2048,256]{1,0:T(8,128)(2,1)} %get-tuple-element.4) | copy-start | bytes 3145732
  81.5 5.5 %copy-start.9 = (bf16[2048,256]{1,0:T(8,128)(2,1)S(1)}, bf16[2048,256]{1,0:T(8,128)(2,1)}, u32[]{:S(2)}) copy-start(bf16[2048,256]{1,0:T(8,128)(2,1)} %get-tuple-element.5) | copy-start | bytes 3145732
  81.5 5.5 %copy-start.11 = (bf16[512,256]{0,1:T(8,128)(2,1)S(1)}, bf16[512,256]{0,1:T(8,128)(2,1)}, u32[]{:S(2)}) copy-start(bf16[512,256]{0,1:T(8,128)(2,1)} %copy-done.10) | copy-start | bytes 786436
  86.9 3.3 copy-start.7
  86.9 3.5 copy-start.3
  86.9 9.0 %collective-permute-start.2 = (f32[16,64,1280]{2,1,0:T(8,128)}, f32[16,64,1280]{2,1,0:T(8,128)}, u32[]{:S(2)}, u32[]{:S(2)}) collective-permute-start(f32[16,64,1280]{2,1,0:T(8,128)} %dynamic-slice_bitcast_fusion), channel_id=1, source_target_pairs={{0,8},{8,0},{1,9},{9,1},{2,10},{10,2},{3,11},{11,3},{4,12},{12,4},... | collective-permute-start | bytes 15728648 | tf_op jit(solution)/shard_map/ppermute | solution.py:80
  95.3 275.4 %reduce-scatter.5.cloned.1.call-start = ((), (), s32[]{:S(2)}) async-start(), calls=%async_computation.3 | async-start | bytes 5570560 | tf_op jit(solution)/shard_map/reduce_scatter | solution.py:81
  103.0 271.0 %copy-start.1 = (bf16[2,256,2048]{2,1,0:T(8,128)(2,1)S(1)}, bf16[2,256,2048]{2,1,0:T(8,128)(2,1)}, u32[]{:S(2)}) copy-start(bf16[2,256,2048]{2,1,0:T(8,128)(2,1)} %param.5) | copy-start | bytes 6291460
Sparse Core Ops, SparseCore 0:
  95.4 53.9 reduce-scatter.2
  153.4 217.1 reduce-scatter.4

commit v3 on v1

--- a/solution.py
+++ b/solution.py
@@ -22,6 +22,31 @@
     return lax.dot_general(
         left, right, (((1,), (1,)), ((), ())), preferred_element_type=jnp.float32
     )
+
+
+def ring_reduce_scatter(x):
+    peers = lax.axis_size("ring")
+    at = lax.axis_index("ring")
+    chunks = x.reshape(peers, x.shape[0] // peers, x.shape[1])
+    half = x.shape[1] // 2
+    sums = []
+    for step, cols in ((1, slice(0, half)), (-1, slice(half, None))):
+        own = chunks[:, :, cols]
+        pairs = [(i, (i + step) % peers) for i in range(peers)]
+        acc = lax.dynamic_index_in_dim(own, (at - step) % peers, 0, keepdims=False)
+        for s in range(peers - 1):
+            got = lax.ppermute(acc, "ring", pairs)
+            acc = got + lax.dynamic_index_in_dim(
+                own, (at - step * (s + 2)) % peers, 0, keepdims=False
+            )
+        sums.append(acc)
+    full = jnp.concatenate(sums, axis=1)
+    pairs_n = lax.axis_size("pair")
+    me = lax.axis_index("pair")
+    parts = full.reshape(pairs_n, full.shape[0] // pairs_n, full.shape[1])
+    keep = lax.dynamic_index_in_dim(parts, me, 0, keepdims=False)
+    give = lax.dynamic_index_in_dim(parts, 1 - me, 0, keepdims=False)
+    return keep + lax.ppermute(give, "pair", [(0, 1), (1, 0)])
 
 
 def local(states, upstream, w_in, w_out, lengths):
@@ -55,9 +80,10 @@
         branch_grads.reshape(traj, window_extent, 2 * blocks), "tm", -receptive_extent
     ).reshape(rows_n, 2 * blocks)
     partial_value = contract_cols(w_now, branch_grads) + contract_cols(w_dil, later)
-    summed = lax.psum_scatter(partial_value, "chan", scatter_dimension=0, tiled=True)
-    share = width // lax.axis_size("chan")
-    own_rows = lax.dynamic_slice_in_dim(grad_rows, lax.axis_index("chan") * share, share, 2)
+    summed = ring_reduce_scatter(partial_value)
+    share = width // (lax.axis_size("ring") * lax.axis_size("pair"))
+    chan_index = lax.axis_index("ring") * lax.axis_size("pair") + lax.axis_index("pair")
+    own_rows = lax.dynamic_slice_in_dim(grad_rows, chan_index * share, share, 2)
     summed = summed.reshape(share, traj, window_extent).transpose(1, 2, 0)
     grad_states = (own_rows.astype(jnp.float32) + summed).astype(jnp.bfloat16)
     weight_terms = jnp.concatenate(
@@ -76,18 +102,23 @@
     return (grad_states, in_summed * scale, out_summed * scale)
 
 
+CHAN = ("ring", "pair")
+
+
 def solution(mesh):
+    tm, chan = mesh.shape["tm"], mesh.shape["chan"]
+    mesh = jax.sharding.Mesh(mesh.devices.reshape(tm, chan // 2, 2), ("tm", "ring", "pair"))
     placed = (
         P(None, "tm", None),
         P(None, "tm", None),
-        P(None, None, None, "chan"),
-        P("chan", None),
+        P(None, None, None, CHAN),
+        P(CHAN, None),
         P(),
     )
     return jax.shard_map(
         local,
         mesh=mesh,
         in_specs=placed,
-        out_specs=(P(None, "tm", "chan"), P(None, None, "tm", "chan"), P("chan", "tm")),
+        out_specs=(P(None, "tm", CHAN), P(None, None, "tm", CHAN), P(CHAN, "tm")),
         check_vma=False,
     )

time: 346 us -> 265 us (0.77)
  waiting for transfers between devices: 263 us -> 166 us
  starting transfers between devices: 7.16 us -> 17.9 us
  other arithmetic: 7.5 us -> 16.4 us
    unnamed x3 -> x2, waiting for transfers between devices: 163 us -> 89.8 us
    reduce_scatter x1 -> x0, waiting for transfers between devices: 69 us -> none  [local(): lax.psum_scatter(partial_value, 'chan', scatter_dimension=0, tiled=True)]
    ppermute x0 -> x7, waiting for transfers between devices: none -> 44.2 us  [the longest x6 24 us: ring_reduce_scatter(): got = lax.ppermute(acc, 'ring', pairs)]
    ppermute x0 -> x7, starting transfers between devices: none -> 10.9 us  [the longest x6 10.3 us: ring_reduce_scatter(): got = lax.ppermute(acc, 'ring', pairs)]
    add x0 -> x7, other arithmetic: none -> 8.73 us  [the longest x6 8.64 us: ring_reduce_scatter(): got + lax.dynamic_index_in_dim(own, (at - step * (s + 2)) % peers, 0, kee...]
  transfers between devices with their start and end apart: 4 -> 10, of which waited for: 4 -> 8; matrix products, arithmetic and copies ran while one was open for 9% -> 10% of each run, Pallas kernels for 0% -> 0%
where the time goes in v3:
time: 265 us; the launch traced here: 261 us
  waiting for transfers between devices  166 us (63%)
  local copies, waits for them, and re-layouts  27.6 us (10%)
  starting transfers between devices  17.9 us (7%)
  matrix products  17.9 us (7%)
  other arithmetic  16.4 us (6%)
  between operations  15 us (6%)
    unnamed x2, waiting for transfers between devices  89.8 us
    ppermute x2, waiting for transfers between devices, shifted(): return lax.ppermute(x, axis, pairs)  32 us
    ppermute x6, waiting for transfers between devices, ring_reduce_scatter(): got = lax.ppermute(acc, 'ring', pairs)  24 us
    ppermute x1, waiting for transfers between devices, ring_reduce_scatter(): return keep + lax.ppermute(give, 'pair', [(0, 1), (1, 0)])  20.2 us
    unnamed x31, local copies, waits for them, and re-layouts  17.7 us
    ppermute x6, starting transfers between devices, ring_reduce_scatter(): got = lax.ppermute(acc, 'ring', pairs)  10.3 us
    dot_general x3, matrix products, contract_cols(): lax.dot_general(left, right, (((1,), (1,)), ((), ())), preferred_element_...  9.36 us
    add x6, other arithmetic, ring_reduce_scatter(): got + lax.dynamic_index_in_dim(own, (at - step * (s + 2)) % peers, 0, kee...  8.64 us
  transfers between devices with their start and end apart: 10, of which 8 were waited for; matrix products, arithmetic and copies ran while one was open for 10% of the time, Pallas kernels for 0%

profile of v3, /device:TPU:98, one launch (start us, length us, event | category | flops | bytes accessed | tf_op | source)
XLA Modules:
  0.0 260.8 jit_solution(11416226470334010093)
XLA Ops:
  7.2 4.0 %slice_bitcast_fusion.1 = (bf16[2048,256]{1,0:T(8,128)(2,1)S(1)}, bf16[2048,256]{1,0:T(8,128)(2,1)}, bf16[2048,256]{1,0:T(8,128)(2,1)}, bf16[2048,256]{1,0:T(8,128)(2,1)S(1)}) fusion(bf16[2,2,2048,256]{3,2,1,0:T(8,128)(2,1)} %param.7), kind=kLoop, calls=%fused_computation.12 | loop fusion | bytes 8388608 | tf_op jit(solution)/shard_map/squeeze | solution.py:59
  11.2 2.2 fusion
  13.4 2.3 copy.23
  15.7 5.0 %collective-permute-start = (f32[2,256,512]{1,0,2:T(2,128)}, f32[2,256,512]{1,0,2:T(2,128)}, u32[]{:S(2)}, u32[]{:S(2)}) collective-permute-start(f32[2,256,512]{1,0,2:T(2,128)} %copy.23), channel_id=1, source_target_pairs={{0,32},{8,40},{16,48},{24,56},{32,64},{40,72},{48,80},{56,88},{64,... | collective-permute-start | bytes 3145736 | tf_op jit(solution)/shard_map/ppermute | solution.py:12
  20.8 3.0 %convolution_bitcast_fusion.2 = f32[512,512]{0,1:T(8,128)S(1)} fusion(bf16[512,2048]{1,0:T(8,128)(2,1)S(1)} %bitcast.69, bf16[2048,256]{1,0:T(8,128)(2,1)} %get-tuple-element.18, bf16[2048,256]{1,0:T(8,128)(2,1)} %get-tuple-element.19), kind=kOutput, calls=%fused_computation.7 | convolution fusion | flops 1077936128 | bytes 5242880 | tf_op jit(solution)/shard_map/dot_general | solution.py:64
  24.1 19.4 %collective-permute-done = f32[2,256,512]{1,0,2:T(2,128)} collective-permute-done((f32[2,256,512]{1,0,2:T(2,128)}, f32[2,256,512]{1,0,2:T(2,128)}, u32[]{:S(2)}, u32[]{:S(2)}) %collective-permute-start) | collective-permute-done | bytes 1048608 | tf_op jit(solution)/shard_map/ppermute | solution.py:12
  43.5 1.3 copy.35
  44.8 0.2 add.121
  45.0 1.0 copy-done.12
  46.0 0.9 multiply_convert_fusion.2
  47.0 1.9 collective-permute-start.1
  48.9 0.8 fusion.5
  49.7 1.3 convolution_bitcast_fusion.1
  51.0 12.7 %collective-permute-done.1 = bf16[2,256,512]{1,2,0:T(8,128)(2,1)S(1)} collective-permute-done((bf16[2,256,512]{1,2,0:T(8,128)(2,1)S(1)}, bf16[2,256,512]{1,2,0:T(8,128)(2,1)S(1)}, u32[]{:S(2)}, u32[]{:S(2)}) %collective-permute-start.1) | collective-permute-done | bytes 524320 | tf_op jit(solution)/shard_map/ppermute | solution.py:12
  63.7 0.8 copy-done.7
  64.4 1.3 convolution_bitcast_fusion
  65.7 4.4 %pad_maximum_fusion = f32[2048,1280]{0,1:T(8,128)} fusion(f32[2048,256]{0,1:T(8,128)S(1)} %fusion.5, f32[2048,512]{0,1:T(8,128)S(1)} %convolution_bitcast_fusion, f32[2048,512]{0,1:T(8,128)S(1)} %convolution_bitcast_fusion.1), kind=kLoop, calls=%fused_computation | loop fusion | flops 5242880 | bytes 20971520 | tf_op jit(solution)/shard_map/concatenate | solution.py:89
  70.2 11.3 %copy.30 = f32[2048,1280]{1,0:T(8,128)} copy(f32[2048,1280]{0,1:T(8,128)} %pad_maximum_fusion) | data formatting | bytes 20971520
  81.5 0.9 copy-done.10
  82.5 5.0 %fusion.1 = f32[2048,512]{1,0:T(8,128)} fusion(bf16[2048,256]{1,0:T(8,128)(2,1)} %get-tuple-element.18, bf16[2048,256]{1,0:T(8,128)(2,1)} %get-tuple-element.19, bf16[512,256]{0,1:T(8,128)(2,1)S(1)} %copy-done.10, bf16[512,256]{0,1:T(8,128)(2,1)S(1)} %get-tuple-element.21), kind=kOutput, calls=%fused_computation.9 | convolution fusion | flops 1078984704 | bytes 6815744 | tf_op jit(solution)/shard_map/dot_general | solution.py:22
  87.4 0.2 copy.25
  87.7 3.5 %convolution_add_fusion = f32[2048,512]{1,0:T(8,128)S(1)} fusion(f32[2048,512]{1,0:T(8,128)} %fusion.1, bf16[512,512]{1,0:T(8,128)(2,1)S(1)} %bitcast.81, bf16[2048,256]{1,0:T(8,128)(2,1)S(1)} %copy-done.4, bf16[2048,256]{1,0:T(8,128)(2,1)S(1)} %get-tuple-element.17), kind=kOutput, calls=%fused_computation.3 | convolution fusion | flops 1078984704 | bytes 11010048 | tf_op jit(solution)/shard_map/dot_general | solution.py:22
  91.1 0.4 fusion.11
  91.6 1.3 copy-done.2
  93.0 1.7 collective-permute-start.2
  94.6 0.8 dynamic-slice_bitcast_fusion.1
  95.5 1.7 collective-permute-start.5
  97.1 9.4 %collective-permute-done.2 = f32[512,256]{1,0:T(8,128)S(1)} collective-permute-done((f32[512,256]{1,0:T(8,128)S(1)}, f32[512,256]{1,0:T(8,128)S(1)}, u32[]{:S(2)}, u32[]{:S(2)}) %collective-permute-start.2) | collective-permute-done | bytes 524320 | tf_op jit(solution)/shard_map/ppermute | solution.py:38
  106.6 1.2 bitcast_add_fusion.6
  107.7 0.4 collective-permute-start.3
  108.1 2.0 bitcast_add_fusion.3
  110.1 2.9 %collective-permute-start.6 = (f32[512,256]{1,0:T(8,128)}, f32[512,256]{1,0:T(8,128)}, u32[]{:S(2)}, u32[]{:S(2)}) collective-permute-start(f32[512,256]{1,0:T(8,128)} %bitcast_add_fusion.3), channel_id=1, source_target_pairs={{0,6},{2,0},{4,2},{6,4},{1,7},{3,1},{5,3},{7,5},{8,14},{10,8},{12,... | collective-permute-start | bytes 1572872 | tf_op jit(solution)/shard_map/ppermute | solution.py:38
  113.0 7.5 %collective-permute-done.3 = f32[512,256]{1,0:T(8,128)} collective-permute-done((f32[512,256]{1,0:T(8,128)S(1)}, f32[512,256]{1,0:T(8,128)}, u32[]{:S(2)}, u32[]{:S(2)}) %collective-permute-start.3) | collective-permute-done | bytes 524320 | tf_op jit(solution)/shard_map/ppermute | solution.py:38
  120.5 1.3 bitcast_add_fusion.5
  121.9 2.0 bitcast_add_fusion.2
  123.9 3.7 %collective-permute-start.7 = (f32[512,256]{1,0:T(8,128)}, f32[512,256]{1,0:T(8,128)}, u32[]{:S(2)}, u32[]{:S(2)}) collective-permute-start(f32[512,256]{1,0:T(8,128)} %bitcast_add_fusion.2), channel_id=1, source_target_pairs={{0,6},{2,0},{4,2},{6,4},{1,7},{3,1},{5,3},{7,5},{8,14},{10,8},{12,... | collective-permute-start | bytes 1572872 | tf_op jit(solution)/shard_map/ppermute | solution.py:38
  127.6 6.1 %collective-permute-done.4 = f32[512,256]{1,0:T(8,128)S(1)} collective-permute-done((f32[512,256]{1,0:T(8,128)S(1)}, f32[512,256]{1,0:T(8,128)S(1)}, u32[]{:S(2)}, u32[]{:S(2)}) %collective-permute-start.4) | collective-permute-done | bytes 524320 | tf_op jit(solution)/shard_map/ppermute | solution.py:38
  133.7 1.1 bitcast_add_fusion.4
  134.8 0.9 collective-permute-done.7
  135.7 1.1 bitcast_add_fusion.1
  137.0 0.6 collective-permute-start.8
  137.6 0.6 convert_reduce_fusion
  138.9 20.2 %collective-permute-done.8 = f32[256,512]{1,0:T(8,128)S(1)} collective-permute-done((f32[256,512]{1,0:T(8,128)S(1)}, f32[256,512]{1,0:T(8,128)S(1)}, u32[]{:S(2)}, u32[]{:S(2)}) %collective-permute-start.8) | collective-permute-done | bytes 524320 | tf_op jit(solution)/shard_map/ppermute | solution.py:49
  159.4 1.9 add_convert_fusion
  161.3 89.7 %reduce-scatter.4.cloned.1.call-done = f32[64,1280]{1,0:T(8,128)} async-done(((f32[2048,1280]{1,0:T(8,128)}), f32[64,1280]{1,0:T(8,128)}) %reduce-scatter.4.cloned.1.call-update) | async-done | bytes 327696
  251.0 1.0 slice.44
  252.2 0.9 copy.27
  253.3 0.7 copy.28
  (43 shorter events, 1.4 us)
Async XLA Ops:
  7.2 4.0 %copy-start = (bf16[2,256,2048]{2,1,0:T(8,128)(2,1)S(1)}, bf16[2,256,2048]{2,1,0:T(8,128)(2,1)}, u32[]{:S(2)}) copy-start(bf16[2,256,2048]{2,1,0:T(8,128)(2,1)} %param.5) | copy-start | bytes 6291460
  7.2 243.8 %reduce-scatter.4.cloned.1.call-start = ((), (), s32[]{:S(2)}) async-start(), calls=%async_computation.1 | async-start | bytes 10813440
  11.2 2.2 copy-start.3
  13.4 7.3 %copy-start.11 = (s32[2]{0:T(128)S(1)}, s32[2]{0:T(128)}, u32[]{:S(2)}) copy-start(s32[2]{0:T(128)} %param.9) | copy-start | bytes 28
  15.7 27.7 %collective-permute-start = (f32[2,256,512]{1,0,2:T(2,128)}, f32[2,256,512]{1,0,2:T(2,128)}, u32[]{:S(2)}, u32[]{:S(2)}) collective-permute-start(f32[2,256,512]{1,0,2:T(2,128)} %copy.23), channel_id=1, source_target_pairs={{0,32},{8,40},{16,48},{24,56},{32,64},{40,72},{48,80},{56,88},{64,... | collective-permute-start | bytes 3145736 | tf_op jit(solution)/shard_map/ppermute | solution.py:12
  20.8 3.0 %copy-start.6 = (bf16[2,256,2048]{2,1,0:T(8,128)(2,1)S(1)}, bf16[2,256,2048]{2,1,0:T(8,128)(2,1)}, u32[]{:S(2)}) copy-start(bf16[2,256,2048]{2,1,0:T(8,128)(2,1)} %param.6) | copy-start | bytes 6291460
  24.1 24.9 %copy-start.5 = (bf16[2,256,2048]{2,1,0:T(8,128)(2,1)}, bf16[2,256,2048]{2,1,0:T(8,128)(2,1)S(1)}, u32[]{:S(2)}) copy-start(bf16[2,256,2048]{2,1,0:T(8,128)(2,1)S(1)} %broadcast_select_fusion) | copy-start | bytes 6291460
  44.8 1.2 copy-start.12
  46.9 2.8 %copy-start.9 = (bf16[512,256]{0,1:T(8,128)(2,1)}, bf16[512,256]{0,1:T(8,128)(2,1)S(1)}, u32[]{:S(2)}) copy-start(bf16[512,256]{0,1:T(8,128)(2,1)S(1)} %get-tuple-element.22) | copy-start | bytes 786436
  47.0 16.7 %collective-permute-start.1 = (bf16[2,256,512]{1,2,0:T(8,128)(2,1)S(1)}, bf16[2,256,512]{1,2,0:T(8,128)(2,1)S(1)}, u32[]{:S(2)}, u32[]{:S(2)}) collective-permute-start(bf16[2,256,512]{1,2,0:T(8,128)(2,1)S(1)} %bitcast.83), channel_id=1, source_target_pairs={{32,0},{40,8},{48,16},{56,24},{64,32},{72,40},{80,48},{88,56},{96,... | collective-permute-start | bytes 1572872 | tf_op jit(solution)/shard_map/ppermute | solution.py:12
  63.7 0.8 copy-start.7
  81.5 0.9 copy-start.10
  82.4 5.0 %copy-start.8 = (bf16[2,256,512]{1,2,0:T(8,128)(2,1)S(1)}, bf16[2,256,512]{1,2,0:T(8,128)(2,1)}, u32[]{:S(2)}) copy-start(bf16[2,256,512]{1,2,0:T(8,128)(2,1)} %copy-done.7) | copy-start | bytes 1572868
  82.4 5.2 %copy-start.4 = (bf16[2048,256]{1,0:T(8,128)(2,1)S(1)}, bf16[2048,256]{1,0:T(8,128)(2,1)}, u32[]{:S(2)}) copy-start(bf16[2048,256]{1,0:T(8,128)(2,1)} %copy-done.3) | copy-start | bytes 3145732
  91.6 1.4 copy-start.2
  93.0 13.6 %collective-permute-start.2 = (f32[512,256]{1,0:T(8,128)S(1)}, f32[512,256]{1,0:T(8,128)S(1)}, u32[]{:S(2)}, u32[]{:S(2)}) collective-permute-start(f32[512,256]{1,0:T(8,128)S(1)} %dynamic-slice_bitcast_fusion.2), channel_id=1, source_target_pairs={{0,2},{2,4},{4,6},{6,0},{1,3},{3,5},{5,7},{7,1},{8,10},{10,12},{12... | collective-permute-start | bytes 1572872 | tf_op jit(solution)/shard_map/ppermute | solution.py:38
  95.5 12.6 %collective-permute-start.5 = (f32[512,256]{1,0:T(8,128)}, f32[512,256]{1,0:T(8,128)}, u32[]{:S(2)}, u32[]{:S(2)}) collective-permute-start(f32[512,256]{1,0:T(8,128)} %dynamic-slice_bitcast_fusion.1), channel_id=1, source_target_pairs={{0,6},{2,0},{4,2},{6,4},{1,7},{3,1},{5,3},{7,5},{8,14},{10,8},{12,... | collective-permute-start | bytes 1572872 | tf_op jit(solution)/shard_map/ppermute | solution.py:38
  107.7 12.8 %collective-permute-start.3 = (f32[512,256]{1,0:T(8,128)S(1)}, f32[512,256]{1,0:T(8,128)}, u32[]{:S(2)}, u32[]{:S(2)}) collective-permute-start(f32[512,256]{1,0:T(8,128)S(1)} %bitcast_add_fusion.6), channel_id=1, source_target_pairs={{0,2},{2,4},{4,6},{6,0},{1,3},{3,5},{5,7},{7,1},{8,10},{10,12},{12... | collective-permute-start | bytes 1572872 | tf_op jit(solution)/shard_map/ppermute | solution.py:38
  110.1 11.9 %collective-permute-start.6 = (f32[512,256]{1,0:T(8,128)}, f32[512,256]{1,0:T(8,128)}, u32[]{:S(2)}, u32[]{:S(2)}) collective-permute-start(f32[512,256]{1,0:T(8,128)} %bitcast_add_fusion.3), channel_id=1, source_target_pairs={{0,6},{2,0},{4,2},{6,4},{1,7},{3,1},{5,3},{7,5},{8,14},{10,8},{12,... | collective-permute-start | bytes 1572872 | tf_op jit(solution)/shard_map/ppermute | solution.py:38
  121.8 11.9 %collective-permute-start.4 = (f32[512,256]{1,0:T(8,128)S(1)}, f32[512,256]{1,0:T(8,128)S(1)}, u32[]{:S(2)}, u32[]{:S(2)}) collective-permute-start(f32[512,256]{1,0:T(8,128)S(1)} %bitcast_add_fusion.5), channel_id=1, source_target_pairs={{0,2},{2,4},{4,6},{6,0},{1,3},{3,5},{5,7},{7,1},{8,10},{10,12},{12... | collective-permute-start | bytes 1572872 | tf_op jit(solution)/shard_map/ppermute | solution.py:38
  123.9 11.8 %collective-permute-start.7 = (f32[512,256]{1,0:T(8,128)}, f32[512,256]{1,0:T(8,128)}, u32[]{:S(2)}, u32[]{:S(2)}) collective-permute-start(f32[512,256]{1,0:T(8,128)} %bitcast_add_fusion.2), channel_id=1, source_target_pairs={{0,6},{2,0},{4,2},{6,4},{1,7},{3,1},{5,3},{7,5},{8,14},{10,8},{12,... | collective-permute-start | bytes 1572872 | tf_op jit(solution)/shard_map/ppermute | solution.py:38
  137.0 22.1 %collective-permute-start.8 = (f32[256,512]{1,0:T(8,128)S(1)}, f32[256,512]{1,0:T(8,128)S(1)}, u32[]{:S(2)}, u32[]{:S(2)}) collective-permute-start(f32[256,512]{1,0:T(8,128)S(1)} %dynamic-slice_bitcast_fusion), channel_id=1, source_target_pairs={{0,1},{1,0},{2,3},{3,2},{4,5},{5,4},{6,7},{7,6},{8,9},{9,8},{10,11... | collective-permute-start | bytes 1572872 | tf_op jit(solution)/shard_map/ppermute | solution.py:49
  159.4 94.6 %copy-start.1 = (bf16[2,256,2048]{2,1,0:T(8,128)(2,1)S(1)}, bf16[2,256,2048]{2,1,0:T(8,128)(2,1)}, u32[]{:S(2)}) copy-start(bf16[2,256,2048]{2,1,0:T(8,128)(2,1)} %param.5) | copy-start | bytes 6291460
  251.0 2.1 slice-start
Sparse Core Ops, SparseCore 0:
  81.6 169.3 reduce-scatter.3

commit v4 on v3

--- a/solution.py
+++ b/solution.py
@@ -86,19 +86,23 @@
     own_rows = lax.dynamic_slice_in_dim(grad_rows, chan_index * share, share, 2)
     summed = summed.reshape(share, traj, window_extent).transpose(1, 2, 0)
     grad_states = (own_rows.astype(jnp.float32) + summed).astype(jnp.bfloat16)
-    weight_terms = jnp.concatenate(
-        [
-            contract_rows(rows, branch_grads),
-            contract_rows(rows, later),
-            contract_rows(grad_flat, mixed),
-        ],
-        axis=1,
+    early = lax.psum_scatter(
+        jnp.concatenate(
+            [contract_rows(rows, branch_grads), contract_rows(grad_flat, mixed)], axis=1
+        ),
+        "tm",
+        scatter_dimension=0,
+        tiled=True,
     )
-    reduced = lax.psum_scatter(weight_terms, "tm", scatter_dimension=0, tiled=True)
+    early, later_rows, grad_states = lax.optimization_barrier((early, later, grad_states))
+    late = lax.psum_scatter(
+        contract_rows(rows, later_rows), "tm", scatter_dimension=0, tiled=True
+    )
     scale = lax.rsqrt(jnp.sum(lengths.astype(jnp.float32)))
-    part = reduced.shape[0]
-    in_summed = reduced[:, : 4 * blocks].reshape(part, 2, 2, blocks).transpose(1, 2, 0, 3)
-    out_summed = reduced[:, 4 * blocks :].T
+    part = early.shape[0]
+    in_summed = jnp.concatenate([early[:, : 2 * blocks], late], axis=1)
+    in_summed = in_summed.reshape(part, 2, 2, blocks).transpose(1, 2, 0, 3)
+    out_summed = early[:, 2 * blocks :].T
     return (grad_states, in_summed * scale, out_summed * scale)
 
 

time: 265 us -> 349 us (1.32)
  waiting for transfers between devices: 166 us -> 246 us
  local copies, waits for them, and re-layouts: 27.6 us -> 33.6 us
    unnamed x2 -> x4, waiting for transfers between devices: 89.8 us -> 179 us
    ppermute x1, waiting for transfers between devices: 20.2 us -> 12.3 us  [ring_reduce_scatter(): return keep + lax.ppermute(give, 'pair', [(0, 1), (1, 0)])]
    dot_general x3, matrix products: 9.36 us -> 5.09 us  [contract_cols(): lax.dot_general(left, right, (((1,), (1,)), ((), ())), preferred_element_...]
    unnamed x31 -> x30, local copies, waits for them, and re-layouts: 17.7 us -> 19.7 us
  transfers between devices with their start and end apart: 10 -> 11, of which waited for: 8 -> 9; matrix products, arithmetic and copies ran while one was open for 10% -> 9% of each run, Pallas kernels for 0% -> 0%
where the time goes in v4:
time: 349 us; the launch traced here: 345 us
  waiting for transfers between devices  246 us (70%)
  local copies, waits for them, and re-layouts  33.6 us (10%)
  starting transfers between devices  17.6 us (5%)
  other arithmetic  17.6 us (5%)
  matrix products  15.6 us (4%)
  between operations  15 us (4%)
    unnamed x4, waiting for transfers between devices  179 us
    ppermute x2, waiting for transfers between devices, shifted(): return lax.ppermute(x, axis, pairs)  31.1 us
    ppermute x6, waiting for transfers between devices, ring_reduce_scatter(): got = lax.ppermute(acc, 'ring', pairs)  23.2 us
    unnamed x30, local copies, waits for them, and re-layouts  19.7 us
    ppermute x1, waiting for transfers between devices, ring_reduce_scatter(): return keep + lax.ppermute(give, 'pair', [(0, 1), (1, 0)])  12.3 us
    add x6, other arithmetic, ring_reduce_scatter(): got + lax.dynamic_index_in_dim(own, (at - step * (s + 2)) % peers, 0, kee...  10.1 us
    ppermute x6, starting transfers between devices, ring_reduce_scatter(): got = lax.ppermute(acc, 'ring', pairs)  9.97 us
  transfers between devices with their start and end apart: 11, of which 9 were waited for; matrix products, arithmetic and copies ran while one was open for 9% of the time, Pallas kernels for 0%

profile of v4, /device:TPU:98, one launch (start us, length us, event | category | flops | bytes accessed | tf_op | source)
XLA Modules:
  0.0 345.3 jit_solution(230249172314067387)
XLA Ops:
  7.2 3.9 %slice_bitcast_fusion.1 = (bf16[2048,256]{1,0:T(8,128)(2,1)S(1)}, bf16[2048,256]{1,0:T(8,128)(2,1)}, bf16[2048,256]{1,0:T(8,128)(2,1)}, bf16[2048,256]{1,0:T(8,128)(2,1)S(1)}) fusion(bf16[2,2,2048,256]{3,2,1,0:T(8,128)(2,1)} %param.7), kind=kLoop, calls=%fused_computation.12 | loop fusion | bytes 8388608 | tf_op jit(solution)/shard_map/squeeze | solution.py:59
  11.1 2.2 fusion
  13.4 1.5 copy.18
  14.9 5.0 %collective-permute-start = (f32[2,256,512]{1,0,2:T(2,128)S(1)}, f32[2,256,512]{1,0,2:T(2,128)}, u32[]{:S(2)}, u32[]{:S(2)}) collective-permute-start(f32[2,256,512]{1,0,2:T(2,128)S(1)} %copy.18), channel_id=1, source_target_pairs={{0,32},{8,40},{16,48},{24,56},{32,64},{40,72},{48,80},{56,88},{64,... | collective-permute-start | bytes 3145736 | tf_op jit(solution)/shard_map/ppermute | solution.py:12
  20.1 3.0 convolution_bitcast_fusion.2
  23.3 19.1 %collective-permute-done = f32[2,256,512]{1,0,2:T(2,128)} collective-permute-done((f32[2,256,512]{1,0,2:T(2,128)S(1)}, f32[2,256,512]{1,0,2:T(2,128)}, u32[]{:S(2)}, u32[]{:S(2)}) %collective-permute-start) | collective-permute-done | bytes 1048608 | tf_op jit(solution)/shard_map/ppermute | solution.py:12
  42.4 1.3 copy.27
  43.9 0.8 fusion.5
  45.1 0.9 multiply_convert_fusion.2
  46.0 1.3 convolution_bitcast_fusion.1
  47.3 3.0 pad_maximum_fusion
  50.3 6.6 %copy.23 = f32[2048,768]{1,0:T(8,128)} copy(f32[2048,768]{0,1:T(8,128)} %pad_maximum_fusion) | data formatting | bytes 12582912
  57.0 0.9 reshape.72
  57.9 1.9 collective-permute-start.1
  59.9 2.9 fusion.1
  62.8 12.1 %collective-permute-done.1 = bf16[2,256,512]{1,0,2:T(2,128)(2,1)S(1)} collective-permute-done((bf16[2,256,512]{1,0,2:T(2,128)(2,1)}, bf16[2,256,512]{1,0,2:T(2,128)(2,1)S(1)}, u32[]{:S(2)}, u32[]{:S(2)}) %collective-permute-start.1) | collective-permute-done | bytes 524320 | tf_op jit(solution)/shard_map/ppermute | solution.py:12
  74.9 0.8 copy-done.9
  75.7 1.1 copy.28
  76.9 1.3 convolution_add_fusion
  78.1 1.8 fusion.11
  79.9 1.4 copy-done.1
  81.3 0.8 dynamic-slice_bitcast_fusion.2
  82.1 1.6 collective-permute-start.2
  83.7 1.9 dynamic-slice_bitcast_fusion.1
  85.6 1.7 collective-permute-start.5
  87.3 8.6 %collective-permute-done.2 = f32[512,256]{1,0:T(8,128)S(1)} collective-permute-done((f32[512,256]{1,0:T(8,128)}, f32[512,256]{1,0:T(8,128)S(1)}, u32[]{:S(2)}, u32[]{:S(2)}) %collective-permute-start.2) | collective-permute-done | bytes 524320 | tf_op jit(solution)/shard_map/ppermute | solution.py:38
  95.9 1.9 bitcast_add_fusion.6
  98.1 2.1 bitcast_add_fusion.3
  100.1 2.9 collective-permute-start.6
  103.1 7.7 %collective-permute-done.3 = f32[512,256]{1,0:T(8,128)} collective-permute-done((f32[512,256]{1,0:T(8,128)}, f32[512,256]{1,0:T(8,128)}, u32[]{:S(2)}, u32[]{:S(2)}) %collective-permute-start.3) | collective-permute-done | bytes 524320 | tf_op jit(solution)/shard_map/ppermute | solution.py:38
  110.7 1.3 bitcast_add_fusion.5
  112.1 2.3 bitcast_add_fusion.2
  114.4 3.4 collective-permute-start.7
  117.9 6.1 %collective-permute-done.4 = f32[512,256]{1,0:T(8,128)} collective-permute-done((f32[512,256]{1,0:T(8,128)S(1)}, f32[512,256]{1,0:T(8,128)}, u32[]{:S(2)}, u32[]{:S(2)}) %collective-permute-start.4) | collective-permute-done | bytes 524320 | tf_op jit(solution)/shard_map/ppermute | solution.py:38
  124.0 1.3 bitcast_add_fusion.4
  126.0 1.3 bitcast_add_fusion.1
  127.5 1.0 copy-done.2
  129.1 12.3 %collective-permute-done.8 = f32[256,512]{1,0:T(8,128)} collective-permute-done((f32[256,512]{1,0:T(8,128)S(1)}, f32[256,512]{1,0:T(8,128)}, u32[]{:S(2)}, u32[]{:S(2)}) %collective-permute-start.8) | collective-permute-done | bytes 524320 | tf_op jit(solution)/shard_map/ppermute | solution.py:49
  141.4 1.3 bitcast_add_fusion
  142.7 1.0 copy.22
  143.7 1.9 add_convert_fusion
  145.6 54.7 %reduce-scatter.7.cloned.1.call-done = f32[64,768]{1,0:T(8,128)} async-done(((f32[2048,768]{1,0:T(8,128)}), f32[64,768]{1,0:T(8,128)}) %reduce-scatter.7.cloned.1.call-update) | async-done | bytes 196624
  200.2 1.1 copy.24
  201.3 3.3 convolution_bitcast_fusion
  204.6 5.3 %copy.25 = f32[2048,512]{1,0:T(8,128)} copy(f32[2048,512]{0,1:T(8,128)} %convolution_bitcast_fusion) | data formatting | bytes 8388608
  212.0 124.5 %reduce-scatter.9.cloned.1.call-done = f32[64,512]{1,0:T(8,128)} async-done(((f32[2048,512]{1,0:T(8,128)}), f32[64,512]{1,0:T(8,128)}) %reduce-scatter.9.cloned.1.call-update) | async-done | bytes 131088
  336.5 1.0 copy.26
  337.5 0.9 copy.20
  (43 shorter events, 4.4 us)
Async XLA Ops:
  7.2 4.0 %copy-start = (bf16[2,256,2048]{2,1,0:T(8,128)(2,1)S(1)}, bf16[2,256,2048]{2,1,0:T(8,128)(2,1)}, u32[]{:S(2)}) copy-start(bf16[2,256,2048]{2,1,0:T(8,128)(2,1)} %param.5) | copy-start | bytes 6291460
  7.2 193.0 %reduce-scatter.7.cloned.1.call-start = ((), (), s32[]{:S(2)}) async-start(), calls=%async_computation.2 | async-start | bytes 6488064
  11.1 2.2 copy-start.3
  11.1 2.2 copy-start.5
  13.4 6.6 %copy-start.10 = (s32[2]{0:T(128)S(1)}, s32[2]{0:T(128)}, u32[]{:S(2)}) copy-start(s32[2]{0:T(128)} %param.9) | copy-start | bytes 28
  14.9 27.4 %collective-permute-start = (f32[2,256,512]{1,0,2:T(2,128)S(1)}, f32[2,256,512]{1,0,2:T(2,128)}, u32[]{:S(2)}, u32[]{:S(2)}) collective-permute-start(f32[2,256,512]{1,0,2:T(2,128)S(1)} %copy.18), channel_id=1, source_target_pairs={{0,32},{8,40},{16,48},{24,56},{32,64},{40,72},{48,80},{56,88},{64,... | collective-permute-start | bytes 3145736 | tf_op jit(solution)/shard_map/ppermute | solution.py:12
  20.1 3.0 copy-start.8
  23.3 21.4 %copy-start.7 = (bf16[2,256,2048]{2,1,0:T(8,128)(2,1)}, bf16[2,256,2048]{2,1,0:T(8,128)(2,1)S(1)}, u32[]{:S(2)}) copy-start(bf16[2,256,2048]{2,1,0:T(8,128)(2,1)S(1)} %broadcast_select_fusion) | copy-start | bytes 6291460
  43.9 1.2 copy-start.11
  56.9 279.5 %reduce-scatter.9.cloned.1.call-start = ((), (), s32[]{:S(2)}) async-start(), calls=%async_computation.3 | async-start | bytes 4325376
  57.9 17.0 %collective-permute-start.1 = (bf16[2,256,512]{1,0,2:T(2,128)(2,1)}, bf16[2,256,512]{1,0,2:T(2,128)(2,1)S(1)}, u32[]{:S(2)}, u32[]{:S(2)}) collective-permute-start(bf16[2,256,512]{1,0,2:T(2,128)(2,1)} %reshape.72), channel_id=1, source_target_pairs={{32,0},{40,8},{48,16},{56,24},{64,32},{72,40},{80,48},{88,56},{96,... | collective-permute-start | bytes 1572872 | tf_op jit(solution)/shard_map/ppermute | solution.py:12
  59.9 17.0 %copy-start.4 = (bf16[2048,256]{1,0:T(8,128)(2,1)S(1)}, bf16[2048,256]{1,0:T(8,128)(2,1)}, u32[]{:S(2)}) copy-start(bf16[2048,256]{1,0:T(8,128)(2,1)} %copy-done.3) | copy-start | bytes 3145732
  59.9 17.0 %copy-start.6 = (bf16[2048,256]{1,0:T(8,128)(2,1)S(1)}, bf16[2048,256]{1,0:T(8,128)(2,1)}, u32[]{:S(2)}) copy-start(bf16[2048,256]{1,0:T(8,128)(2,1)} %copy-done.5) | copy-start | bytes 3145732
  74.9 0.8 copy-start.9
  79.9 1.4 copy-start.1
  82.1 13.7 %collective-permute-start.2 = (f32[512,256]{1,0:T(8,128)}, f32[512,256]{1,0:T(8,128)S(1)}, u32[]{:S(2)}, u32[]{:S(2)}) collective-permute-start(f32[512,256]{1,0:T(8,128)} %dynamic-slice_bitcast_fusion.2), channel_id=1, source_target_pairs={{0,2},{2,4},{4,6},{6,0},{1,3},{3,5},{5,7},{7,1},{8,10},{10,12},{12... | collective-permute-start | bytes 1572872 | tf_op jit(solution)/shard_map/ppermute | solution.py:38
  85.6 12.5 %collective-permute-start.5 = (f32[512,256]{1,0:T(8,128)}, f32[512,256]{1,0:T(8,128)}, u32[]{:S(2)}, u32[]{:S(2)}) collective-permute-start(f32[512,256]{1,0:T(8,128)} %dynamic-slice_bitcast_fusion.1), channel_id=1, source_target_pairs={{0,6},{2,0},{4,2},{6,4},{1,7},{3,1},{5,3},{7,5},{8,14},{10,8},{12,... | collective-permute-start | bytes 1572872 | tf_op jit(solution)/shard_map/ppermute | solution.py:38
  97.8 13.0 %collective-permute-start.3 = (f32[512,256]{1,0:T(8,128)}, f32[512,256]{1,0:T(8,128)}, u32[]{:S(2)}, u32[]{:S(2)}) collective-permute-start(f32[512,256]{1,0:T(8,128)} %bitcast_add_fusion.6), channel_id=1, source_target_pairs={{0,2},{2,4},{4,6},{6,0},{1,3},{3,5},{5,7},{7,1},{8,10},{10,12},{12... | collective-permute-start | bytes 1572872 | tf_op jit(solution)/shard_map/ppermute | solution.py:38
  100.1 12.0 %collective-permute-start.6 = (f32[512,256]{1,0:T(8,128)}, f32[512,256]{1,0:T(8,128)}, u32[]{:S(2)}, u32[]{:S(2)}) collective-permute-start(f32[512,256]{1,0:T(8,128)} %bitcast_add_fusion.3), channel_id=1, source_target_pairs={{0,6},{2,0},{4,2},{6,4},{1,7},{3,1},{5,3},{7,5},{8,14},{10,8},{12,... | collective-permute-start | bytes 1572872 | tf_op jit(solution)/shard_map/ppermute | solution.py:38
  112.0 12.0 %collective-permute-start.4 = (f32[512,256]{1,0:T(8,128)S(1)}, f32[512,256]{1,0:T(8,128)}, u32[]{:S(2)}, u32[]{:S(2)}) collective-permute-start(f32[512,256]{1,0:T(8,128)S(1)} %bitcast_add_fusion.5), channel_id=1, source_target_pairs={{0,2},{2,4},{4,6},{6,0},{1,3},{3,5},{5,7},{7,1},{8,10},{10,12},{12... | collective-permute-start | bytes 1572872 | tf_op jit(solution)/shard_map/ppermute | solution.py:38
  114.4 11.6 %collective-permute-start.7 = (f32[512,256]{1,0:T(8,128)}, f32[512,256]{1,0:T(8,128)}, u32[]{:S(2)}, u32[]{:S(2)}) collective-permute-start(f32[512,256]{1,0:T(8,128)} %bitcast_add_fusion.2), channel_id=1, source_target_pairs={{0,6},{2,0},{4,2},{6,4},{1,7},{3,1},{5,3},{7,5},{8,14},{10,8},{12,... | collective-permute-start | bytes 1572872 | tf_op jit(solution)/shard_map/ppermute | solution.py:38
  127.4 1.0 copy-start.2
  128.5 12.9 %collective-permute-start.8 = (f32[256,512]{1,0:T(8,128)S(1)}, f32[256,512]{1,0:T(8,128)}, u32[]{:S(2)}, u32[]{:S(2)}) collective-permute-start(f32[256,512]{1,0:T(8,128)S(1)} %dynamic-slice_bitcast_fusion), channel_id=1, source_target_pairs={{0,1},{1,0},{2,3},{3,2},{4,5},{5,4},{6,7},{7,6},{8,9},{9,8},{10,11... | collective-permute-start | bytes 1572872 | tf_op jit(solution)/shard_map/ppermute | solution.py:49
Sparse Core Ops, SparseCore 0:
  57.0 143.1 reduce-scatter.6
  210.1 126.3 reduce-scatter.8

commit v5 on v1

--- a/solution.py
+++ b/solution.py
@@ -6,8 +6,11 @@
 DILATION_STEPS = 1024
 
 
+TIME = ("tz", "tx", "tc")
+
+
 def shifted(x, axis, by):
-    peers = lax.axis_size(axis)
+    peers = lax.axis_size(axis[0]) * lax.axis_size(axis[1]) * lax.axis_size(axis[2])
     pairs = [(i, i + by) for i in range(peers) if 0 <= i + by < peers]
     return lax.ppermute(x, axis, pairs)
 
@@ -24,6 +27,39 @@
     )
 
 
+def ring_sum(chunks, axis):
+    peers = lax.axis_size(axis)
+    at = lax.axis_index(axis)
+    half = chunks.shape[-1] // 2
+    sums = []
+    for step, cols in ((1, slice(0, half)), (-1, slice(half, None))):
+        own = chunks[..., cols]
+        pairs = [(i, (i + step) % peers) for i in range(peers)]
+        acc = lax.dynamic_index_in_dim(own, (at - step) % peers, 0, keepdims=False)
+        for s in range(peers - 1):
+            got = lax.ppermute(acc, axis, pairs)
+            acc = got + lax.dynamic_index_in_dim(
+                own, (at - step * (s + 2)) % peers, 0, keepdims=False
+            )
+        sums.append(acc)
+    return jnp.concatenate(sums, axis=-1)
+
+
+def swap_sum(parts, axis):
+    me = lax.axis_index(axis)
+    keep = lax.dynamic_index_in_dim(parts, me, 0, keepdims=False)
+    give = lax.dynamic_index_in_dim(parts, 1 - me, 0, keepdims=False)
+    return keep + lax.ppermute(give, axis, [(0, 1), (1, 0)])
+
+
+def time_reduce_scatter(x):
+    outer, mid, inner = (lax.axis_size(a) for a in TIME)
+    blocks = x.reshape(outer, mid, inner, x.shape[0] // (outer * mid * inner), x.shape[1])
+    blocks = swap_sum(jnp.moveaxis(blocks, 2, 0), TIME[2])
+    blocks = ring_sum(blocks, TIME[0])
+    return swap_sum(blocks, TIME[1])
+
+
 def local(states, upstream, w_in, w_out, lengths):
     traj, window_extent, width = states.shape
     blocks = w_in.shape[3]
@@ -34,12 +70,12 @@
     w_dil = jnp.concatenate([w_in[1, 0], w_in[1, 1]], axis=1)
     dilated = jnp.dot(rows, w_dil, preferred_element_type=jnp.float32)
     dilated_prior = shifted(
-        dilated.reshape(traj, window_extent, 2 * blocks), "tm", receptive_extent
+        dilated.reshape(traj, window_extent, 2 * blocks), TIME, receptive_extent
     ).reshape(rows_n, 2 * blocks)
     pre = jnp.dot(rows, w_now, preferred_element_type=jnp.float32) + dilated_prior
     filt = pre[:, :blocks]
     gate = pre[:, blocks:]
-    first = lax.axis_index("tm") * window_extent
+    first = lax.axis_index(TIME) * window_extent
     positions = first + jnp.arange(window_extent, dtype=jnp.int32)
     valid = positions[None, :] < lengths[:, None]
     grad_rows = jnp.where(valid[:, :, None], upstream, jnp.zeros_like(upstream))
@@ -52,7 +88,7 @@
     gate_gradient = (dmix * tangent * sigma * (1.0 - sigma)).astype(jnp.bfloat16)
     branch_grads = jnp.concatenate([filter_gradient, gate_gradient], axis=1)
     later = shifted(
-        branch_grads.reshape(traj, window_extent, 2 * blocks), "tm", -receptive_extent
+        branch_grads.reshape(traj, window_extent, 2 * blocks), TIME, -receptive_extent
     ).reshape(rows_n, 2 * blocks)
     partial_value = contract_cols(w_now, branch_grads) + contract_cols(w_dil, later)
     summed = lax.psum_scatter(partial_value, "chan", scatter_dimension=0, tiled=True)
@@ -68,7 +104,7 @@
         ],
         axis=1,
     )
-    reduced = lax.psum_scatter(weight_terms, "tm", scatter_dimension=0, tiled=True)
+    reduced = time_reduce_scatter(weight_terms)
     scale = lax.rsqrt(jnp.sum(lengths.astype(jnp.float32)))
     part = reduced.shape[0]
     in_summed = reduced[:, : 4 * blocks].reshape(part, 2, 2, blocks).transpose(1, 2, 0, 3)
@@ -77,9 +113,11 @@
 
 
 def solution(mesh):
+    tm, chan = mesh.shape["tm"], mesh.shape["chan"]
+    mesh = jax.sharding.Mesh(mesh.devices.reshape(tm // 4, 2, 2, chan), TIME + ("chan",))
     placed = (
-        P(None, "tm", None),
-        P(None, "tm", None),
+        P(None, TIME, None),
+        P(None, TIME, None),
         P(None, None, None, "chan"),
         P("chan", None),
         P(),
@@ -88,6 +126,6 @@
         local,
         mesh=mesh,
         in_specs=placed,
-        out_specs=(P(None, "tm", "chan"), P(None, None, "tm", "chan"), P("chan", "tm")),
+        out_specs=(P(None, TIME, "chan"), P(None, None, TIME, "chan"), P("chan", TIME)),
         check_vma=False,
     )

time: 346 us -> 209 us (0.60)
  waiting for transfers between devices: 263 us -> 80.1 us
  starting transfers between devices: 7.16 us -> 33.9 us
  other arithmetic: 7.5 us -> 26.8 us
  local copies, waits for them, and re-layouts: 27.5 us -> 32.1 us
    unnamed x3 -> x1, waiting for transfers between devices: 163 us -> 0.02 us
    reduce_scatter x1, waiting for transfers between devices: 69 us -> 0.01 us  [local(): lax.psum_scatter(partial_value, 'chan', scatter_dimension=0, tiled=True)]
    ppermute x0 -> x16, waiting for transfers between devices: none -> 48 us  [the longest x14 35.7 us: ring_sum(): got = lax.ppermute(acc, axis, pairs)]
    ppermute x0 -> x16, starting transfers between devices: none -> 26.9 us  [the longest x14 24.8 us: ring_sum(): got = lax.ppermute(acc, axis, pairs)]
    add x0 -> x16, other arithmetic: none -> 19 us  [the longest x14 14.1 us: ring_sum(): got + lax.dynamic_index_in_dim(own, (at - step * (s + 2)) % peers, 0, kee...]
    unnamed x31, local copies, waits for them, and re-layouts: 16.1 us -> 3.79 us
    concatenate x0 -> x1, local copies, waits for them, and re-layouts: none -> 11.3 us  [local(): jnp.concatenate([contract_rows(rows, branch_grads), contract_rows(rows, l...]
    squeeze x0 -> x3, local copies, waits for them, and re-layouts: none -> 6.44 us  [the longest x1 5.43 us: swap_sum(): give = lax.dynamic_index_in_dim(parts, 1 - me, 0, keepdims=False)]
  transfers between devices with their start and end apart: 4 -> 19, of which waited for: 4 -> 12; matrix products, arithmetic and copies ran while one was open for 9% -> 19% of each run, Pallas kernels for 0% -> 0%
where the time goes in v5:
time: 209 us; the launch traced here: 207 us
  waiting for transfers between devices  80.1 us (38%)
  starting transfers between devices  33.9 us (16%)
  local copies, waits for them, and re-layouts  32.1 us (15%)
  other arithmetic  26.8 us (13%)
  matrix products  18.3 us (9%)
  between operations  15.3 us (7%)
    ppermute x14, waiting for transfers between devices, ring_sum(): got = lax.ppermute(acc, axis, pairs)  35.7 us
    ppermute x2, waiting for transfers between devices, shifted(): return lax.ppermute(x, axis, pairs)  32 us
    ppermute x14, starting transfers between devices, ring_sum(): got = lax.ppermute(acc, axis, pairs)  24.8 us
    add x14, other arithmetic, ring_sum(): got + lax.dynamic_index_in_dim(own, (at - step * (s + 2)) % peers, 0, kee...  14.1 us
    ppermute x2, waiting for transfers between devices, swap_sum(): return keep + lax.ppermute(give, axis, [(0, 1), (1, 0)])  12.4 us
    concatenate x1, local copies, waits for them, and re-layouts, local(): jnp.concatenate([contract_rows(rows, branch_grads), contract_rows(rows, l...  11.3 us
    dot_general x3, matrix products, contract_cols(): lax.dot_general(left, right, (((1,), (1,)), ((), ())), preferred_element_...  9.69 us
    ppermute x2, starting transfers between devices, shifted(): return lax.ppermute(x, axis, pairs)  6.95 us
  transfers between devices with their start and end apart: 19, of which 12 were waited for; matrix products, arithmetic and copies ran while one was open for 19% of the time, Pallas kernels for 0%

profile of v5, /device:TPU:98, one launch (start us, length us, event | category | flops | bytes accessed | tf_op | source)
XLA Modules:
  0.0 206.5 jit_solution(11285796585017515428)
XLA Ops:
  7.2 4.0 %slice_bitcast_fusion.1 = (bf16[2048,256]{1,0:T(8,128)(2,1)S(1)}, bf16[2048,256]{1,0:T(8,128)(2,1)}, bf16[2048,256]{1,0:T(8,128)(2,1)}, bf16[2048,256]{1,0:T(8,128)(2,1)S(1)}) fusion(bf16[2,2,2048,256]{3,2,1,0:T(8,128)(2,1)} %param.7), kind=kLoop, calls=%fused_computation.13 | loop fusion | bytes 8388608 | tf_op jit(solution)/shard_map/squeeze | solution.py:70
  11.2 2.3 %fusion = f32[512,512]{0,1:T(8,128)} fusion(bf16[512,2048]{1,0:T(8,128)(2,1)S(1)} %bitcast.91, bf16[2048,256]{1,0:T(8,128)(2,1)S(1)} %get-tuple-element.8, bf16[2048,256]{1,0:T(8,128)(2,1)S(1)} %get-tuple-element.5), kind=kOutput, calls=%fused_computation.10 | convolution fusion | flops 1077936128 | bytes 5242880 | tf_op jit(solution)/shard_map/dot_general | solution.py:71
  13.5 2.2 %copy.28 = f32[2,256,512]{1,0,2:T(2,128)} copy(f32[2,256,512]{2,1,0:T(8,128)} %bitcast.101) | data formatting | bytes 2097152 | tf_op jit(solution)/shard_map/reshape | solution.py:73
  15.8 5.0 %collective-permute-start = (f32[2,256,512]{1,0,2:T(2,128)}, f32[2,256,512]{1,0,2:T(2,128)}, u32[]{:S(2)}, u32[]{:S(2)}) collective-permute-start(f32[2,256,512]{1,0,2:T(2,128)} %copy.28), channel_id=1, source_target_pairs={{0,32},{8,40},{16,48},{24,56},{32,64},{40,72},{48,80},{56,88},{64,... | collective-permute-start | bytes 3145736 | tf_op jit(solution)/shard_map/ppermute | solution.py:15
  20.9 3.0 %convolution_bitcast_fusion.2 = f32[512,512]{0,1:T(8,128)S(1)} fusion(bf16[512,2048]{1,0:T(8,128)(2,1)S(1)} %bitcast.90, bf16[2048,256]{1,0:T(8,128)(2,1)} %get-tuple-element.6, bf16[2048,256]{1,0:T(8,128)(2,1)} %get-tuple-element.7), kind=kOutput, calls=%fused_computation.9 | convolution fusion | flops 1077936128 | bytes 5242880 | tf_op jit(solution)/shard_map/dot_general | solution.py:75
  24.1 19.4 %collective-permute-done = f32[2,256,512]{1,0,2:T(2,128)} collective-permute-done((f32[2,256,512]{1,0,2:T(2,128)}, f32[2,256,512]{1,0,2:T(2,128)}, u32[]{:S(2)}, u32[]{:S(2)}) %collective-permute-start) | collective-permute-done | bytes 1048608 | tf_op jit(solution)/shard_map/ppermute | solution.py:15
  43.5 1.4 copy.36
  46.2 1.9 collective-permute-start.1
  48.9 1.3 convolution_bitcast_fusion.1
  50.2 12.6 %collective-permute-done.1 = bf16[2,256,512]{1,2,0:T(8,128)(2,1)S(1)} collective-permute-done((bf16[2,256,512]{1,2,0:T(8,128)(2,1)S(1)}, bf16[2,256,512]{1,2,0:T(8,128)(2,1)S(1)}, u32[]{:S(2)}, u32[]{:S(2)}) %collective-permute-start.1) | collective-permute-done | bytes 524320 | tf_op jit(solution)/shard_map/ppermute | solution.py:15
  63.6 1.3 convolution_bitcast_fusion
  64.9 4.3 %pad_maximum_fusion = f32[2048,1280]{0,1:T(8,128)} fusion(f32[2048,256]{0,1:T(8,128)S(1)} %fusion.10, f32[2048,512]{0,1:T(8,128)S(1)} %convolution_bitcast_fusion, f32[2048,512]{0,1:T(8,128)S(1)} %convolution_bitcast_fusion.1), kind=kLoop, calls=%fused_computation | loop fusion | flops 5242880 | bytes 20971520 | tf_op jit(solution)/shard_map/concatenate | solution.py:99
  69.2 11.3 %copy.32 = f32[2048,1280]{1,0:T(8,128)} copy(f32[2048,1280]{0,1:T(8,128)} %pad_maximum_fusion) | data formatting | bytes 20971520 | tf_op jit(solution)/shard_map/concatenate | solution.py:99
  80.5 5.4 %dynamic-slice_bitcast_fusion = f32[8,2,64,1280]{3,2,1,0:T(8,128)} fusion(f32[8,2,2,64,1280]{4,3,2,1,0:T(8,128)} %bitcast.93, s32[]{:T(128)S(6)} %select_n.140), kind=kLoop, calls=%fused_computation.2 | loop fusion | bytes 10485764 | tf_op jit(solution)/shard_map/jit(dynamic_index_in_dim)/squeeze | solution.py:51
  86.0 3.3 %fusion.1 = f32[2048,512]{1,0:T(8,128)} fusion(bf16[2048,256]{1,0:T(8,128)(2,1)S(1)} %copy-done.9, bf16[2048,256]{1,0:T(8,128)(2,1)S(1)} %copy-done.10, bf16[512,256]{0,1:T(8,128)(2,1)S(1)} %copy-done.12, bf16[512,256]{0,1:T(8,128)(2,1)S(1)} %get-tuple-element.9), kind=kOutput, calls=%fused_computation.11 | convolution fusion | flops 1078984704 | bytes 6815744 | tf_op jit(solution)/shard_map/dot_general | solution.py:25
  89.5 5.5 %convolution_add_fusion = f32[2048,512]{1,0:T(8,128)} fusion(f32[2048,512]{1,0:T(8,128)} %fusion.1, bf16[512,512]{1,0:T(8,128)(2,1)S(1)} %bitcast.100, bf16[2048,256]{1,0:T(8,128)(2,1)S(1)} %copy-done.4, bf16[2048,256]{1,0:T(8,128)(2,1)S(1)} %get-tuple-element.5), kind=kOutput, calls=%fused_computation.5 | convolution fusion | flops 1078984704 | bytes 11010048 | tf_op jit(solution)/shard_map/dot_general | solution.py:25
  95.1 4.8 %bitcast_add_fusion = f32[8,2,64,1280]{3,2,1,0:T(8,128)S(1)} fusion(f32[8,2,64,1280]{3,2,1,0:T(8,128)} %collective-permute-done.2, f32[8,2,2,64,1280]{4,3,2,1,0:T(8,128)} %bitcast.94, s32[]{:T(128)S(6)} %select_n.139), kind=kLoop, calls=%fused_computation.1 | loop fusion | flops 1310720 | bytes 15728644 | tf_op jit(solution)/shard_map/add | solution.py:52
  99.9 1.9 fusion.17
  101.8 1.5 copy-done.2
  103.4 1.8 collective-permute-start.3
  106.5 7.0 %collective-permute-done.3 = f32[2,64,640]{2,1,0:T(8,128)S(1)} collective-permute-done((f32[2,64,640]{2,1,0:T(8,128)S(1)}, f32[2,64,640]{2,1,0:T(8,128)S(1)}, u32[]{:S(2)}, u32[]{:S(2)}) %collective-permute-start.3) | collective-permute-done | bytes 327712 | tf_op jit(solution)/shard_map/ppermute | solution.py:40
  113.5 1.0 bitcast_add_fusion.14
  114.5 3.0 %collective-permute-start.4 = (f32[2,64,640]{2,1,0:T(8,128)S(1)}, f32[2,64,640]{2,1,0:T(8,128)S(1)}, u32[]{:S(2)}, u32[]{:S(2)}) collective-permute-start(f32[2,64,640]{2,1,0:T(8,128)S(1)} %bitcast_add_fusion.14), channel_id=1, source_target_pairs={{0,32},{32,64},{64,96},{96,128},{128,160},{160,192},{192,224},{224... | collective-permute-start | bytes 983048 | tf_op jit(solution)/shard_map/ppermute | solution.py:40
  117.6 1.0 bitcast_add_fusion.7
  118.7 5.6 %collective-permute-done.4 = f32[2,64,640]{2,1,0:T(8,128)S(1)} collective-permute-done((f32[2,64,640]{2,1,0:T(8,128)S(1)}, f32[2,64,640]{2,1,0:T(8,128)S(1)}, u32[]{:S(2)}, u32[]{:S(2)}) %collective-permute-start.4) | collective-permute-done | bytes 327712 | tf_op jit(solution)/shard_map/ppermute | solution.py:40
  124.3 1.0 bitcast_add_fusion.13
  125.3 3.8 %collective-permute-start.5 = (f32[2,64,640]{2,1,0:T(8,128)S(1)}, f32[2,64,640]{2,1,0:T(8,128)S(1)}, u32[]{:S(2)}, u32[]{:S(2)}) collective-permute-start(f32[2,64,640]{2,1,0:T(8,128)S(1)} %bitcast_add_fusion.13), channel_id=1, source_target_pairs={{0,32},{32,64},{64,96},{96,128},{128,160},{160,192},{192,224},{224... | collective-permute-start | bytes 983048 | tf_op jit(solution)/shard_map/ppermute | solution.py:40
  129.1 1.0 bitcast_add_fusion.6
  130.3 4.8 %collective-permute-done.5 = f32[2,64,640]{2,1,0:T(8,128)S(1)} collective-permute-done((f32[2,64,640]{2,1,0:T(8,128)S(1)}, f32[2,64,640]{2,1,0:T(8,128)S(1)}, u32[]{:S(2)}, u32[]{:S(2)}) %collective-permute-start.5) | collective-permute-done | bytes 327712 | tf_op jit(solution)/shard_map/ppermute | solution.py:40
  136.0 3.8 %collective-permute-start.6 = (f32[2,64,640]{2,1,0:T(8,128)S(1)}, f32[2,64,640]{2,1,0:T(8,128)S(1)}, u32[]{:S(2)}, u32[]{:S(2)}) collective-permute-start(f32[2,64,640]{2,1,0:T(8,128)S(1)} %bitcast_add_fusion.12), channel_id=1, source_target_pairs={{0,32},{32,64},{64,96},{96,128},{128,160},{160,192},{192,224},{224... | collective-permute-start | bytes 983048 | tf_op jit(solution)/shard_map/ppermute | solution.py:40
  139.8 1.0 bitcast_add_fusion.5
  141.0 3.9 %collective-permute-done.6 = f32[2,64,640]{2,1,0:T(8,128)S(1)} collective-permute-done((f32[2,64,640]{2,1,0:T(8,128)S(1)}, f32[2,64,640]{2,1,0:T(8,128)S(1)}, u32[]{:S(2)}, u32[]{:S(2)}) %collective-permute-start.6) | collective-permute-done | bytes 327712 | tf_op jit(solution)/shard_map/ppermute | solution.py:40
  145.9 3.8 %collective-permute-start.7 = (f32[2,64,640]{2,1,0:T(8,128)S(1)}, f32[2,64,640]{2,1,0:T(8,128)S(1)}, u32[]{:S(2)}, u32[]{:S(2)}) collective-permute-start(f32[2,64,640]{2,1,0:T(8,128)S(1)} %bitcast_add_fusion.11), channel_id=1, source_target_pairs={{0,32},{32,64},{64,96},{96,128},{128,160},{160,192},{192,224},{224... | collective-permute-start | bytes 983048 | tf_op jit(solution)/shard_map/ppermute | solution.py:40
  149.6 1.0 bitcast_add_fusion.4
  150.8 3.4 %collective-permute-done.7 = f32[2,64,640]{2,1,0:T(8,128)S(1)} collective-permute-done((f32[2,64,640]{2,1,0:T(8,128)S(1)}, f32[2,64,640]{2,1,0:T(8,128)S(1)}, u32[]{:S(2)}, u32[]{:S(2)}) %collective-permute-start.7) | collective-permute-done | bytes 327712 | tf_op jit(solution)/shard_map/ppermute | solution.py:40
  155.2 4.0 %collective-permute-start.8 = (f32[2,64,640]{2,1,0:T(8,128)S(1)}, f32[2,64,640]{2,1,0:T(8,128)S(1)}, u32[]{:S(2)}, u32[]{:S(2)}) collective-permute-start(f32[2,64,640]{2,1,0:T(8,128)S(1)} %bitcast_add_fusion.10), channel_id=1, source_target_pairs={{0,32},{32,64},{64,96},{96,128},{128,160},{160,192},{192,224},{224... | collective-permute-start | bytes 983048 | tf_op jit(solution)/shard_map/ppermute | solution.py:40
  159.2 1.0 bitcast_add_fusion.3
  160.4 3.5 %collective-permute-done.8 = f32[2,64,640]{2,1,0:T(8,128)S(1)} collective-permute-done((f32[2,64,640]{2,1,0:T(8,128)S(1)}, f32[2,64,640]{2,1,0:T(8,128)S(1)}, u32[]{:S(2)}, u32[]{:S(2)}) %collective-permute-start.8) | collective-permute-done | bytes 327712 | tf_op jit(solution)/shard_map/ppermute | solution.py:40
  163.8 1.0 bitcast_add_fusion.9
  164.9 3.8 %collective-permute-start.9 = (f32[2,64,640]{2,1,0:T(8,128)S(1)}, f32[2,64,640]{2,1,0:T(8,128)S(1)}, u32[]{:S(2)}, u32[]{:S(2)}) collective-permute-start(f32[2,64,640]{2,1,0:T(8,128)S(1)} %bitcast_add_fusion.9), channel_id=1, source_target_pairs={{0,32},{32,64},{64,96},{96,128},{128,160},{160,192},{192,224},{224... | collective-permute-start | bytes 983048 | tf_op jit(solution)/shard_map/ppermute | solution.py:40
  168.9 1.0 bitcast_add_fusion.2
  170.0 3.2 %collective-permute-done.9 = f32[2,64,640]{2,1,0:T(8,128)S(1)} collective-permute-done((f32[2,64,640]{2,1,0:T(8,128)S(1)}, f32[2,64,640]{2,1,0:T(8,128)S(1)}, u32[]{:S(2)}, u32[]{:S(2)}) %collective-permute-start.9) | collective-permute-done | bytes 327712 | tf_op jit(solution)/shard_map/ppermute | solution.py:40
  174.2 4.0 %collective-permute-done.16 = f32[2,64,640]{2,1,0:T(8,128)S(1)} collective-permute-done((f32[2,64,640]{2,1,0:T(8,128)S(1)}, f32[2,64,640]{2,1,0:T(8,128)S(1)}, u32[]{:S(2)}, u32[]{:S(2)}) %collective-permute-start.16) | collective-permute-done | bytes 327712 | tf_op jit(solution)/shard_map/ppermute | solution.py:40
  178.2 1.0 bitcast_add_fusion.1
  179.3 2.1 %collective-permute-start.17 = (f32[64,1280]{1,0:T(8,128)S(1)}, f32[64,1280]{1,0:T(8,128)S(1)}, u32[]{:S(2)}, u32[]{:S(2)}) collective-permute-start(f32[64,1280]{1,0:T(8,128)S(1)} %fusion.6), channel_id=1, source_target_pairs={{0,16},{16,0},{1,17},{17,1},{2,18},{18,2},{3,19},{19,3},{4,20},{20... | collective-permute-start | bytes 983048 | tf_op jit(solution)/shard_map/ppermute | solution.py:52
  182.7 12.4 %collective-permute-done.17 = f32[64,1280]{1,0:T(8,128)S(1)} collective-permute-done((f32[64,1280]{1,0:T(8,128)S(1)}, f32[64,1280]{1,0:T(8,128)S(1)}, u32[]{:S(2)}, u32[]{:S(2)}) %collective-permute-start.17) | collective-permute-done | bytes 327712 | tf_op jit(solution)/shard_map/ppermute | solution.py:52
  196.7 1.2 copy.34
  198.0 1.7 add_convert_fusion
  (69 shorter events, 11.9 us)
Async XLA Ops:
  7.2 4.0 %copy-start = (bf16[2,256,2048]{2,1,0:T(8,128)(2,1)S(1)}, bf16[2,256,2048]{2,1,0:T(8,128)(2,1)}, u32[]{:S(2)}) copy-start(bf16[2,256,2048]{2,1,0:T(8,128)(2,1)} %param.5) | copy-start | bytes 6291460
  7.2 189.5 %reduce-scatter.2.cloned.1.call-start = ((), (), s32[]{:S(2)}) async-start(), calls=%async_computation.1 | async-start | bytes 4718592 | tf_op jit(solution)/shard_map/reduce_scatter | solution.py:94
  11.2 2.3 %copy-start.3 = (bf16[2048,256]{1,0:T(8,128)(2,1)}, bf16[2048,256]{1,0:T(8,128)(2,1)S(1)}, u32[]{:S(2)}) copy-start(bf16[2048,256]{1,0:T(8,128)(2,1)S(1)} %get-tuple-element.8) | copy-start | bytes 3145732
  11.2 9.6 %copy-start.13 = (s32[2]{0:T(128)S(1)}, s32[2]{0:T(128)}, u32[]{:S(2)}) copy-start(s32[2]{0:T(128)} %param.9) | copy-start | bytes 28
  15.8 27.7 %collective-permute-start = (f32[2,256,512]{1,0,2:T(2,128)}, f32[2,256,512]{1,0,2:T(2,128)}, u32[]{:S(2)}, u32[]{:S(2)}) collective-permute-start(f32[2,256,512]{1,0,2:T(2,128)} %copy.28), channel_id=1, source_target_pairs={{0,32},{8,40},{16,48},{24,56},{32,64},{40,72},{48,80},{56,88},{64,... | collective-permute-start | bytes 3145736 | tf_op jit(solution)/shard_map/ppermute | solution.py:15
  20.9 3.0 %copy-start.6 = (bf16[2,256,2048]{2,1,0:T(8,128)(2,1)S(1)}, bf16[2,256,2048]{2,1,0:T(8,128)(2,1)}, u32[]{:S(2)}) copy-start(bf16[2,256,2048]{2,1,0:T(8,128)(2,1)} %param.6) | copy-start | bytes 6291460
  24.1 23.9 %copy-start.5 = (bf16[2,256,2048]{2,1,0:T(8,128)(2,1)}, bf16[2,256,2048]{2,1,0:T(8,128)(2,1)S(1)}, u32[]{:S(2)}) copy-start(bf16[2,256,2048]{2,1,0:T(8,128)(2,1)S(1)} %broadcast_select_fusion) | copy-start | bytes 6291460
  43.5 1.6 copy-start.14
  46.1 2.8 %copy-start.11 = (bf16[512,256]{0,1:T(8,128)(2,1)}, bf16[512,256]{0,1:T(8,128)(2,1)S(1)}, u32[]{:S(2)}) copy-start(bf16[512,256]{0,1:T(8,128)(2,1)S(1)} %get-tuple-element.10) | copy-start | bytes 786436
  46.2 16.7 %collective-permute-start.1 = (bf16[2,256,512]{1,2,0:T(8,128)(2,1)S(1)}, bf16[2,256,512]{1,2,0:T(8,128)(2,1)S(1)}, u32[]{:S(2)}, u32[]{:S(2)}) collective-permute-start(bf16[2,256,512]{1,2,0:T(8,128)(2,1)S(1)} %bitcast.102), channel_id=1, source_target_pairs={{32,0},{40,8},{48,16},{56,24},{64,32},{72,40},{80,48},{88,56},{96,... | collective-permute-start | bytes 1572872 | tf_op jit(solution)/shard_map/ppermute | solution.py:15
  62.8 0.8 copy-start.7
  80.5 5.4 %copy-start.9 = (bf16[2048,256]{1,0:T(8,128)(2,1)S(1)}, bf16[2048,256]{1,0:T(8,128)(2,1)}, u32[]{:S(2)}) copy-start(bf16[2048,256]{1,0:T(8,128)(2,1)} %get-tuple-element.6) | copy-start | bytes 3145732
  80.5 5.5 %copy-start.10 = (bf16[2048,256]{1,0:T(8,128)(2,1)S(1)}, bf16[2048,256]{1,0:T(8,128)(2,1)}, u32[]{:S(2)}) copy-start(bf16[2048,256]{1,0:T(8,128)(2,1)} %get-tuple-element.7) | copy-start | bytes 3145732
  80.5 5.5 %copy-start.12 = (bf16[512,256]{0,1:T(8,128)(2,1)S(1)}, bf16[512,256]{0,1:T(8,128)(2,1)}, u32[]{:S(2)}) copy-start(bf16[512,256]{0,1:T(8,128)(2,1)} %copy-done.11) | copy-start | bytes 786436
  85.9 3.3 %copy-start.8 = (bf16[2,256,512]{1,2,0:T(8,128)(2,1)S(1)}, bf16[2,256,512]{1,2,0:T(8,128)(2,1)}, u32[]{:S(2)}) copy-start(bf16[2,256,512]{1,2,0:T(8,128)(2,1)} %copy-done.7) | copy-start | bytes 1572868
  86.0 3.5 %copy-start.4 = (bf16[2048,256]{1,0:T(8,128)(2,1)S(1)}, bf16[2048,256]{1,0:T(8,128)(2,1)}, u32[]{:S(2)}) copy-start(bf16[2048,256]{1,0:T(8,128)(2,1)} %copy-done.3) | copy-start | bytes 3145732
  86.0 9.1 %collective-permute-start.2 = (f32[8,2,64,1280]{3,2,1,0:T(8,128)}, f32[8,2,64,1280]{3,2,1,0:T(8,128)}, u32[]{:S(2)}, u32[]{:S(2)}) collective-permute-start(f32[8,2,64,1280]{3,2,1,0:T(8,128)} %dynamic-slice_bitcast_fusion), channel_id=1, source_target_pairs={{0,8},{8,0},{1,9},{9,1},{2,10},{10,2},{3,11},{11,3},{4,12},{12,4},... | collective-permute-start | bytes 15728648 | tf_op jit(solution)/shard_map/ppermute | solution.py:52
  101.8 1.5 copy-start.2
  103.4 10.2 %collective-permute-start.3 = (f32[2,64,640]{2,1,0:T(8,128)S(1)}, f32[2,64,640]{2,1,0:T(8,128)S(1)}, u32[]{:S(2)}, u32[]{:S(2)}) collective-permute-start(f32[2,64,640]{2,1,0:T(8,128)S(1)} %dynamic-slice_bitcast_fusion.2), channel_id=1, source_target_pairs={{0,32},{32,64},{64,96},{96,128},{128,160},{160,192},{192,224},{224... | collective-permute-start | bytes 983048 | tf_op jit(solution)/shard_map/ppermute | solution.py:40
  106.2 11.4 %collective-permute-start.10 = (f32[2,64,640]{2,1,0:T(8,128)S(1)}, f32[2,64,640]{2,1,0:T(8,128)S(1)}, u32[]{:S(2)}, u32[]{:S(2)}) collective-permute-start(f32[2,64,640]{2,1,0:T(8,128)S(1)} %dynamic-slice_bitcast_fusion.1), channel_id=1, source_target_pairs={{0,224},{32,0},{64,32},{96,64},{128,96},{160,128},{192,160},{224,1... | collective-permute-start | bytes 983048 | tf_op jit(solution)/shard_map/ppermute | solution.py:40
  114.5 9.8 %collective-permute-start.4 = (f32[2,64,640]{2,1,0:T(8,128)S(1)}, f32[2,64,640]{2,1,0:T(8,128)S(1)}, u32[]{:S(2)}, u32[]{:S(2)}) collective-permute-start(f32[2,64,640]{2,1,0:T(8,128)S(1)} %bitcast_add_fusion.14), channel_id=1, source_target_pairs={{0,32},{32,64},{64,96},{96,128},{128,160},{160,192},{192,224},{224... | collective-permute-start | bytes 983048 | tf_op jit(solution)/shard_map/ppermute | solution.py:40
  118.6 10.5 %collective-permute-start.11 = (f32[2,64,640]{2,1,0:T(8,128)S(1)}, f32[2,64,640]{2,1,0:T(8,128)S(1)}, u32[]{:S(2)}, u32[]{:S(2)}) collective-permute-start(f32[2,64,640]{2,1,0:T(8,128)S(1)} %bitcast_add_fusion.7), channel_id=1, source_target_pairs={{0,224},{32,0},{64,32},{96,64},{128,96},{160,128},{192,160},{224,1... | collective-permute-start | bytes 983048 | tf_op jit(solution)/shard_map/ppermute | solution.py:40
  125.3 9.7 %collective-permute-start.5 = (f32[2,64,640]{2,1,0:T(8,128)S(1)}, f32[2,64,640]{2,1,0:T(8,128)S(1)}, u32[]{:S(2)}, u32[]{:S(2)}) collective-permute-start(f32[2,64,640]{2,1,0:T(8,128)S(1)} %bitcast_add_fusion.13), channel_id=1, source_target_pairs={{0,32},{32,64},{64,96},{96,128},{128,160},{160,192},{192,224},{224... | collective-permute-start | bytes 983048 | tf_op jit(solution)/shard_map/ppermute | solution.py:40
  130.1 9.7 %collective-permute-start.12 = (f32[2,64,640]{2,1,0:T(8,128)S(1)}, f32[2,64,640]{2,1,0:T(8,128)S(1)}, u32[]{:S(2)}, u32[]{:S(2)}) collective-permute-start(f32[2,64,640]{2,1,0:T(8,128)S(1)} %bitcast_add_fusion.6), channel_id=1, source_target_pairs={{0,224},{32,0},{64,32},{96,64},{128,96},{160,128},{192,160},{224,1... | collective-permute-start | bytes 983048 | tf_op jit(solution)/shard_map/ppermute | solution.py:40
  136.0 8.8 %collective-permute-start.6 = (f32[2,64,640]{2,1,0:T(8,128)S(1)}, f32[2,64,640]{2,1,0:T(8,128)S(1)}, u32[]{:S(2)}, u32[]{:S(2)}) collective-permute-start(f32[2,64,640]{2,1,0:T(8,128)S(1)} %bitcast_add_fusion.12), channel_id=1, source_target_pairs={{0,32},{32,64},{64,96},{96,128},{128,160},{160,192},{192,224},{224... | collective-permute-start | bytes 983048 | tf_op jit(solution)/shard_map/ppermute | solution.py:40
  140.8 8.8 %collective-permute-start.13 = (f32[2,64,640]{2,1,0:T(8,128)S(1)}, f32[2,64,640]{2,1,0:T(8,128)S(1)}, u32[]{:S(2)}, u32[]{:S(2)}) collective-permute-start(f32[2,64,640]{2,1,0:T(8,128)S(1)} %bitcast_add_fusion.5), channel_id=1, source_target_pairs={{0,224},{32,0},{64,32},{96,64},{128,96},{160,128},{192,160},{224,1... | collective-permute-start | bytes 983048 | tf_op jit(solution)/shard_map/ppermute | solution.py:40
  145.9 8.4 %collective-permute-start.7 = (f32[2,64,640]{2,1,0:T(8,128)S(1)}, f32[2,64,640]{2,1,0:T(8,128)S(1)}, u32[]{:S(2)}, u32[]{:S(2)}) collective-permute-start(f32[2,64,640]{2,1,0:T(8,128)S(1)} %bitcast_add_fusion.11), channel_id=1, source_target_pairs={{0,32},{32,64},{64,96},{96,128},{128,160},{160,192},{192,224},{224... | collective-permute-start | bytes 983048 | tf_op jit(solution)/shard_map/ppermute | solution.py:40
  150.7 8.6 %collective-permute-start.14 = (f32[2,64,640]{2,1,0:T(8,128)S(1)}, f32[2,64,640]{2,1,0:T(8,128)S(1)}, u32[]{:S(2)}, u32[]{:S(2)}) collective-permute-start(f32[2,64,640]{2,1,0:T(8,128)S(1)} %bitcast_add_fusion.4), channel_id=1, source_target_pairs={{0,224},{32,0},{64,32},{96,64},{128,96},{160,128},{192,160},{224,1... | collective-permute-start | bytes 983048 | tf_op jit(solution)/shard_map/ppermute | solution.py:40
  155.2 8.6 %collective-permute-start.8 = (f32[2,64,640]{2,1,0:T(8,128)S(1)}, f32[2,64,640]{2,1,0:T(8,128)S(1)}, u32[]{:S(2)}, u32[]{:S(2)}) collective-permute-start(f32[2,64,640]{2,1,0:T(8,128)S(1)} %bitcast_add_fusion.10), channel_id=1, source_target_pairs={{0,32},{32,64},{64,96},{96,128},{128,160},{160,192},{192,224},{224... | collective-permute-start | bytes 983048 | tf_op jit(solution)/shard_map/ppermute | solution.py:40
  160.3 8.6 %collective-permute-start.15 = (f32[2,64,640]{2,1,0:T(8,128)S(1)}, f32[2,64,640]{2,1,0:T(8,128)S(1)}, u32[]{:S(2)}, u32[]{:S(2)}) collective-permute-start(f32[2,64,640]{2,1,0:T(8,128)S(1)} %bitcast_add_fusion.3), channel_id=1, source_target_pairs={{0,224},{32,0},{64,32},{96,64},{128,96},{160,128},{192,160},{224,1... | collective-permute-start | bytes 983048 | tf_op jit(solution)/shard_map/ppermute | solution.py:40
  164.9 8.4 %collective-permute-start.9 = (f32[2,64,640]{2,1,0:T(8,128)S(1)}, f32[2,64,640]{2,1,0:T(8,128)S(1)}, u32[]{:S(2)}, u32[]{:S(2)}) collective-permute-start(f32[2,64,640]{2,1,0:T(8,128)S(1)} %bitcast_add_fusion.9), channel_id=1, source_target_pairs={{0,32},{32,64},{64,96},{96,128},{128,160},{160,192},{192,224},{224... | collective-permute-start | bytes 983048 | tf_op jit(solution)/shard_map/ppermute | solution.py:40
  169.9 8.4 %collective-permute-start.16 = (f32[2,64,640]{2,1,0:T(8,128)S(1)}, f32[2,64,640]{2,1,0:T(8,128)S(1)}, u32[]{:S(2)}, u32[]{:S(2)}) collective-permute-start(f32[2,64,640]{2,1,0:T(8,128)S(1)} %bitcast_add_fusion.2), channel_id=1, source_target_pairs={{0,224},{32,0},{64,32},{96,64},{128,96},{160,128},{192,160},{224,1... | collective-permute-start | bytes 983048 | tf_op jit(solution)/shard_map/ppermute | solution.py:40
  179.2 20.4 %copy-start.1 = (bf16[2,256,2048]{2,1,0:T(8,128)(2,1)S(1)}, bf16[2,256,2048]{2,1,0:T(8,128)(2,1)}, u32[]{:S(2)}) copy-start(bf16[2,256,2048]{2,1,0:T(8,128)(2,1)} %param.5) | copy-start | bytes 6291460
  179.3 15.7 %collective-permute-start.17 = (f32[64,1280]{1,0:T(8,128)S(1)}, f32[64,1280]{1,0:T(8,128)S(1)}, u32[]{:S(2)}, u32[]{:S(2)}) collective-permute-start(f32[64,1280]{1,0:T(8,128)S(1)} %fusion.6), channel_id=1, source_target_pairs={{0,16},{16,0},{1,17},{17,1},{2,18},{18,2},{3,19},{19,3},{4,20},{20... | collective-permute-start | bytes 983048 | tf_op jit(solution)/shard_map/ppermute | solution.py:52
Sparse Core Ops, SparseCore 0:
  95.1 99.2 reduce-scatter.1

commit v6 on v5

--- a/solution.py
+++ b/solution.py
@@ -30,10 +30,9 @@
 def ring_sum(chunks, axis):
     peers = lax.axis_size(axis)
     at = lax.axis_index(axis)
-    half = chunks.shape[-1] // 2
     sums = []
-    for step, cols in ((1, slice(0, half)), (-1, slice(half, None))):
-        own = chunks[..., cols]
+    for step, half in ((1, 0), (-1, 1)):
+        own = chunks[:, half]
         pairs = [(i, (i + step) % peers) for i in range(peers)]
         acc = lax.dynamic_index_in_dim(own, (at - step) % peers, 0, keepdims=False)
         for s in range(peers - 1):
@@ -42,7 +41,7 @@
                 own, (at - step * (s + 2)) % peers, 0, keepdims=False
             )
         sums.append(acc)
-    return jnp.concatenate(sums, axis=-1)
+    return jnp.stack(sums)
 
 
 def swap_sum(parts, axis):
@@ -52,10 +51,16 @@
     return keep + lax.ppermute(give, axis, [(0, 1), (1, 0)])
 
 
-def time_reduce_scatter(x):
+def time_reduce_scatter(left, right):
     outer, mid, inner = (lax.axis_size(a) for a in TIME)
-    blocks = x.reshape(outer, mid, inner, x.shape[0] // (outer * mid * inner), x.shape[1])
-    blocks = swap_sum(jnp.moveaxis(blocks, 2, 0), TIME[2])
+    split = left.reshape(left.shape[0], outer, mid, inner, -1)
+    me = lax.axis_index(TIME[2])
+    keep = lax.dynamic_index_in_dim(split, me, 3, keepdims=False)
+    give = lax.dynamic_index_in_dim(split, 1 - me, 3, keepdims=False)
+    keep = contract_rows(keep.reshape(left.shape[0], -1), right)
+    give = contract_rows(give.reshape(left.shape[0], -1), right)
+    blocks = keep + lax.ppermute(give, TIME[2], [(0, 1), (1, 0)])
+    blocks = blocks.reshape(outer, mid, -1, right.shape[1])
     blocks = ring_sum(blocks, TIME[0])
     return swap_sum(blocks, TIME[1])
 
@@ -96,15 +101,16 @@
     own_rows = lax.dynamic_slice_in_dim(grad_rows, lax.axis_index("chan") * share, share, 2)
     summed = summed.reshape(share, traj, window_extent).transpose(1, 2, 0)
     grad_states = (own_rows.astype(jnp.float32) + summed).astype(jnp.bfloat16)
-    weight_terms = jnp.concatenate(
+    left = jnp.concatenate([rows, grad_flat], axis=0)
+    zeros = jnp.zeros_like(branch_grads)
+    right = jnp.concatenate(
         [
-            contract_rows(rows, branch_grads),
-            contract_rows(rows, later),
-            contract_rows(grad_flat, mixed),
+            jnp.concatenate([branch_grads, later, jnp.zeros_like(mixed)], axis=1),
+            jnp.concatenate([zeros, zeros, mixed], axis=1),
         ],
-        axis=1,
+        axis=0,
     )
-    reduced = time_reduce_scatter(weight_terms)
+    reduced = time_reduce_scatter(left, right)
     scale = lax.rsqrt(jnp.sum(lengths.astype(jnp.float32)))
     part = reduced.shape[0]
     in_summed = reduced[:, : 4 * blocks].reshape(part, 2, 2, blocks).transpose(1, 2, 0, 3)

time: 209 us -> 212 us (1.014)
  other arithmetic: 26.8 us -> 12.6 us
  matrix products: 18.3 us -> 31.3 us
  waiting for transfers between devices: 80.1 us -> 84.8 us
    ppermute x2, waiting for transfers between devices: 32 us -> 14.8 us  [shifted(): return lax.ppermute(x, axis, pairs)]
    dot_general x3 -> x2, matrix products: 3.32 us -> 17.7 us  [contract_rows(): lax.dot_general(left, right, (((0,), (0,)), ((), ())), preferred_element_...]
    reduce_scatter x1, waiting for transfers between devices: 0.01 us -> 12.8 us  [local(): lax.psum_scatter(partial_value, 'chan', scatter_dimension=0, tiled=True)]
    add x14 -> x12, other arithmetic: 14.1 us -> 6.31 us  [ring_sum(): got + lax.dynamic_index_in_dim(own, (at - step * (s + 2)) % peers, 0, kee...]
    ppermute x0 -> x1, waiting for transfers between devices: none -> 6.15 us  [time_reduce_scatter(): blocks = keep + lax.ppermute(give, TIME[2], [(0, 1), (1, 0)])]
    squeeze x1 -> x0, local copies, waits for them, and re-layouts: 5.43 us -> none  [swap_sum(): give = lax.dynamic_index_in_dim(parts, 1 - me, 0, keepdims=False)]
    add x2 -> x1, other arithmetic: 4.83 us -> 0.07 us  [swap_sum(): return keep + lax.ppermute(give, axis, [(0, 1), (1, 0)])]
    concatenate x1 -> x0, other arithmetic: 4.34 us -> none  [local(): jnp.concatenate([contract_rows(rows, branch_grads), contract_rows(rows, l...]
  transfers between devices with their start and end apart: 19 -> 19, of which waited for: 12 -> 15; matrix products, arithmetic and copies ran while one was open for 19% -> 18% of each run, Pallas kernels for 0% -> 0%
where the time goes in v6:
time: 212 us; the launch traced here: 209 us
  waiting for transfers between devices  84.8 us (40%)
  starting transfers between devices  33.6 us (16%)
  local copies, waits for them, and re-layouts  31.5 us (15%)
  matrix products  31.3 us (15%)
  between operations  15.2 us (7%)
  other arithmetic  12.6 us (6%)
    ppermute x14, waiting for transfers between devices, ring_sum(): got = lax.ppermute(acc, axis, pairs)  37.4 us
    ppermute x14, starting transfers between devices, ring_sum(): got = lax.ppermute(acc, axis, pairs)  24.7 us
    dot_general x2, matrix products, contract_rows(): lax.dot_general(left, right, (((0,), (0,)), ((), ())), preferred_element_...  17.7 us
    ppermute x2, waiting for transfers between devices, shifted(): return lax.ppermute(x, axis, pairs)  14.8 us
    ppermute x1, waiting for transfers between devices, swap_sum(): return keep + lax.ppermute(give, axis, [(0, 1), (1, 0)])  13.6 us
    reduce_scatter x1, waiting for transfers between devices, local(): lax.psum_scatter(partial_value, 'chan', scatter_dimension=0, tiled=True)  12.8 us
    dot_general x3, matrix products, contract_cols(): lax.dot_general(left, right, (((1,), (1,)), ((), ())), preferred_element_...  7.76 us
    concatenate x3, local copies, waits for them, and re-layouts, local(): left = jnp.concatenate([rows, grad_flat], axis=0)  7.29 us
  transfers between devices with their start and end apart: 19, of which 15 were waited for; matrix products, arithmetic and copies ran while one was open for 18% of the time, Pallas kernels for 0%

profile of v6, /device:TPU:98, one launch (start us, length us, event | category | flops | bytes accessed | tf_op | source)
XLA Modules:
  0.0 209.1 jit_solution(11345489757947312250)
XLA Ops:
  7.2 3.9 %slice_bitcast_fusion.1 = (bf16[2048,256]{1,0:T(8,128)(2,1)S(1)}, bf16[2048,256]{1,0:T(8,128)(2,1)}, bf16[2048,256]{1,0:T(8,128)(2,1)}, bf16[2048,256]{1,0:T(8,128)(2,1)S(1)}) fusion(bf16[2,2,2048,256]{3,2,1,0:T(8,128)(2,1)} %param.7), kind=kLoop, calls=%fused_computation.12 | loop fusion | bytes 8388608 | tf_op jit(solution)/shard_map/squeeze | solution.py:75
  11.1 2.3 %fusion.2 = f32[512,512]{0,1:T(8,128)} fusion(bf16[512,2048]{1,0:T(8,128)(2,1)S(1)} %bitcast.99, bf16[2048,256]{1,0:T(8,128)(2,1)S(1)} %get-tuple-element.10, bf16[2048,256]{1,0:T(8,128)(2,1)S(1)} %get-tuple-element.7), kind=kOutput, calls=%fused_computation.9 | convolution fusion | flops 1077936128 | bytes 5242880 | tf_op jit(solution)/shard_map/dot_general | solution.py:76
  13.5 2.2 %copy.11 = f32[2,256,512]{1,0,2:T(2,128)} copy(f32[2,256,512]{2,1,0:T(8,128)} %bitcast.104) | data formatting | bytes 2097152 | tf_op jit(solution)/shard_map/reshape | solution.py:78
  15.7 5.0 %collective-permute-start = (f32[2,256,512]{1,0,2:T(2,128)}, f32[2,256,512]{1,0,2:T(2,128)}, u32[]{:S(2)}, u32[]{:S(2)}) collective-permute-start(f32[2,256,512]{1,0,2:T(2,128)} %copy.11), channel_id=1, source_target_pairs={{0,32},{8,40},{16,48},{24,56},{32,64},{40,72},{48,80},{56,88},{64,... | collective-permute-start | bytes 3145736 | tf_op jit(solution)/shard_map/ppermute | solution.py:15
  20.7 4.8 %copy.13 = bf16[2,256,2048]{1,0,2:T(2,128)(2,1)S(1)} copy(bf16[2,256,2048]{2,1,0:T(8,128)(2,1)} %param.5) | data formatting | bytes 4194304 | tf_op args[0]
  25.6 2.6 %concatenate.31 = bf16[512,8,2,2,64]{0,4,3,2,1:T(8,128)(2,1)} reshape(bf16[2,256,2048]{1,0,2:T(2,128)(2,1)S(1)} %copy.13) | data formatting | bytes 4194304 | tf_op jit(solution)/shard_map/concatenate | solution.py:104
  28.3 1.8 broadcast_select_fusion
  30.1 4.2 %copy.14 = bf16[2,256,2048]{1,0,2:T(2,128)(2,1)} copy(bf16[2,256,2048]{2,1,0:T(8,128)(2,1)S(1)} %broadcast_select_fusion) | data formatting | bytes 4194304 | tf_op jit(solution)/shard_map/jit(_where)/select_n | solution.py:86
  34.3 4.4 %concatenate.32 = bf16[512,8,2,2,64]{0,4,3,2,1:T(8,128)(2,1)} reshape(bf16[2,256,2048]{1,0,2:T(2,128)(2,1)} %copy.14) | data formatting | bytes 4194304 | tf_op jit(solution)/shard_map/concatenate | solution.py:104
  38.7 3.5 %convolution_bitcast_fusion = f32[512,512]{0,1:T(8,128)S(1)} fusion(bf16[512,2048]{1,0:T(8,128)(2,1)} %bitcast.98, bf16[2048,256]{1,0:T(8,128)(2,1)} %get-tuple-element.8, bf16[2048,256]{1,0:T(8,128)(2,1)} %get-tuple-element.9), kind=kOutput, calls=%fused_computation.8 | convolution fusion | flops 1077936128 | bytes 5242880 | tf_op jit(solution)/shard_map/dot_general | solution.py:80
  42.3 1.2 collective-permute-done
  43.5 1.3 copy.17
  45.0 1.6 multiply_convert_fusion.2
  47.5 2.1 collective-permute-start.1
  50.7 13.6 %collective-permute-done.1 = bf16[2,256,512]{1,0,2:T(2,128)(2,1)S(1)} collective-permute-done((bf16[2,256,512]{1,0,2:T(2,128)(2,1)S(1)}, bf16[2,256,512]{1,0,2:T(2,128)(2,1)S(1)}, u32[]{:S(2)}, u32[]{:S(2)}) %collective-permute-start.1) | collective-permute-done | bytes 524320 | tf_op jit(solution)/shard_map/ppermute | solution.py:15
  64.4 5.2 %fusion.19 = f32[1024,1280]{1,0:T(8,128)} fusion(bf16[1024,1024]{0,1:T(8,128)(2,1)S(1)} %bitcast.97, bf16[512,256]{0,1:T(8,128)(2,1)S(1)} %copy-done.14, bf16[512,256]{0,1:T(8,128)(2,1)S(1)} %broadcast_in_dim.19, bf16[512,512]{0,1:T(8,128)(2,1)S(1)} %bitcast.101, bf16[512,256]{0,1:T(8,128)(2,1)S(1)} %copy-done.11, bf16[512,256]{0,1:T(8,128)(2,1)S(1)} %get-tuple-element.11), kind=kOutput, calls=%fused_computation.67 | convolution fusion | flops 2700083200 | bytes 8912896 | tf_op jit(solution)/shard_map/dot_general | solution.py:19
  69.7 2.8 %fusion.3 = f32[2048,512]{1,0:T(8,128)S(1)} fusion(bf16[2048,256]{1,0:T(8,128)(2,1)} %get-tuple-element.8, bf16[2048,256]{1,0:T(8,128)(2,1)} %get-tuple-element.9, bf16[512,256]{0,1:T(8,128)(2,1)S(1)} %copy-done.12, bf16[512,256]{0,1:T(8,128)(2,1)S(1)} %get-tuple-element.11), kind=kOutput, calls=%fused_computation.10 | convolution fusion | flops 1078984704 | bytes 6815744 | tf_op jit(solution)/shard_map/dot_general | solution.py:25
  72.5 6.2 %collective-permute-done.2 = f32[1024,1280]{1,0:T(8,128)} collective-permute-done((f32[1024,1280]{1,0:T(8,128)}, f32[1024,1280]{1,0:T(8,128)}, u32[]{:S(2)}, u32[]{:S(2)}) %collective-permute-start.2) | collective-permute-done | bytes 5242912 | tf_op jit(solution)/shard_map/ppermute | solution.py:62
  78.7 12.5 %convolution_add_fusion = f32[1024,1280]{1,0:T(8,128)S(1)} fusion(f32[1024,1280]{1,0:T(8,128)} %collective-permute-done.2, bf16[1024,1024]{0,1:T(8,128)(2,1)S(1)} %bitcast.96, bf16[512,256]{0,1:T(8,128)(2,1)S(1)} %copy-done.15, bf16[512,256]{0,1:T(8,128)(2,1)S(1)} %broadcast_in_dim.19, bf16[512,512]{0,1:T(8,128)(2,1)S(1)} %bitcast.102, ...), kind=kOutput, calls=%fused_computation.2 | convolution fusion | flops 2701393920 | bytes 14155776 | tf_op jit(solution)/shard_map/dot_general | solution.py:19
  91.2 2.0 fusion.22
  93.2 1.7 dynamic-slice_bitcast_fusion.1
  94.9 1.7 collective-permute-start.3
  96.7 3.3 %convolution_add_fusion.1 = f32[2048,512]{1,0:T(8,128)} fusion(f32[2048,512]{1,0:T(8,128)S(1)} %fusion.3, bf16[512,512]{0,1:T(8,128)(2,1)S(1)} %bitcast.103, bf16[2048,256]{1,0:T(8,128)(2,1)S(1)} %copy-done.8, bf16[2048,256]{1,0:T(8,128)(2,1)S(1)} %copy-done.6), kind=kOutput, calls=%fused_computation.3 | convolution fusion | flops 1078984704 | bytes 11010048 | tf_op jit(solution)/shard_map/dot_general | solution.py:25
  100.5 4.4 %collective-permute-done.3 = f32[64,1280]{1,0:T(8,128)S(1)} collective-permute-done((f32[64,1280]{1,0:T(8,128)}, f32[64,1280]{1,0:T(8,128)S(1)}, u32[]{:S(2)}, u32[]{:S(2)}) %collective-permute-start.3) | collective-permute-done | bytes 327712 | tf_op jit(solution)/shard_map/ppermute | solution.py:39
  105.9 3.0 %collective-permute-start.4 = (f32[64,1280]{1,0:T(8,128)S(1)}, f32[64,1280]{1,0:T(8,128)S(1)}, u32[]{:S(2)}, u32[]{:S(2)}) collective-permute-start(f32[64,1280]{1,0:T(8,128)S(1)} %bitcast_add_fusion.13), channel_id=1, source_target_pairs={{0,32},{32,64},{64,96},{96,128},{128,160},{160,192},{192,224},{224... | collective-permute-start | bytes 983048 | tf_op jit(solution)/shard_map/ppermute | solution.py:39
  108.9 1.9 collective-permute-done.10
  111.0 4.4 %collective-permute-done.4 = f32[64,1280]{1,0:T(8,128)S(1)} collective-permute-done((f32[64,1280]{1,0:T(8,128)S(1)}, f32[64,1280]{1,0:T(8,128)S(1)}, u32[]{:S(2)}, u32[]{:S(2)}) %collective-permute-start.4) | collective-permute-done | bytes 327712 | tf_op jit(solution)/shard_map/ppermute | solution.py:39
  115.4 1.0 bitcast_add_fusion.12
  116.4 3.8 %collective-permute-start.5 = (f32[64,1280]{1,0:T(8,128)S(1)}, f32[64,1280]{1,0:T(8,128)S(1)}, u32[]{:S(2)}, u32[]{:S(2)}) collective-permute-start(f32[64,1280]{1,0:T(8,128)S(1)} %bitcast_add_fusion.12), channel_id=1, source_target_pairs={{0,32},{32,64},{64,96},{96,128},{128,160},{160,192},{192,224},{224... | collective-permute-start | bytes 983048 | tf_op jit(solution)/shard_map/ppermute | solution.py:39
  121.1 4.6 %collective-permute-done.5 = f32[64,1280]{1,0:T(8,128)S(1)} collective-permute-done((f32[64,1280]{1,0:T(8,128)S(1)}, f32[64,1280]{1,0:T(8,128)S(1)}, u32[]{:S(2)}, u32[]{:S(2)}) %collective-permute-start.5) | collective-permute-done | bytes 327712 | tf_op jit(solution)/shard_map/ppermute | solution.py:39
  125.7 1.0 bitcast_add_fusion.11
  126.8 3.8 %collective-permute-start.6 = (f32[64,1280]{1,0:T(8,128)S(1)}, f32[64,1280]{1,0:T(8,128)S(1)}, u32[]{:S(2)}, u32[]{:S(2)}) collective-permute-start(f32[64,1280]{1,0:T(8,128)S(1)} %bitcast_add_fusion.11), channel_id=1, source_target_pairs={{0,32},{32,64},{64,96},{96,128},{128,160},{160,192},{192,224},{224... | collective-permute-start | bytes 983048 | tf_op jit(solution)/shard_map/ppermute | solution.py:39
  130.7 4.7 %collective-permute-done.6 = f32[64,1280]{1,0:T(8,128)S(1)} collective-permute-done((f32[64,1280]{1,0:T(8,128)S(1)}, f32[64,1280]{1,0:T(8,128)S(1)}, u32[]{:S(2)}, u32[]{:S(2)}) %collective-permute-start.6) | collective-permute-done | bytes 327712 | tf_op jit(solution)/shard_map/ppermute | solution.py:39
  135.3 1.0 bitcast_add_fusion.10
  136.3 3.8 %collective-permute-start.7 = (f32[64,1280]{1,0:T(8,128)S(1)}, f32[64,1280]{1,0:T(8,128)S(1)}, u32[]{:S(2)}, u32[]{:S(2)}) collective-permute-start(f32[64,1280]{1,0:T(8,128)S(1)} %bitcast_add_fusion.10), channel_id=1, source_target_pairs={{0,32},{32,64},{64,96},{96,128},{128,160},{160,192},{192,224},{224... | collective-permute-start | bytes 983048 | tf_op jit(solution)/shard_map/ppermute | solution.py:39
  140.3 4.5 %collective-permute-done.7 = f32[64,1280]{1,0:T(8,128)S(1)} collective-permute-done((f32[64,1280]{1,0:T(8,128)S(1)}, f32[64,1280]{1,0:T(8,128)S(1)}, u32[]{:S(2)}, u32[]{:S(2)}) %collective-permute-start.7) | collective-permute-done | bytes 327712 | tf_op jit(solution)/shard_map/ppermute | solution.py:39
  144.7 1.0 bitcast_add_fusion.9
  145.7 3.8 %collective-permute-start.8 = (f32[64,1280]{1,0:T(8,128)S(1)}, f32[64,1280]{1,0:T(8,128)S(1)}, u32[]{:S(2)}, u32[]{:S(2)}) collective-permute-start(f32[64,1280]{1,0:T(8,128)S(1)} %bitcast_add_fusion.9), channel_id=1, source_target_pairs={{0,32},{32,64},{64,96},{96,128},{128,160},{160,192},{192,224},{224... | collective-permute-start | bytes 983048 | tf_op jit(solution)/shard_map/ppermute | solution.py:39
  149.6 5.0 %collective-permute-done.8 = f32[64,1280]{1,0:T(8,128)S(1)} collective-permute-done((f32[64,1280]{1,0:T(8,128)S(1)}, f32[64,1280]{1,0:T(8,128)S(1)}, u32[]{:S(2)}, u32[]{:S(2)}) %collective-permute-start.8) | collective-permute-done | bytes 327712 | tf_op jit(solution)/shard_map/ppermute | solution.py:39
  154.7 1.0 bitcast_add_fusion.8
  155.7 3.8 %collective-permute-start.9 = (f32[64,1280]{1,0:T(8,128)S(1)}, f32[64,1280]{1,0:T(8,128)S(1)}, u32[]{:S(2)}, u32[]{:S(2)}) collective-permute-start(f32[64,1280]{1,0:T(8,128)S(1)} %bitcast_add_fusion.8), channel_id=1, source_target_pairs={{0,32},{32,64},{64,96},{96,128},{128,160},{160,192},{192,224},{224... | collective-permute-start | bytes 983048 | tf_op jit(solution)/shard_map/ppermute | solution.py:39
  159.6 4.5 %collective-permute-done.9 = f32[64,1280]{1,0:T(8,128)S(1)} collective-permute-done((f32[64,1280]{1,0:T(8,128)S(1)}, f32[64,1280]{1,0:T(8,128)S(1)}, u32[]{:S(2)}, u32[]{:S(2)}) %collective-permute-start.9) | collective-permute-done | bytes 327712 | tf_op jit(solution)/shard_map/ppermute | solution.py:39
  165.1 2.8 %collective-permute-done.16 = f32[64,1280]{1,0:T(8,128)S(1)} collective-permute-done((f32[64,1280]{1,0:T(8,128)S(1)}, f32[64,1280]{1,0:T(8,128)S(1)}, u32[]{:S(2)}, u32[]{:S(2)}) %collective-permute-start.16) | collective-permute-done | bytes 327712 | tf_op jit(solution)/shard_map/ppermute | solution.py:39
  168.0 1.8 collective-permute-start.17
  171.1 13.6 %collective-permute-done.17 = f32[64,1280]{1,0:T(8,128)S(1)} collective-permute-done((f32[64,1280]{1,0:T(8,128)S(1)}, f32[64,1280]{1,0:T(8,128)S(1)}, u32[]{:S(2)}, u32[]{:S(2)}) %collective-permute-start.17) | collective-permute-done | bytes 327712 | tf_op jit(solution)/shard_map/ppermute | solution.py:51
  186.4 12.8 %reduce-scatter.2.cloned.1.call-done = f32[256,512]{1,0:T(8,128)} async-done(((f32[2048,512]{1,0:T(8,128)}), f32[256,512]{1,0:T(8,128)}) %reduce-scatter.2.cloned.1.call-update) | async-done | bytes 524304 | tf_op jit(solution)/shard_map/reduce_scatter | solution.py:99
  199.3 1.2 copy.16
  200.5 1.7 add_convert_fusion
  (74 shorter events, 8.9 us)
Async XLA Ops:
  7.2 37.8 %copy-start = (bf16[256,2048]{1,0:T(8,128)(2,1)S(1)}, bf16[256,2048]{1,0:T(8,128)(2,1)}, u32[]{:S(2)}) copy-start(bf16[256,2048]{1,0:T(8,128)(2,1)} %param.8) | copy-start | bytes 3145732
  7.2 4.0 %copy-start.9 = (bf16[2,256,2048]{2,1,0:T(8,128)(2,1)S(1)}, bf16[2,256,2048]{2,1,0:T(8,128)(2,1)}, u32[]{:S(2)}) copy-start(bf16[2,256,2048]{2,1,0:T(8,128)(2,1)} %param.5) | copy-start | bytes 6291460
  7.2 192.1 %reduce-scatter.2.cloned.1.call-start = ((), (), s32[]{:S(2)}) async-start(), calls=%async_computation.1 | async-start | bytes 4718592 | tf_op jit(solution)/shard_map/reduce_scatter | solution.py:99
  11.1 2.3 %copy-start.5 = (bf16[2048,256]{1,0:T(8,128)(2,1)}, bf16[2048,256]{1,0:T(8,128)(2,1)S(1)}, u32[]{:S(2)}) copy-start(bf16[2048,256]{1,0:T(8,128)(2,1)S(1)} %get-tuple-element.7) | copy-start | bytes 3145732
  11.1 2.3 %copy-start.7 = (bf16[2048,256]{1,0:T(8,128)(2,1)}, bf16[2048,256]{1,0:T(8,128)(2,1)S(1)}, u32[]{:S(2)}) copy-start(bf16[2048,256]{1,0:T(8,128)(2,1)S(1)} %get-tuple-element.10) | copy-start | bytes 3145732
  15.7 27.7 %collective-permute-start = (f32[2,256,512]{1,0,2:T(2,128)}, f32[2,256,512]{1,0,2:T(2,128)}, u32[]{:S(2)}, u32[]{:S(2)}) collective-permute-start(f32[2,256,512]{1,0,2:T(2,128)} %copy.11), channel_id=1, source_target_pairs={{0,32},{8,40},{16,48},{24,56},{32,64},{40,72},{48,80},{56,88},{64,... | collective-permute-start | bytes 3145736 | tf_op jit(solution)/shard_map/ppermute | solution.py:15
  25.6 2.7 %copy-start.13 = (s32[2]{0:T(128)S(1)}, s32[2]{0:T(128)}, u32[]{:S(2)}) copy-start(s32[2]{0:T(128)} %param.9) | copy-start | bytes 28
  30.1 14.8 %copy-start.2 = (bf16[2,256,2048]{2,1,0:T(8,128)(2,1)}, bf16[2,256,2048]{2,1,0:T(8,128)(2,1)S(1)}, u32[]{:S(2)}) copy-start(bf16[2,256,2048]{2,1,0:T(8,128)(2,1)S(1)} %broadcast_select_fusion) | copy-start | bytes 6291460
  46.6 0.7 copy-start.10
  46.6 2.9 %copy-start.3 = (bf16[512,8,2,2,64]{0,4,3,2,1:T(8,128)(2,1)S(1)}, bf16[512,8,2,2,64]{0,4,3,2,1:T(8,128)(2,1)}, u32[]{:S(2)}) copy-start(bf16[512,8,2,2,64]{0,4,3,2,1:T(8,128)(2,1)} %concatenate.31) | copy-start | bytes 6291460
  47.5 2.3 %copy-start.4 = (bf16[512,8,2,2,64]{0,4,3,2,1:T(8,128)(2,1)S(1)}, bf16[512,8,2,2,64]{0,4,3,2,1:T(8,128)(2,1)}, u32[]{:S(2)}) copy-start(bf16[512,8,2,2,64]{0,4,3,2,1:T(8,128)(2,1)} %concatenate.32) | copy-start | bytes 6291460
  47.5 16.8 %collective-permute-start.1 = (bf16[2,256,512]{1,0,2:T(2,128)(2,1)S(1)}, bf16[2,256,512]{1,0,2:T(2,128)(2,1)S(1)}, u32[]{:S(2)}, u32[]{:S(2)}) collective-permute-start(bf16[2,256,512]{1,0,2:T(2,128)(2,1)S(1)} %reshape.114), channel_id=1, source_target_pairs={{32,0},{40,8},{48,16},{56,24},{64,32},{72,40},{80,48},{88,56},{96,... | collective-permute-start | bytes 1572872 | tf_op jit(solution)/shard_map/ppermute | solution.py:15
  50.1 14.3 %copy-start.11 = (bf16[512,256]{0,1:T(8,128)(2,1)S(1)}, bf16[512,256]{0,1:T(8,128)(2,1)}, u32[]{:S(2)}) copy-start(bf16[512,256]{0,1:T(8,128)(2,1)} %copy-done.10) | copy-start | bytes 786436
  50.1 14.3 %copy-start.14 = (bf16[512,256]{0,1:T(8,128)(2,1)S(1)}, bf16[512,256]{0,1:T(8,128)(2,1)}, u32[]{:S(2)}) copy-start(bf16[512,256]{0,1:T(8,128)(2,1)} %get-tuple-element.13) | copy-start | bytes 786436
  64.4 5.3 %copy-start.12 = (bf16[512,256]{0,1:T(8,128)(2,1)S(1)}, bf16[512,256]{0,1:T(8,128)(2,1)}, u32[]{:S(2)}) copy-start(bf16[512,256]{0,1:T(8,128)(2,1)} %copy-done.10) | copy-start | bytes 786436
  69.7 9.0 %collective-permute-start.2 = (f32[1024,1280]{1,0:T(8,128)}, f32[1024,1280]{1,0:T(8,128)}, u32[]{:S(2)}, u32[]{:S(2)}) collective-permute-start(f32[1024,1280]{1,0:T(8,128)} %fusion.19), channel_id=1, source_target_pairs={{0,8},{8,0},{1,9},{9,1},{2,10},{10,2},{3,11},{11,3},{4,12},{12,4},... | collective-permute-start | bytes 15728648 | tf_op jit(solution)/shard_map/ppermute | solution.py:62
  69.7 9.0 %copy-start.15 = (bf16[512,256]{0,1:T(8,128)(2,1)S(1)}, bf16[512,256]{0,1:T(8,128)(2,1)}, u32[]{:S(2)}) copy-start(bf16[512,256]{0,1:T(8,128)(2,1)} %get-tuple-element.13) | copy-start | bytes 786436
  91.2 5.5 %copy-start.6 = (bf16[2048,256]{1,0:T(8,128)(2,1)S(1)}, bf16[2048,256]{1,0:T(8,128)(2,1)}, u32[]{:S(2)}) copy-start(bf16[2048,256]{1,0:T(8,128)(2,1)} %copy-done.5) | copy-start | bytes 3145732
  91.2 5.5 %copy-start.8 = (bf16[2048,256]{1,0:T(8,128)(2,1)S(1)}, bf16[2048,256]{1,0:T(8,128)(2,1)}, u32[]{:S(2)}) copy-start(bf16[2048,256]{1,0:T(8,128)(2,1)} %copy-done.7) | copy-start | bytes 3145732
  94.9 10.0 %collective-permute-start.3 = (f32[64,1280]{1,0:T(8,128)}, f32[64,1280]{1,0:T(8,128)S(1)}, u32[]{:S(2)}, u32[]{:S(2)}) collective-permute-start(f32[64,1280]{1,0:T(8,128)} %dynamic-slice_bitcast_fusion.1), channel_id=1, source_target_pairs={{0,32},{32,64},{64,96},{96,128},{128,160},{160,192},{192,224},{224... | collective-permute-start | bytes 983048 | tf_op jit(solution)/shard_map/ppermute | solution.py:39
  100.1 10.8 %collective-permute-start.10 = (f32[64,1280]{1,0:T(8,128)S(1)}, f32[64,1280]{1,0:T(8,128)S(1)}, u32[]{:S(2)}, u32[]{:S(2)}) collective-permute-start(f32[64,1280]{1,0:T(8,128)S(1)} %dynamic-slice_bitcast_fusion), channel_id=1, source_target_pairs={{0,224},{32,0},{64,32},{96,64},{128,96},{160,128},{192,160},{224,1... | collective-permute-start | bytes 983048 | tf_op jit(solution)/shard_map/ppermute | solution.py:39
  105.9 9.4 %collective-permute-start.4 = (f32[64,1280]{1,0:T(8,128)S(1)}, f32[64,1280]{1,0:T(8,128)S(1)}, u32[]{:S(2)}, u32[]{:S(2)}) collective-permute-start(f32[64,1280]{1,0:T(8,128)S(1)} %bitcast_add_fusion.13), channel_id=1, source_target_pairs={{0,32},{32,64},{64,96},{96,128},{128,160},{160,192},{192,224},{224... | collective-permute-start | bytes 983048 | tf_op jit(solution)/shard_map/ppermute | solution.py:39
  110.9 9.9 %collective-permute-start.11 = (f32[64,1280]{1,0:T(8,128)S(1)}, f32[64,1280]{1,0:T(8,128)S(1)}, u32[]{:S(2)}, u32[]{:S(2)}) collective-permute-start(f32[64,1280]{1,0:T(8,128)S(1)} %bitcast_add_fusion.6), channel_id=1, source_target_pairs={{0,224},{32,0},{64,32},{96,64},{128,96},{160,128},{192,160},{224,1... | collective-permute-start | bytes 983048 | tf_op jit(solution)/shard_map/ppermute | solution.py:39
  116.4 9.4 %collective-permute-start.5 = (f32[64,1280]{1,0:T(8,128)S(1)}, f32[64,1280]{1,0:T(8,128)S(1)}, u32[]{:S(2)}, u32[]{:S(2)}) collective-permute-start(f32[64,1280]{1,0:T(8,128)S(1)} %bitcast_add_fusion.12), channel_id=1, source_target_pairs={{0,32},{32,64},{64,96},{96,128},{128,160},{160,192},{192,224},{224... | collective-permute-start | bytes 983048 | tf_op jit(solution)/shard_map/ppermute | solution.py:39
  120.8 9.7 %collective-permute-start.12 = (f32[64,1280]{1,0:T(8,128)S(1)}, f32[64,1280]{1,0:T(8,128)S(1)}, u32[]{:S(2)}, u32[]{:S(2)}) collective-permute-start(f32[64,1280]{1,0:T(8,128)S(1)} %bitcast_add_fusion.5), channel_id=1, source_target_pairs={{0,224},{32,0},{64,32},{96,64},{128,96},{160,128},{192,160},{224,1... | collective-permute-start | bytes 983048 | tf_op jit(solution)/shard_map/ppermute | solution.py:39
  126.8 8.6 %collective-permute-start.6 = (f32[64,1280]{1,0:T(8,128)S(1)}, f32[64,1280]{1,0:T(8,128)S(1)}, u32[]{:S(2)}, u32[]{:S(2)}) collective-permute-start(f32[64,1280]{1,0:T(8,128)S(1)} %bitcast_add_fusion.11), channel_id=1, source_target_pairs={{0,32},{32,64},{64,96},{96,128},{128,160},{160,192},{192,224},{224... | collective-permute-start | bytes 983048 | tf_op jit(solution)/shard_map/ppermute | solution.py:39
  130.6 9.5 %collective-permute-start.13 = (f32[64,1280]{1,0:T(8,128)S(1)}, f32[64,1280]{1,0:T(8,128)S(1)}, u32[]{:S(2)}, u32[]{:S(2)}) collective-permute-start(f32[64,1280]{1,0:T(8,128)S(1)} %bitcast_add_fusion.4), channel_id=1, source_target_pairs={{0,224},{32,0},{64,32},{96,64},{128,96},{160,128},{192,160},{224,1... | collective-permute-start | bytes 983048 | tf_op jit(solution)/shard_map/ppermute | solution.py:39
  136.3 8.4 %collective-permute-start.7 = (f32[64,1280]{1,0:T(8,128)S(1)}, f32[64,1280]{1,0:T(8,128)S(1)}, u32[]{:S(2)}, u32[]{:S(2)}) collective-permute-start(f32[64,1280]{1,0:T(8,128)S(1)} %bitcast_add_fusion.10), channel_id=1, source_target_pairs={{0,32},{32,64},{64,96},{96,128},{128,160},{160,192},{192,224},{224... | collective-permute-start | bytes 983048 | tf_op jit(solution)/shard_map/ppermute | solution.py:39
  140.2 9.3 %collective-permute-start.14 = (f32[64,1280]{1,0:T(8,128)S(1)}, f32[64,1280]{1,0:T(8,128)S(1)}, u32[]{:S(2)}, u32[]{:S(2)}) collective-permute-start(f32[64,1280]{1,0:T(8,128)S(1)} %bitcast_add_fusion.3), channel_id=1, source_target_pairs={{0,224},{32,0},{64,32},{96,64},{128,96},{160,128},{192,160},{224,1... | collective-permute-start | bytes 983048 | tf_op jit(solution)/shard_map/ppermute | solution.py:39
  145.7 8.9 %collective-permute-start.8 = (f32[64,1280]{1,0:T(8,128)S(1)}, f32[64,1280]{1,0:T(8,128)S(1)}, u32[]{:S(2)}, u32[]{:S(2)}) collective-permute-start(f32[64,1280]{1,0:T(8,128)S(1)} %bitcast_add_fusion.9), channel_id=1, source_target_pairs={{0,32},{32,64},{64,96},{96,128},{128,160},{160,192},{192,224},{224... | collective-permute-start | bytes 983048 | tf_op jit(solution)/shard_map/ppermute | solution.py:39
  149.5 9.9 %collective-permute-start.15 = (f32[64,1280]{1,0:T(8,128)S(1)}, f32[64,1280]{1,0:T(8,128)S(1)}, u32[]{:S(2)}, u32[]{:S(2)}) collective-permute-start(f32[64,1280]{1,0:T(8,128)S(1)} %bitcast_add_fusion.2), channel_id=1, source_target_pairs={{0,224},{32,0},{64,32},{96,64},{128,96},{160,128},{192,160},{224,1... | collective-permute-start | bytes 983048 | tf_op jit(solution)/shard_map/ppermute | solution.py:39
  155.7 8.4 %collective-permute-start.9 = (f32[64,1280]{1,0:T(8,128)S(1)}, f32[64,1280]{1,0:T(8,128)S(1)}, u32[]{:S(2)}, u32[]{:S(2)}) collective-permute-start(f32[64,1280]{1,0:T(8,128)S(1)} %bitcast_add_fusion.8), channel_id=1, source_target_pairs={{0,32},{32,64},{64,96},{96,128},{128,160},{160,192},{192,224},{224... | collective-permute-start | bytes 983048 | tf_op jit(solution)/shard_map/ppermute | solution.py:39
  159.5 8.4 %collective-permute-start.16 = (f32[64,1280]{1,0:T(8,128)S(1)}, f32[64,1280]{1,0:T(8,128)S(1)}, u32[]{:S(2)}, u32[]{:S(2)}) collective-permute-start(f32[64,1280]{1,0:T(8,128)S(1)} %bitcast_add_fusion.1), channel_id=1, source_target_pairs={{0,224},{32,0},{64,32},{96,64},{128,96},{160,128},{192,160},{224,1... | collective-permute-start | bytes 983048 | tf_op jit(solution)/shard_map/ppermute | solution.py:39
  167.9 34.3 %copy-start.1 = (bf16[256,2048]{1,0:T(8,128)(2,1)S(1)}, bf16[256,2048]{1,0:T(8,128)(2,1)}, u32[]{:S(2)}) copy-start(bf16[256,2048]{1,0:T(8,128)(2,1)} %param.8) | copy-start | bytes 3145732
  168.0 16.7 %collective-permute-start.17 = (f32[64,1280]{1,0:T(8,128)S(1)}, f32[64,1280]{1,0:T(8,128)S(1)}, u32[]{:S(2)}, u32[]{:S(2)}) collective-permute-start(f32[64,1280]{1,0:T(8,128)S(1)} %fusion.8), channel_id=1, source_target_pairs={{0,16},{16,0},{1,17},{17,1},{2,18},{18,2},{3,19},{19,3},{4,20},{20... | collective-permute-start | bytes 983048 | tf_op jit(solution)/shard_map/ppermute | solution.py:51
Sparse Core Ops, SparseCore 0:
  100.1 99.1 reduce-scatter.1

commit v7 on v5

--- a/solution.py
+++ b/solution.py
@@ -7,6 +7,7 @@
 
 
 TIME = ("tz", "tx", "tc")
+CHAN = ("cy", "cx")
 
 
 def shifted(x, axis, by):
@@ -52,6 +53,26 @@
     return keep + lax.ppermute(give, axis, [(0, 1), (1, 0)])
 
 
+def chan_ring_reduce_scatter(x):
+    peers = lax.axis_size("cy")
+    at = lax.axis_index("cy")
+    chunks = x.reshape(peers, x.shape[0] // peers, x.shape[1])
+    half = x.shape[1] // 2
+    sums = []
+    for step, cols in ((1, slice(0, half)), (-1, slice(half, None))):
+        own = chunks[:, :, cols]
+        pairs = [(i, (i + step) % peers) for i in range(peers)]
+        acc = lax.dynamic_index_in_dim(own, (at - step) % peers, 0, keepdims=False)
+        for s in range(peers - 1):
+            got = lax.ppermute(acc, "cy", pairs)
+            acc = got + lax.dynamic_index_in_dim(
+                own, (at - step * (s + 2)) % peers, 0, keepdims=False
+            )
+        sums.append(acc)
+    full = jnp.concatenate(sums, axis=1)
+    return swap_sum(full.reshape(2, full.shape[0] // 2, full.shape[1]), "cx")
+
+
 def time_reduce_scatter(x):
     outer, mid, inner = (lax.axis_size(a) for a in TIME)
     blocks = x.reshape(outer, mid, inner, x.shape[0] // (outer * mid * inner), x.shape[1])
@@ -91,9 +112,16 @@
         branch_grads.reshape(traj, window_extent, 2 * blocks), TIME, -receptive_extent
     ).reshape(rows_n, 2 * blocks)
     partial_value = contract_cols(w_now, branch_grads) + contract_cols(w_dil, later)
-    summed = lax.psum_scatter(partial_value, "chan", scatter_dimension=0, tiled=True)
-    share = width // lax.axis_size("chan")
-    own_rows = lax.dynamic_slice_in_dim(grad_rows, lax.axis_index("chan") * share, share, 2)
+    cut = partial_value.shape[1] // 2
+    summed = jnp.concatenate(
+        [
+            lax.psum_scatter(partial_value[:, :cut], CHAN, scatter_dimension=0, tiled=True),
+            chan_ring_reduce_scatter(partial_value[:, cut:]),
+        ],
+        axis=1,
+    )
+    share = width // (lax.axis_size("cy") * lax.axis_size("cx"))
+    own_rows = lax.dynamic_slice_in_dim(grad_rows, lax.axis_index(CHAN) * share, share, 2)
     summed = summed.reshape(share, traj, window_extent).transpose(1, 2, 0)
     grad_states = (own_rows.astype(jnp.float32) + summed).astype(jnp.bfloat16)
     weight_terms = jnp.concatenate(
@@ -114,18 +142,18 @@
 
 def solution(mesh):
     tm, chan = mesh.shape["tm"], mesh.shape["chan"]
-    mesh = jax.sharding.Mesh(mesh.devices.reshape(tm // 4, 2, 2, chan), TIME + ("chan",))
+    mesh = jax.sharding.Mesh(mesh.devices.reshape(tm // 4, 2, 2, chan // 2, 2), TIME + CHAN)
     placed = (
         P(None, TIME, None),
         P(None, TIME, None),
-        P(None, None, None, "chan"),
-        P("chan", None),
+        P(None, None, None, CHAN),
+        P(CHAN, None),
         P(),
     )
     return jax.shard_map(
         local,
         mesh=mesh,
         in_specs=placed,
-        out_specs=(P(None, TIME, "chan"), P(None, None, TIME, "chan"), P("chan", TIME)),
+        out_specs=(P(None, TIME, CHAN), P(None, None, TIME, CHAN), P(CHAN, TIME)),
         check_vma=False,
     )

time: 209 us -> 206 us (0.986)
  starting transfers between devices: 33.9 us -> 44.6 us
  other arithmetic: 26.8 us -> 17.5 us
  waiting for transfers between devices: 80.1 us -> 77.8 us
    add x14, other arithmetic: 14.1 us -> 0.64 us  [ring_sum(): got + lax.dynamic_index_in_dim(own, (at - step * (s + 2)) % peers, 0, kee...]
    ppermute x0 -> x6, starting transfers between devices: none -> 10.6 us  [chan_ring_reduce_scatter(): got = lax.ppermute(acc, 'cy', pairs)]
    ppermute x2 -> x3, waiting for transfers between devices: 12.4 us -> 1.86 us  [swap_sum(): return keep + lax.ppermute(give, axis, [(0, 1), (1, 0)])]
    ppermute x0 -> x6, waiting for transfers between devices: none -> 4.72 us  [chan_ring_reduce_scatter(): got = lax.ppermute(acc, 'cy', pairs)]
    ppermute x14, waiting for transfers between devices: 35.7 us -> 39.2 us  [ring_sum(): got = lax.ppermute(acc, axis, pairs)]
    add x2 -> x3, other arithmetic: 4.83 us -> 6.02 us  [swap_sum(): return keep + lax.ppermute(give, axis, [(0, 1), (1, 0)])]
    squeeze x1 -> x2, local copies, waits for them, and re-layouts: 5.43 us -> 5.37 us  [swap_sum(): give = lax.dynamic_index_in_dim(parts, 1 - me, 0, keepdims=False)]
  transfers between devices with their start and end apart: 19 -> 26, of which waited for: 12 -> 14; matrix products, arithmetic and copies ran while one was open for 19% -> 14% of each run, Pallas kernels for 0% -> 0%
where the time goes in v7:
time: 206 us; the launch traced here: 204 us
  waiting for transfers between devices  77.8 us (38%)
  starting transfers between devices  44.6 us (22%)
  local copies, waits for them, and re-layouts  31.1 us (15%)
  matrix products  17.8 us (9%)
  other arithmetic  17.5 us (8%)
  between operations  15.3 us (7%)
    ppermute x14, waiting for transfers between devices, ring_sum(): got = lax.ppermute(acc, axis, pairs)  39.2 us
    ppermute x2, waiting for transfers between devices, shifted(): return lax.ppermute(x, axis, pairs)  32 us
    ppermute x14, starting transfers between devices, ring_sum(): got = lax.ppermute(acc, axis, pairs)  24.8 us
    concatenate x1, local copies, waits for them, and re-layouts, local(): jnp.concatenate([contract_rows(rows, branch_grads), contract_rows(rows, l...  11.3 us
    ppermute x6, starting transfers between devices, chan_ring_reduce_scatter(): got = lax.ppermute(acc, 'cy', pairs)  10.6 us
    dot_general x3, matrix products, contract_cols(): lax.dot_general(left, right, (((1,), (1,)), ((), ())), preferred_element_...  9.32 us
    ppermute x2, starting transfers between devices, shifted(): return lax.ppermute(x, axis, pairs)  6.95 us
    add x3, other arithmetic, swap_sum(): return keep + lax.ppermute(give, axis, [(0, 1), (1, 0)])  6.02 us
  transfers between devices with their start and end apart: 26, of which 14 were waited for; matrix products, arithmetic and copies ran while one was open for 14% of the time, Pallas kernels for 0%

profile of v7, /device:TPU:98, one launch (start us, length us, event | category | flops | bytes accessed | tf_op | source)
XLA Modules:
  0.0 204.1 jit_solution(15902019716086214246)
XLA Ops:
  7.2 3.9 %slice_bitcast_fusion.1 = (bf16[2048,256]{1,0:T(8,128)(2,1)S(1)}, bf16[2048,256]{1,0:T(8,128)(2,1)}, bf16[2048,256]{1,0:T(8,128)(2,1)}, bf16[2048,256]{1,0:T(8,128)(2,1)S(1)}) fusion(bf16[2,2,2048,256]{3,2,1,0:T(8,128)(2,1)} %param.7), kind=kLoop, calls=%fused_computation.13 | loop fusion | bytes 8388608 | tf_op jit(solution)/shard_map/squeeze | solution.py:91
  11.2 2.2 %fusion = f32[512,512]{0,1:T(8,128)} fusion(bf16[512,2048]{1,0:T(8,128)(2,1)S(1)} %bitcast.113, bf16[2048,256]{1,0:T(8,128)(2,1)S(1)} %get-tuple-element.10, bf16[2048,256]{1,0:T(8,128)(2,1)S(1)} %get-tuple-element.7), kind=kOutput, calls=%fused_computation.10 | convolution fusion | flops 1077936128 | bytes 5242880 | tf_op jit(solution)/shard_map/dot_general | solution.py:92
  13.4 2.3 %copy.28 = f32[2,256,512]{1,0,2:T(2,128)} copy(f32[2,256,512]{2,1,0:T(8,128)} %bitcast.126) | data formatting | bytes 2097152 | tf_op jit(solution)/shard_map/reshape | solution.py:94
  15.7 5.0 %collective-permute-start = (f32[2,256,512]{1,0,2:T(2,128)}, f32[2,256,512]{1,0,2:T(2,128)}, u32[]{:S(2)}, u32[]{:S(2)}) collective-permute-start(f32[2,256,512]{1,0,2:T(2,128)} %copy.28), channel_id=1, source_target_pairs={{0,32},{8,40},{16,48},{24,56},{32,64},{40,72},{48,80},{56,88},{64,... | collective-permute-start | bytes 3145736 | tf_op jit(solution)/shard_map/ppermute | solution.py:16
  20.8 3.0 %convolution_bitcast_fusion.2 = f32[512,512]{0,1:T(8,128)S(1)} fusion(bf16[512,2048]{1,0:T(8,128)(2,1)S(1)} %bitcast.112, bf16[2048,256]{1,0:T(8,128)(2,1)} %get-tuple-element.8, bf16[2048,256]{1,0:T(8,128)(2,1)} %get-tuple-element.9), kind=kOutput, calls=%fused_computation.9 | convolution fusion | flops 1077936128 | bytes 5242880 | tf_op jit(solution)/shard_map/dot_general | solution.py:96
  24.0 19.4 %collective-permute-done = f32[2,256,512]{1,0,2:T(2,128)} collective-permute-done((f32[2,256,512]{1,0,2:T(2,128)}, f32[2,256,512]{1,0,2:T(2,128)}, u32[]{:S(2)}, u32[]{:S(2)}) %collective-permute-start) | collective-permute-done | bytes 1048608 | tf_op jit(solution)/shard_map/ppermute | solution.py:16
  43.4 1.4 copy.36
  45.0 0.9 multiply_convert_fusion.2
  46.0 1.9 collective-permute-start.1
  48.0 0.8 fusion.10
  48.8 1.3 convolution_bitcast_fusion.1
  50.1 12.7 %collective-permute-done.1 = bf16[2,256,512]{1,2,0:T(8,128)(2,1)S(1)} collective-permute-done((bf16[2,256,512]{1,2,0:T(8,128)(2,1)S(1)}, bf16[2,256,512]{1,2,0:T(8,128)(2,1)S(1)}, u32[]{:S(2)}, u32[]{:S(2)}) %collective-permute-start.1) | collective-permute-done | bytes 524320 | tf_op jit(solution)/shard_map/ppermute | solution.py:16
  62.7 0.8 copy-done.8
  63.5 1.3 convolution_bitcast_fusion
  64.8 4.4 %pad_maximum_fusion = f32[2048,1280]{0,1:T(8,128)} fusion(f32[2048,256]{0,1:T(8,128)S(1)} %fusion.10, f32[2048,512]{0,1:T(8,128)S(1)} %convolution_bitcast_fusion, f32[2048,512]{0,1:T(8,128)S(1)} %convolution_bitcast_fusion.1), kind=kLoop, calls=%fused_computation | loop fusion | flops 5242880 | bytes 20971520 | tf_op jit(solution)/shard_map/concatenate | solution.py:127
  69.1 11.3 %copy.32 = f32[2048,1280]{1,0:T(8,128)} copy(f32[2048,1280]{0,1:T(8,128)} %pad_maximum_fusion) | data formatting | bytes 20971520 | tf_op jit(solution)/shard_map/concatenate | solution.py:127
  80.4 5.3 %dynamic-slice_bitcast_fusion = f32[8,2,64,1280]{3,2,1,0:T(8,128)} fusion(f32[8,2,2,64,1280]{4,3,2,1,0:T(8,128)} %bitcast.115, s32[]{:T(128)S(6)} %select_n.222), kind=kLoop, calls=%fused_computation.2 | loop fusion | bytes 10485764 | tf_op jit(solution)/shard_map/jit(dynamic_index_in_dim)/squeeze | solution.py:52
  85.8 4.9 %fusion.1 = f32[2048,512]{1,0:T(8,128)} fusion(bf16[2048,256]{1,0:T(8,128)(2,1)} %get-tuple-element.8, bf16[2048,256]{1,0:T(8,128)(2,1)} %get-tuple-element.9, bf16[512,256]{0,1:T(8,128)(2,1)S(1)} %copy-done.11, bf16[512,256]{0,1:T(8,128)(2,1)S(1)} %get-tuple-element.13), kind=kOutput, calls=%fused_computation.11 | convolution fusion | flops 1078984704 | bytes 6815744 | tf_op jit(solution)/shard_map/dot_general | solution.py:26
  91.0 3.5 %convolution_add_fusion = f32[2048,512]{1,0:T(8,128)S(1)} fusion(f32[2048,512]{1,0:T(8,128)} %fusion.1, bf16[512,512]{1,0:T(8,128)(2,1)S(1)} %bitcast.125, bf16[2048,256]{1,0:T(8,128)(2,1)S(1)} %copy-done.5, bf16[2048,256]{1,0:T(8,128)(2,1)S(1)} %get-tuple-element.7), kind=kOutput, calls=%fused_computation.5 | convolution fusion | flops 1078984704 | bytes 11010048 | tf_op jit(solution)/shard_map/dot_general | solution.py:26
  94.4 1.7 fusion.18
  96.3 1.0 copy-done.2
  97.3 3.3 %collective-permute-start.5 = (f32[512,128]{1,0:T(8,128)S(1)}, f32[512,128]{1,0:T(8,128)S(1)}, u32[]{:S(2)}, u32[]{:S(2)}) collective-permute-start(f32[512,128]{1,0:T(8,128)S(1)} %dynamic-slice_bitcast_fusion.4), channel_id=1, source_target_pairs={{0,6},{2,0},{4,2},{6,4},{1,7},{3,1},{5,3},{7,5},{8,14},{10,8},{12,... | collective-permute-start | bytes 786440 | tf_op jit(solution)/shard_map/ppermute | solution.py:67
  102.1 4.7 %collective-permute-done.5 = f32[512,128]{1,0:T(8,128)S(1)} collective-permute-done((f32[512,128]{1,0:T(8,128)S(1)}, f32[512,128]{1,0:T(8,128)S(1)}, u32[]{:S(2)}, u32[]{:S(2)}) %collective-permute-start.5) | collective-permute-done | bytes 262176 | tf_op jit(solution)/shard_map/ppermute | solution.py:67
  106.8 3.8 %collective-permute-start.6 = (f32[512,128]{1,0:T(8,128)S(1)}, f32[512,128]{1,0:T(8,128)S(1)}, u32[]{:S(2)}, u32[]{:S(2)}) collective-permute-start(f32[512,128]{1,0:T(8,128)S(1)} %bitcast_add_fusion.18), channel_id=1, source_target_pairs={{0,6},{2,0},{4,2},{6,4},{1,7},{3,1},{5,3},{7,5},{8,14},{10,8},{12,... | collective-permute-start | bytes 786440 | tf_op jit(solution)/shard_map/ppermute | solution.py:67
  110.7 5.0 %bitcast_add_fusion = f32[8,2,64,1280]{3,2,1,0:T(8,128)S(1)} fusion(f32[8,2,64,1280]{3,2,1,0:T(8,128)} %collective-permute-done.9, f32[8,2,2,64,1280]{4,3,2,1,0:T(8,128)} %bitcast.116, s32[]{:T(128)S(6)} %select_n.221), kind=kLoop, calls=%fused_computation.1 | loop fusion | flops 1310720 | bytes 15728644 | tf_op jit(solution)/shard_map/add | solution.py:53
  116.4 1.6 collective-permute-start.10
  118.7 3.3 %collective-permute-start.7 = (f32[512,128]{1,0:T(8,128)S(1)}, f32[512,128]{1,0:T(8,128)S(1)}, u32[]{:S(2)}, u32[]{:S(2)}) collective-permute-start(f32[512,128]{1,0:T(8,128)S(1)} %bitcast_add_fusion.17), channel_id=1, source_target_pairs={{0,6},{2,0},{4,2},{6,4},{1,7},{3,1},{5,3},{7,5},{8,14},{10,8},{12,... | collective-permute-start | bytes 786440 | tf_op jit(solution)/shard_map/ppermute | solution.py:67
  122.0 3.3 %collective-permute-done.10 = f32[2,64,640]{2,1,0:T(8,128)S(1)} collective-permute-done((f32[2,64,640]{2,1,0:T(8,128)S(1)}, f32[2,64,640]{2,1,0:T(8,128)S(1)}, u32[]{:S(2)}, u32[]{:S(2)}) %collective-permute-start.10) | collective-permute-done | bytes 327712 | tf_op jit(solution)/shard_map/ppermute | solution.py:41
  125.3 3.0 %collective-permute-start.11 = (f32[2,64,640]{2,1,0:T(8,128)S(1)}, f32[2,64,640]{2,1,0:T(8,128)S(1)}, u32[]{:S(2)}, u32[]{:S(2)}) collective-permute-start(f32[2,64,640]{2,1,0:T(8,128)S(1)} %bitcast_add_fusion.14), channel_id=1, source_target_pairs={{0,32},{32,64},{64,96},{96,128},{128,160},{160,192},{192,224},{224... | collective-permute-start | bytes 983048 | tf_op jit(solution)/shard_map/ppermute | solution.py:41
  128.7 5.4 %collective-permute-done.11 = f32[2,64,640]{2,1,0:T(8,128)S(1)} collective-permute-done((f32[2,64,640]{2,1,0:T(8,128)S(1)}, f32[2,64,640]{2,1,0:T(8,128)S(1)}, u32[]{:S(2)}, u32[]{:S(2)}) %collective-permute-start.11) | collective-permute-done | bytes 327712 | tf_op jit(solution)/shard_map/ppermute | solution.py:41
  134.1 3.8 %collective-permute-start.12 = (f32[2,64,640]{2,1,0:T(8,128)S(1)}, f32[2,64,640]{2,1,0:T(8,128)S(1)}, u32[]{:S(2)}, u32[]{:S(2)}) collective-permute-start(f32[2,64,640]{2,1,0:T(8,128)S(1)} %bitcast_add_fusion.13), channel_id=1, source_target_pairs={{0,32},{32,64},{64,96},{96,128},{128,160},{160,192},{192,224},{224... | collective-permute-start | bytes 983048 | tf_op jit(solution)/shard_map/ppermute | solution.py:41
  138.0 4.6 %collective-permute-done.12 = f32[2,64,640]{2,1,0:T(8,128)S(1)} collective-permute-done((f32[2,64,640]{2,1,0:T(8,128)S(1)}, f32[2,64,640]{2,1,0:T(8,128)S(1)}, u32[]{:S(2)}, u32[]{:S(2)}) %collective-permute-start.12) | collective-permute-done | bytes 327712 | tf_op jit(solution)/shard_map/ppermute | solution.py:41
  142.7 3.8 %collective-permute-start.13 = (f32[2,64,640]{2,1,0:T(8,128)S(1)}, f32[2,64,640]{2,1,0:T(8,128)S(1)}, u32[]{:S(2)}, u32[]{:S(2)}) collective-permute-start(f32[2,64,640]{2,1,0:T(8,128)S(1)} %bitcast_add_fusion.12), channel_id=1, source_target_pairs={{0,32},{32,64},{64,96},{96,128},{128,160},{160,192},{192,224},{224... | collective-permute-start | bytes 983048 | tf_op jit(solution)/shard_map/ppermute | solution.py:41
  146.6 4.6 %collective-permute-done.13 = f32[2,64,640]{2,1,0:T(8,128)S(1)} collective-permute-done((f32[2,64,640]{2,1,0:T(8,128)S(1)}, f32[2,64,640]{2,1,0:T(8,128)S(1)}, u32[]{:S(2)}, u32[]{:S(2)}) %collective-permute-start.13) | collective-permute-done | bytes 327712 | tf_op jit(solution)/shard_map/ppermute | solution.py:41
  151.3 4.0 %collective-permute-start.14 = (f32[2,64,640]{2,1,0:T(8,128)S(1)}, f32[2,64,640]{2,1,0:T(8,128)S(1)}, u32[]{:S(2)}, u32[]{:S(2)}) collective-permute-start(f32[2,64,640]{2,1,0:T(8,128)S(1)} %bitcast_add_fusion.11), channel_id=1, source_target_pairs={{0,32},{32,64},{64,96},{96,128},{128,160},{160,192},{192,224},{224... | collective-permute-start | bytes 983048 | tf_op jit(solution)/shard_map/ppermute | solution.py:41
  155.5 5.9 %collective-permute-done.14 = f32[2,64,640]{2,1,0:T(8,128)S(1)} collective-permute-done((f32[2,64,640]{2,1,0:T(8,128)S(1)}, f32[2,64,640]{2,1,0:T(8,128)S(1)}, u32[]{:S(2)}, u32[]{:S(2)}) %collective-permute-start.14) | collective-permute-done | bytes 327712 | tf_op jit(solution)/shard_map/ppermute | solution.py:41
  161.4 3.8 %collective-permute-start.15 = (f32[2,64,640]{2,1,0:T(8,128)S(1)}, f32[2,64,640]{2,1,0:T(8,128)S(1)}, u32[]{:S(2)}, u32[]{:S(2)}) collective-permute-start(f32[2,64,640]{2,1,0:T(8,128)S(1)} %bitcast_add_fusion.10), channel_id=1, source_target_pairs={{0,32},{32,64},{64,96},{96,128},{128,160},{160,192},{192,224},{224... | collective-permute-start | bytes 983048 | tf_op jit(solution)/shard_map/ppermute | solution.py:41
  165.7 6.8 %collective-permute-done.15 = f32[2,64,640]{2,1,0:T(8,128)S(1)} collective-permute-done((f32[2,64,640]{2,1,0:T(8,128)S(1)}, f32[2,64,640]{2,1,0:T(8,128)S(1)}, u32[]{:S(2)}, u32[]{:S(2)}) %collective-permute-start.15) | collective-permute-done | bytes 327712 | tf_op jit(solution)/shard_map/ppermute | solution.py:41
  172.5 3.8 %collective-permute-start.16 = (f32[2,64,640]{2,1,0:T(8,128)S(1)}, f32[2,64,640]{2,1,0:T(8,128)S(1)}, u32[]{:S(2)}, u32[]{:S(2)}) collective-permute-start(f32[2,64,640]{2,1,0:T(8,128)S(1)} %bitcast_add_fusion.9), channel_id=1, source_target_pairs={{0,32},{32,64},{64,96},{96,128},{128,160},{160,192},{192,224},{224... | collective-permute-start | bytes 983048 | tf_op jit(solution)/shard_map/ppermute | solution.py:41
  176.7 4.2 %collective-permute-done.16 = f32[2,64,640]{2,1,0:T(8,128)S(1)} collective-permute-done((f32[2,64,640]{2,1,0:T(8,128)S(1)}, f32[2,64,640]{2,1,0:T(8,128)S(1)}, u32[]{:S(2)}, u32[]{:S(2)}) %collective-permute-start.16) | collective-permute-done | bytes 327712 | tf_op jit(solution)/shard_map/ppermute | solution.py:41
  181.0 4.0 %collective-permute-done.23 = f32[2,64,640]{2,1,0:T(8,128)S(1)} collective-permute-done((f32[2,64,640]{2,1,0:T(8,128)S(1)}, f32[2,64,640]{2,1,0:T(8,128)S(1)}, u32[]{:S(2)}, u32[]{:S(2)}) %collective-permute-start.23) | collective-permute-done | bytes 327712 | tf_op jit(solution)/shard_map/ppermute | solution.py:41
  185.0 0.8 fusion.6
  185.8 2.1 %collective-permute-start.24 = (f32[64,1280]{1,0:T(8,128)}, f32[64,1280]{1,0:T(8,128)}, u32[]{:S(2)}, u32[]{:S(2)}) collective-permute-start(f32[64,1280]{1,0:T(8,128)} %fusion.6), channel_id=1, source_target_pairs={{0,16},{16,0},{1,17},{17,1},{2,18},{18,2},{3,19},{19,3},{4,20},{20... | collective-permute-start | bytes 983048 | tf_op jit(solution)/shard_map/ppermute | solution.py:53
  187.9 1.9 pad_maximum_fusion.9
  189.8 1.2 copy.34
  191.1 1.7 add_convert_fusion
  192.8 1.9 collective-permute-done.24
  194.6 1.0 fusion.9
  (95 shorter events, 6.8 us)
Async XLA Ops:
  7.2 4.0 %copy-start = (bf16[2,256,2048]{2,1,0:T(8,128)(2,1)S(1)}, bf16[2,256,2048]{2,1,0:T(8,128)(2,1)}, u32[]{:S(2)}) copy-start(bf16[2,256,2048]{2,1,0:T(8,128)(2,1)} %param.5) | copy-start | bytes 6291460
  7.2 180.7 %reduce-scatter.2.cloned.1.call-start = ((), (), s32[]{:S(2)}) async-start(), calls=%async_computation.1 | async-start | bytes 2359296 | tf_op jit(solution)/shard_map/reduce_scatter | solution.py:118
  11.2 2.2 %copy-start.4 = (bf16[2048,256]{1,0:T(8,128)(2,1)}, bf16[2048,256]{1,0:T(8,128)(2,1)S(1)}, u32[]{:S(2)}) copy-start(bf16[2048,256]{1,0:T(8,128)(2,1)S(1)} %get-tuple-element.10) | copy-start | bytes 3145732
  11.2 9.6 %copy-start.12 = (s32[2]{0:T(128)S(1)}, s32[2]{0:T(128)}, u32[]{:S(2)}) copy-start(s32[2]{0:T(128)} %param.9) | copy-start | bytes 28
  15.7 27.7 %collective-permute-start = (f32[2,256,512]{1,0,2:T(2,128)}, f32[2,256,512]{1,0,2:T(2,128)}, u32[]{:S(2)}, u32[]{:S(2)}) collective-permute-start(f32[2,256,512]{1,0,2:T(2,128)} %copy.28), channel_id=1, source_target_pairs={{0,32},{8,40},{16,48},{24,56},{32,64},{40,72},{48,80},{56,88},{64,... | collective-permute-start | bytes 3145736 | tf_op jit(solution)/shard_map/ppermute | solution.py:16
  20.8 3.0 %copy-start.7 = (bf16[2,256,2048]{2,1,0:T(8,128)(2,1)S(1)}, bf16[2,256,2048]{2,1,0:T(8,128)(2,1)}, u32[]{:S(2)}) copy-start(bf16[2,256,2048]{2,1,0:T(8,128)(2,1)} %param.6) | copy-start | bytes 6291460
  24.0 23.9 %copy-start.6 = (bf16[2,256,2048]{2,1,0:T(8,128)(2,1)}, bf16[2,256,2048]{2,1,0:T(8,128)(2,1)S(1)}, u32[]{:S(2)}) copy-start(bf16[2,256,2048]{2,1,0:T(8,128)(2,1)S(1)} %broadcast_select_fusion) | copy-start | bytes 6291460
  43.4 1.6 copy-start.13
  45.9 2.8 %copy-start.10 = (bf16[512,256]{0,1:T(8,128)(2,1)}, bf16[512,256]{0,1:T(8,128)(2,1)S(1)}, u32[]{:S(2)}) copy-start(bf16[512,256]{0,1:T(8,128)(2,1)S(1)} %get-tuple-element.14) | copy-start | bytes 786436
  46.0 16.7 %collective-permute-start.1 = (bf16[2,256,512]{1,2,0:T(8,128)(2,1)S(1)}, bf16[2,256,512]{1,2,0:T(8,128)(2,1)S(1)}, u32[]{:S(2)}, u32[]{:S(2)}) collective-permute-start(bf16[2,256,512]{1,2,0:T(8,128)(2,1)S(1)} %bitcast.127), channel_id=1, source_target_pairs={{32,0},{40,8},{48,16},{56,24},{64,32},{72,40},{80,48},{88,56},{96,... | collective-permute-start | bytes 1572872 | tf_op jit(solution)/shard_map/ppermute | solution.py:16
  62.7 0.8 copy-start.8
  80.4 5.4 %copy-start.11 = (bf16[512,256]{0,1:T(8,128)(2,1)S(1)}, bf16[512,256]{0,1:T(8,128)(2,1)}, u32[]{:S(2)}) copy-start(bf16[512,256]{0,1:T(8,128)(2,1)} %copy-done.10) | copy-start | bytes 786436
  85.8 25.0 %collective-permute-start.9 = (f32[8,2,64,1280]{3,2,1,0:T(8,128)}, f32[8,2,64,1280]{3,2,1,0:T(8,128)}, u32[]{:S(2)}, u32[]{:S(2)}) collective-permute-start(f32[8,2,64,1280]{3,2,1,0:T(8,128)} %dynamic-slice_bitcast_fusion), channel_id=1, source_target_pairs={{0,8},{8,0},{1,9},{9,1},{2,10},{10,2},{3,11},{11,3},{4,12},{12,4},... | collective-permute-start | bytes 15728648 | tf_op jit(solution)/shard_map/ppermute | solution.py:53
  85.8 5.0 %copy-start.9 = (bf16[2,256,512]{1,2,0:T(8,128)(2,1)S(1)}, bf16[2,256,512]{1,2,0:T(8,128)(2,1)}, u32[]{:S(2)}) copy-start(bf16[2,256,512]{1,2,0:T(8,128)(2,1)} %copy-done.8) | copy-start | bytes 1572868
  85.8 5.2 %copy-start.5 = (bf16[2048,256]{1,0:T(8,128)(2,1)S(1)}, bf16[2048,256]{1,0:T(8,128)(2,1)}, u32[]{:S(2)}) copy-start(bf16[2048,256]{1,0:T(8,128)(2,1)} %copy-done.4) | copy-start | bytes 3145732
  96.3 1.0 copy-start.2
  97.3 9.5 %copy-start.3 = (f32[4,512,128]{2,1,0:T(8,128)S(1)}, f32[4,512,128]{2,1,0:T(8,128)}, u32[]{:S(2)}) copy-start(f32[4,512,128]{2,1,0:T(8,128)} %copy-done.2) | copy-start | bytes 3145732
  97.3 9.5 %collective-permute-start.5 = (f32[512,128]{1,0:T(8,128)S(1)}, f32[512,128]{1,0:T(8,128)S(1)}, u32[]{:S(2)}, u32[]{:S(2)}) collective-permute-start(f32[512,128]{1,0:T(8,128)S(1)} %dynamic-slice_bitcast_fusion.4), channel_id=1, source_target_pairs={{0,6},{2,0},{4,2},{6,4},{1,7},{3,1},{5,3},{7,5},{8,14},{10,8},{12,... | collective-permute-start | bytes 786440 | tf_op jit(solution)/shard_map/ppermute | solution.py:67
  100.6 10.0 %collective-permute-start.2 = (f32[512,128]{1,0:T(8,128)S(1)}, f32[512,128]{1,0:T(8,128)S(1)}, u32[]{:S(2)}, u32[]{:S(2)}) collective-permute-start(f32[512,128]{1,0:T(8,128)S(1)} %dynamic-slice_bitcast_fusion.5), channel_id=1, source_target_pairs={{0,2},{2,4},{4,6},{6,0},{1,3},{3,5},{5,7},{7,1},{8,10},{10,12},{12... | collective-permute-start | bytes 786440 | tf_op jit(solution)/shard_map/ppermute | solution.py:67
  106.8 11.8 %collective-permute-start.6 = (f32[512,128]{1,0:T(8,128)S(1)}, f32[512,128]{1,0:T(8,128)S(1)}, u32[]{:S(2)}, u32[]{:S(2)}) collective-permute-start(f32[512,128]{1,0:T(8,128)S(1)} %bitcast_add_fusion.18), channel_id=1, source_target_pairs={{0,6},{2,0},{4,2},{6,4},{1,7},{3,1},{5,3},{7,5},{8,14},{10,8},{12,... | collective-permute-start | bytes 786440 | tf_op jit(solution)/shard_map/ppermute | solution.py:67
  110.6 17.9 %collective-permute-start.3 = (f32[512,128]{1,0:T(8,128)S(1)}, f32[512,128]{1,0:T(8,128)S(1)}, u32[]{:S(2)}, u32[]{:S(2)}) collective-permute-start(f32[512,128]{1,0:T(8,128)S(1)} %bitcast_add_fusion.21), channel_id=1, source_target_pairs={{0,2},{2,4},{4,6},{6,0},{1,3},{3,5},{5,7},{7,1},{8,10},{10,12},{12... | collective-permute-start | bytes 786440 | tf_op jit(solution)/shard_map/ppermute | solution.py:67
  116.4 8.9 %collective-permute-start.10 = (f32[2,64,640]{2,1,0:T(8,128)S(1)}, f32[2,64,640]{2,1,0:T(8,128)S(1)}, u32[]{:S(2)}, u32[]{:S(2)}) collective-permute-start(f32[2,64,640]{2,1,0:T(8,128)S(1)} %dynamic-slice_bitcast_fusion.2), channel_id=1, source_target_pairs={{0,32},{32,64},{64,96},{96,128},{128,160},{160,192},{192,224},{224... | collective-permute-start | bytes 983048 | tf_op jit(solution)/shard_map/ppermute | solution.py:41
  118.1 10.3 %collective-permute-start.17 = (f32[2,64,640]{2,1,0:T(8,128)S(1)}, f32[2,64,640]{2,1,0:T(8,128)S(1)}, u32[]{:S(2)}, u32[]{:S(2)}) collective-permute-start(f32[2,64,640]{2,1,0:T(8,128)S(1)} %dynamic-slice_bitcast_fusion.1), channel_id=1, source_target_pairs={{0,224},{32,0},{64,32},{96,64},{128,96},{160,128},{192,160},{224,1... | collective-permute-start | bytes 983048 | tf_op jit(solution)/shard_map/ppermute | solution.py:41
  118.7 19.3 %collective-permute-start.7 = (f32[512,128]{1,0:T(8,128)S(1)}, f32[512,128]{1,0:T(8,128)S(1)}, u32[]{:S(2)}, u32[]{:S(2)}) collective-permute-start(f32[512,128]{1,0:T(8,128)S(1)} %bitcast_add_fusion.17), channel_id=1, source_target_pairs={{0,6},{2,0},{4,2},{6,4},{1,7},{3,1},{5,3},{7,5},{8,14},{10,8},{12,... | collective-permute-start | bytes 786440 | tf_op jit(solution)/shard_map/ppermute | solution.py:67
  125.3 8.7 %collective-permute-start.11 = (f32[2,64,640]{2,1,0:T(8,128)S(1)}, f32[2,64,640]{2,1,0:T(8,128)S(1)}, u32[]{:S(2)}, u32[]{:S(2)}) collective-permute-start(f32[2,64,640]{2,1,0:T(8,128)S(1)} %bitcast_add_fusion.14), channel_id=1, source_target_pairs={{0,32},{32,64},{64,96},{96,128},{128,160},{160,192},{192,224},{224... | collective-permute-start | bytes 983048 | tf_op jit(solution)/shard_map/ppermute | solution.py:41
  128.4 9.4 %collective-permute-start.18 = (f32[2,64,640]{2,1,0:T(8,128)S(1)}, f32[2,64,640]{2,1,0:T(8,128)S(1)}, u32[]{:S(2)}, u32[]{:S(2)}) collective-permute-start(f32[2,64,640]{2,1,0:T(8,128)S(1)} %bitcast_add_fusion.7), channel_id=1, source_target_pairs={{0,224},{32,0},{64,32},{96,64},{128,96},{160,128},{192,160},{224,1... | collective-permute-start | bytes 983048 | tf_op jit(solution)/shard_map/ppermute | solution.py:41
  128.6 18.0 %collective-permute-start.4 = (f32[512,128]{1,0:T(8,128)S(1)}, f32[512,128]{1,0:T(8,128)S(1)}, u32[]{:S(2)}, u32[]{:S(2)}) collective-permute-start(f32[512,128]{1,0:T(8,128)S(1)} %bitcast_add_fusion.20), channel_id=1, source_target_pairs={{0,2},{2,4},{4,6},{6,0},{1,3},{3,5},{5,7},{7,1},{8,10},{10,12},{12... | collective-permute-start | bytes 786440 | tf_op jit(solution)/shard_map/ppermute | solution.py:67
  134.1 8.6 %collective-permute-start.12 = (f32[2,64,640]{2,1,0:T(8,128)S(1)}, f32[2,64,640]{2,1,0:T(8,128)S(1)}, u32[]{:S(2)}, u32[]{:S(2)}) collective-permute-start(f32[2,64,640]{2,1,0:T(8,128)S(1)} %bitcast_add_fusion.13), channel_id=1, source_target_pairs={{0,32},{32,64},{64,96},{96,128},{128,160},{160,192},{192,224},{224... | collective-permute-start | bytes 983048 | tf_op jit(solution)/shard_map/ppermute | solution.py:41
  137.9 8.6 %collective-permute-start.19 = (f32[2,64,640]{2,1,0:T(8,128)S(1)}, f32[2,64,640]{2,1,0:T(8,128)S(1)}, u32[]{:S(2)}, u32[]{:S(2)}) collective-permute-start(f32[2,64,640]{2,1,0:T(8,128)S(1)} %bitcast_add_fusion.6), channel_id=1, source_target_pairs={{0,224},{32,0},{64,32},{96,64},{128,96},{160,128},{192,160},{224,1... | collective-permute-start | bytes 983048 | tf_op jit(solution)/shard_map/ppermute | solution.py:41
  142.7 8.6 %collective-permute-start.13 = (f32[2,64,640]{2,1,0:T(8,128)S(1)}, f32[2,64,640]{2,1,0:T(8,128)S(1)}, u32[]{:S(2)}, u32[]{:S(2)}) collective-permute-start(f32[2,64,640]{2,1,0:T(8,128)S(1)} %bitcast_add_fusion.12), channel_id=1, source_target_pairs={{0,32},{32,64},{64,96},{96,128},{128,160},{160,192},{192,224},{224... | collective-permute-start | bytes 983048 | tf_op jit(solution)/shard_map/ppermute | solution.py:41
  146.5 8.8 %collective-permute-start.20 = (f32[2,64,640]{2,1,0:T(8,128)S(1)}, f32[2,64,640]{2,1,0:T(8,128)S(1)}, u32[]{:S(2)}, u32[]{:S(2)}) collective-permute-start(f32[2,64,640]{2,1,0:T(8,128)S(1)} %bitcast_add_fusion.5), channel_id=1, source_target_pairs={{0,224},{32,0},{64,32},{96,64},{128,96},{160,128},{192,160},{224,1... | collective-permute-start | bytes 983048 | tf_op jit(solution)/shard_map/ppermute | solution.py:41
  151.3 10.1 %collective-permute-start.14 = (f32[2,64,640]{2,1,0:T(8,128)S(1)}, f32[2,64,640]{2,1,0:T(8,128)S(1)}, u32[]{:S(2)}, u32[]{:S(2)}) collective-permute-start(f32[2,64,640]{2,1,0:T(8,128)S(1)} %bitcast_add_fusion.11), channel_id=1, source_target_pairs={{0,32},{32,64},{64,96},{96,128},{128,160},{160,192},{192,224},{224... | collective-permute-start | bytes 983048 | tf_op jit(solution)/shard_map/ppermute | solution.py:41
  155.4 10.0 %collective-permute-start.21 = (f32[2,64,640]{2,1,0:T(8,128)S(1)}, f32[2,64,640]{2,1,0:T(8,128)S(1)}, u32[]{:S(2)}, u32[]{:S(2)}) collective-permute-start(f32[2,64,640]{2,1,0:T(8,128)S(1)} %bitcast_add_fusion.4), channel_id=1, source_target_pairs={{0,224},{32,0},{64,32},{96,64},{128,96},{160,128},{192,160},{224,1... | collective-permute-start | bytes 983048 | tf_op jit(solution)/shard_map/ppermute | solution.py:41
  161.4 11.1 %collective-permute-start.15 = (f32[2,64,640]{2,1,0:T(8,128)S(1)}, f32[2,64,640]{2,1,0:T(8,128)S(1)}, u32[]{:S(2)}, u32[]{:S(2)}) collective-permute-start(f32[2,64,640]{2,1,0:T(8,128)S(1)} %bitcast_add_fusion.10), channel_id=1, source_target_pairs={{0,32},{32,64},{64,96},{96,128},{128,160},{160,192},{192,224},{224... | collective-permute-start | bytes 983048 | tf_op jit(solution)/shard_map/ppermute | solution.py:41
  165.4 11.1 %collective-permute-start.22 = (f32[2,64,640]{2,1,0:T(8,128)S(1)}, f32[2,64,640]{2,1,0:T(8,128)S(1)}, u32[]{:S(2)}, u32[]{:S(2)}) collective-permute-start(f32[2,64,640]{2,1,0:T(8,128)S(1)} %bitcast_add_fusion.3), channel_id=1, source_target_pairs={{0,224},{32,0},{64,32},{96,64},{128,96},{160,128},{192,160},{224,1... | collective-permute-start | bytes 983048 | tf_op jit(solution)/shard_map/ppermute | solution.py:41
  165.5 11.2 %collective-permute-start.8 = (f32[256,256]{1,0:T(8,128)S(1)}, f32[256,256]{1,0:T(8,128)S(1)}, u32[]{:S(2)}, u32[]{:S(2)}) collective-permute-start(f32[256,256]{1,0:T(8,128)S(1)} %dynamic-slice_bitcast_fusion.3), channel_id=1, source_target_pairs={{0,1},{1,0},{2,3},{3,2},{4,5},{5,4},{6,7},{7,6},{8,9},{9,8},{10,11... | collective-permute-start | bytes 786440 | tf_op jit(solution)/shard_map/ppermute | solution.py:53
  172.5 8.4 %collective-permute-start.16 = (f32[2,64,640]{2,1,0:T(8,128)S(1)}, f32[2,64,640]{2,1,0:T(8,128)S(1)}, u32[]{:S(2)}, u32[]{:S(2)}) collective-permute-start(f32[2,64,640]{2,1,0:T(8,128)S(1)} %bitcast_add_fusion.9), channel_id=1, source_target_pairs={{0,32},{32,64},{64,96},{96,128},{128,160},{160,192},{192,224},{224... | collective-permute-start | bytes 983048 | tf_op jit(solution)/shard_map/ppermute | solution.py:41
  176.6 8.4 %collective-permute-start.23 = (f32[2,64,640]{2,1,0:T(8,128)S(1)}, f32[2,64,640]{2,1,0:T(8,128)S(1)}, u32[]{:S(2)}, u32[]{:S(2)}) collective-permute-start(f32[2,64,640]{2,1,0:T(8,128)S(1)} %bitcast_add_fusion.2), channel_id=1, source_target_pairs={{0,224},{32,0},{64,32},{96,64},{128,96},{160,128},{192,160},{224,1... | collective-permute-start | bytes 983048 | tf_op jit(solution)/shard_map/ppermute | solution.py:41
  185.8 8.9 %collective-permute-start.24 = (f32[64,1280]{1,0:T(8,128)}, f32[64,1280]{1,0:T(8,128)}, u32[]{:S(2)}, u32[]{:S(2)}) collective-permute-start(f32[64,1280]{1,0:T(8,128)} %fusion.6), channel_id=1, source_target_pairs={{0,16},{16,0},{1,17},{17,1},{2,18},{18,2},{3,19},{19,3},{4,20},{20... | collective-permute-start | bytes 983048 | tf_op jit(solution)/shard_map/ppermute | solution.py:53
  187.9 9.4 %copy-start.1 = (bf16[2,256,2048]{2,1,0:T(8,128)(2,1)S(1)}, bf16[2,256,2048]{2,1,0:T(8,128)(2,1)}, u32[]{:S(2)}) copy-start(bf16[2,256,2048]{2,1,0:T(8,128)(2,1)} %param.5) | copy-start | bytes 6291460
Sparse Core Ops, SparseCore 0:
  102.2 53.8 reduce-scatter.1

commit v8 on v7

--- a/solution.py
+++ b/solution.py
@@ -112,7 +112,7 @@
         branch_grads.reshape(traj, window_extent, 2 * blocks), TIME, -receptive_extent
     ).reshape(rows_n, 2 * blocks)
     partial_value = contract_cols(w_now, branch_grads) + contract_cols(w_dil, later)
-    cut = partial_value.shape[1] // 2
+    cut = partial_value.shape[1] * 3 // 4
     summed = jnp.concatenate(
         [
             lax.psum_scatter(partial_value[:, :cut], CHAN, scatter_dimension=0, tiled=True),

time: 206 us -> 210 us (1.019)
  local copies, waits for them, and re-layouts: 31.1 us -> 34 us
  waiting for transfers between devices: 77.8 us -> 80.6 us
  transfers between devices with their start and end apart: 26 -> 26, of which waited for: 14 -> 16; matrix products, arithmetic and copies ran while one was open for 14% -> 15% of each run, Pallas kernels for 0% -> 0%
where the time goes in v8:
time: 210 us
  waiting for transfers between devices  80.6 us (38%)
  starting transfers between devices  44.1 us (21%)
  local copies, waits for them, and re-layouts  34 us (16%)
  matrix products  17.9 us (9%)
  other arithmetic  17.7 us (8%)
  between operations  15.3 us (7%)
    ppermute x14, waiting for transfers between devices, ring_sum(): got = lax.ppermute(acc, axis, pairs)  40.8 us
    ppermute x2, waiting for transfers between devices, shifted(): return lax.ppermute(x, axis, pairs)  32 us
    ppermute x14, starting transfers between devices, ring_sum(): got = lax.ppermute(acc, axis, pairs)  24.5 us
    concatenate x1, local copies, waits for them, and re-layouts, local(): jnp.concatenate([contract_rows(rows, branch_grads), contract_rows(rows, l...  11.3 us
    ppermute x6, starting transfers between devices, chan_ring_reduce_scatter(): got = lax.ppermute(acc, 'cy', pairs)  10.6 us
    dot_general x3, matrix products, contract_cols(): lax.dot_general(left, right, (((1,), (1,)), ((), ())), preferred_element_...  9.42 us
    ppermute x2, starting transfers between devices, shifted(): return lax.ppermute(x, axis, pairs)  6.95 us
    add x3, other arithmetic, swap_sum(): return keep + lax.ppermute(give, axis, [(0, 1), (1, 0)])  6.13 us
  transfers between devices with their start and end apart: 26, of which 16 were waited for; matrix products, arithmetic and copies ran while one was open for 15% of the time, Pallas kernels for 0%

profile of v8, /device:TPU:98, one launch (start us, length us, event | category | flops | bytes accessed | tf_op | source)
XLA Modules:
  0.0 209.6 jit_solution(8132026271208421202)
XLA Ops:
  7.2 3.9 %slice_bitcast_fusion.1 = (bf16[2048,256]{1,0:T(8,128)(2,1)S(1)}, bf16[2048,256]{1,0:T(8,128)(2,1)}, bf16[2048,256]{1,0:T(8,128)(2,1)}, bf16[2048,256]{1,0:T(8,128)(2,1)S(1)}) fusion(bf16[2,2,2048,256]{3,2,1,0:T(8,128)(2,1)} %param.7), kind=kLoop, calls=%fused_computation.13 | loop fusion | bytes 8388608 | tf_op jit(solution)/shard_map/squeeze | solution.py:91
  11.1 2.2 %fusion = f32[512,512]{0,1:T(8,128)} fusion(bf16[512,2048]{1,0:T(8,128)(2,1)S(1)} %bitcast.113, bf16[2048,256]{1,0:T(8,128)(2,1)S(1)} %get-tuple-element.8, bf16[2048,256]{1,0:T(8,128)(2,1)S(1)} %get-tuple-element.5), kind=kOutput, calls=%fused_computation.10 | convolution fusion | flops 1077936128 | bytes 5242880 | tf_op jit(solution)/shard_map/dot_general | solution.py:92
  13.4 2.3 %copy.28 = f32[2,256,512]{1,0,2:T(2,128)} copy(f32[2,256,512]{2,1,0:T(8,128)} %bitcast.126) | data formatting | bytes 2097152 | tf_op jit(solution)/shard_map/reshape | solution.py:94
  15.6 5.0 %collective-permute-start = (f32[2,256,512]{1,0,2:T(2,128)}, f32[2,256,512]{1,0,2:T(2,128)}, u32[]{:S(2)}, u32[]{:S(2)}) collective-permute-start(f32[2,256,512]{1,0,2:T(2,128)} %copy.28), channel_id=1, source_target_pairs={{0,32},{8,40},{16,48},{24,56},{32,64},{40,72},{48,80},{56,88},{64,... | collective-permute-start | bytes 3145736 | tf_op jit(solution)/shard_map/ppermute | solution.py:16
  20.8 3.0 %convolution_bitcast_fusion.2 = f32[512,512]{0,1:T(8,128)S(1)} fusion(bf16[512,2048]{1,0:T(8,128)(2,1)S(1)} %bitcast.112, bf16[2048,256]{1,0:T(8,128)(2,1)} %get-tuple-element.6, bf16[2048,256]{1,0:T(8,128)(2,1)} %get-tuple-element.7), kind=kOutput, calls=%fused_computation.9 | convolution fusion | flops 1077936128 | bytes 5242880 | tf_op jit(solution)/shard_map/dot_general | solution.py:96
  24.0 19.4 %collective-permute-done = f32[2,256,512]{1,0,2:T(2,128)} collective-permute-done((f32[2,256,512]{1,0,2:T(2,128)}, f32[2,256,512]{1,0,2:T(2,128)}, u32[]{:S(2)}, u32[]{:S(2)}) %collective-permute-start) | collective-permute-done | bytes 1048608 | tf_op jit(solution)/shard_map/ppermute | solution.py:16
  43.4 1.4 copy.36
  45.0 0.9 multiply_convert_fusion.2
  46.0 1.9 collective-permute-start.1
  48.7 1.3 convolution_bitcast_fusion.1
  50.0 12.6 %collective-permute-done.1 = bf16[2,256,512]{1,2,0:T(8,128)(2,1)S(1)} collective-permute-done((bf16[2,256,512]{1,2,0:T(8,128)(2,1)S(1)}, bf16[2,256,512]{1,2,0:T(8,128)(2,1)S(1)}, u32[]{:S(2)}, u32[]{:S(2)}) %collective-permute-start.1) | collective-permute-done | bytes 524320 | tf_op jit(solution)/shard_map/ppermute | solution.py:16
  63.4 1.3 convolution_bitcast_fusion
  64.7 4.4 %pad_maximum_fusion = f32[2048,1280]{0,1:T(8,128)} fusion(f32[2048,256]{0,1:T(8,128)S(1)} %fusion.10, f32[2048,512]{0,1:T(8,128)S(1)} %convolution_bitcast_fusion, f32[2048,512]{0,1:T(8,128)S(1)} %convolution_bitcast_fusion.1), kind=kLoop, calls=%fused_computation | loop fusion | flops 5242880 | bytes 20971520 | tf_op jit(solution)/shard_map/concatenate | solution.py:127
  69.1 11.3 %copy.32 = f32[2048,1280]{1,0:T(8,128)} copy(f32[2048,1280]{0,1:T(8,128)} %pad_maximum_fusion) | data formatting | bytes 20971520 | tf_op jit(solution)/shard_map/concatenate | solution.py:127
  80.4 5.3 %dynamic-slice_bitcast_fusion = f32[8,2,64,1280]{3,2,1,0:T(8,128)} fusion(f32[8,2,2,64,1280]{4,3,2,1,0:T(8,128)} %bitcast.115, s32[]{:T(128)S(6)} %select_n.222), kind=kLoop, calls=%fused_computation.2 | loop fusion | bytes 10485764 | tf_op jit(solution)/shard_map/jit(dynamic_index_in_dim)/squeeze | solution.py:52
  86.3 4.9 %fusion.1 = f32[2048,512]{1,0:T(8,128)} fusion(bf16[2048,256]{1,0:T(8,128)(2,1)} %get-tuple-element.6, bf16[2048,256]{1,0:T(8,128)(2,1)} %get-tuple-element.7, bf16[512,256]{0,1:T(8,128)(2,1)S(1)} %copy-done.10, bf16[512,256]{0,1:T(8,128)(2,1)S(1)} %get-tuple-element.9), kind=kOutput, calls=%fused_computation.11 | convolution fusion | flops 1078984704 | bytes 6815744 | tf_op jit(solution)/shard_map/dot_general | solution.py:26
  91.5 3.6 %convolution_add_fusion = f32[2048,512]{1,0:T(8,128)S(1)} fusion(f32[2048,512]{1,0:T(8,128)} %fusion.1, bf16[512,512]{1,0:T(8,128)(2,1)S(1)} %bitcast.123, bf16[2048,256]{1,0:T(8,128)(2,1)S(1)} %copy-done.4, bf16[2048,256]{1,0:T(8,128)(2,1)S(1)} %get-tuple-element.5), kind=kOutput, calls=%fused_computation.5 | convolution fusion | flops 1078984704 | bytes 11010048 | tf_op jit(solution)/shard_map/dot_general | solution.py:26
  95.6 1.5 copy-done.2
  97.1 3.3 %collective-permute-start.5 = (f32[512,64]{1,0:T(8,128)S(1)}, f32[512,64]{1,0:T(8,128)S(1)}, u32[]{:S(2)}, u32[]{:S(2)}) collective-permute-start(f32[512,64]{1,0:T(8,128)S(1)} %dynamic-slice_bitcast_fusion.3), channel_id=1, source_target_pairs={{0,6},{2,0},{4,2},{6,4},{1,7},{3,1},{5,3},{7,5},{8,14},{10,8},{12,... | collective-permute-start | bytes 393224 | tf_op jit(solution)/shard_map/ppermute | solution.py:67
  101.2 3.7 %slice.58 = f32[2048,384]{1,0:T(8,128)} slice(f32[2048,512]{1,0:T(8,128)} %copy-done.2), slice={[0:2048], [0:384]} | slice | bytes 6291456 | tf_op jit(solution)/shard_map/slice | solution.py:118
  105.1 1.6 collective-permute-done.5
  106.7 3.8 %collective-permute-start.6 = (f32[512,64]{1,0:T(8,128)S(1)}, f32[512,64]{1,0:T(8,128)S(1)}, u32[]{:S(2)}, u32[]{:S(2)}) collective-permute-start(f32[512,64]{1,0:T(8,128)S(1)} %bitcast_add_fusion.17), channel_id=1, source_target_pairs={{0,6},{2,0},{4,2},{6,4},{1,7},{3,1},{5,3},{7,5},{8,14},{10,8},{12,... | collective-permute-start | bytes 393224 | tf_op jit(solution)/shard_map/ppermute | solution.py:67
  110.4 4.2 %collective-permute-done.2 = f32[512,64]{1,0:T(8,128)S(1)} collective-permute-done((f32[512,64]{1,0:T(8,128)S(1)}, f32[512,64]{1,0:T(8,128)S(1)}, u32[]{:S(2)}, u32[]{:S(2)}) %collective-permute-start.2) | collective-permute-done | bytes 131104 | tf_op jit(solution)/shard_map/ppermute | solution.py:67
  114.8 5.1 %bitcast_add_fusion = f32[8,2,64,1280]{3,2,1,0:T(8,128)S(1)} fusion(f32[8,2,64,1280]{3,2,1,0:T(8,128)} %collective-permute-done.9, f32[8,2,2,64,1280]{4,3,2,1,0:T(8,128)} %bitcast.116, s32[]{:T(128)S(6)} %select_n.221), kind=kLoop, calls=%fused_computation.1 | loop fusion | flops 1310720 | bytes 15728644 | tf_op jit(solution)/shard_map/add | solution.py:53
  120.6 1.8 collective-permute-start.10
  122.9 3.3 %collective-permute-start.7 = (f32[512,64]{1,0:T(8,128)S(1)}, f32[512,64]{1,0:T(8,128)S(1)}, u32[]{:S(2)}, u32[]{:S(2)}) collective-permute-start(f32[512,64]{1,0:T(8,128)S(1)} %bitcast_add_fusion.16), channel_id=1, source_target_pairs={{0,6},{2,0},{4,2},{6,4},{1,7},{3,1},{5,3},{7,5},{8,14},{10,8},{12,... | collective-permute-start | bytes 393224 | tf_op jit(solution)/shard_map/ppermute | solution.py:67
  126.1 3.5 %collective-permute-done.10 = f32[2,64,640]{2,1,0:T(8,128)S(1)} collective-permute-done((f32[2,64,640]{2,1,0:T(8,128)S(1)}, f32[2,64,640]{2,1,0:T(8,128)S(1)}, u32[]{:S(2)}, u32[]{:S(2)}) %collective-permute-start.10) | collective-permute-done | bytes 327712 | tf_op jit(solution)/shard_map/ppermute | solution.py:41
  129.7 2.8 %collective-permute-start.11 = (f32[2,64,640]{2,1,0:T(8,128)S(1)}, f32[2,64,640]{2,1,0:T(8,128)S(1)}, u32[]{:S(2)}, u32[]{:S(2)}) collective-permute-start(f32[2,64,640]{2,1,0:T(8,128)S(1)} %bitcast_add_fusion.14), channel_id=1, source_target_pairs={{0,32},{32,64},{64,96},{96,128},{128,160},{160,192},{192,224},{224... | collective-permute-start | bytes 983048 | tf_op jit(solution)/shard_map/ppermute | solution.py:41
  132.7 5.1 %collective-permute-done.11 = f32[2,64,640]{2,1,0:T(8,128)S(1)} collective-permute-done((f32[2,64,640]{2,1,0:T(8,128)S(1)}, f32[2,64,640]{2,1,0:T(8,128)S(1)}, u32[]{:S(2)}, u32[]{:S(2)}) %collective-permute-start.11) | collective-permute-done | bytes 327712 | tf_op jit(solution)/shard_map/ppermute | solution.py:41
  137.9 3.7 %collective-permute-start.12 = (f32[2,64,640]{2,1,0:T(8,128)S(1)}, f32[2,64,640]{2,1,0:T(8,128)S(1)}, u32[]{:S(2)}, u32[]{:S(2)}) collective-permute-start(f32[2,64,640]{2,1,0:T(8,128)S(1)} %bitcast_add_fusion.13), channel_id=1, source_target_pairs={{0,32},{32,64},{64,96},{96,128},{128,160},{160,192},{192,224},{224... | collective-permute-start | bytes 983048 | tf_op jit(solution)/shard_map/ppermute | solution.py:41
  141.8 4.4 %collective-permute-done.12 = f32[2,64,640]{2,1,0:T(8,128)S(1)} collective-permute-done((f32[2,64,640]{2,1,0:T(8,128)S(1)}, f32[2,64,640]{2,1,0:T(8,128)S(1)}, u32[]{:S(2)}, u32[]{:S(2)}) %collective-permute-start.12) | collective-permute-done | bytes 327712 | tf_op jit(solution)/shard_map/ppermute | solution.py:41
  146.3 3.8 %collective-permute-start.13 = (f32[2,64,640]{2,1,0:T(8,128)S(1)}, f32[2,64,640]{2,1,0:T(8,128)S(1)}, u32[]{:S(2)}, u32[]{:S(2)}) collective-permute-start(f32[2,64,640]{2,1,0:T(8,128)S(1)} %bitcast_add_fusion.12), channel_id=1, source_target_pairs={{0,32},{32,64},{64,96},{96,128},{128,160},{160,192},{192,224},{224... | collective-permute-start | bytes 983048 | tf_op jit(solution)/shard_map/ppermute | solution.py:41
  150.5 4.9 %collective-permute-done.13 = f32[2,64,640]{2,1,0:T(8,128)S(1)} collective-permute-done((f32[2,64,640]{2,1,0:T(8,128)S(1)}, f32[2,64,640]{2,1,0:T(8,128)S(1)}, u32[]{:S(2)}, u32[]{:S(2)}) %collective-permute-start.13) | collective-permute-done | bytes 327712 | tf_op jit(solution)/shard_map/ppermute | solution.py:41
  155.4 3.8 %collective-permute-start.14 = (f32[2,64,640]{2,1,0:T(8,128)S(1)}, f32[2,64,640]{2,1,0:T(8,128)S(1)}, u32[]{:S(2)}, u32[]{:S(2)}) collective-permute-start(f32[2,64,640]{2,1,0:T(8,128)S(1)} %bitcast_add_fusion.11), channel_id=1, source_target_pairs={{0,32},{32,64},{64,96},{96,128},{128,160},{160,192},{192,224},{224... | collective-permute-start | bytes 983048 | tf_op jit(solution)/shard_map/ppermute | solution.py:41
  160.0 5.5 %collective-permute-done.14 = f32[2,64,640]{2,1,0:T(8,128)S(1)} collective-permute-done((f32[2,64,640]{2,1,0:T(8,128)S(1)}, f32[2,64,640]{2,1,0:T(8,128)S(1)}, u32[]{:S(2)}, u32[]{:S(2)}) %collective-permute-start.14) | collective-permute-done | bytes 327712 | tf_op jit(solution)/shard_map/ppermute | solution.py:41
  165.5 3.8 %collective-permute-start.15 = (f32[2,64,640]{2,1,0:T(8,128)S(1)}, f32[2,64,640]{2,1,0:T(8,128)S(1)}, u32[]{:S(2)}, u32[]{:S(2)}) collective-permute-start(f32[2,64,640]{2,1,0:T(8,128)S(1)} %bitcast_add_fusion.10), channel_id=1, source_target_pairs={{0,32},{32,64},{64,96},{96,128},{128,160},{160,192},{192,224},{224... | collective-permute-start | bytes 983048 | tf_op jit(solution)/shard_map/ppermute | solution.py:41
  169.3 1.0 collective-permute-done.21
  170.5 5.8 %collective-permute-done.15 = f32[2,64,640]{2,1,0:T(8,128)S(1)} collective-permute-done((f32[2,64,640]{2,1,0:T(8,128)S(1)}, f32[2,64,640]{2,1,0:T(8,128)S(1)}, u32[]{:S(2)}, u32[]{:S(2)}) %collective-permute-start.15) | collective-permute-done | bytes 327712 | tf_op jit(solution)/shard_map/ppermute | solution.py:41
  176.4 3.8 %collective-permute-start.16 = (f32[2,64,640]{2,1,0:T(8,128)S(1)}, f32[2,64,640]{2,1,0:T(8,128)S(1)}, u32[]{:S(2)}, u32[]{:S(2)}) collective-permute-start(f32[2,64,640]{2,1,0:T(8,128)S(1)} %bitcast_add_fusion.9), channel_id=1, source_target_pairs={{0,32},{32,64},{64,96},{96,128},{128,160},{160,192},{192,224},{224... | collective-permute-start | bytes 983048 | tf_op jit(solution)/shard_map/ppermute | solution.py:41
  180.2 1.8 collective-permute-done.22
  182.2 2.6 %collective-permute-done.16 = f32[2,64,640]{2,1,0:T(8,128)S(1)} collective-permute-done((f32[2,64,640]{2,1,0:T(8,128)S(1)}, f32[2,64,640]{2,1,0:T(8,128)S(1)}, u32[]{:S(2)}, u32[]{:S(2)}) %collective-permute-start.16) | collective-permute-done | bytes 327712 | tf_op jit(solution)/shard_map/ppermute | solution.py:41
  184.8 5.6 %collective-permute-done.23 = f32[2,64,640]{2,1,0:T(8,128)S(1)} collective-permute-done((f32[2,64,640]{2,1,0:T(8,128)S(1)}, f32[2,64,640]{2,1,0:T(8,128)S(1)}, u32[]{:S(2)}, u32[]{:S(2)}) %collective-permute-start.23) | collective-permute-done | bytes 327712 | tf_op jit(solution)/shard_map/ppermute | solution.py:41
  191.2 2.0 collective-permute-start.24
  193.2 2.0 pad_maximum_fusion.8
  195.2 1.2 copy.34
  196.4 1.7 add_convert_fusion
  198.1 2.0 collective-permute-done.24
  200.1 1.0 fusion.9
  (94 shorter events, 9.6 us)
Async XLA Ops:
  7.2 4.0 %copy-start = (bf16[2,256,2048]{2,1,0:T(8,128)(2,1)S(1)}, bf16[2,256,2048]{2,1,0:T(8,128)(2,1)}, u32[]{:S(2)}) copy-start(bf16[2,256,2048]{2,1,0:T(8,128)(2,1)} %param.5) | copy-start | bytes 6291460
  7.2 186.0 %reduce-scatter.2.cloned.1.call-start = ((), (), s32[]{:S(2)}) async-start(), calls=%async_computation.1 | async-start | bytes 3538944 | tf_op jit(solution)/shard_map/reduce_scatter | solution.py:118
  11.1 2.2 %copy-start.3 = (bf16[2048,256]{1,0:T(8,128)(2,1)}, bf16[2048,256]{1,0:T(8,128)(2,1)S(1)}, u32[]{:S(2)}) copy-start(bf16[2048,256]{1,0:T(8,128)(2,1)S(1)} %get-tuple-element.8) | copy-start | bytes 3145732
  11.1 9.6 %copy-start.11 = (s32[2]{0:T(128)S(1)}, s32[2]{0:T(128)}, u32[]{:S(2)}) copy-start(s32[2]{0:T(128)} %param.9) | copy-start | bytes 28
  15.6 27.7 %collective-permute-start = (f32[2,256,512]{1,0,2:T(2,128)}, f32[2,256,512]{1,0,2:T(2,128)}, u32[]{:S(2)}, u32[]{:S(2)}) collective-permute-start(f32[2,256,512]{1,0,2:T(2,128)} %copy.28), channel_id=1, source_target_pairs={{0,32},{8,40},{16,48},{24,56},{32,64},{40,72},{48,80},{56,88},{64,... | collective-permute-start | bytes 3145736 | tf_op jit(solution)/shard_map/ppermute | solution.py:16
  20.8 3.0 %copy-start.6 = (bf16[2,256,2048]{2,1,0:T(8,128)(2,1)S(1)}, bf16[2,256,2048]{2,1,0:T(8,128)(2,1)}, u32[]{:S(2)}) copy-start(bf16[2,256,2048]{2,1,0:T(8,128)(2,1)} %param.6) | copy-start | bytes 6291460
  24.0 23.9 %copy-start.5 = (bf16[2,256,2048]{2,1,0:T(8,128)(2,1)}, bf16[2,256,2048]{2,1,0:T(8,128)(2,1)S(1)}, u32[]{:S(2)}) copy-start(bf16[2,256,2048]{2,1,0:T(8,128)(2,1)S(1)} %broadcast_select_fusion) | copy-start | bytes 6291460
  43.4 1.6 copy-start.12
  45.9 2.8 %copy-start.9 = (bf16[512,256]{0,1:T(8,128)(2,1)}, bf16[512,256]{0,1:T(8,128)(2,1)S(1)}, u32[]{:S(2)}) copy-start(bf16[512,256]{0,1:T(8,128)(2,1)S(1)} %get-tuple-element.10) | copy-start | bytes 786436
  46.0 16.7 %collective-permute-start.1 = (bf16[2,256,512]{1,2,0:T(8,128)(2,1)S(1)}, bf16[2,256,512]{1,2,0:T(8,128)(2,1)S(1)}, u32[]{:S(2)}, u32[]{:S(2)}) collective-permute-start(bf16[2,256,512]{1,2,0:T(8,128)(2,1)S(1)} %bitcast.127), channel_id=1, source_target_pairs={{32,0},{40,8},{48,16},{56,24},{64,32},{72,40},{80,48},{88,56},{96,... | collective-permute-start | bytes 1572872 | tf_op jit(solution)/shard_map/ppermute | solution.py:16
  62.6 0.8 copy-start.7
  80.4 5.9 %copy-start.10 = (bf16[512,256]{0,1:T(8,128)(2,1)S(1)}, bf16[512,256]{0,1:T(8,128)(2,1)}, u32[]{:S(2)}) copy-start(bf16[512,256]{0,1:T(8,128)(2,1)} %copy-done.9) | copy-start | bytes 786436
  85.7 29.1 %collective-permute-start.9 = (f32[8,2,64,1280]{3,2,1,0:T(8,128)}, f32[8,2,64,1280]{3,2,1,0:T(8,128)}, u32[]{:S(2)}, u32[]{:S(2)}) collective-permute-start(f32[8,2,64,1280]{3,2,1,0:T(8,128)} %dynamic-slice_bitcast_fusion), channel_id=1, source_target_pairs={{0,8},{8,0},{1,9},{9,1},{2,10},{10,2},{3,11},{11,3},{4,12},{12,4},... | collective-permute-start | bytes 15728648 | tf_op jit(solution)/shard_map/ppermute | solution.py:53
  86.3 5.0 %copy-start.8 = (bf16[2,256,512]{1,2,0:T(8,128)(2,1)S(1)}, bf16[2,256,512]{1,2,0:T(8,128)(2,1)}, u32[]{:S(2)}) copy-start(bf16[2,256,512]{1,2,0:T(8,128)(2,1)} %copy-done.7) | copy-start | bytes 1572868
  86.3 5.2 %copy-start.4 = (bf16[2048,256]{1,0:T(8,128)(2,1)S(1)}, bf16[2048,256]{1,0:T(8,128)(2,1)}, u32[]{:S(2)}) copy-start(bf16[2048,256]{1,0:T(8,128)(2,1)} %copy-done.3) | copy-start | bytes 3145732
  95.1 2.0 copy-start.2
  97.1 9.5 %collective-permute-start.5 = (f32[512,64]{1,0:T(8,128)S(1)}, f32[512,64]{1,0:T(8,128)S(1)}, u32[]{:S(2)}, u32[]{:S(2)}) collective-permute-start(f32[512,64]{1,0:T(8,128)S(1)} %dynamic-slice_bitcast_fusion.3), channel_id=1, source_target_pairs={{0,6},{2,0},{4,2},{6,4},{1,7},{3,1},{5,3},{7,5},{8,14},{10,8},{12,... | collective-permute-start | bytes 393224 | tf_op jit(solution)/shard_map/ppermute | solution.py:67
  104.9 9.7 %collective-permute-start.2 = (f32[512,64]{1,0:T(8,128)S(1)}, f32[512,64]{1,0:T(8,128)S(1)}, u32[]{:S(2)}, u32[]{:S(2)}) collective-permute-start(f32[512,64]{1,0:T(8,128)S(1)} %dynamic-slice_bitcast_fusion.4), channel_id=1, source_target_pairs={{0,2},{2,4},{4,6},{6,0},{1,3},{3,5},{5,7},{7,1},{8,10},{10,12},{12... | collective-permute-start | bytes 393224 | tf_op jit(solution)/shard_map/ppermute | solution.py:67
  106.7 16.1 %collective-permute-start.6 = (f32[512,64]{1,0:T(8,128)S(1)}, f32[512,64]{1,0:T(8,128)S(1)}, u32[]{:S(2)}, u32[]{:S(2)}) collective-permute-start(f32[512,64]{1,0:T(8,128)S(1)} %bitcast_add_fusion.17), channel_id=1, source_target_pairs={{0,6},{2,0},{4,2},{6,4},{1,7},{3,1},{5,3},{7,5},{8,14},{10,8},{12,... | collective-permute-start | bytes 393224 | tf_op jit(solution)/shard_map/ppermute | solution.py:67
  114.7 17.9 %collective-permute-start.3 = (f32[512,64]{1,0:T(8,128)S(1)}, f32[512,64]{1,0:T(8,128)S(1)}, u32[]{:S(2)}, u32[]{:S(2)}) collective-permute-start(f32[512,64]{1,0:T(8,128)S(1)} %bitcast_add_fusion.20), channel_id=1, source_target_pairs={{0,2},{2,4},{4,6},{6,0},{1,3},{3,5},{5,7},{7,1},{8,10},{10,12},{12... | collective-permute-start | bytes 393224 | tf_op jit(solution)/shard_map/ppermute | solution.py:67
  120.6 9.0 %collective-permute-start.10 = (f32[2,64,640]{2,1,0:T(8,128)S(1)}, f32[2,64,640]{2,1,0:T(8,128)S(1)}, u32[]{:S(2)}, u32[]{:S(2)}) collective-permute-start(f32[2,64,640]{2,1,0:T(8,128)S(1)} %dynamic-slice_bitcast_fusion.2), channel_id=1, source_target_pairs={{0,32},{32,64},{64,96},{96,128},{128,160},{160,192},{192,224},{224... | collective-permute-start | bytes 983048 | tf_op jit(solution)/shard_map/ppermute | solution.py:41
  122.4 10.0 %collective-permute-start.17 = (f32[2,64,640]{2,1,0:T(8,128)S(1)}, f32[2,64,640]{2,1,0:T(8,128)S(1)}, u32[]{:S(2)}, u32[]{:S(2)}) collective-permute-start(f32[2,64,640]{2,1,0:T(8,128)S(1)} %dynamic-slice_bitcast_fusion.1), channel_id=1, source_target_pairs={{0,224},{32,0},{64,32},{96,64},{128,96},{160,128},{192,160},{224,1... | collective-permute-start | bytes 983048 | tf_op jit(solution)/shard_map/ppermute | solution.py:41
  122.9 18.9 %collective-permute-start.7 = (f32[512,64]{1,0:T(8,128)S(1)}, f32[512,64]{1,0:T(8,128)S(1)}, u32[]{:S(2)}, u32[]{:S(2)}) collective-permute-start(f32[512,64]{1,0:T(8,128)S(1)} %bitcast_add_fusion.16), channel_id=1, source_target_pairs={{0,6},{2,0},{4,2},{6,4},{1,7},{3,1},{5,3},{7,5},{8,14},{10,8},{12,... | collective-permute-start | bytes 393224 | tf_op jit(solution)/shard_map/ppermute | solution.py:67
  129.7 8.2 %collective-permute-start.11 = (f32[2,64,640]{2,1,0:T(8,128)S(1)}, f32[2,64,640]{2,1,0:T(8,128)S(1)}, u32[]{:S(2)}, u32[]{:S(2)}) collective-permute-start(f32[2,64,640]{2,1,0:T(8,128)S(1)} %bitcast_add_fusion.14), channel_id=1, source_target_pairs={{0,32},{32,64},{64,96},{96,128},{128,160},{160,192},{192,224},{224... | collective-permute-start | bytes 983048 | tf_op jit(solution)/shard_map/ppermute | solution.py:41
  132.5 9.1 %collective-permute-start.18 = (f32[2,64,640]{2,1,0:T(8,128)S(1)}, f32[2,64,640]{2,1,0:T(8,128)S(1)}, u32[]{:S(2)}, u32[]{:S(2)}) collective-permute-start(f32[2,64,640]{2,1,0:T(8,128)S(1)} %bitcast_add_fusion.7), channel_id=1, source_target_pairs={{0,224},{32,0},{64,32},{96,64},{128,96},{160,128},{192,160},{224,1... | collective-permute-start | bytes 983048 | tf_op jit(solution)/shard_map/ppermute | solution.py:41
  132.6 17.8 %collective-permute-start.4 = (f32[512,64]{1,0:T(8,128)S(1)}, f32[512,64]{1,0:T(8,128)S(1)}, u32[]{:S(2)}, u32[]{:S(2)}) collective-permute-start(f32[512,64]{1,0:T(8,128)S(1)} %bitcast_add_fusion.19), channel_id=1, source_target_pairs={{0,2},{2,4},{4,6},{6,0},{1,3},{3,5},{5,7},{7,1},{8,10},{10,12},{12... | collective-permute-start | bytes 393224 | tf_op jit(solution)/shard_map/ppermute | solution.py:67
  137.9 8.3 %collective-permute-start.12 = (f32[2,64,640]{2,1,0:T(8,128)S(1)}, f32[2,64,640]{2,1,0:T(8,128)S(1)}, u32[]{:S(2)}, u32[]{:S(2)}) collective-permute-start(f32[2,64,640]{2,1,0:T(8,128)S(1)} %bitcast_add_fusion.13), channel_id=1, source_target_pairs={{0,32},{32,64},{64,96},{96,128},{128,160},{160,192},{192,224},{224... | collective-permute-start | bytes 983048 | tf_op jit(solution)/shard_map/ppermute | solution.py:41
  141.7 8.4 %collective-permute-start.19 = (f32[2,64,640]{2,1,0:T(8,128)S(1)}, f32[2,64,640]{2,1,0:T(8,128)S(1)}, u32[]{:S(2)}, u32[]{:S(2)}) collective-permute-start(f32[2,64,640]{2,1,0:T(8,128)S(1)} %bitcast_add_fusion.6), channel_id=1, source_target_pairs={{0,224},{32,0},{64,32},{96,64},{128,96},{160,128},{192,160},{224,1... | collective-permute-start | bytes 983048 | tf_op jit(solution)/shard_map/ppermute | solution.py:41
  146.3 9.1 %collective-permute-start.13 = (f32[2,64,640]{2,1,0:T(8,128)S(1)}, f32[2,64,640]{2,1,0:T(8,128)S(1)}, u32[]{:S(2)}, u32[]{:S(2)}) collective-permute-start(f32[2,64,640]{2,1,0:T(8,128)S(1)} %bitcast_add_fusion.12), channel_id=1, source_target_pairs={{0,32},{32,64},{64,96},{96,128},{128,160},{160,192},{192,224},{224... | collective-permute-start | bytes 983048 | tf_op jit(solution)/shard_map/ppermute | solution.py:41
  150.1 9.6 %collective-permute-start.20 = (f32[2,64,640]{2,1,0:T(8,128)S(1)}, f32[2,64,640]{2,1,0:T(8,128)S(1)}, u32[]{:S(2)}, u32[]{:S(2)}) collective-permute-start(f32[2,64,640]{2,1,0:T(8,128)S(1)} %bitcast_add_fusion.5), channel_id=1, source_target_pairs={{0,224},{32,0},{64,32},{96,64},{128,96},{160,128},{192,160},{224,1... | collective-permute-start | bytes 983048 | tf_op jit(solution)/shard_map/ppermute | solution.py:41
  155.4 10.0 %collective-permute-start.14 = (f32[2,64,640]{2,1,0:T(8,128)S(1)}, f32[2,64,640]{2,1,0:T(8,128)S(1)}, u32[]{:S(2)}, u32[]{:S(2)}) collective-permute-start(f32[2,64,640]{2,1,0:T(8,128)S(1)} %bitcast_add_fusion.11), channel_id=1, source_target_pairs={{0,32},{32,64},{64,96},{96,128},{128,160},{160,192},{192,224},{224... | collective-permute-start | bytes 983048 | tf_op jit(solution)/shard_map/ppermute | solution.py:41
  159.8 10.5 %collective-permute-start.21 = (f32[2,64,640]{2,1,0:T(8,128)S(1)}, f32[2,64,640]{2,1,0:T(8,128)S(1)}, u32[]{:S(2)}, u32[]{:S(2)}) collective-permute-start(f32[2,64,640]{2,1,0:T(8,128)S(1)} %bitcast_add_fusion.4), channel_id=1, source_target_pairs={{0,224},{32,0},{64,32},{96,64},{128,96},{160,128},{192,160},{224,1... | collective-permute-start | bytes 983048 | tf_op jit(solution)/shard_map/ppermute | solution.py:41
  165.5 10.9 %collective-permute-start.15 = (f32[2,64,640]{2,1,0:T(8,128)S(1)}, f32[2,64,640]{2,1,0:T(8,128)S(1)}, u32[]{:S(2)}, u32[]{:S(2)}) collective-permute-start(f32[2,64,640]{2,1,0:T(8,128)S(1)} %bitcast_add_fusion.10), channel_id=1, source_target_pairs={{0,32},{32,64},{64,96},{96,128},{128,160},{160,192},{192,224},{224... | collective-permute-start | bytes 983048 | tf_op jit(solution)/shard_map/ppermute | solution.py:41
  170.3 11.7 %collective-permute-start.22 = (f32[2,64,640]{2,1,0:T(8,128)S(1)}, f32[2,64,640]{2,1,0:T(8,128)S(1)}, u32[]{:S(2)}, u32[]{:S(2)}) collective-permute-start(f32[2,64,640]{2,1,0:T(8,128)S(1)} %bitcast_add_fusion.3), channel_id=1, source_target_pairs={{0,224},{32,0},{64,32},{96,64},{128,96},{160,128},{192,160},{224,1... | collective-permute-start | bytes 983048 | tf_op jit(solution)/shard_map/ppermute | solution.py:41
  170.4 11.7 %collective-permute-start.8 = (f32[256,128]{1,0:T(8,128)S(1)}, f32[256,128]{1,0:T(8,128)S(1)}, u32[]{:S(2)}, u32[]{:S(2)}) collective-permute-start(f32[256,128]{1,0:T(8,128)S(1)} %dynamic-slice_bitcast_fusion.5), channel_id=1, source_target_pairs={{0,1},{1,0},{2,3},{3,2},{4,5},{5,4},{6,7},{7,6},{8,9},{9,8},{10,11... | collective-permute-start | bytes 393224 | tf_op jit(solution)/shard_map/ppermute | solution.py:53
  176.4 8.4 %collective-permute-start.16 = (f32[2,64,640]{2,1,0:T(8,128)S(1)}, f32[2,64,640]{2,1,0:T(8,128)S(1)}, u32[]{:S(2)}, u32[]{:S(2)}) collective-permute-start(f32[2,64,640]{2,1,0:T(8,128)S(1)} %bitcast_add_fusion.9), channel_id=1, source_target_pairs={{0,32},{32,64},{64,96},{96,128},{128,160},{160,192},{192,224},{224... | collective-permute-start | bytes 983048 | tf_op jit(solution)/shard_map/ppermute | solution.py:41
  182.0 8.4 %collective-permute-start.23 = (f32[2,64,640]{2,1,0:T(8,128)S(1)}, f32[2,64,640]{2,1,0:T(8,128)S(1)}, u32[]{:S(2)}, u32[]{:S(2)}) collective-permute-start(f32[2,64,640]{2,1,0:T(8,128)S(1)} %bitcast_add_fusion.2), channel_id=1, source_target_pairs={{0,224},{32,0},{64,32},{96,64},{128,96},{160,128},{192,160},{224,1... | collective-permute-start | bytes 983048 | tf_op jit(solution)/shard_map/ppermute | solution.py:41
  191.2 8.9 %collective-permute-start.24 = (f32[64,1280]{1,0:T(8,128)}, f32[64,1280]{1,0:T(8,128)}, u32[]{:S(2)}, u32[]{:S(2)}) collective-permute-start(f32[64,1280]{1,0:T(8,128)} %fusion.6), channel_id=1, source_target_pairs={{0,16},{16,0},{1,17},{17,1},{2,18},{18,2},{3,19},{19,3},{4,20},{20... | collective-permute-start | bytes 983048 | tf_op jit(solution)/shard_map/ppermute | solution.py:53
  193.2 9.6 %copy-start.1 = (bf16[2,256,2048]{2,1,0:T(8,128)(2,1)S(1)}, bf16[2,256,2048]{2,1,0:T(8,128)(2,1)}, u32[]{:S(2)}) copy-start(bf16[2,256,2048]{2,1,0:T(8,128)(2,1)} %param.5) | copy-start | bytes 6291460
Sparse Core Ops, SparseCore 0:
  105.2 76.3 reduce-scatter.1

commit v9 on v7

--- a/solution.py
+++ b/solution.py
@@ -31,10 +31,9 @@
 def ring_sum(chunks, axis):
     peers = lax.axis_size(axis)
     at = lax.axis_index(axis)
-    half = chunks.shape[-1] // 2
     sums = []
-    for step, cols in ((1, slice(0, half)), (-1, slice(half, None))):
-        own = chunks[..., cols]
+    for step, half in ((1, 0), (-1, 1)):
+        own = chunks[:, half]
         pairs = [(i, (i + step) % peers) for i in range(peers)]
         acc = lax.dynamic_index_in_dim(own, (at - step) % peers, 0, keepdims=False)
         for s in range(peers - 1):
@@ -43,7 +42,7 @@
                 own, (at - step * (s + 2)) % peers, 0, keepdims=False
             )
         sums.append(acc)
-    return jnp.concatenate(sums, axis=-1)
+    return jnp.stack(sums)
 
 
 def swap_sum(parts, axis):

time: 206 us -> 228 us (1.11)
  waiting for transfers between devices: 77.8 us -> 101 us
  starting transfers between devices: 44.6 us -> 41.1 us
  other arithmetic: 17.5 us -> 20.2 us
    ppermute x6, waiting for transfers between devices: 4.72 us -> 16.8 us  [chan_ring_reduce_scatter(): got = lax.ppermute(acc, 'cy', pairs)]
    ppermute x14, waiting for transfers between devices: 39.2 us -> 50.6 us  [ring_sum(): got = lax.ppermute(acc, axis, pairs)]
    ppermute x14, starting transfers between devices: 24.8 us -> 20.3 us  [ring_sum(): got = lax.ppermute(acc, axis, pairs)]
    add x6, other arithmetic: 0.19 us -> 3.02 us  [chan_ring_reduce_scatter(): got + lax.dynamic_index_in_dim(own, (at - step * (s + 2)) % peers, 0, kee...]
  transfers between devices with their start and end apart: 26 -> 26, of which waited for: 14 -> 21; matrix products, arithmetic and copies ran while one was open for 14% -> 14% of each run, Pallas kernels for 0% -> 0%
where the time goes in v9:
time: 228 us; the launch traced here: 227 us
  waiting for transfers between devices  101 us (44%)
  starting transfers between devices  41.1 us (18%)
  local copies, waits for them, and re-layouts  30.9 us (14%)
  other arithmetic  20.2 us (9%)
  matrix products  17.8 us (8%)
  between operations  15.3 us (7%)
    ppermute x14, waiting for transfers between devices, ring_sum(): got = lax.ppermute(acc, axis, pairs)  50.6 us
    ppermute x2, waiting for transfers between devices, shifted(): return lax.ppermute(x, axis, pairs)  32 us
    ppermute x14, starting transfers between devices, ring_sum(): got = lax.ppermute(acc, axis, pairs)  20.3 us
    ppermute x6, waiting for transfers between devices, chan_ring_reduce_scatter(): got = lax.ppermute(acc, 'cy', pairs)  16.8 us
    concatenate x1, local copies, waits for them, and re-layouts, local(): jnp.concatenate([contract_rows(rows, branch_grads), contract_rows(rows, l...  11.3 us
    ppermute x6, starting transfers between devices, chan_ring_reduce_scatter(): got = lax.ppermute(acc, 'cy', pairs)  11 us
    dot_general x3, matrix products, contract_cols(): lax.dot_general(left, right, (((1,), (1,)), ((), ())), preferred_element_...  9.32 us
    ppermute x2, starting transfers between devices, shifted(): return lax.ppermute(x, axis, pairs)  6.95 us
  transfers between devices with their start and end apart: 26, of which 21 were waited for; matrix products, arithmetic and copies ran while one was open for 14% of the time, Pallas kernels for 0%

profile of v9, /device:TPU:98, one launch (start us, length us, event | category | flops | bytes accessed | tf_op | source)
XLA Modules:
  0.0 226.6 jit_solution(7068871007427551196)
XLA Ops:
  7.2 3.9 %slice_bitcast_fusion.1 = (bf16[2048,256]{1,0:T(8,128)(2,1)S(1)}, bf16[2048,256]{1,0:T(8,128)(2,1)}, bf16[2048,256]{1,0:T(8,128)(2,1)}, bf16[2048,256]{1,0:T(8,128)(2,1)S(1)}) fusion(bf16[2,2,2048,256]{3,2,1,0:T(8,128)(2,1)} %param.7), kind=kLoop, calls=%fused_computation.13 | loop fusion | bytes 8388608 | tf_op jit(solution)/shard_map/squeeze | solution.py:90
  11.2 2.2 fusion
  13.4 2.3 copy.28
  15.7 5.0 %collective-permute-start = (f32[2,256,512]{1,0,2:T(2,128)}, f32[2,256,512]{1,0,2:T(2,128)}, u32[]{:S(2)}, u32[]{:S(2)}) collective-permute-start(f32[2,256,512]{1,0,2:T(2,128)} %copy.28), channel_id=1, source_target_pairs={{0,32},{8,40},{16,48},{24,56},{32,64},{40,72},{48,80},{56,88},{64,... | collective-permute-start | bytes 3145736 | tf_op jit(solution)/shard_map/ppermute | solution.py:16
  20.8 3.0 %convolution_bitcast_fusion.2 = f32[512,512]{0,1:T(8,128)S(1)} fusion(bf16[512,2048]{1,0:T(8,128)(2,1)S(1)} %bitcast.120, bf16[2048,256]{1,0:T(8,128)(2,1)} %get-tuple-element.8, bf16[2048,256]{1,0:T(8,128)(2,1)} %get-tuple-element.9), kind=kOutput, calls=%fused_computation.9 | convolution fusion | flops 1077936128 | bytes 5242880 | tf_op jit(solution)/shard_map/dot_general | solution.py:95
  24.0 19.4 %collective-permute-done = f32[2,256,512]{1,0,2:T(2,128)} collective-permute-done((f32[2,256,512]{1,0,2:T(2,128)}, f32[2,256,512]{1,0,2:T(2,128)}, u32[]{:S(2)}, u32[]{:S(2)}) %collective-permute-start) | collective-permute-done | bytes 1048608 | tf_op jit(solution)/shard_map/ppermute | solution.py:16
  43.4 1.4 copy.36
  46.0 1.9 collective-permute-start.1
  48.8 1.3 convolution_bitcast_fusion.1
  50.1 12.6 %collective-permute-done.1 = bf16[2,256,512]{1,2,0:T(8,128)(2,1)S(1)} collective-permute-done((bf16[2,256,512]{1,2,0:T(8,128)(2,1)S(1)}, bf16[2,256,512]{1,2,0:T(8,128)(2,1)S(1)}, u32[]{:S(2)}, u32[]{:S(2)}) %collective-permute-start.1) | collective-permute-done | bytes 524320 | tf_op jit(solution)/shard_map/ppermute | solution.py:16
  63.5 1.3 convolution_bitcast_fusion
  64.7 4.4 %pad_maximum_fusion = f32[2048,1280]{0,1:T(8,128)} fusion(f32[2048,256]{0,1:T(8,128)S(1)} %fusion.12, f32[2048,512]{0,1:T(8,128)S(1)} %convolution_bitcast_fusion, f32[2048,512]{0,1:T(8,128)S(1)} %convolution_bitcast_fusion.1), kind=kLoop, calls=%fused_computation | loop fusion | flops 5242880 | bytes 20971520 | tf_op jit(solution)/shard_map/concatenate | solution.py:126
  69.2 11.3 %copy.32 = f32[2048,1280]{1,0:T(8,128)} copy(f32[2048,1280]{0,1:T(8,128)} %pad_maximum_fusion) | data formatting | bytes 20971520 | tf_op jit(solution)/shard_map/concatenate | solution.py:126
  80.5 5.4 %dynamic-slice_bitcast_fusion = f32[8,2,64,1280]{3,2,1,0:T(8,128)} fusion(f32[8,2,2,64,1280]{4,3,2,1,0:T(8,128)} %bitcast.123, s32[]{:T(128)S(6)} %select_n.222), kind=kLoop, calls=%fused_computation.2 | loop fusion | bytes 10485764 | tf_op jit(solution)/shard_map/jit(dynamic_index_in_dim)/squeeze | solution.py:51
  85.9 4.9 %fusion.1 = f32[2048,512]{1,0:T(8,128)} fusion(bf16[2048,256]{1,0:T(8,128)(2,1)} %get-tuple-element.8, bf16[2048,256]{1,0:T(8,128)(2,1)} %get-tuple-element.9, bf16[512,256]{0,1:T(8,128)(2,1)S(1)} %copy-done.10, bf16[512,256]{0,1:T(8,128)(2,1)S(1)} %get-tuple-element.13), kind=kOutput, calls=%fused_computation.11 | convolution fusion | flops 1078984704 | bytes 6815744 | tf_op jit(solution)/shard_map/dot_general | solution.py:26
  91.1 3.5 %convolution_add_fusion = f32[2048,512]{1,0:T(8,128)S(1)} fusion(f32[2048,512]{1,0:T(8,128)} %fusion.1, bf16[512,512]{1,0:T(8,128)(2,1)S(1)} %bitcast.133, bf16[2048,256]{1,0:T(8,128)(2,1)S(1)} %copy-done.4, bf16[2048,256]{1,0:T(8,128)(2,1)S(1)} %get-tuple-element.7), kind=kOutput, calls=%fused_computation.5 | convolution fusion | flops 1078984704 | bytes 11010048 | tf_op jit(solution)/shard_map/dot_general | solution.py:26
  94.6 1.7 fusion.20
  97.4 3.3 %collective-permute-start.5 = (f32[512,128]{1,0:T(8,128)S(1)}, f32[512,128]{1,0:T(8,128)S(1)}, u32[]{:S(2)}, u32[]{:S(2)}) collective-permute-start(f32[512,128]{1,0:T(8,128)S(1)} %dynamic-slice_bitcast_fusion.4), channel_id=1, source_target_pairs={{0,6},{2,0},{4,2},{6,4},{1,7},{3,1},{5,3},{7,5},{8,14},{10,8},{12,... | collective-permute-start | bytes 786440 | tf_op jit(solution)/shard_map/ppermute | solution.py:66
  100.8 6.1 %collective-permute-done.5 = f32[512,128]{1,0:T(8,128)S(1)} collective-permute-done((f32[512,128]{1,0:T(8,128)S(1)}, f32[512,128]{1,0:T(8,128)S(1)}, u32[]{:S(2)}, u32[]{:S(2)}) %collective-permute-start.5) | collective-permute-done | bytes 262176 | tf_op jit(solution)/shard_map/ppermute | solution.py:66
  106.9 1.0 bitcast_add_fusion.18
  107.9 3.8 %collective-permute-start.6 = (f32[512,128]{1,0:T(8,128)S(1)}, f32[512,128]{1,0:T(8,128)S(1)}, u32[]{:S(2)}, u32[]{:S(2)}) collective-permute-start(f32[512,128]{1,0:T(8,128)S(1)} %bitcast_add_fusion.18), channel_id=1, source_target_pairs={{0,6},{2,0},{4,2},{6,4},{1,7},{3,1},{5,3},{7,5},{8,14},{10,8},{12,... | collective-permute-start | bytes 786440 | tf_op jit(solution)/shard_map/ppermute | solution.py:66
  111.8 5.2 %collective-permute-done.6 = f32[512,128]{1,0:T(8,128)S(1)} collective-permute-done((f32[512,128]{1,0:T(8,128)S(1)}, f32[512,128]{1,0:T(8,128)S(1)}, u32[]{:S(2)}, u32[]{:S(2)}) %collective-permute-start.6) | collective-permute-done | bytes 262176 | tf_op jit(solution)/shard_map/ppermute | solution.py:66
  118.0 3.8 %collective-permute-start.7 = (f32[512,128]{1,0:T(8,128)S(1)}, f32[512,128]{1,0:T(8,128)S(1)}, u32[]{:S(2)}, u32[]{:S(2)}) collective-permute-start(f32[512,128]{1,0:T(8,128)S(1)} %bitcast_add_fusion.17), channel_id=1, source_target_pairs={{0,6},{2,0},{4,2},{6,4},{1,7},{3,1},{5,3},{7,5},{8,14},{10,8},{12,... | collective-permute-start | bytes 786440 | tf_op jit(solution)/shard_map/ppermute | solution.py:66
  123.3 3.0 %collective-permute-done.7 = f32[512,128]{1,0:T(8,128)S(1)} collective-permute-done((f32[512,128]{1,0:T(8,128)S(1)}, f32[512,128]{1,0:T(8,128)S(1)}, u32[]{:S(2)}, u32[]{:S(2)}) %collective-permute-start.7) | collective-permute-done | bytes 262176 | tf_op jit(solution)/shard_map/ppermute | solution.py:66
  126.3 1.0 bitcast_add_fusion.16
  127.2 2.5 %collective-permute-done.4 = f32[512,128]{1,0:T(8,128)S(1)} collective-permute-done((f32[512,128]{1,0:T(8,128)S(1)}, f32[512,128]{1,0:T(8,128)S(1)}, u32[]{:S(2)}, u32[]{:S(2)}) %collective-permute-start.4) | collective-permute-done | bytes 262176 | tf_op jit(solution)/shard_map/ppermute | solution.py:66
  130.6 4.8 %bitcast_add_fusion = f32[8,2,64,1280]{3,2,1,0:T(8,128)S(1)} fusion(f32[8,2,64,1280]{3,2,1,0:T(8,128)} %collective-permute-done.9, f32[8,2,2,64,1280]{4,3,2,1,0:T(8,128)} %bitcast.124, s32[]{:T(128)S(6)} %select_n.221), kind=kLoop, calls=%fused_computation.1 | loop fusion | flops 1310720 | bytes 15728644 | tf_op jit(solution)/shard_map/add | solution.py:52
  135.8 1.8 collective-permute-start.10
  138.1 5.9 %collective-permute-done.10 = f32[64,1280]{1,0:T(8,128)S(1)} collective-permute-done((f32[64,1280]{1,0:T(8,128)S(1)}, f32[64,1280]{1,0:T(8,128)S(1)}, u32[]{:S(2)}, u32[]{:S(2)}) %collective-permute-start.10) | collective-permute-done | bytes 327712 | tf_op jit(solution)/shard_map/ppermute | solution.py:40
  144.1 1.9 collective-permute-start.11
  146.3 6.7 %collective-permute-done.11 = f32[64,1280]{1,0:T(8,128)S(1)} collective-permute-done((f32[64,1280]{1,0:T(8,128)S(1)}, f32[64,1280]{1,0:T(8,128)S(1)}, u32[]{:S(2)}, u32[]{:S(2)}) %collective-permute-start.11) | collective-permute-done | bytes 327712 | tf_op jit(solution)/shard_map/ppermute | solution.py:40
  153.0 2.1 collective-permute-start.12
  155.7 7.1 %collective-permute-done.12 = f32[64,1280]{1,0:T(8,128)S(1)} collective-permute-done((f32[64,1280]{1,0:T(8,128)S(1)}, f32[64,1280]{1,0:T(8,128)S(1)}, u32[]{:S(2)}, u32[]{:S(2)}) %collective-permute-start.12) | collective-permute-done | bytes 327712 | tf_op jit(solution)/shard_map/ppermute | solution.py:40
  162.9 2.6 %collective-permute-start.13 = (f32[64,1280]{1,0:T(8,128)S(1)}, f32[64,1280]{1,0:T(8,128)S(1)}, u32[]{:S(2)}, u32[]{:S(2)}) collective-permute-start(f32[64,1280]{1,0:T(8,128)S(1)} %bitcast_add_fusion.12), channel_id=1, source_target_pairs={{0,32},{32,64},{64,96},{96,128},{128,160},{160,192},{192,224},{224... | collective-permute-start | bytes 983048 | tf_op jit(solution)/shard_map/ppermute | solution.py:40
  166.1 7.4 %collective-permute-done.13 = f32[64,1280]{1,0:T(8,128)S(1)} collective-permute-done((f32[64,1280]{1,0:T(8,128)S(1)}, f32[64,1280]{1,0:T(8,128)S(1)}, u32[]{:S(2)}, u32[]{:S(2)}) %collective-permute-start.13) | collective-permute-done | bytes 327712 | tf_op jit(solution)/shard_map/ppermute | solution.py:40
  173.5 3.2 %collective-permute-start.14 = (f32[64,1280]{1,0:T(8,128)S(1)}, f32[64,1280]{1,0:T(8,128)S(1)}, u32[]{:S(2)}, u32[]{:S(2)}) collective-permute-start(f32[64,1280]{1,0:T(8,128)S(1)} %bitcast_add_fusion.11), channel_id=1, source_target_pairs={{0,32},{32,64},{64,96},{96,128},{128,160},{160,192},{192,224},{224... | collective-permute-start | bytes 983048 | tf_op jit(solution)/shard_map/ppermute | solution.py:40
  177.6 6.8 %collective-permute-done.14 = f32[64,1280]{1,0:T(8,128)S(1)} collective-permute-done((f32[64,1280]{1,0:T(8,128)S(1)}, f32[64,1280]{1,0:T(8,128)S(1)}, u32[]{:S(2)}, u32[]{:S(2)}) %collective-permute-start.14) | collective-permute-done | bytes 327712 | tf_op jit(solution)/shard_map/ppermute | solution.py:40
  184.4 3.8 %collective-permute-start.15 = (f32[64,1280]{1,0:T(8,128)S(1)}, f32[64,1280]{1,0:T(8,128)S(1)}, u32[]{:S(2)}, u32[]{:S(2)}) collective-permute-start(f32[64,1280]{1,0:T(8,128)S(1)} %bitcast_add_fusion.10), channel_id=1, source_target_pairs={{0,32},{32,64},{64,96},{96,128},{128,160},{160,192},{192,224},{224... | collective-permute-start | bytes 983048 | tf_op jit(solution)/shard_map/ppermute | solution.py:40
  188.8 6.2 %collective-permute-done.15 = f32[64,1280]{1,0:T(8,128)S(1)} collective-permute-done((f32[64,1280]{1,0:T(8,128)S(1)}, f32[64,1280]{1,0:T(8,128)S(1)}, u32[]{:S(2)}, u32[]{:S(2)}) %collective-permute-start.15) | collective-permute-done | bytes 327712 | tf_op jit(solution)/shard_map/ppermute | solution.py:40
  195.0 3.8 %collective-permute-start.16 = (f32[64,1280]{1,0:T(8,128)S(1)}, f32[64,1280]{1,0:T(8,128)S(1)}, u32[]{:S(2)}, u32[]{:S(2)}) collective-permute-start(f32[64,1280]{1,0:T(8,128)S(1)} %bitcast_add_fusion.9), channel_id=1, source_target_pairs={{0,32},{32,64},{64,96},{96,128},{128,160},{160,192},{192,224},{224... | collective-permute-start | bytes 983048 | tf_op jit(solution)/shard_map/ppermute | solution.py:40
  199.1 4.2 %collective-permute-done.16 = f32[64,1280]{1,0:T(8,128)S(1)} collective-permute-done((f32[64,1280]{1,0:T(8,128)S(1)}, f32[64,1280]{1,0:T(8,128)S(1)}, u32[]{:S(2)}, u32[]{:S(2)}) %collective-permute-start.16) | collective-permute-done | bytes 327712 | tf_op jit(solution)/shard_map/ppermute | solution.py:40
  203.4 4.0 %collective-permute-done.23 = f32[64,1280]{1,0:T(8,128)S(1)} collective-permute-done((f32[64,1280]{1,0:T(8,128)S(1)}, f32[64,1280]{1,0:T(8,128)S(1)}, u32[]{:S(2)}, u32[]{:S(2)}) %collective-permute-start.23) | collective-permute-done | bytes 327712 | tf_op jit(solution)/shard_map/ppermute | solution.py:40
  208.2 2.1 collective-permute-start.24
  210.3 2.0 pad_maximum_fusion.9
  212.2 1.2 copy.34
  213.5 1.7 add_convert_fusion
  215.2 1.9 collective-permute-done.24
  217.1 1.0 fusion.9
  (93 shorter events, 14.0 us)
Async XLA Ops:
  7.2 4.0 %copy-start = (bf16[2,256,2048]{2,1,0:T(8,128)(2,1)S(1)}, bf16[2,256,2048]{2,1,0:T(8,128)(2,1)}, u32[]{:S(2)}) copy-start(bf16[2,256,2048]{2,1,0:T(8,128)(2,1)} %param.5) | copy-start | bytes 6291460
  7.2 203.1 %reduce-scatter.2.cloned.1.call-start = ((), (), s32[]{:S(2)}) async-start(), calls=%async_computation.1 | async-start | bytes 2359296 | tf_op jit(solution)/shard_map/reduce_scatter | solution.py:117
  11.2 2.2 copy-start.3
  11.2 9.6 %copy-start.11 = (s32[2]{0:T(128)S(1)}, s32[2]{0:T(128)}, u32[]{:S(2)}) copy-start(s32[2]{0:T(128)} %param.9) | copy-start | bytes 28
  15.7 27.7 %collective-permute-start = (f32[2,256,512]{1,0,2:T(2,128)}, f32[2,256,512]{1,0,2:T(2,128)}, u32[]{:S(2)}, u32[]{:S(2)}) collective-permute-start(f32[2,256,512]{1,0,2:T(2,128)} %copy.28), channel_id=1, source_target_pairs={{0,32},{8,40},{16,48},{24,56},{32,64},{40,72},{48,80},{56,88},{64,... | collective-permute-start | bytes 3145736 | tf_op jit(solution)/shard_map/ppermute | solution.py:16
  20.8 3.0 %copy-start.6 = (bf16[2,256,2048]{2,1,0:T(8,128)(2,1)S(1)}, bf16[2,256,2048]{2,1,0:T(8,128)(2,1)}, u32[]{:S(2)}) copy-start(bf16[2,256,2048]{2,1,0:T(8,128)(2,1)} %param.6) | copy-start | bytes 6291460
  24.0 23.9 %copy-start.5 = (bf16[2,256,2048]{2,1,0:T(8,128)(2,1)}, bf16[2,256,2048]{2,1,0:T(8,128)(2,1)S(1)}, u32[]{:S(2)}) copy-start(bf16[2,256,2048]{2,1,0:T(8,128)(2,1)S(1)} %broadcast_select_fusion) | copy-start | bytes 6291460
  43.4 1.6 copy-start.12
  45.9 2.8 %copy-start.9 = (bf16[512,256]{0,1:T(8,128)(2,1)}, bf16[512,256]{0,1:T(8,128)(2,1)S(1)}, u32[]{:S(2)}) copy-start(bf16[512,256]{0,1:T(8,128)(2,1)S(1)} %get-tuple-element.14) | copy-start | bytes 786436
  46.0 16.7 %collective-permute-start.1 = (bf16[2,256,512]{1,2,0:T(8,128)(2,1)S(1)}, bf16[2,256,512]{1,2,0:T(8,128)(2,1)S(1)}, u32[]{:S(2)}, u32[]{:S(2)}) collective-permute-start(bf16[2,256,512]{1,2,0:T(8,128)(2,1)S(1)} %bitcast.135), channel_id=1, source_target_pairs={{32,0},{40,8},{48,16},{56,24},{64,32},{72,40},{80,48},{88,56},{96,... | collective-permute-start | bytes 1572872 | tf_op jit(solution)/shard_map/ppermute | solution.py:16
  62.7 0.8 copy-start.7
  80.5 5.4 %copy-start.10 = (bf16[512,256]{0,1:T(8,128)(2,1)S(1)}, bf16[512,256]{0,1:T(8,128)(2,1)}, u32[]{:S(2)}) copy-start(bf16[512,256]{0,1:T(8,128)(2,1)} %copy-done.9) | copy-start | bytes 786436
  85.9 44.7 %collective-permute-start.9 = (f32[8,2,64,1280]{3,2,1,0:T(8,128)}, f32[8,2,64,1280]{3,2,1,0:T(8,128)}, u32[]{:S(2)}, u32[]{:S(2)}) collective-permute-start(f32[8,2,64,1280]{3,2,1,0:T(8,128)} %dynamic-slice_bitcast_fusion), channel_id=1, source_target_pairs={{0,8},{8,0},{1,9},{9,1},{2,10},{10,2},{3,11},{11,3},{4,12},{12,4},... | collective-permute-start | bytes 15728648 | tf_op jit(solution)/shard_map/ppermute | solution.py:52
  85.9 5.0 %copy-start.8 = (bf16[2,256,512]{1,2,0:T(8,128)(2,1)S(1)}, bf16[2,256,512]{1,2,0:T(8,128)(2,1)}, u32[]{:S(2)}) copy-start(bf16[2,256,512]{1,2,0:T(8,128)(2,1)} %copy-done.7) | copy-start | bytes 1572868
  85.9 5.2 %copy-start.4 = (bf16[2048,256]{1,0:T(8,128)(2,1)S(1)}, bf16[2048,256]{1,0:T(8,128)(2,1)}, u32[]{:S(2)}) copy-start(bf16[2048,256]{1,0:T(8,128)(2,1)} %copy-done.3) | copy-start | bytes 3145732
  96.4 1.0 copy-start.2
  97.4 9.5 %collective-permute-start.5 = (f32[512,128]{1,0:T(8,128)S(1)}, f32[512,128]{1,0:T(8,128)S(1)}, u32[]{:S(2)}, u32[]{:S(2)}) collective-permute-start(f32[512,128]{1,0:T(8,128)S(1)} %dynamic-slice_bitcast_fusion.4), channel_id=1, source_target_pairs={{0,6},{2,0},{4,2},{6,4},{1,7},{3,1},{5,3},{7,5},{8,14},{10,8},{12,... | collective-permute-start | bytes 786440 | tf_op jit(solution)/shard_map/ppermute | solution.py:66
  100.7 10.9 %collective-permute-start.2 = (f32[512,128]{1,0:T(8,128)S(1)}, f32[512,128]{1,0:T(8,128)S(1)}, u32[]{:S(2)}, u32[]{:S(2)}) collective-permute-start(f32[512,128]{1,0:T(8,128)S(1)} %dynamic-slice_bitcast_fusion.5), channel_id=1, source_target_pairs={{0,2},{2,4},{4,6},{6,0},{1,3},{3,5},{5,7},{7,1},{8,10},{10,12},{12... | collective-permute-start | bytes 786440 | tf_op jit(solution)/shard_map/ppermute | solution.py:66
  107.9 9.1 %collective-permute-start.6 = (f32[512,128]{1,0:T(8,128)S(1)}, f32[512,128]{1,0:T(8,128)S(1)}, u32[]{:S(2)}, u32[]{:S(2)}) collective-permute-start(f32[512,128]{1,0:T(8,128)S(1)} %bitcast_add_fusion.18), channel_id=1, source_target_pairs={{0,6},{2,0},{4,2},{6,4},{1,7},{3,1},{5,3},{7,5},{8,14},{10,8},{12,... | collective-permute-start | bytes 786440 | tf_op jit(solution)/shard_map/ppermute | solution.py:66
  111.7 10.1 %collective-permute-start.3 = (f32[512,128]{1,0:T(8,128)S(1)}, f32[512,128]{1,0:T(8,128)S(1)}, u32[]{:S(2)}, u32[]{:S(2)}) collective-permute-start(f32[512,128]{1,0:T(8,128)S(1)} %bitcast_add_fusion.21), channel_id=1, source_target_pairs={{0,2},{2,4},{4,6},{6,0},{1,3},{3,5},{5,7},{7,1},{8,10},{10,12},{12... | collective-permute-start | bytes 786440 | tf_op jit(solution)/shard_map/ppermute | solution.py:66
  118.0 8.3 %collective-permute-start.7 = (f32[512,128]{1,0:T(8,128)S(1)}, f32[512,128]{1,0:T(8,128)S(1)}, u32[]{:S(2)}, u32[]{:S(2)}) collective-permute-start(f32[512,128]{1,0:T(8,128)S(1)} %bitcast_add_fusion.17), channel_id=1, source_target_pairs={{0,6},{2,0},{4,2},{6,4},{1,7},{3,1},{5,3},{7,5},{8,14},{10,8},{12,... | collective-permute-start | bytes 786440 | tf_op jit(solution)/shard_map/ppermute | solution.py:66
  121.8 8.0 %collective-permute-start.4 = (f32[512,128]{1,0:T(8,128)S(1)}, f32[512,128]{1,0:T(8,128)S(1)}, u32[]{:S(2)}, u32[]{:S(2)}) collective-permute-start(f32[512,128]{1,0:T(8,128)S(1)} %bitcast_add_fusion.20), channel_id=1, source_target_pairs={{0,2},{2,4},{4,6},{6,0},{1,3},{3,5},{5,7},{7,1},{8,10},{10,12},{12... | collective-permute-start | bytes 786440 | tf_op jit(solution)/shard_map/ppermute | solution.py:66
  129.9 7.7 %collective-permute-start.8 = (f32[256,256]{1,0:T(8,128)S(1)}, f32[256,256]{1,0:T(8,128)S(1)}, u32[]{:S(2)}, u32[]{:S(2)}) collective-permute-start(f32[256,256]{1,0:T(8,128)S(1)} %dynamic-slice_bitcast_fusion.3), channel_id=1, source_target_pairs={{0,1},{1,0},{2,3},{3,2},{4,5},{5,4},{6,7},{7,6},{8,9},{9,8},{10,11... | collective-permute-start | bytes 786440 | tf_op jit(solution)/shard_map/ppermute | solution.py:52
  135.8 8.2 %collective-permute-start.10 = (f32[64,1280]{1,0:T(8,128)S(1)}, f32[64,1280]{1,0:T(8,128)S(1)}, u32[]{:S(2)}, u32[]{:S(2)}) collective-permute-start(f32[64,1280]{1,0:T(8,128)S(1)} %dynamic-slice_bitcast_fusion.2), channel_id=1, source_target_pairs={{0,32},{32,64},{64,96},{96,128},{128,160},{160,192},{192,224},{224... | collective-permute-start | bytes 983048 | tf_op jit(solution)/shard_map/ppermute | solution.py:40
  137.7 8.5 %collective-permute-start.17 = (f32[64,1280]{1,0:T(8,128)S(1)}, f32[64,1280]{1,0:T(8,128)S(1)}, u32[]{:S(2)}, u32[]{:S(2)}) collective-permute-start(f32[64,1280]{1,0:T(8,128)S(1)} %dynamic-slice_bitcast_fusion.1), channel_id=1, source_target_pairs={{0,224},{32,0},{64,32},{96,64},{128,96},{160,128},{192,160},{224,1... | collective-permute-start | bytes 983048 | tf_op jit(solution)/shard_map/ppermute | solution.py:40
  144.1 9.0 %collective-permute-start.11 = (f32[64,1280]{1,0:T(8,128)S(1)}, f32[64,1280]{1,0:T(8,128)S(1)}, u32[]{:S(2)}, u32[]{:S(2)}) collective-permute-start(f32[64,1280]{1,0:T(8,128)S(1)} %bitcast_add_fusion.14), channel_id=1, source_target_pairs={{0,32},{32,64},{64,96},{96,128},{128,160},{160,192},{192,224},{224... | collective-permute-start | bytes 983048 | tf_op jit(solution)/shard_map/ppermute | solution.py:40
  146.2 9.4 %collective-permute-start.18 = (f32[64,1280]{1,0:T(8,128)S(1)}, f32[64,1280]{1,0:T(8,128)S(1)}, u32[]{:S(2)}, u32[]{:S(2)}) collective-permute-start(f32[64,1280]{1,0:T(8,128)S(1)} %bitcast_add_fusion.7), channel_id=1, source_target_pairs={{0,224},{32,0},{64,32},{96,64},{128,96},{160,128},{192,160},{224,1... | collective-permute-start | bytes 983048 | tf_op jit(solution)/shard_map/ppermute | solution.py:40
  153.0 9.8 %collective-permute-start.12 = (f32[64,1280]{1,0:T(8,128)S(1)}, f32[64,1280]{1,0:T(8,128)S(1)}, u32[]{:S(2)}, u32[]{:S(2)}) collective-permute-start(f32[64,1280]{1,0:T(8,128)S(1)} %bitcast_add_fusion.13), channel_id=1, source_target_pairs={{0,32},{32,64},{64,96},{96,128},{128,160},{160,192},{192,224},{224... | collective-permute-start | bytes 983048 | tf_op jit(solution)/shard_map/ppermute | solution.py:40
  155.6 10.1 %collective-permute-start.19 = (f32[64,1280]{1,0:T(8,128)S(1)}, f32[64,1280]{1,0:T(8,128)S(1)}, u32[]{:S(2)}, u32[]{:S(2)}) collective-permute-start(f32[64,1280]{1,0:T(8,128)S(1)} %bitcast_add_fusion.6), channel_id=1, source_target_pairs={{0,224},{32,0},{64,32},{96,64},{128,96},{160,128},{192,160},{224,1... | collective-permute-start | bytes 983048 | tf_op jit(solution)/shard_map/ppermute | solution.py:40
  162.9 10.5 %collective-permute-start.13 = (f32[64,1280]{1,0:T(8,128)S(1)}, f32[64,1280]{1,0:T(8,128)S(1)}, u32[]{:S(2)}, u32[]{:S(2)}) collective-permute-start(f32[64,1280]{1,0:T(8,128)S(1)} %bitcast_add_fusion.12), channel_id=1, source_target_pairs={{0,32},{32,64},{64,96},{96,128},{128,160},{160,192},{192,224},{224... | collective-permute-start | bytes 983048 | tf_op jit(solution)/shard_map/ppermute | solution.py:40
  165.8 11.7 %collective-permute-start.20 = (f32[64,1280]{1,0:T(8,128)S(1)}, f32[64,1280]{1,0:T(8,128)S(1)}, u32[]{:S(2)}, u32[]{:S(2)}) collective-permute-start(f32[64,1280]{1,0:T(8,128)S(1)} %bitcast_add_fusion.5), channel_id=1, source_target_pairs={{0,224},{32,0},{64,32},{96,64},{128,96},{160,128},{192,160},{224,1... | collective-permute-start | bytes 983048 | tf_op jit(solution)/shard_map/ppermute | solution.py:40
  173.5 10.9 %collective-permute-start.14 = (f32[64,1280]{1,0:T(8,128)S(1)}, f32[64,1280]{1,0:T(8,128)S(1)}, u32[]{:S(2)}, u32[]{:S(2)}) collective-permute-start(f32[64,1280]{1,0:T(8,128)S(1)} %bitcast_add_fusion.11), channel_id=1, source_target_pairs={{0,32},{32,64},{64,96},{96,128},{128,160},{160,192},{192,224},{224... | collective-permute-start | bytes 983048 | tf_op jit(solution)/shard_map/ppermute | solution.py:40
  177.5 11.2 %collective-permute-start.21 = (f32[64,1280]{1,0:T(8,128)S(1)}, f32[64,1280]{1,0:T(8,128)S(1)}, u32[]{:S(2)}, u32[]{:S(2)}) collective-permute-start(f32[64,1280]{1,0:T(8,128)S(1)} %bitcast_add_fusion.4), channel_id=1, source_target_pairs={{0,224},{32,0},{64,32},{96,64},{128,96},{160,128},{192,160},{224,1... | collective-permute-start | bytes 983048 | tf_op jit(solution)/shard_map/ppermute | solution.py:40
  184.4 10.5 %collective-permute-start.15 = (f32[64,1280]{1,0:T(8,128)S(1)}, f32[64,1280]{1,0:T(8,128)S(1)}, u32[]{:S(2)}, u32[]{:S(2)}) collective-permute-start(f32[64,1280]{1,0:T(8,128)S(1)} %bitcast_add_fusion.10), channel_id=1, source_target_pairs={{0,32},{32,64},{64,96},{96,128},{128,160},{160,192},{192,224},{224... | collective-permute-start | bytes 983048 | tf_op jit(solution)/shard_map/ppermute | solution.py:40
  188.7 10.3 %collective-permute-start.22 = (f32[64,1280]{1,0:T(8,128)S(1)}, f32[64,1280]{1,0:T(8,128)S(1)}, u32[]{:S(2)}, u32[]{:S(2)}) collective-permute-start(f32[64,1280]{1,0:T(8,128)S(1)} %bitcast_add_fusion.3), channel_id=1, source_target_pairs={{0,224},{32,0},{64,32},{96,64},{128,96},{160,128},{192,160},{224,1... | collective-permute-start | bytes 983048 | tf_op jit(solution)/shard_map/ppermute | solution.py:40
  195.0 8.4 %collective-permute-start.16 = (f32[64,1280]{1,0:T(8,128)S(1)}, f32[64,1280]{1,0:T(8,128)S(1)}, u32[]{:S(2)}, u32[]{:S(2)}) collective-permute-start(f32[64,1280]{1,0:T(8,128)S(1)} %bitcast_add_fusion.9), channel_id=1, source_target_pairs={{0,32},{32,64},{64,96},{96,128},{128,160},{160,192},{192,224},{224... | collective-permute-start | bytes 983048 | tf_op jit(solution)/shard_map/ppermute | solution.py:40
  199.0 8.4 %collective-permute-start.23 = (f32[64,1280]{1,0:T(8,128)S(1)}, f32[64,1280]{1,0:T(8,128)S(1)}, u32[]{:S(2)}, u32[]{:S(2)}) collective-permute-start(f32[64,1280]{1,0:T(8,128)S(1)} %bitcast_add_fusion.2), channel_id=1, source_target_pairs={{0,224},{32,0},{64,32},{96,64},{128,96},{160,128},{192,160},{224,1... | collective-permute-start | bytes 983048 | tf_op jit(solution)/shard_map/ppermute | solution.py:40
  208.2 8.9 %collective-permute-start.24 = (f32[64,1280]{1,0:T(8,128)}, f32[64,1280]{1,0:T(8,128)}, u32[]{:S(2)}, u32[]{:S(2)}) collective-permute-start(f32[64,1280]{1,0:T(8,128)} %fusion.6), channel_id=1, source_target_pairs={{0,16},{16,0},{1,17},{17,1},{2,18},{18,2},{3,19},{19,3},{4,20},{20... | collective-permute-start | bytes 983048 | tf_op jit(solution)/shard_map/ppermute | solution.py:52
  210.3 9.5 %copy-start.1 = (bf16[2,256,2048]{2,1,0:T(8,128)(2,1)S(1)}, bf16[2,256,2048]{2,1,0:T(8,128)(2,1)}, u32[]{:S(2)}) copy-start(bf16[2,256,2048]{2,1,0:T(8,128)(2,1)} %param.5) | copy-start | bytes 6291460
Sparse Core Ops, SparseCore 0:
  123.4 53.8 reduce-scatter.1

commit v10 on v7

--- a/solution.py
+++ b/solution.py
@@ -124,14 +124,15 @@
     own_rows = lax.dynamic_slice_in_dim(grad_rows, lax.axis_index(CHAN) * share, share, 2)
     summed = summed.reshape(share, traj, window_extent).transpose(1, 2, 0)
     grad_states = (own_rows.astype(jnp.float32) + summed).astype(jnp.bfloat16)
-    weight_terms = jnp.concatenate(
+    zeros = jnp.zeros_like(branch_grads)
+    right = jnp.concatenate(
         [
-            contract_rows(rows, branch_grads),
-            contract_rows(rows, later),
-            contract_rows(grad_flat, mixed),
+            jnp.concatenate([branch_grads, later, jnp.zeros_like(mixed)], axis=1),
+            jnp.concatenate([zeros, zeros, mixed], axis=1),
         ],
-        axis=1,
+        axis=0,
     )
+    weight_terms = contract_rows(jnp.concatenate([rows, grad_flat], axis=0), right)
     reduced = time_reduce_scatter(weight_terms)
     scale = lax.rsqrt(jnp.sum(lengths.astype(jnp.float32)))
     part = reduced.shape[0]

time: 206 us -> 194 us (0.942)
  local copies, waits for them, and re-layouts: 31.1 us -> 19.8 us
  other arithmetic: 17.5 us -> 11.5 us
  waiting for transfers between devices: 77.8 us -> 80.3 us
    concatenate x1 -> x0, local copies, waits for them, and re-layouts: 11.3 us -> none  [local(): jnp.concatenate([contract_rows(rows, branch_grads), contract_rows(rows, l...]
    dot_general x3 -> x1, matrix products: 3.33 us -> 8.13 us  [contract_rows(): lax.dot_general(left, right, (((0,), (0,)), ((), ())), preferred_element_...]
    concatenate x1 -> x0, other arithmetic: 4.35 us -> none  [local(): jnp.concatenate([contract_rows(rows, branch_grads), contract_rows(rows, l...]
    dot_general x3, matrix products: 9.32 us -> 5.67 us  [contract_cols(): lax.dot_general(left, right, (((1,), (1,)), ((), ())), preferred_element_...]
    unnamed x29 -> x22, local copies, waits for them, and re-layouts: 3.17 us -> 6.64 us
    squeeze x2, local copies, waits for them, and re-layouts: 5.37 us -> 2.98 us  [swap_sum(): give = lax.dynamic_index_in_dim(parts, 1 - me, 0, keepdims=False)]
  transfers between devices with their start and end apart: 26 -> 26, of which waited for: 14 -> 15; matrix products, arithmetic and copies ran while one was open for 14% -> 11% of each run, Pallas kernels for 0% -> 0%
where the time goes in v10:
time: 194 us; the launch traced here: 192 us
  waiting for transfers between devices  80.3 us (41%)
  starting transfers between devices  45.3 us (23%)
  local copies, waits for them, and re-layouts  19.8 us (10%)
  matrix products  19.7 us (10%)
  between operations  15.3 us (8%)
  other arithmetic  11.5 us (6%)
    ppermute x14, waiting for transfers between devices, ring_sum(): got = lax.ppermute(acc, axis, pairs)  39.3 us
    ppermute x2, waiting for transfers between devices, shifted(): return lax.ppermute(x, axis, pairs)  33.4 us
    ppermute x14, starting transfers between devices, ring_sum(): got = lax.ppermute(acc, axis, pairs)  24.8 us
    ppermute x6, starting transfers between devices, chan_ring_reduce_scatter(): got = lax.ppermute(acc, 'cy', pairs)  10.4 us
    dot_general x1, matrix products, contract_rows(): lax.dot_general(left, right, (((0,), (0,)), ((), ())), preferred_element_...  8.13 us
    ppermute x2, starting transfers between devices, shifted(): return lax.ppermute(x, axis, pairs)  6.95 us
    unnamed x22, local copies, waits for them, and re-layouts  6.64 us
    add x3, other arithmetic, swap_sum(): return keep + lax.ppermute(give, axis, [(0, 1), (1, 0)])  6.02 us
  transfers between devices with their start and end apart: 26, of which 15 were waited for; matrix products, arithmetic and copies ran while one was open for 11% of the time, Pallas kernels for 0%

profile of v10, /device:TPU:98, one launch (start us, length us, event | category | flops | bytes accessed | tf_op | source)
XLA Modules:
  0.0 191.9 jit_solution(5296957516597840269)
XLA Ops:
  7.2 4.0 %slice_bitcast_fusion.1 = (bf16[2048,256]{1,0:T(8,128)(2,1)S(1)}, bf16[2048,256]{1,0:T(8,128)(2,1)}, bf16[2048,256]{1,0:T(8,128)(2,1)}, bf16[2048,256]{1,0:T(8,128)(2,1)S(1)}) fusion(bf16[2,2,2048,256]{3,2,1,0:T(8,128)(2,1)} %param.7), kind=kLoop, calls=%fused_computation.27 | loop fusion | bytes 8388608 | tf_op jit(solution)/shard_map/squeeze | solution.py:91
  11.2 2.2 %fusion.16 = f32[512,512]{0,1:T(8,128)} fusion(bf16[512,2048]{1,0:T(8,128)(2,1)S(1)} %bitcast.119, bf16[2048,256]{1,0:T(8,128)(2,1)S(1)} %get-tuple-element.10, bf16[2048,256]{1,0:T(8,128)(2,1)S(1)} %get-tuple-element.7), kind=kOutput, calls=%fused_computation.23 | convolution fusion | flops 1077936128 | bytes 5242880 | tf_op jit(solution)/shard_map/dot_general | solution.py:92
  13.5 2.3 %copy.8 = f32[2,256,512]{1,0,2:T(2,128)} copy(f32[2,256,512]{2,1,0:T(8,128)} %bitcast.114) | data formatting | bytes 2097152 | tf_op jit(solution)/shard_map/reshape | solution.py:94
  15.7 5.0 %collective-permute-start = (f32[2,256,512]{1,0,2:T(2,128)}, f32[2,256,512]{1,0,2:T(2,128)}, u32[]{:S(2)}, u32[]{:S(2)}) collective-permute-start(f32[2,256,512]{1,0,2:T(2,128)} %copy.8), channel_id=1, source_target_pairs={{0,32},{8,40},{16,48},{24,56},{32,64},{40,72},{48,80},{56,88},{64,... | collective-permute-start | bytes 3145736 | tf_op jit(solution)/shard_map/ppermute | solution.py:16
  20.9 3.7 %convolution_bitcast_fusion = f32[512,512]{0,1:T(8,128)S(1)} fusion(bf16[512,2048]{1,0:T(8,128)(2,1)} %bitcast.117, bf16[2048,256]{1,0:T(8,128)(2,1)} %get-tuple-element.8, bf16[2048,256]{1,0:T(8,128)(2,1)} %get-tuple-element.9), kind=kOutput, calls=%fused_computation.22 | convolution fusion | flops 1077936128 | bytes 5242880 | tf_op jit(solution)/shard_map/dot_general | solution.py:96
  24.8 18.7 %collective-permute-done = f32[2,256,512]{1,0,2:T(2,128)} collective-permute-done((f32[2,256,512]{1,0,2:T(2,128)}, f32[2,256,512]{1,0,2:T(2,128)}, u32[]{:S(2)}, u32[]{:S(2)}) %collective-permute-start) | collective-permute-done | bytes 1048608 | tf_op jit(solution)/shard_map/ppermute | solution.py:16
  43.5 1.3 copy.12
  45.0 1.6 multiply_convert_fusion.2
  46.6 0.7 copy-done.6
  47.5 1.9 %collective-permute-start.1 = (bf16[2,256,512]{1,0,2:T(2,128)(2,1)S(1)}, bf16[2,256,512]{1,0,2:T(2,128)(2,1)S(1)}, u32[]{:S(2)}, u32[]{:S(2)}) collective-permute-start(bf16[2,256,512]{1,0,2:T(2,128)(2,1)S(1)} %reshape.79), channel_id=1, source_target_pairs={{32,0},{40,8},{48,16},{56,24},{64,32},{72,40},{80,48},{88,56},{96,... | collective-permute-start | bytes 1572872 | tf_op jit(solution)/shard_map/ppermute | solution.py:16
  49.4 14.7 %collective-permute-done.1 = bf16[2,256,512]{1,0,2:T(2,128)(2,1)S(1)} collective-permute-done((bf16[2,256,512]{1,0,2:T(2,128)(2,1)S(1)}, bf16[2,256,512]{1,0,2:T(2,128)(2,1)S(1)}, u32[]{:S(2)}, u32[]{:S(2)}) %collective-permute-start.1) | collective-permute-done | bytes 524320 | tf_op jit(solution)/shard_map/ppermute | solution.py:16
  64.2 0.8 copy-done.5
  65.0 1.1 copy.13
  66.1 8.1 %fusion.1 = f32[2048,1280]{1,0:T(8,128)S(1)} fusion(bf16[512,2048]{1,0:T(8,128)(2,1)} %bitcast.108, bf16[512,2048]{1,0:T(8,128)(2,1)} %bitcast.118, bf16[512,256]{0,1:T(8,128)(2,1)} %get-tuple-element.15, bf16[512,256]{0,1:T(8,128)(2,1)S(1)} %broadcast_in_dim.19, bf16[512,512]{0,1:T(8,128)(2,1)S(1)} %bitcast.112, bf16[512,256]{0,1:T(8,128)(2,1)} %copy-done.6, ...), kind=kOutput, calls=%fused_computation.4 | convolution fusion | flops 5392826368 | bytes 16252928 | tf_op jit(solution)/shard_map/dot_general | solution.py:20
  74.3 3.0 %dynamic-slice_bitcast_fusion = f32[8,2,64,1280]{3,2,1,0:T(8,128)} fusion(f32[8,2,2,64,1280]{4,3,2,1,0:T(8,128)S(1)} %bitcast.103, s32[]{:T(128)S(6)} %select_n.222), kind=kLoop, calls=%fused_computation.2 | loop fusion | bytes 10485764 | tf_op jit(solution)/shard_map/jit(dynamic_index_in_dim)/squeeze | solution.py:52
  77.2 2.7 %copy-done.2 = f32[2048,1280]{1,0:T(8,128)} copy-done((f32[2048,1280]{1,0:T(8,128)}, f32[2048,1280]{1,0:T(8,128)S(1)}, u32[]{:S(2)}) %copy-start.2) | copy-done | bytes 10485784
  79.9 2.8 %fusion.17 = f32[2048,512]{1,0:T(8,128)S(1)} fusion(bf16[2048,256]{1,0:T(8,128)(2,1)} %get-tuple-element.8, bf16[2048,256]{1,0:T(8,128)(2,1)} %get-tuple-element.9, bf16[512,256]{0,1:T(8,128)(2,1)S(1)} %copy-done.7, bf16[512,256]{0,1:T(8,128)(2,1)S(1)} %get-tuple-element.13), kind=kOutput, calls=%fused_computation.24 | convolution fusion | flops 1078984704 | bytes 6815744 | tf_op jit(solution)/shard_map/dot_general | solution.py:26
  82.7 1.3 convolution_add_fusion
  84.0 1.7 fusion.36
  85.9 3.1 %collective-permute-start.5 = (f32[512,128]{1,0:T(8,128)S(1)}, f32[512,128]{1,0:T(8,128)S(1)}, u32[]{:S(2)}, u32[]{:S(2)}) collective-permute-start(f32[512,128]{1,0:T(8,128)S(1)} %dynamic-slice_bitcast_fusion.4), channel_id=1, source_target_pairs={{0,6},{2,0},{4,2},{6,4},{1,7},{3,1},{5,3},{7,5},{8,14},{10,8},{12,... | collective-permute-start | bytes 786440 | tf_op jit(solution)/shard_map/ppermute | solution.py:67
  90.5 4.7 %collective-permute-done.5 = f32[512,128]{1,0:T(8,128)S(1)} collective-permute-done((f32[512,128]{1,0:T(8,128)S(1)}, f32[512,128]{1,0:T(8,128)S(1)}, u32[]{:S(2)}, u32[]{:S(2)}) %collective-permute-start.5) | collective-permute-done | bytes 262176 | tf_op jit(solution)/shard_map/ppermute | solution.py:67
  95.3 3.8 %collective-permute-start.6 = (f32[512,128]{1,0:T(8,128)S(1)}, f32[512,128]{1,0:T(8,128)S(1)}, u32[]{:S(2)}, u32[]{:S(2)}) collective-permute-start(f32[512,128]{1,0:T(8,128)S(1)} %bitcast_add_fusion.18), channel_id=1, source_target_pairs={{0,6},{2,0},{4,2},{6,4},{1,7},{3,1},{5,3},{7,5},{8,14},{10,8},{12,... | collective-permute-start | bytes 786440 | tf_op jit(solution)/shard_map/ppermute | solution.py:67
  99.2 5.0 %bitcast_add_fusion = f32[8,2,64,1280]{3,2,1,0:T(8,128)S(1)} fusion(f32[8,2,64,1280]{3,2,1,0:T(8,128)} %collective-permute-done.9, f32[8,2,2,64,1280]{4,3,2,1,0:T(8,128)} %bitcast.104, s32[]{:T(128)S(6)} %select_n.221), kind=kLoop, calls=%fused_computation.1 | loop fusion | flops 1310720 | bytes 15728644 | tf_op jit(solution)/shard_map/add | solution.py:53
  104.2 0.7 fusion.35
  104.9 1.6 collective-permute-start.10
  107.1 3.3 %collective-permute-start.7 = (f32[512,128]{1,0:T(8,128)S(1)}, f32[512,128]{1,0:T(8,128)S(1)}, u32[]{:S(2)}, u32[]{:S(2)}) collective-permute-start(f32[512,128]{1,0:T(8,128)S(1)} %bitcast_add_fusion.17), channel_id=1, source_target_pairs={{0,6},{2,0},{4,2},{6,4},{1,7},{3,1},{5,3},{7,5},{8,14},{10,8},{12,... | collective-permute-start | bytes 786440 | tf_op jit(solution)/shard_map/ppermute | solution.py:67
  110.4 3.3 %collective-permute-done.10 = f32[2,64,640]{2,1,0:T(8,128)S(1)} collective-permute-done((f32[2,64,640]{2,1,0:T(8,128)S(1)}, f32[2,64,640]{2,1,0:T(8,128)S(1)}, u32[]{:S(2)}, u32[]{:S(2)}) %collective-permute-start.10) | collective-permute-done | bytes 327712 | tf_op jit(solution)/shard_map/ppermute | solution.py:41
  113.8 3.0 %collective-permute-start.11 = (f32[2,64,640]{2,1,0:T(8,128)S(1)}, f32[2,64,640]{2,1,0:T(8,128)S(1)}, u32[]{:S(2)}, u32[]{:S(2)}) collective-permute-start(f32[2,64,640]{2,1,0:T(8,128)S(1)} %bitcast_add_fusion.14), channel_id=1, source_target_pairs={{0,32},{32,64},{64,96},{96,128},{128,160},{160,192},{192,224},{224... | collective-permute-start | bytes 983048 | tf_op jit(solution)/shard_map/ppermute | solution.py:41
  117.1 5.4 %collective-permute-done.11 = f32[2,64,640]{2,1,0:T(8,128)S(1)} collective-permute-done((f32[2,64,640]{2,1,0:T(8,128)S(1)}, f32[2,64,640]{2,1,0:T(8,128)S(1)}, u32[]{:S(2)}, u32[]{:S(2)}) %collective-permute-start.11) | collective-permute-done | bytes 327712 | tf_op jit(solution)/shard_map/ppermute | solution.py:41
  122.5 4.0 %collective-permute-start.12 = (f32[2,64,640]{2,1,0:T(8,128)S(1)}, f32[2,64,640]{2,1,0:T(8,128)S(1)}, u32[]{:S(2)}, u32[]{:S(2)}) collective-permute-start(f32[2,64,640]{2,1,0:T(8,128)S(1)} %bitcast_add_fusion.13), channel_id=1, source_target_pairs={{0,32},{32,64},{64,96},{96,128},{128,160},{160,192},{192,224},{224... | collective-permute-start | bytes 983048 | tf_op jit(solution)/shard_map/ppermute | solution.py:41
  126.7 4.6 %collective-permute-done.12 = f32[2,64,640]{2,1,0:T(8,128)S(1)} collective-permute-done((f32[2,64,640]{2,1,0:T(8,128)S(1)}, f32[2,64,640]{2,1,0:T(8,128)S(1)}, u32[]{:S(2)}, u32[]{:S(2)}) %collective-permute-start.12) | collective-permute-done | bytes 327712 | tf_op jit(solution)/shard_map/ppermute | solution.py:41
  131.3 3.8 %collective-permute-start.13 = (f32[2,64,640]{2,1,0:T(8,128)S(1)}, f32[2,64,640]{2,1,0:T(8,128)S(1)}, u32[]{:S(2)}, u32[]{:S(2)}) collective-permute-start(f32[2,64,640]{2,1,0:T(8,128)S(1)} %bitcast_add_fusion.12), channel_id=1, source_target_pairs={{0,32},{32,64},{64,96},{96,128},{128,160},{160,192},{192,224},{224... | collective-permute-start | bytes 983048 | tf_op jit(solution)/shard_map/ppermute | solution.py:41
  135.3 4.6 %collective-permute-done.13 = f32[2,64,640]{2,1,0:T(8,128)S(1)} collective-permute-done((f32[2,64,640]{2,1,0:T(8,128)S(1)}, f32[2,64,640]{2,1,0:T(8,128)S(1)}, u32[]{:S(2)}, u32[]{:S(2)}) %collective-permute-start.13) | collective-permute-done | bytes 327712 | tf_op jit(solution)/shard_map/ppermute | solution.py:41
  139.9 3.8 %collective-permute-start.14 = (f32[2,64,640]{2,1,0:T(8,128)S(1)}, f32[2,64,640]{2,1,0:T(8,128)S(1)}, u32[]{:S(2)}, u32[]{:S(2)}) collective-permute-start(f32[2,64,640]{2,1,0:T(8,128)S(1)} %bitcast_add_fusion.11), channel_id=1, source_target_pairs={{0,32},{32,64},{64,96},{96,128},{128,160},{160,192},{192,224},{224... | collective-permute-start | bytes 983048 | tf_op jit(solution)/shard_map/ppermute | solution.py:41
  144.2 5.4 %collective-permute-done.14 = f32[2,64,640]{2,1,0:T(8,128)S(1)} collective-permute-done((f32[2,64,640]{2,1,0:T(8,128)S(1)}, f32[2,64,640]{2,1,0:T(8,128)S(1)}, u32[]{:S(2)}, u32[]{:S(2)}) %collective-permute-start.14) | collective-permute-done | bytes 327712 | tf_op jit(solution)/shard_map/ppermute | solution.py:41
  149.6 3.8 %collective-permute-start.15 = (f32[2,64,640]{2,1,0:T(8,128)S(1)}, f32[2,64,640]{2,1,0:T(8,128)S(1)}, u32[]{:S(2)}, u32[]{:S(2)}) collective-permute-start(f32[2,64,640]{2,1,0:T(8,128)S(1)} %bitcast_add_fusion.10), channel_id=1, source_target_pairs={{0,32},{32,64},{64,96},{96,128},{128,160},{160,192},{192,224},{224... | collective-permute-start | bytes 983048 | tf_op jit(solution)/shard_map/ppermute | solution.py:41
  154.3 6.1 %collective-permute-done.15 = f32[2,64,640]{2,1,0:T(8,128)S(1)} collective-permute-done((f32[2,64,640]{2,1,0:T(8,128)S(1)}, f32[2,64,640]{2,1,0:T(8,128)S(1)}, u32[]{:S(2)}, u32[]{:S(2)}) %collective-permute-start.15) | collective-permute-done | bytes 327712 | tf_op jit(solution)/shard_map/ppermute | solution.py:41
  160.5 3.8 %collective-permute-start.16 = (f32[2,64,640]{2,1,0:T(8,128)S(1)}, f32[2,64,640]{2,1,0:T(8,128)S(1)}, u32[]{:S(2)}, u32[]{:S(2)}) collective-permute-start(f32[2,64,640]{2,1,0:T(8,128)S(1)} %bitcast_add_fusion.9), channel_id=1, source_target_pairs={{0,32},{32,64},{64,96},{96,128},{128,160},{160,192},{192,224},{224... | collective-permute-start | bytes 983048 | tf_op jit(solution)/shard_map/ppermute | solution.py:41
  164.3 0.8 collective-permute-done.22
  165.3 3.6 %collective-permute-done.16 = f32[2,64,640]{2,1,0:T(8,128)S(1)} collective-permute-done((f32[2,64,640]{2,1,0:T(8,128)S(1)}, f32[2,64,640]{2,1,0:T(8,128)S(1)}, u32[]{:S(2)}, u32[]{:S(2)}) %collective-permute-start.16) | collective-permute-done | bytes 327712 | tf_op jit(solution)/shard_map/ppermute | solution.py:41
  168.9 4.6 %collective-permute-done.23 = f32[2,64,640]{2,1,0:T(8,128)S(1)} collective-permute-done((f32[2,64,640]{2,1,0:T(8,128)S(1)}, f32[2,64,640]{2,1,0:T(8,128)S(1)}, u32[]{:S(2)}, u32[]{:S(2)}) %collective-permute-start.23) | collective-permute-done | bytes 327712 | tf_op jit(solution)/shard_map/ppermute | solution.py:41
  173.6 3.0 %collective-permute-start.24 = (f32[64,1280]{1,0:T(8,128)S(1)}, f32[64,1280]{1,0:T(8,128)}, u32[]{:S(2)}, u32[]{:S(2)}) collective-permute-start(f32[64,1280]{1,0:T(8,128)S(1)} %fusion.23), channel_id=1, source_target_pairs={{0,16},{16,0},{1,17},{17,1},{2,18},{18,2},{3,19},{19,3},{4,20},{20... | collective-permute-start | bytes 983048 | tf_op jit(solution)/shard_map/ppermute | solution.py:53
  176.5 1.1 pad_maximum_fusion.8
  177.9 1.7 add_convert_fusion
  179.6 2.8 %collective-permute-done.24 = f32[64,1280]{1,0:T(8,128)} collective-permute-done((f32[64,1280]{1,0:T(8,128)S(1)}, f32[64,1280]{1,0:T(8,128)}, u32[]{:S(2)}, u32[]{:S(2)}) %collective-permute-start.24) | collective-permute-done | bytes 327712 | tf_op jit(solution)/shard_map/ppermute | solution.py:53
  182.4 1.0 fusion.26
  183.4 0.6 fusion.27
  184.3 0.8 copy.15
  (84 shorter events, 5.4 us)
Async XLA Ops:
  7.2 37.8 %copy-start = (bf16[256,2048]{1,0:T(8,128)(2,1)S(1)}, bf16[256,2048]{1,0:T(8,128)(2,1)}, u32[]{:S(2)}) copy-start(bf16[256,2048]{1,0:T(8,128)(2,1)} %param.8) | copy-start | bytes 3145732
  7.2 169.4 %reduce-scatter.2.cloned.1.call-start = ((), (), s32[]{:S(2)}) async-start(), calls=%async_computation.1 | async-start | bytes 2359296 | tf_op jit(solution)/shard_map/reduce_scatter | solution.py:118
  7.2 4.0 %copy-start.9 = (bf16[2,256,2048]{2,1,0:T(8,128)(2,1)S(1)}, bf16[2,256,2048]{2,1,0:T(8,128)(2,1)}, u32[]{:S(2)}) copy-start(bf16[2,256,2048]{2,1,0:T(8,128)(2,1)} %param.5) | copy-start | bytes 6291460
  11.2 9.5 %copy-start.8 = (s32[2]{0:T(128)S(1)}, s32[2]{0:T(128)}, u32[]{:S(2)}) copy-start(s32[2]{0:T(128)} %param.9) | copy-start | bytes 28
  15.7 27.7 %collective-permute-start = (f32[2,256,512]{1,0,2:T(2,128)}, f32[2,256,512]{1,0,2:T(2,128)}, u32[]{:S(2)}, u32[]{:S(2)}) collective-permute-start(f32[2,256,512]{1,0,2:T(2,128)} %copy.8), channel_id=1, source_target_pairs={{0,32},{8,40},{16,48},{24,56},{32,64},{40,72},{48,80},{56,88},{64,... | collective-permute-start | bytes 3145736 | tf_op jit(solution)/shard_map/ppermute | solution.py:16
  20.9 3.7 %copy-start.4 = (bf16[2,256,2048]{2,1,0:T(8,128)(2,1)S(1)}, bf16[2,256,2048]{2,1,0:T(8,128)(2,1)}, u32[]{:S(2)}) copy-start(bf16[2,256,2048]{2,1,0:T(8,128)(2,1)} %param.6) | copy-start | bytes 6291460
  24.8 20.2 %copy-start.3 = (bf16[2,256,2048]{2,1,0:T(8,128)(2,1)}, bf16[2,256,2048]{2,1,0:T(8,128)(2,1)S(1)}, u32[]{:S(2)}) copy-start(bf16[2,256,2048]{2,1,0:T(8,128)(2,1)S(1)} %broadcast_select_fusion) | copy-start | bytes 6291460
  46.6 0.7 copy-start.6
  47.5 16.7 %collective-permute-start.1 = (bf16[2,256,512]{1,0,2:T(2,128)(2,1)S(1)}, bf16[2,256,512]{1,0,2:T(2,128)(2,1)S(1)}, u32[]{:S(2)}, u32[]{:S(2)}) collective-permute-start(bf16[2,256,512]{1,0,2:T(2,128)(2,1)S(1)} %reshape.79), channel_id=1, source_target_pairs={{32,0},{40,8},{48,16},{56,24},{64,32},{72,40},{80,48},{88,56},{96,... | collective-permute-start | bytes 1572872 | tf_op jit(solution)/shard_map/ppermute | solution.py:16
  64.2 0.8 copy-start.5
  74.3 5.7 %copy-start.2 = (f32[2048,1280]{1,0:T(8,128)}, f32[2048,1280]{1,0:T(8,128)S(1)}, u32[]{:S(2)}) copy-start(f32[2048,1280]{1,0:T(8,128)S(1)} %fusion.1) | copy-start | bytes 31457284
  74.3 5.7 %copy-start.7 = (bf16[512,256]{0,1:T(8,128)(2,1)S(1)}, bf16[512,256]{0,1:T(8,128)(2,1)}, u32[]{:S(2)}) copy-start(bf16[512,256]{0,1:T(8,128)(2,1)} %copy-done.6) | copy-start | bytes 786436
  79.9 19.2 %collective-permute-start.9 = (f32[8,2,64,1280]{3,2,1,0:T(8,128)}, f32[8,2,64,1280]{3,2,1,0:T(8,128)}, u32[]{:S(2)}, u32[]{:S(2)}) collective-permute-start(f32[8,2,64,1280]{3,2,1,0:T(8,128)} %dynamic-slice_bitcast_fusion), channel_id=1, source_target_pairs={{0,8},{8,0},{1,9},{9,1},{2,10},{10,2},{3,11},{11,3},{4,12},{12,4},... | collective-permute-start | bytes 15728648 | tf_op jit(solution)/shard_map/ppermute | solution.py:53
  85.9 9.3 %collective-permute-start.5 = (f32[512,128]{1,0:T(8,128)S(1)}, f32[512,128]{1,0:T(8,128)S(1)}, u32[]{:S(2)}, u32[]{:S(2)}) collective-permute-start(f32[512,128]{1,0:T(8,128)S(1)} %dynamic-slice_bitcast_fusion.4), channel_id=1, source_target_pairs={{0,6},{2,0},{4,2},{6,4},{1,7},{3,1},{5,3},{7,5},{8,14},{10,8},{12,... | collective-permute-start | bytes 786440 | tf_op jit(solution)/shard_map/ppermute | solution.py:67
  89.0 10.0 %collective-permute-start.2 = (f32[512,128]{1,0:T(8,128)S(1)}, f32[512,128]{1,0:T(8,128)S(1)}, u32[]{:S(2)}, u32[]{:S(2)}) collective-permute-start(f32[512,128]{1,0:T(8,128)S(1)} %dynamic-slice_bitcast_fusion.5), channel_id=1, source_target_pairs={{0,2},{2,4},{4,6},{6,0},{1,3},{3,5},{5,7},{7,1},{8,10},{10,12},{12... | collective-permute-start | bytes 786440 | tf_op jit(solution)/shard_map/ppermute | solution.py:67
  95.3 11.8 %collective-permute-start.6 = (f32[512,128]{1,0:T(8,128)S(1)}, f32[512,128]{1,0:T(8,128)S(1)}, u32[]{:S(2)}, u32[]{:S(2)}) collective-permute-start(f32[512,128]{1,0:T(8,128)S(1)} %bitcast_add_fusion.18), channel_id=1, source_target_pairs={{0,6},{2,0},{4,2},{6,4},{1,7},{3,1},{5,3},{7,5},{8,14},{10,8},{12,... | collective-permute-start | bytes 786440 | tf_op jit(solution)/shard_map/ppermute | solution.py:67
  99.1 17.9 %collective-permute-start.3 = (f32[512,128]{1,0:T(8,128)S(1)}, f32[512,128]{1,0:T(8,128)S(1)}, u32[]{:S(2)}, u32[]{:S(2)}) collective-permute-start(f32[512,128]{1,0:T(8,128)S(1)} %bitcast_add_fusion.21), channel_id=1, source_target_pairs={{0,2},{2,4},{4,6},{6,0},{1,3},{3,5},{5,7},{7,1},{8,10},{10,12},{12... | collective-permute-start | bytes 786440 | tf_op jit(solution)/shard_map/ppermute | solution.py:67
  104.9 8.9 %collective-permute-start.10 = (f32[2,64,640]{2,1,0:T(8,128)S(1)}, f32[2,64,640]{2,1,0:T(8,128)S(1)}, u32[]{:S(2)}, u32[]{:S(2)}) collective-permute-start(f32[2,64,640]{2,1,0:T(8,128)S(1)} %dynamic-slice_bitcast_fusion.2), channel_id=1, source_target_pairs={{0,32},{32,64},{64,96},{96,128},{128,160},{160,192},{192,224},{224... | collective-permute-start | bytes 983048 | tf_op jit(solution)/shard_map/ppermute | solution.py:41
  106.5 10.3 %collective-permute-start.17 = (f32[2,64,640]{2,1,0:T(8,128)S(1)}, f32[2,64,640]{2,1,0:T(8,128)S(1)}, u32[]{:S(2)}, u32[]{:S(2)}) collective-permute-start(f32[2,64,640]{2,1,0:T(8,128)S(1)} %dynamic-slice_bitcast_fusion.1), channel_id=1, source_target_pairs={{0,224},{32,0},{64,32},{96,64},{128,96},{160,128},{192,160},{224,1... | collective-permute-start | bytes 983048 | tf_op jit(solution)/shard_map/ppermute | solution.py:41
  107.1 19.5 %collective-permute-start.7 = (f32[512,128]{1,0:T(8,128)S(1)}, f32[512,128]{1,0:T(8,128)S(1)}, u32[]{:S(2)}, u32[]{:S(2)}) collective-permute-start(f32[512,128]{1,0:T(8,128)S(1)} %bitcast_add_fusion.17), channel_id=1, source_target_pairs={{0,6},{2,0},{4,2},{6,4},{1,7},{3,1},{5,3},{7,5},{8,14},{10,8},{12,... | collective-permute-start | bytes 786440 | tf_op jit(solution)/shard_map/ppermute | solution.py:67
  113.8 8.7 %collective-permute-start.11 = (f32[2,64,640]{2,1,0:T(8,128)S(1)}, f32[2,64,640]{2,1,0:T(8,128)S(1)}, u32[]{:S(2)}, u32[]{:S(2)}) collective-permute-start(f32[2,64,640]{2,1,0:T(8,128)S(1)} %bitcast_add_fusion.14), channel_id=1, source_target_pairs={{0,32},{32,64},{64,96},{96,128},{128,160},{160,192},{192,224},{224... | collective-permute-start | bytes 983048 | tf_op jit(solution)/shard_map/ppermute | solution.py:41
  116.8 9.6 %collective-permute-start.18 = (f32[2,64,640]{2,1,0:T(8,128)S(1)}, f32[2,64,640]{2,1,0:T(8,128)S(1)}, u32[]{:S(2)}, u32[]{:S(2)}) collective-permute-start(f32[2,64,640]{2,1,0:T(8,128)S(1)} %bitcast_add_fusion.7), channel_id=1, source_target_pairs={{0,224},{32,0},{64,32},{96,64},{128,96},{160,128},{192,160},{224,1... | collective-permute-start | bytes 983048 | tf_op jit(solution)/shard_map/ppermute | solution.py:41
  117.0 18.2 %collective-permute-start.4 = (f32[512,128]{1,0:T(8,128)S(1)}, f32[512,128]{1,0:T(8,128)S(1)}, u32[]{:S(2)}, u32[]{:S(2)}) collective-permute-start(f32[512,128]{1,0:T(8,128)S(1)} %bitcast_add_fusion.20), channel_id=1, source_target_pairs={{0,2},{2,4},{4,6},{6,0},{1,3},{3,5},{5,7},{7,1},{8,10},{10,12},{12... | collective-permute-start | bytes 786440 | tf_op jit(solution)/shard_map/ppermute | solution.py:67
  122.5 8.8 %collective-permute-start.12 = (f32[2,64,640]{2,1,0:T(8,128)S(1)}, f32[2,64,640]{2,1,0:T(8,128)S(1)}, u32[]{:S(2)}, u32[]{:S(2)}) collective-permute-start(f32[2,64,640]{2,1,0:T(8,128)S(1)} %bitcast_add_fusion.13), channel_id=1, source_target_pairs={{0,32},{32,64},{64,96},{96,128},{128,160},{160,192},{192,224},{224... | collective-permute-start | bytes 983048 | tf_op jit(solution)/shard_map/ppermute | solution.py:41
  126.5 8.6 %collective-permute-start.19 = (f32[2,64,640]{2,1,0:T(8,128)S(1)}, f32[2,64,640]{2,1,0:T(8,128)S(1)}, u32[]{:S(2)}, u32[]{:S(2)}) collective-permute-start(f32[2,64,640]{2,1,0:T(8,128)S(1)} %bitcast_add_fusion.6), channel_id=1, source_target_pairs={{0,224},{32,0},{64,32},{96,64},{128,96},{160,128},{192,160},{224,1... | collective-permute-start | bytes 983048 | tf_op jit(solution)/shard_map/ppermute | solution.py:41
  131.3 8.5 %collective-permute-start.13 = (f32[2,64,640]{2,1,0:T(8,128)S(1)}, f32[2,64,640]{2,1,0:T(8,128)S(1)}, u32[]{:S(2)}, u32[]{:S(2)}) collective-permute-start(f32[2,64,640]{2,1,0:T(8,128)S(1)} %bitcast_add_fusion.12), channel_id=1, source_target_pairs={{0,32},{32,64},{64,96},{96,128},{128,160},{160,192},{192,224},{224... | collective-permute-start | bytes 983048 | tf_op jit(solution)/shard_map/ppermute | solution.py:41
  135.1 8.8 %collective-permute-start.20 = (f32[2,64,640]{2,1,0:T(8,128)S(1)}, f32[2,64,640]{2,1,0:T(8,128)S(1)}, u32[]{:S(2)}, u32[]{:S(2)}) collective-permute-start(f32[2,64,640]{2,1,0:T(8,128)S(1)} %bitcast_add_fusion.5), channel_id=1, source_target_pairs={{0,224},{32,0},{64,32},{96,64},{128,96},{160,128},{192,160},{224,1... | collective-permute-start | bytes 983048 | tf_op jit(solution)/shard_map/ppermute | solution.py:41
  139.9 9.7 %collective-permute-start.14 = (f32[2,64,640]{2,1,0:T(8,128)S(1)}, f32[2,64,640]{2,1,0:T(8,128)S(1)}, u32[]{:S(2)}, u32[]{:S(2)}) collective-permute-start(f32[2,64,640]{2,1,0:T(8,128)S(1)} %bitcast_add_fusion.11), channel_id=1, source_target_pairs={{0,32},{32,64},{64,96},{96,128},{128,160},{160,192},{192,224},{224... | collective-permute-start | bytes 983048 | tf_op jit(solution)/shard_map/ppermute | solution.py:41
  144.0 10.0 %collective-permute-start.21 = (f32[2,64,640]{2,1,0:T(8,128)S(1)}, f32[2,64,640]{2,1,0:T(8,128)S(1)}, u32[]{:S(2)}, u32[]{:S(2)}) collective-permute-start(f32[2,64,640]{2,1,0:T(8,128)S(1)} %bitcast_add_fusion.4), channel_id=1, source_target_pairs={{0,224},{32,0},{64,32},{96,64},{128,96},{160,128},{192,160},{224,1... | collective-permute-start | bytes 983048 | tf_op jit(solution)/shard_map/ppermute | solution.py:41
  149.6 10.8 %collective-permute-start.15 = (f32[2,64,640]{2,1,0:T(8,128)S(1)}, f32[2,64,640]{2,1,0:T(8,128)S(1)}, u32[]{:S(2)}, u32[]{:S(2)}) collective-permute-start(f32[2,64,640]{2,1,0:T(8,128)S(1)} %bitcast_add_fusion.10), channel_id=1, source_target_pairs={{0,32},{32,64},{64,96},{96,128},{128,160},{160,192},{192,224},{224... | collective-permute-start | bytes 983048 | tf_op jit(solution)/shard_map/ppermute | solution.py:41
  154.0 11.1 %collective-permute-start.22 = (f32[2,64,640]{2,1,0:T(8,128)S(1)}, f32[2,64,640]{2,1,0:T(8,128)S(1)}, u32[]{:S(2)}, u32[]{:S(2)}) collective-permute-start(f32[2,64,640]{2,1,0:T(8,128)S(1)} %bitcast_add_fusion.3), channel_id=1, source_target_pairs={{0,224},{32,0},{64,32},{96,64},{128,96},{160,128},{192,160},{224,1... | collective-permute-start | bytes 983048 | tf_op jit(solution)/shard_map/ppermute | solution.py:41
  154.1 11.1 %collective-permute-start.8 = (f32[256,256]{1,0:T(8,128)S(1)}, f32[256,256]{1,0:T(8,128)S(1)}, u32[]{:S(2)}, u32[]{:S(2)}) collective-permute-start(f32[256,256]{1,0:T(8,128)S(1)} %dynamic-slice_bitcast_fusion.3), channel_id=1, source_target_pairs={{0,1},{1,0},{2,3},{3,2},{4,5},{5,4},{6,7},{7,6},{8,9},{9,8},{10,11... | collective-permute-start | bytes 786440 | tf_op jit(solution)/shard_map/ppermute | solution.py:53
  160.5 8.4 %collective-permute-start.16 = (f32[2,64,640]{2,1,0:T(8,128)S(1)}, f32[2,64,640]{2,1,0:T(8,128)S(1)}, u32[]{:S(2)}, u32[]{:S(2)}) collective-permute-start(f32[2,64,640]{2,1,0:T(8,128)S(1)} %bitcast_add_fusion.9), channel_id=1, source_target_pairs={{0,32},{32,64},{64,96},{96,128},{128,160},{160,192},{192,224},{224... | collective-permute-start | bytes 983048 | tf_op jit(solution)/shard_map/ppermute | solution.py:41
  165.1 8.4 %collective-permute-start.23 = (f32[2,64,640]{2,1,0:T(8,128)S(1)}, f32[2,64,640]{2,1,0:T(8,128)S(1)}, u32[]{:S(2)}, u32[]{:S(2)}) collective-permute-start(f32[2,64,640]{2,1,0:T(8,128)S(1)} %bitcast_add_fusion.2), channel_id=1, source_target_pairs={{0,224},{32,0},{64,32},{96,64},{128,96},{160,128},{192,160},{224,1... | collective-permute-start | bytes 983048 | tf_op jit(solution)/shard_map/ppermute | solution.py:41
  173.6 8.8 %collective-permute-start.24 = (f32[64,1280]{1,0:T(8,128)S(1)}, f32[64,1280]{1,0:T(8,128)}, u32[]{:S(2)}, u32[]{:S(2)}) collective-permute-start(f32[64,1280]{1,0:T(8,128)S(1)} %fusion.23), channel_id=1, source_target_pairs={{0,16},{16,0},{1,17},{17,1},{2,18},{18,2},{3,19},{19,3},{4,20},{20... | collective-permute-start | bytes 983048 | tf_op jit(solution)/shard_map/ppermute | solution.py:53
  176.5 8.5 %copy-start.1 = (bf16[256,2048]{1,0:T(8,128)(2,1)S(1)}, bf16[256,2048]{1,0:T(8,128)(2,1)}, u32[]{:S(2)}) copy-start(bf16[256,2048]{1,0:T(8,128)(2,1)} %param.8) | copy-start | bytes 3145732
Sparse Core Ops, SparseCore 0:
  90.6 53.8 reduce-scatter.1

commit v11 on v10

--- a/solution.py
+++ b/solution.py
@@ -73,10 +73,16 @@
     return swap_sum(full.reshape(2, full.shape[0] // 2, full.shape[1]), "cx")
 
 
-def time_reduce_scatter(x):
+def time_reduce_scatter(left, right):
     outer, mid, inner = (lax.axis_size(a) for a in TIME)
-    blocks = x.reshape(outer, mid, inner, x.shape[0] // (outer * mid * inner), x.shape[1])
-    blocks = swap_sum(jnp.moveaxis(blocks, 2, 0), TIME[2])
+    split = left.reshape(left.shape[0], outer, mid, inner, -1)
+    me = lax.axis_index(TIME[2])
+    pair = [(0, 1), (1, 0)]
+    keep = lax.dynamic_index_in_dim(split, me, 3, keepdims=False).reshape(left.shape[0], -1)
+    give = lax.dynamic_index_in_dim(split, 1 - me, 3, keepdims=False).reshape(left.shape[0], -1)
+    both_left = jnp.concatenate([keep, lax.ppermute(give, TIME[2], pair)], axis=0)
+    both_right = jnp.concatenate([right, lax.ppermute(right, TIME[2], pair)], axis=0)
+    blocks = contract_rows(both_left, both_right).reshape(outer, mid, -1, right.shape[1])
     blocks = ring_sum(blocks, TIME[0])
     return swap_sum(blocks, TIME[1])
 
@@ -132,8 +138,7 @@
         ],
         axis=0,
     )
-    weight_terms = contract_rows(jnp.concatenate([rows, grad_flat], axis=0), right)
-    reduced = time_reduce_scatter(weight_terms)
+    reduced = time_reduce_scatter(jnp.concatenate([rows, grad_flat], axis=0), right)
     scale = lax.rsqrt(jnp.sum(lengths.astype(jnp.float32)))
     part = reduced.shape[0]
     in_summed = reduced[:, : 4 * blocks].reshape(part, 2, 2, blocks).transpose(1, 2, 0, 3)

time: 194 us -> 228 us (1.18); the launches traced: 192 us -> 223 us
  local copies, waits for them, and re-layouts: 19.8 us -> 46.4 us
  waiting for transfers between devices: 80.3 us -> 62.5 us
  starting transfers between devices: 45.3 us -> 57.1 us
  other arithmetic: 11.5 us -> 20.9 us
    ppermute x2, waiting for transfers between devices: 33.4 us -> 18.7 us  [shifted(): return lax.ppermute(x, axis, pairs)]
    ppermute x14, starting transfers between devices: 24.8 us -> 36.9 us  [ring_sum(): got = lax.ppermute(acc, axis, pairs)]
    concatenate x0 -> x1, other arithmetic: none -> 9.95 us  [local(): jnp.concatenate([jnp.concatenate([branch_grads, later, jnp.zeros_like(mix...]
    concatenate x0 -> x4, local copies, waits for them, and re-layouts: none -> 9.13 us  [the longest x3 9.05 us: local(): jnp.concatenate([rows, grad_flat], axis=0)]
    unnamed x22 -> x42, local copies, waits for them, and re-layouts: 6.64 us -> 14.8 us
    add x3 -> x2, other arithmetic: 6.02 us -> 1.79 us  [swap_sum(): return keep + lax.ppermute(give, axis, [(0, 1), (1, 0)])]
    select_n x0 -> x1, local copies, waits for them, and re-layouts: none -> 3.87 us  [local(): grad_rows = jnp.where(valid[:, :, None], upstream, jnp.zeros_like(upstream))]
    squeeze x2 -> x1, local copies, waits for them, and re-layouts: 2.98 us -> 0.03 us  [swap_sum(): give = lax.dynamic_index_in_dim(parts, 1 - me, 0, keepdims=False)]
  transfers between devices with their start and end apart: 26 -> 27, of which waited for: 15 -> 16; matrix products, arithmetic and copies ran while one was open for 11% -> 26% of each run, Pallas kernels for 0% -> 0%
where the time goes in v11:
time: 228 us; the launch traced here: 223 us
  waiting for transfers between devices  62.5 us (27%)
  starting transfers between devices  57.1 us (25%)
  local copies, waits for them, and re-layouts  46.4 us (20%)
  other arithmetic  20.9 us (9%)
  matrix products  20.7 us (9%)
  between operations  15.5 us (7%)
    ppermute x14, waiting for transfers between devices, ring_sum(): got = lax.ppermute(acc, axis, pairs)  39.6 us
    ppermute x14, starting transfers between devices, ring_sum(): got = lax.ppermute(acc, axis, pairs)  36.9 us
    ppermute x2, waiting for transfers between devices, shifted(): return lax.ppermute(x, axis, pairs)  18.7 us
    unnamed x42, local copies, waits for them, and re-layouts  14.8 us
    ppermute x6, starting transfers between devices, chan_ring_reduce_scatter(): got = lax.ppermute(acc, 'cy', pairs)  10.2 us
    concatenate x1, other arithmetic, local(): jnp.concatenate([jnp.concatenate([branch_grads, later, jnp.zeros_like(mix...  9.95 us
    concatenate x3, local copies, waits for them, and re-layouts, local(): jnp.concatenate([rows, grad_flat], axis=0)  9.05 us
    dot_general x1, matrix products, contract_rows(): lax.dot_general(left, right, (((0,), (0,)), ((), ())), preferred_element_...  8.93 us
  transfers between devices with their start and end apart: 27, of which 16 were waited for; matrix products, arithmetic and copies ran while one was open for 26% of the time, Pallas kernels for 0%

profile of v11, /device:TPU:98, one launch (start us, length us, event | category | flops | bytes accessed | tf_op | source)
XLA Modules:
  0.0 223.2 jit_solution(8009673858782357632)
XLA Ops:
  7.2 3.9 %slice_bitcast_fusion.1 = (bf16[2048,256]{1,0:T(8,128)(2,1)S(1)}, bf16[2048,256]{1,0:T(8,128)(2,1)}, bf16[2048,256]{1,0:T(8,128)(2,1)}, bf16[2048,256]{1,0:T(8,128)(2,1)S(1)}) fusion(bf16[2,2,2048,256]{3,2,1,0:T(8,128)(2,1)} %param.7), kind=kLoop, calls=%fused_computation.24 | loop fusion | bytes 8388608 | tf_op jit(solution)/shard_map/squeeze | solution.py:97
  11.2 2.3 %fusion.15 = f32[512,512]{0,1:T(8,128)} fusion(bf16[512,2048]{1,0:T(8,128)(2,1)S(1)} %bitcast.114, bf16[2048,256]{1,0:T(8,128)(2,1)S(1)} %get-tuple-element.12, bf16[2048,256]{1,0:T(8,128)(2,1)S(1)} %get-tuple-element.9), kind=kOutput, calls=%fused_computation.21 | convolution fusion | flops 1077936128 | bytes 5242880 | tf_op jit(solution)/shard_map/dot_general | solution.py:98
  13.4 2.3 %copy.11 = f32[2,256,512]{1,0,2:T(2,128)} copy(f32[2,256,512]{2,1,0:T(8,128)} %bitcast.118) | data formatting | bytes 2097152 | tf_op jit(solution)/shard_map/reshape | solution.py:100
  15.7 5.0 %collective-permute-start = (f32[2,256,512]{1,0,2:T(2,128)}, f32[2,256,512]{1,0,2:T(2,128)}, u32[]{:S(2)}, u32[]{:S(2)}) collective-permute-start(f32[2,256,512]{1,0,2:T(2,128)} %copy.11), channel_id=1, source_target_pairs={{0,32},{8,40},{16,48},{24,56},{32,64},{40,72},{48,80},{56,88},{64,... | collective-permute-start | bytes 3145736 | tf_op jit(solution)/shard_map/ppermute | solution.py:16
  20.9 3.7 %convolution_bitcast_fusion = f32[512,512]{0,1:T(8,128)S(1)} fusion(bf16[512,2048]{1,0:T(8,128)(2,1)} %bitcast.113, bf16[2048,256]{1,0:T(8,128)(2,1)} %get-tuple-element.10, bf16[2048,256]{1,0:T(8,128)(2,1)} %get-tuple-element.11), kind=kOutput, calls=%fused_computation.20 | convolution fusion | flops 1077936128 | bytes 5242880 | tf_op jit(solution)/shard_map/dot_general | solution.py:102
  24.8 18.7 %collective-permute-done = f32[2,256,512]{1,0,2:T(2,128)} collective-permute-done((f32[2,256,512]{1,0,2:T(2,128)}, f32[2,256,512]{1,0,2:T(2,128)}, u32[]{:S(2)}, u32[]{:S(2)}) %collective-permute-start) | collective-permute-done | bytes 1048608 | tf_op jit(solution)/shard_map/ppermute | solution.py:16
  43.5 1.3 copy.17
  45.0 1.6 multiply_convert_fusion.2
  48.3 1.9 collective-permute-start.1
  50.3 6.2 %copy.13 = bf16[2,256,2048]{1,0,2:T(2,128)(2,1)} copy(bf16[2,256,2048]{2,1,0:T(8,128)(2,1)} %param.5) | data formatting | bytes 4194304 | tf_op args[0]
  56.4 3.9 %copy.14 = bf16[2,256,2048]{1,0,2:T(2,128)(2,1)} copy(bf16[2,256,2048]{2,1,0:T(8,128)(2,1)S(1)} %broadcast_select_fusion) | data formatting | bytes 4194304 | tf_op jit(solution)/shard_map/jit(_where)/select_n | solution.py:108
  60.3 4.4 %concatenate.49 = bf16[512,8,2,2,64]{0,4,3,2,1:T(8,128)(2,1)} reshape(bf16[2,256,2048]{1,0,2:T(2,128)(2,1)} %copy.13) | data formatting | bytes 4194304 | tf_op jit(solution)/shard_map/concatenate | solution.py:141
  64.7 4.4 %concatenate.50 = bf16[512,8,2,2,64]{0,4,3,2,1:T(8,128)(2,1)} reshape(bf16[2,256,2048]{1,0,2:T(2,128)(2,1)} %copy.14) | data formatting | bytes 4194304 | tf_op jit(solution)/shard_map/concatenate | solution.py:141
  69.1 2.0 constant_dynamic-update-slice_fusion.1
  73.2 1.1 copy.18
  74.4 9.9 %pad_maximum_fusion = bf16[1024,1280]{0,1:T(8,128)(2,1)} fusion(bf16[512,1280]{0,1:T(8,128)(2,1)S(1)} %concatenate.54, bf16[512,256]{0,1:T(8,128)(2,1)S(1)} %broadcast_in_dim.19, bf16[512,512]{0,1:T(8,128)(2,1)S(1)} %bitcast.108, bf16[512,256]{0,1:T(8,128)(2,1)S(1)} %copy-done.15, bf16[512,256]{0,1:T(8,128)(2,1)S(1)} %get-tuple-element.15), kind=kLoop, calls=%fused_computation.16 | loop fusion | flops 13107200 | bytes 5242880 | tf_op jit(solution)/shard_map/concatenate | solution.py:134
  84.6 2.5 %constant_dynamic-slice_fusion.1 = (bf16[1024,8,2,1,64]{0,4,3,2,1:T(8,128)(2,1)}, bf16[1024,8,2,1,64]{0,4,3,2,1:T(8,128)(2,1)}) fusion(bf16[1024,8,2,2,64]{0,4,3,2,1:T(8,128)(2,1)S(1)} %constant_dynamic-update-slice_fusion, s32[]{:T(128)S(6)} %select_n.221, s32[]{:T(128)S(6)} %select_n.222), kind=kLoop, calls=%fused_computation.79 | loop fusion | bytes 8388616 | tf_op jit(solution)/shard_map/jit(dynamic_index_in_dim)/dynamic_slice | solution.py:81
  87.6 2.9 %fusion.16 = f32[2048,512]{1,0:T(8,128)S(1)} fusion(bf16[2048,256]{1,0:T(8,128)(2,1)} %get-tuple-element.10, bf16[2048,256]{1,0:T(8,128)(2,1)} %get-tuple-element.11, bf16[512,256]{0,1:T(8,128)(2,1)S(1)} %copy-done.15, bf16[512,256]{0,1:T(8,128)(2,1)S(1)} %get-tuple-element.15), kind=kOutput, calls=%fused_computation.22 | convolution fusion | flops 1078984704 | bytes 6815744 | tf_op jit(solution)/shard_map/dot_general | solution.py:26
  90.6 1.3 convolution_add_fusion
  91.8 1.6 fusion.32
  93.5 1.1 fusion.33
  96.3 3.0 %collective-permute-start.5 = (f32[512,128]{1,0:T(8,128)}, f32[512,128]{1,0:T(8,128)}, u32[]{:S(2)}, u32[]{:S(2)}) collective-permute-start(f32[512,128]{1,0:T(8,128)} %dynamic-slice_bitcast_fusion.3), channel_id=1, source_target_pairs={{0,6},{2,0},{4,2},{6,4},{1,7},{3,1},{5,3},{7,5},{8,14},{10,8},{12,... | collective-permute-start | bytes 786440 | tf_op jit(solution)/shard_map/ppermute | solution.py:67
  99.3 1.7 dynamic-slice_bitcast_fusion.4
  102.4 3.0 %collective-permute-done.5 = f32[512,128]{1,0:T(8,128)} collective-permute-done((f32[512,128]{1,0:T(8,128)}, f32[512,128]{1,0:T(8,128)}, u32[]{:S(2)}, u32[]{:S(2)}) %collective-permute-start.5) | collective-permute-done | bytes 262176 | tf_op jit(solution)/shard_map/ppermute | solution.py:67
  105.4 1.1 bitcast_add_fusion.17
  106.5 3.8 %collective-permute-start.6 = (f32[512,128]{1,0:T(8,128)S(1)}, f32[512,128]{1,0:T(8,128)S(1)}, u32[]{:S(2)}, u32[]{:S(2)}) collective-permute-start(f32[512,128]{1,0:T(8,128)S(1)} %bitcast_add_fusion.17), channel_id=1, source_target_pairs={{0,6},{2,0},{4,2},{6,4},{1,7},{3,1},{5,3},{7,5},{8,14},{10,8},{12,... | collective-permute-start | bytes 786440 | tf_op jit(solution)/shard_map/ppermute | solution.py:67
  110.5 1.1 bitcast_add_fusion.20
  111.7 8.9 %fusion = f32[1024,1280]{1,0:T(8,128)S(1)} fusion(bf16[1024,1280]{0,1:T(8,128)(2,1)} %collective-permute-done.10, bf16[512,1280]{0,1:T(8,128)(2,1)} %copy-done.3, bf16[512,256]{0,1:T(8,128)(2,1)S(1)} %broadcast_in_dim.19, bf16[512,512]{0,1:T(8,128)(2,1)S(1)} %bitcast.110, bf16[512,256]{0,1:T(8,128)(2,1)S(1)} %copy-done.15, ...), kind=kOutput, calls=%fused_computation | convolution fusion | flops 5408555008 | bytes 14680064 | tf_op jit(solution)/shard_map/dot_general | solution.py:20
  121.3 13.7 %collective-permute-start.11 = (f32[2,64,640]{2,1,0:T(8,128)S(1)}, f32[2,64,640]{2,1,0:T(8,128)S(1)}, u32[]{:S(2)}, u32[]{:S(2)}) collective-permute-start(f32[2,64,640]{2,1,0:T(8,128)S(1)} %dynamic-slice_bitcast_fusion.1), channel_id=1, source_target_pairs={{0,32},{32,64},{64,96},{96,128},{128,160},{160,192},{192,224},{224... | collective-permute-start | bytes 983048 | tf_op jit(solution)/shard_map/ppermute | solution.py:41
  135.2 3.3 %collective-permute-start.7 = (f32[512,128]{1,0:T(8,128)S(1)}, f32[512,128]{1,0:T(8,128)S(1)}, u32[]{:S(2)}, u32[]{:S(2)}) collective-permute-start(f32[512,128]{1,0:T(8,128)S(1)} %bitcast_add_fusion.16), channel_id=1, source_target_pairs={{0,6},{2,0},{4,2},{6,4},{1,7},{3,1},{5,3},{7,5},{8,14},{10,8},{12,... | collective-permute-start | bytes 786440 | tf_op jit(solution)/shard_map/ppermute | solution.py:67
  138.5 2.6 %collective-permute-done.11 = f32[2,64,640]{2,1,0:T(8,128)S(1)} collective-permute-done((f32[2,64,640]{2,1,0:T(8,128)S(1)}, f32[2,64,640]{2,1,0:T(8,128)S(1)}, u32[]{:S(2)}, u32[]{:S(2)}) %collective-permute-start.11) | collective-permute-done | bytes 327712 | tf_op jit(solution)/shard_map/ppermute | solution.py:41
  141.1 3.8 %collective-permute-start.12 = (f32[2,64,640]{2,1,0:T(8,128)S(1)}, f32[2,64,640]{2,1,0:T(8,128)S(1)}, u32[]{:S(2)}, u32[]{:S(2)}) collective-permute-start(f32[2,64,640]{2,1,0:T(8,128)S(1)} %bitcast_add_fusion.13), channel_id=1, source_target_pairs={{0,32},{32,64},{64,96},{96,128},{128,160},{160,192},{192,224},{224... | collective-permute-start | bytes 983048 | tf_op jit(solution)/shard_map/ppermute | solution.py:41
  145.1 4.9 %collective-permute-done.12 = f32[2,64,640]{2,1,0:T(8,128)S(1)} collective-permute-done((f32[2,64,640]{2,1,0:T(8,128)S(1)}, f32[2,64,640]{2,1,0:T(8,128)S(1)}, u32[]{:S(2)}, u32[]{:S(2)}) %collective-permute-start.12) | collective-permute-done | bytes 327712 | tf_op jit(solution)/shard_map/ppermute | solution.py:41
  150.1 3.8 %collective-permute-start.13 = (f32[2,64,640]{2,1,0:T(8,128)S(1)}, f32[2,64,640]{2,1,0:T(8,128)S(1)}, u32[]{:S(2)}, u32[]{:S(2)}) collective-permute-start(f32[2,64,640]{2,1,0:T(8,128)S(1)} %bitcast_add_fusion.12), channel_id=1, source_target_pairs={{0,32},{32,64},{64,96},{96,128},{128,160},{160,192},{192,224},{224... | collective-permute-start | bytes 983048 | tf_op jit(solution)/shard_map/ppermute | solution.py:41
  154.0 4.4 %collective-permute-done.13 = f32[2,64,640]{2,1,0:T(8,128)S(1)} collective-permute-done((f32[2,64,640]{2,1,0:T(8,128)S(1)}, f32[2,64,640]{2,1,0:T(8,128)S(1)}, u32[]{:S(2)}, u32[]{:S(2)}) %collective-permute-start.13) | collective-permute-done | bytes 327712 | tf_op jit(solution)/shard_map/ppermute | solution.py:41
  158.5 3.8 %collective-permute-start.14 = (f32[2,64,640]{2,1,0:T(8,128)S(1)}, f32[2,64,640]{2,1,0:T(8,128)S(1)}, u32[]{:S(2)}, u32[]{:S(2)}) collective-permute-start(f32[2,64,640]{2,1,0:T(8,128)S(1)} %bitcast_add_fusion.11), channel_id=1, source_target_pairs={{0,32},{32,64},{64,96},{96,128},{128,160},{160,192},{192,224},{224... | collective-permute-start | bytes 983048 | tf_op jit(solution)/shard_map/ppermute | solution.py:41
  162.5 5.3 %collective-permute-done.14 = f32[2,64,640]{2,1,0:T(8,128)S(1)} collective-permute-done((f32[2,64,640]{2,1,0:T(8,128)S(1)}, f32[2,64,640]{2,1,0:T(8,128)S(1)}, u32[]{:S(2)}, u32[]{:S(2)}) %collective-permute-start.14) | collective-permute-done | bytes 327712 | tf_op jit(solution)/shard_map/ppermute | solution.py:41
  167.8 3.8 %collective-permute-start.15 = (f32[2,64,640]{2,1,0:T(8,128)S(1)}, f32[2,64,640]{2,1,0:T(8,128)S(1)}, u32[]{:S(2)}, u32[]{:S(2)}) collective-permute-start(f32[2,64,640]{2,1,0:T(8,128)S(1)} %bitcast_add_fusion.10), channel_id=1, source_target_pairs={{0,32},{32,64},{64,96},{96,128},{128,160},{160,192},{192,224},{224... | collective-permute-start | bytes 983048 | tf_op jit(solution)/shard_map/ppermute | solution.py:41
  172.1 6.2 %collective-permute-done.15 = f32[2,64,640]{2,1,0:T(8,128)S(1)} collective-permute-done((f32[2,64,640]{2,1,0:T(8,128)S(1)}, f32[2,64,640]{2,1,0:T(8,128)S(1)}, u32[]{:S(2)}, u32[]{:S(2)}) %collective-permute-start.15) | collective-permute-done | bytes 327712 | tf_op jit(solution)/shard_map/ppermute | solution.py:41
  178.3 3.8 %collective-permute-start.16 = (f32[2,64,640]{2,1,0:T(8,128)S(1)}, f32[2,64,640]{2,1,0:T(8,128)S(1)}, u32[]{:S(2)}, u32[]{:S(2)}) collective-permute-start(f32[2,64,640]{2,1,0:T(8,128)S(1)} %bitcast_add_fusion.9), channel_id=1, source_target_pairs={{0,32},{32,64},{64,96},{96,128},{128,160},{160,192},{192,224},{224... | collective-permute-start | bytes 983048 | tf_op jit(solution)/shard_map/ppermute | solution.py:41
  183.0 6.9 %collective-permute-done.16 = f32[2,64,640]{2,1,0:T(8,128)S(1)} collective-permute-done((f32[2,64,640]{2,1,0:T(8,128)S(1)}, f32[2,64,640]{2,1,0:T(8,128)S(1)}, u32[]{:S(2)}, u32[]{:S(2)}) %collective-permute-start.16) | collective-permute-done | bytes 327712 | tf_op jit(solution)/shard_map/ppermute | solution.py:41
  190.0 3.8 %collective-permute-start.17 = (f32[2,64,640]{2,1,0:T(8,128)S(1)}, f32[2,64,640]{2,1,0:T(8,128)S(1)}, u32[]{:S(2)}, u32[]{:S(2)}) collective-permute-start(f32[2,64,640]{2,1,0:T(8,128)S(1)} %bitcast_add_fusion.8), channel_id=1, source_target_pairs={{0,32},{32,64},{64,96},{96,128},{128,160},{160,192},{192,224},{224... | collective-permute-start | bytes 983048 | tf_op jit(solution)/shard_map/ppermute | solution.py:41
  195.5 2.8 %collective-permute-done.17 = f32[2,64,640]{2,1,0:T(8,128)S(1)} collective-permute-done((f32[2,64,640]{2,1,0:T(8,128)S(1)}, f32[2,64,640]{2,1,0:T(8,128)S(1)}, u32[]{:S(2)}, u32[]{:S(2)}) %collective-permute-start.17) | collective-permute-done | bytes 327712 | tf_op jit(solution)/shard_map/ppermute | solution.py:41
  198.4 4.6 %collective-permute-done.24 = f32[2,64,640]{2,1,0:T(8,128)S(1)} collective-permute-done((f32[2,64,640]{2,1,0:T(8,128)S(1)}, f32[2,64,640]{2,1,0:T(8,128)S(1)}, u32[]{:S(2)}, u32[]{:S(2)}) %collective-permute-start.24) | collective-permute-done | bytes 327712 | tf_op jit(solution)/shard_map/ppermute | solution.py:41
  204.5 2.1 collective-permute-start.25
  206.7 2.0 pad_maximum_fusion.9
  208.6 2.1 copy.16
  210.7 1.8 add_convert_fusion
  (111 shorter events, 17.8 us)
Async XLA Ops:
  7.2 37.8 %copy-start = (bf16[256,2048]{1,0:T(8,128)(2,1)S(1)}, bf16[256,2048]{1,0:T(8,128)(2,1)}, u32[]{:S(2)}) copy-start(bf16[256,2048]{1,0:T(8,128)(2,1)} %param.8) | copy-start | bytes 3145732
  7.2 199.5 %reduce-scatter.2.cloned.1.call-start = ((), (), s32[]{:S(2)}) async-start(), calls=%async_computation.1 | async-start | bytes 2359296 | tf_op jit(solution)/shard_map/reduce_scatter | solution.py:124
  7.2 3.9 %copy-start.13 = (bf16[2,256,2048]{2,1,0:T(8,128)(2,1)S(1)}, bf16[2,256,2048]{2,1,0:T(8,128)(2,1)}, u32[]{:S(2)}) copy-start(bf16[2,256,2048]{2,1,0:T(8,128)(2,1)} %param.5) | copy-start | bytes 6291460
  11.2 2.3 %copy-start.7 = (bf16[2048,256]{1,0:T(8,128)(2,1)}, bf16[2048,256]{1,0:T(8,128)(2,1)S(1)}, u32[]{:S(2)}) copy-start(bf16[2048,256]{1,0:T(8,128)(2,1)S(1)} %get-tuple-element.9) | copy-start | bytes 3145732
  11.2 2.3 %copy-start.9 = (bf16[2048,256]{1,0:T(8,128)(2,1)}, bf16[2048,256]{1,0:T(8,128)(2,1)S(1)}, u32[]{:S(2)}) copy-start(bf16[2048,256]{1,0:T(8,128)(2,1)S(1)} %get-tuple-element.12) | copy-start | bytes 3145732
  11.2 9.6 %copy-start.18 = (s32[2]{0:T(128)S(1)}, s32[2]{0:T(128)}, u32[]{:S(2)}) copy-start(s32[2]{0:T(128)} %param.9) | copy-start | bytes 28
  15.7 27.7 %collective-permute-start = (f32[2,256,512]{1,0,2:T(2,128)}, f32[2,256,512]{1,0,2:T(2,128)}, u32[]{:S(2)}, u32[]{:S(2)}) collective-permute-start(f32[2,256,512]{1,0,2:T(2,128)} %copy.11), channel_id=1, source_target_pairs={{0,32},{8,40},{16,48},{24,56},{32,64},{40,72},{48,80},{56,88},{64,... | collective-permute-start | bytes 3145736 | tf_op jit(solution)/shard_map/ppermute | solution.py:16
  20.9 3.7 %copy-start.12 = (bf16[2,256,2048]{2,1,0:T(8,128)(2,1)S(1)}, bf16[2,256,2048]{2,1,0:T(8,128)(2,1)}, u32[]{:S(2)}) copy-start(bf16[2,256,2048]{2,1,0:T(8,128)(2,1)} %param.6) | copy-start | bytes 6291460
  46.6 0.7 copy-start.14
  48.3 24.0 %collective-permute-start.1 = (bf16[2,256,512]{1,0,2:T(2,128)(2,1)}, bf16[2,256,512]{1,0,2:T(2,128)(2,1)S(1)}, u32[]{:S(2)}, u32[]{:S(2)}) collective-permute-start(bf16[2,256,512]{1,0,2:T(2,128)(2,1)} %reshape.88), channel_id=1, source_target_pairs={{32,0},{40,8},{48,16},{56,24},{64,32},{72,40},{80,48},{88,56},{96,... | collective-permute-start | bytes 1572872 | tf_op jit(solution)/shard_map/ppermute | solution.py:16
  69.1 2.2 copy-start.2
  71.3 0.9 copy-start.17
  71.3 3.0 %copy-start.15 = (bf16[512,256]{0,1:T(8,128)(2,1)S(1)}, bf16[512,256]{0,1:T(8,128)(2,1)}, u32[]{:S(2)}) copy-start(bf16[512,256]{0,1:T(8,128)(2,1)} %copy-done.14) | copy-start | bytes 786436
  72.4 12.0 %copy-start.3 = (bf16[512,1280]{0,1:T(8,128)(2,1)}, bf16[512,1280]{0,1:T(8,128)(2,1)S(1)}, u32[]{:S(2)}) copy-start(bf16[512,1280]{0,1:T(8,128)(2,1)S(1)} %concatenate.54) | copy-start | bytes 3932164
  72.4 0.8 copy-start.16
  84.3 27.3 %collective-permute-start.10 = (bf16[1024,1280]{0,1:T(8,128)(2,1)}, bf16[1024,1280]{0,1:T(8,128)(2,1)}, u32[]{:S(2)}, u32[]{:S(2)}) collective-permute-start(bf16[1024,1280]{0,1:T(8,128)(2,1)} %pad_maximum_fusion), channel_id=1, source_target_pairs={{0,8},{8,0},{1,9},{9,1},{2,10},{10,2},{3,11},{11,3},{4,12},{12,4},... | collective-permute-start | bytes 7864328 | tf_op jit(solution)/shard_map/ppermute | solution.py:84
  87.1 24.5 %collective-permute-start.9 = (bf16[1024,1024]{0,1:T(8,128)(2,1)}, bf16[1024,1024]{0,1:T(8,128)(2,1)}, u32[]{:S(2)}, u32[]{:S(2)}) collective-permute-start(bf16[1024,1024]{0,1:T(8,128)(2,1)} %bitcast.24), channel_id=1, source_target_pairs={{0,8},{8,0},{1,9},{9,1},{2,10},{10,2},{3,11},{11,3},{4,12},{12,4},... | collective-permute-start | bytes 6291464 | tf_op jit(solution)/shard_map/ppermute | solution.py:83
  87.6 2.9 %copy-start.8 = (bf16[2048,256]{1,0:T(8,128)(2,1)S(1)}, bf16[2048,256]{1,0:T(8,128)(2,1)}, u32[]{:S(2)}) copy-start(bf16[2048,256]{1,0:T(8,128)(2,1)} %copy-done.7) | copy-start | bytes 3145732
  87.6 3.0 %copy-start.10 = (bf16[2048,256]{1,0:T(8,128)(2,1)S(1)}, bf16[2048,256]{1,0:T(8,128)(2,1)}, u32[]{:S(2)}) copy-start(bf16[2048,256]{1,0:T(8,128)(2,1)} %copy-done.9) | copy-start | bytes 3145732
  94.6 1.0 copy-start.5
  96.3 9.1 %collective-permute-start.5 = (f32[512,128]{1,0:T(8,128)}, f32[512,128]{1,0:T(8,128)}, u32[]{:S(2)}, u32[]{:S(2)}) collective-permute-start(f32[512,128]{1,0:T(8,128)} %dynamic-slice_bitcast_fusion.3), channel_id=1, source_target_pairs={{0,6},{2,0},{4,2},{6,4},{1,7},{3,1},{5,3},{7,5},{8,14},{10,8},{12,... | collective-permute-start | bytes 786440 | tf_op jit(solution)/shard_map/ppermute | solution.py:67
  101.0 9.5 %collective-permute-start.2 = (f32[512,128]{1,0:T(8,128)}, f32[512,128]{1,0:T(8,128)}, u32[]{:S(2)}, u32[]{:S(2)}) collective-permute-start(f32[512,128]{1,0:T(8,128)} %dynamic-slice_bitcast_fusion.4), channel_id=1, source_target_pairs={{0,2},{2,4},{4,6},{6,0},{1,3},{3,5},{5,7},{7,1},{8,10},{10,12},{12... | collective-permute-start | bytes 786440 | tf_op jit(solution)/shard_map/ppermute | solution.py:67
  106.5 28.7 %collective-permute-start.6 = (f32[512,128]{1,0:T(8,128)S(1)}, f32[512,128]{1,0:T(8,128)S(1)}, u32[]{:S(2)}, u32[]{:S(2)}) collective-permute-start(f32[512,128]{1,0:T(8,128)S(1)} %bitcast_add_fusion.17), channel_id=1, source_target_pairs={{0,6},{2,0},{4,2},{6,4},{1,7},{3,1},{5,3},{7,5},{8,14},{10,8},{12,... | collective-permute-start | bytes 786440 | tf_op jit(solution)/shard_map/ppermute | solution.py:67
  111.5 33.4 %collective-permute-start.3 = (f32[512,128]{1,0:T(8,128)S(1)}, f32[512,128]{1,0:T(8,128)S(1)}, u32[]{:S(2)}, u32[]{:S(2)}) collective-permute-start(f32[512,128]{1,0:T(8,128)S(1)} %bitcast_add_fusion.20), channel_id=1, source_target_pairs={{0,2},{2,4},{4,6},{6,0},{1,3},{3,5},{5,7},{7,1},{8,10},{10,12},{12... | collective-permute-start | bytes 786440 | tf_op jit(solution)/shard_map/ppermute | solution.py:67
  120.6 14.5 %copy-start.6 = (f32[4,512,128]{2,1,0:T(8,128)S(1)}, f32[4,512,128]{2,1,0:T(8,128)}, u32[]{:S(2)}) copy-start(f32[4,512,128]{2,1,0:T(8,128)} %copy-done.5) | copy-start | bytes 3145732
  121.3 23.7 %copy-start.4 = (f32[4,512,128]{2,1,0:T(8,128)S(1)}, f32[4,512,128]{2,1,0:T(8,128)}, u32[]{:S(2)}) copy-start(f32[4,512,128]{2,1,0:T(8,128)} %get-tuple-element.13) | copy-start | bytes 3145732
  121.3 19.7 %collective-permute-start.11 = (f32[2,64,640]{2,1,0:T(8,128)S(1)}, f32[2,64,640]{2,1,0:T(8,128)S(1)}, u32[]{:S(2)}, u32[]{:S(2)}) collective-permute-start(f32[2,64,640]{2,1,0:T(8,128)S(1)} %dynamic-slice_bitcast_fusion.1), channel_id=1, source_target_pairs={{0,32},{32,64},{64,96},{96,128},{128,160},{160,192},{192,224},{224... | collective-permute-start | bytes 983048 | tf_op jit(solution)/shard_map/ppermute | solution.py:41
  135.0 9.8 %collective-permute-start.18 = (f32[2,64,640]{2,1,0:T(8,128)S(1)}, f32[2,64,640]{2,1,0:T(8,128)S(1)}, u32[]{:S(2)}, u32[]{:S(2)}) collective-permute-start(f32[2,64,640]{2,1,0:T(8,128)S(1)} %dynamic-slice_bitcast_fusion), channel_id=1, source_target_pairs={{0,224},{32,0},{64,32},{96,64},{128,96},{160,128},{192,160},{224,1... | collective-permute-start | bytes 983048 | tf_op jit(solution)/shard_map/ppermute | solution.py:41
  135.2 18.8 %collective-permute-start.7 = (f32[512,128]{1,0:T(8,128)S(1)}, f32[512,128]{1,0:T(8,128)S(1)}, u32[]{:S(2)}, u32[]{:S(2)}) collective-permute-start(f32[512,128]{1,0:T(8,128)S(1)} %bitcast_add_fusion.16), channel_id=1, source_target_pairs={{0,6},{2,0},{4,2},{6,4},{1,7},{3,1},{5,3},{7,5},{8,14},{10,8},{12,... | collective-permute-start | bytes 786440 | tf_op jit(solution)/shard_map/ppermute | solution.py:67
  141.1 8.9 %collective-permute-start.12 = (f32[2,64,640]{2,1,0:T(8,128)S(1)}, f32[2,64,640]{2,1,0:T(8,128)S(1)}, u32[]{:S(2)}, u32[]{:S(2)}) collective-permute-start(f32[2,64,640]{2,1,0:T(8,128)S(1)} %bitcast_add_fusion.13), channel_id=1, source_target_pairs={{0,32},{32,64},{64,96},{96,128},{128,160},{160,192},{192,224},{224... | collective-permute-start | bytes 983048 | tf_op jit(solution)/shard_map/ppermute | solution.py:41
  144.9 8.9 %collective-permute-start.19 = (f32[2,64,640]{2,1,0:T(8,128)S(1)}, f32[2,64,640]{2,1,0:T(8,128)S(1)}, u32[]{:S(2)}, u32[]{:S(2)}) collective-permute-start(f32[2,64,640]{2,1,0:T(8,128)S(1)} %bitcast_add_fusion.6), channel_id=1, source_target_pairs={{0,224},{32,0},{64,32},{96,64},{128,96},{160,128},{192,160},{224,1... | collective-permute-start | bytes 983048 | tf_op jit(solution)/shard_map/ppermute | solution.py:41
  145.0 17.4 %collective-permute-start.4 = (f32[512,128]{1,0:T(8,128)S(1)}, f32[512,128]{1,0:T(8,128)S(1)}, u32[]{:S(2)}, u32[]{:S(2)}) collective-permute-start(f32[512,128]{1,0:T(8,128)S(1)} %bitcast_add_fusion.19), channel_id=1, source_target_pairs={{0,2},{2,4},{4,6},{6,0},{1,3},{3,5},{5,7},{7,1},{8,10},{10,12},{12... | collective-permute-start | bytes 786440 | tf_op jit(solution)/shard_map/ppermute | solution.py:67
  150.1 8.4 %collective-permute-start.13 = (f32[2,64,640]{2,1,0:T(8,128)S(1)}, f32[2,64,640]{2,1,0:T(8,128)S(1)}, u32[]{:S(2)}, u32[]{:S(2)}) collective-permute-start(f32[2,64,640]{2,1,0:T(8,128)S(1)} %bitcast_add_fusion.12), channel_id=1, source_target_pairs={{0,32},{32,64},{64,96},{96,128},{128,160},{160,192},{192,224},{224... | collective-permute-start | bytes 983048 | tf_op jit(solution)/shard_map/ppermute | solution.py:41
  153.9 8.4 %collective-permute-start.20 = (f32[2,64,640]{2,1,0:T(8,128)S(1)}, f32[2,64,640]{2,1,0:T(8,128)S(1)}, u32[]{:S(2)}, u32[]{:S(2)}) collective-permute-start(f32[2,64,640]{2,1,0:T(8,128)S(1)} %bitcast_add_fusion.5), channel_id=1, source_target_pairs={{0,224},{32,0},{64,32},{96,64},{128,96},{160,128},{192,160},{224,1... | collective-permute-start | bytes 983048 | tf_op jit(solution)/shard_map/ppermute | solution.py:41
  158.5 9.3 %collective-permute-start.14 = (f32[2,64,640]{2,1,0:T(8,128)S(1)}, f32[2,64,640]{2,1,0:T(8,128)S(1)}, u32[]{:S(2)}, u32[]{:S(2)}) collective-permute-start(f32[2,64,640]{2,1,0:T(8,128)S(1)} %bitcast_add_fusion.11), channel_id=1, source_target_pairs={{0,32},{32,64},{64,96},{96,128},{128,160},{160,192},{192,224},{224... | collective-permute-start | bytes 983048 | tf_op jit(solution)/shard_map/ppermute | solution.py:41
  162.4 9.6 %collective-permute-start.21 = (f32[2,64,640]{2,1,0:T(8,128)S(1)}, f32[2,64,640]{2,1,0:T(8,128)S(1)}, u32[]{:S(2)}, u32[]{:S(2)}) collective-permute-start(f32[2,64,640]{2,1,0:T(8,128)S(1)} %bitcast_add_fusion.4), channel_id=1, source_target_pairs={{0,224},{32,0},{64,32},{96,64},{128,96},{160,128},{192,160},{224,1... | collective-permute-start | bytes 983048 | tf_op jit(solution)/shard_map/ppermute | solution.py:41
  167.8 10.5 %collective-permute-start.15 = (f32[2,64,640]{2,1,0:T(8,128)S(1)}, f32[2,64,640]{2,1,0:T(8,128)S(1)}, u32[]{:S(2)}, u32[]{:S(2)}) collective-permute-start(f32[2,64,640]{2,1,0:T(8,128)S(1)} %bitcast_add_fusion.10), channel_id=1, source_target_pairs={{0,32},{32,64},{64,96},{96,128},{128,160},{160,192},{192,224},{224... | collective-permute-start | bytes 983048 | tf_op jit(solution)/shard_map/ppermute | solution.py:41
  172.0 10.7 %collective-permute-start.22 = (f32[2,64,640]{2,1,0:T(8,128)S(1)}, f32[2,64,640]{2,1,0:T(8,128)S(1)}, u32[]{:S(2)}, u32[]{:S(2)}) collective-permute-start(f32[2,64,640]{2,1,0:T(8,128)S(1)} %bitcast_add_fusion.3), channel_id=1, source_target_pairs={{0,224},{32,0},{64,32},{96,64},{128,96},{160,128},{192,160},{224,1... | collective-permute-start | bytes 983048 | tf_op jit(solution)/shard_map/ppermute | solution.py:41
  178.3 11.6 %collective-permute-start.16 = (f32[2,64,640]{2,1,0:T(8,128)S(1)}, f32[2,64,640]{2,1,0:T(8,128)S(1)}, u32[]{:S(2)}, u32[]{:S(2)}) collective-permute-start(f32[2,64,640]{2,1,0:T(8,128)S(1)} %bitcast_add_fusion.9), channel_id=1, source_target_pairs={{0,32},{32,64},{64,96},{96,128},{128,160},{160,192},{192,224},{224... | collective-permute-start | bytes 983048 | tf_op jit(solution)/shard_map/ppermute | solution.py:41
  182.8 11.9 %collective-permute-start.23 = (f32[2,64,640]{2,1,0:T(8,128)S(1)}, f32[2,64,640]{2,1,0:T(8,128)S(1)}, u32[]{:S(2)}, u32[]{:S(2)}) collective-permute-start(f32[2,64,640]{2,1,0:T(8,128)S(1)} %bitcast_add_fusion.2), channel_id=1, source_target_pairs={{0,224},{32,0},{64,32},{96,64},{128,96},{160,128},{192,160},{224,1... | collective-permute-start | bytes 983048 | tf_op jit(solution)/shard_map/ppermute | solution.py:41
  182.9 11.9 %collective-permute-start.8 = (f32[256,256]{1,0:T(8,128)S(1)}, f32[256,256]{1,0:T(8,128)S(1)}, u32[]{:S(2)}, u32[]{:S(2)}) collective-permute-start(f32[256,256]{1,0:T(8,128)S(1)} %dynamic-slice_bitcast_fusion.2), channel_id=1, source_target_pairs={{0,1},{1,0},{2,3},{3,2},{4,5},{5,4},{6,7},{7,6},{8,9},{9,8},{10,11... | collective-permute-start | bytes 786440 | tf_op jit(solution)/shard_map/ppermute | solution.py:53
  190.0 8.4 %collective-permute-start.17 = (f32[2,64,640]{2,1,0:T(8,128)S(1)}, f32[2,64,640]{2,1,0:T(8,128)S(1)}, u32[]{:S(2)}, u32[]{:S(2)}) collective-permute-start(f32[2,64,640]{2,1,0:T(8,128)S(1)} %bitcast_add_fusion.8), channel_id=1, source_target_pairs={{0,32},{32,64},{64,96},{96,128},{128,160},{160,192},{192,224},{224... | collective-permute-start | bytes 983048 | tf_op jit(solution)/shard_map/ppermute | solution.py:41
  194.7 8.4 %collective-permute-start.24 = (f32[2,64,640]{2,1,0:T(8,128)S(1)}, f32[2,64,640]{2,1,0:T(8,128)S(1)}, u32[]{:S(2)}, u32[]{:S(2)}) collective-permute-start(f32[2,64,640]{2,1,0:T(8,128)S(1)} %bitcast_add_fusion.1), channel_id=1, source_target_pairs={{0,224},{32,0},{64,32},{96,64},{128,96},{160,128},{192,160},{224,1... | collective-permute-start | bytes 983048 | tf_op jit(solution)/shard_map/ppermute | solution.py:41
  203.1 0.7 copy-start.11
  204.5 8.9 %collective-permute-start.25 = (f32[64,1280]{1,0:T(8,128)}, f32[64,1280]{1,0:T(8,128)}, u32[]{:S(2)}, u32[]{:S(2)}) collective-permute-start(f32[64,1280]{1,0:T(8,128)} %fusion.21), channel_id=1, source_target_pairs={{0,16},{16,0},{1,17},{17,1},{2,18},{18,2},{3,19},{19,3},{4,20},{20... | collective-permute-start | bytes 983048 | tf_op jit(solution)/shard_map/ppermute | solution.py:53
  206.6 9.5 %copy-start.1 = (bf16[256,2048]{1,0:T(8,128)(2,1)S(1)}, bf16[256,2048]{1,0:T(8,128)(2,1)}, u32[]{:S(2)}) copy-start(bf16[256,2048]{1,0:T(8,128)(2,1)} %param.8) | copy-start | bytes 3145732
Sparse Core Ops, SparseCore 0:
  102.5 56.3 reduce-scatter.1

commit v12 on v10

--- a/solution.py
+++ b/solution.py
@@ -90,27 +90,29 @@
     w_now = jnp.concatenate([w_in[0, 0], w_in[0, 1]], axis=1)
     w_dil = jnp.concatenate([w_in[1, 0], w_in[1, 1]], axis=1)
     dilated = jnp.dot(rows, w_dil, preferred_element_type=jnp.float32)
-    dilated_prior = shifted(
-        dilated.reshape(traj, window_extent, 2 * blocks), TIME, receptive_extent
-    ).reshape(rows_n, 2 * blocks)
-    pre = jnp.dot(rows, w_now, preferred_element_type=jnp.float32) + dilated_prior
-    filt = pre[:, :blocks]
-    gate = pre[:, blocks:]
+    present = jnp.dot(rows, w_now, preferred_element_type=jnp.float32)
     first = lax.axis_index(TIME) * window_extent
     positions = first + jnp.arange(window_extent, dtype=jnp.int32)
     valid = positions[None, :] < lengths[:, None]
     grad_rows = jnp.where(valid[:, :, None], upstream, jnp.zeros_like(upstream))
     grad_flat = grad_rows.reshape(rows_n, width)
-    tangent = jnp.tanh(filt)
-    sigma = jax.nn.sigmoid(gate)
-    mixed = (tangent * sigma).astype(jnp.bfloat16)
     dmix = contract_cols(grad_flat, w_out)
-    filter_gradient = (dmix * (1.0 - tangent * tangent) * sigma).astype(jnp.bfloat16)
-    gate_gradient = (dmix * tangent * sigma * (1.0 - sigma)).astype(jnp.bfloat16)
-    branch_grads = jnp.concatenate([filter_gradient, gate_gradient], axis=1)
-    later = shifted(
-        branch_grads.reshape(traj, window_extent, 2 * blocks), TIME, -receptive_extent
-    ).reshape(rows_n, 2 * blocks)
+    mixed_parts, grad_parts, later_parts = [], [], []
+    for b in range(traj):
+        rows_b = slice(b * window_extent, (b + 1) * window_extent)
+        pre = present[rows_b] + shifted(dilated[rows_b], TIME, receptive_extent)
+        tangent = jnp.tanh(pre[:, :blocks])
+        sigma = jax.nn.sigmoid(pre[:, blocks:])
+        mixed_parts.append((tangent * sigma).astype(jnp.bfloat16))
+        dmix_b = dmix[rows_b]
+        filter_gradient = (dmix_b * (1.0 - tangent * tangent) * sigma).astype(jnp.bfloat16)
+        gate_gradient = (dmix_b * tangent * sigma * (1.0 - sigma)).astype(jnp.bfloat16)
+        grad_b = jnp.concatenate([filter_gradient, gate_gradient], axis=1)
+        grad_parts.append(grad_b)
+        later_parts.append(shifted(grad_b, TIME, -receptive_extent))
+    mixed = jnp.concatenate(mixed_parts, axis=0)
+    branch_grads = jnp.concatenate(grad_parts, axis=0)
+    later = jnp.concatenate(later_parts, axis=0)
     partial_value = contract_cols(w_now, branch_grads) + contract_cols(w_dil, later)
     cut = partial_value.shape[1] // 2
     summed = jnp.concatenate(

time: 194 us -> 186 us (0.959)
  waiting for transfers between devices: 80.3 us -> 71 us
  starting transfers between devices: 45.3 us -> 50.3 us
  local copies, waits for them, and re-layouts: 19.8 us -> 16.1 us
  matrix products: 19.7 us -> 16.3 us
  other arithmetic: 11.5 us -> 14.7 us
    ppermute x2 -> x4, waiting for transfers between devices: 33.4 us -> 24.1 us  [shifted(): return lax.ppermute(x, axis, pairs)]
    ppermute x2 -> x4, starting transfers between devices: 6.95 us -> 12.1 us  [shifted(): return lax.ppermute(x, axis, pairs)]
    unnamed x22 -> x23, local copies, waits for them, and re-layouts: 6.64 us -> 4.11 us
    reshape x2 -> x0, local copies, waits for them, and re-layouts: 2.38 us -> none  [the longest x1 2.26 us: local(): dilated.reshape(traj, window_extent, 2 * blocks)]
    dot_general x1, matrix products: 8.13 us -> 5.88 us  [contract_rows(): lax.dot_general(left, right, (((0,), (0,)), ((), ())), preferred_element_...]
  transfers between devices with their start and end apart: 26 -> 28, of which waited for: 15 -> 17; matrix products, arithmetic and copies ran while one was open for 11% -> 13% of each run, Pallas kernels for 0% -> 0%
where the time goes in v12:
time: 186 us; the launch traced here: 184 us
  waiting for transfers between devices  71 us (38%)
  starting transfers between devices  50.3 us (27%)
  matrix products  16.3 us (9%)
  local copies, waits for them, and re-layouts  16.1 us (9%)
  between operations  15.3 us (8%)
  other arithmetic  14.7 us (8%)
    ppermute x14, waiting for transfers between devices, ring_sum(): got = lax.ppermute(acc, axis, pairs)  39.4 us
    ppermute x14, starting transfers between devices, ring_sum(): got = lax.ppermute(acc, axis, pairs)  24.8 us
    ppermute x4, waiting for transfers between devices, shifted(): return lax.ppermute(x, axis, pairs)  24.1 us
    ppermute x4, starting transfers between devices, shifted(): return lax.ppermute(x, axis, pairs)  12.1 us
    ppermute x6, starting transfers between devices, chan_ring_reduce_scatter(): got = lax.ppermute(acc, 'cy', pairs)  10.4 us
    add x3, other arithmetic, swap_sum(): return keep + lax.ppermute(give, axis, [(0, 1), (1, 0)])  6.02 us
    dot_general x1, matrix products, contract_rows(): lax.dot_general(left, right, (((0,), (0,)), ((), ())), preferred_element_...  5.88 us
    dot_general x3, matrix products, contract_cols(): lax.dot_general(left, right, (((1,), (1,)), ((), ())), preferred_element_...  5.59 us
  transfers between devices with their start and end apart: 28, of which 17 were waited for; matrix products, arithmetic and copies ran while one was open for 13% of the time, Pallas kernels for 0%

profile of v12, /device:TPU:98, one launch (start us, length us, event | category | flops | bytes accessed | tf_op | source)
XLA Modules:
  0.0 183.7 jit_solution(6649233704785194793)
XLA Ops:
  7.2 4.0 %slice_bitcast_fusion.1 = (bf16[2048,256]{1,0:T(8,128)(2,1)S(1)}, bf16[2048,256]{1,0:T(8,128)(2,1)}, bf16[2048,256]{1,0:T(8,128)(2,1)}, bf16[2048,256]{1,0:T(8,128)(2,1)S(1)}) fusion(bf16[2,2,2048,256]{3,2,1,0:T(8,128)(2,1)} %param.7), kind=kLoop, calls=%fused_computation.31 | loop fusion | bytes 8388608 | tf_op jit(solution)/shard_map/squeeze | solution.py:91
  11.2 1.3 convolution_bitcast_fusion
  12.5 1.1 fusion.48
  13.6 5.0 %collective-permute-start = (f32[256,512]{0,1:T(8,128)}, f32[256,512]{0,1:T(8,128)}, u32[]{:S(2)}, u32[]{:S(2)}) collective-permute-start(f32[256,512]{0,1:T(8,128)} %get-tuple-element.17), channel_id=1, source_target_pairs={{0,32},{8,40},{16,48},{24,56},{32,64},{40,72},{48,80},{56,88},{64,... | collective-permute-start | bytes 1572872 | tf_op jit(solution)/shard_map/ppermute | solution.py:16
  18.7 2.9 %collective-permute-start.1 = (f32[256,512]{0,1:T(8,128)}, f32[256,512]{0,1:T(8,128)}, u32[]{:S(2)}, u32[]{:S(2)}) collective-permute-start(f32[256,512]{0,1:T(8,128)} %get-tuple-element.18), channel_id=1, source_target_pairs={{0,32},{8,40},{16,48},{24,56},{32,64},{40,72},{48,80},{56,88},{64,... | collective-permute-start | bytes 1572872 | tf_op jit(solution)/shard_map/ppermute | solution.py:16
  21.7 1.8 broadcast_select_fusion
  23.5 1.4 copy-done.3
  24.9 1.5 fusion.49
  26.4 3.5 %convolution_bitcast_fusion.1 = f32[512,512]{0,1:T(8,128)S(1)} fusion(bf16[512,2048]{1,0:T(8,128)(2,1)} %bitcast.101, bf16[2048,256]{1,0:T(8,128)(2,1)} %get-tuple-element.8, bf16[2048,256]{1,0:T(8,128)(2,1)} %get-tuple-element.9), kind=kOutput, calls=%fused_computation.27 | convolution fusion | flops 1077936128 | bytes 5242880 | tf_op jit(solution)/shard_map/dot_general | solution.py:93
  30.0 1.3 collective-permute-done
  31.3 10.1 %collective-permute-done.1 = f32[256,512]{0,1:T(8,128)} collective-permute-done((f32[256,512]{0,1:T(8,128)}, f32[256,512]{0,1:T(8,128)}, u32[]{:S(2)}, u32[]{:S(2)}) %collective-permute-start.1) | collective-permute-done | bytes 524320 | tf_op jit(solution)/shard_map/ppermute | solution.py:16
  41.4 1.4 slice_add_fusion.1
  43.2 2.2 %collective-permute-start.2 = (bf16[256,512]{0,1:T(8,128)(2,1)S(1)}, bf16[256,512]{0,1:T(8,128)(2,1)S(1)}, u32[]{:S(2)}, u32[]{:S(2)}) collective-permute-start(bf16[256,512]{0,1:T(8,128)(2,1)S(1)} %pad_maximum_fusion.8), channel_id=1, source_target_pairs={{32,0},{40,8},{48,16},{56,24},{64,32},{72,40},{80,48},{88,56},{96,... | collective-permute-start | bytes 786440 | tf_op jit(solution)/shard_map/ppermute | solution.py:16
  45.4 1.9 %collective-permute-start.3 = (bf16[256,512]{0,1:T(8,128)(2,1)S(1)}, bf16[256,512]{0,1:T(8,128)(2,1)S(1)}, u32[]{:S(2)}, u32[]{:S(2)}) collective-permute-start(bf16[256,512]{0,1:T(8,128)(2,1)S(1)} %pad_maximum_fusion.9), channel_id=1, source_target_pairs={{32,0},{40,8},{48,16},{56,24},{64,32},{72,40},{80,48},{88,56},{96,... | collective-permute-start | bytes 786440 | tf_op jit(solution)/shard_map/ppermute | solution.py:16
  47.4 8.8 %collective-permute-done.2 = bf16[256,512]{0,1:T(8,128)(2,1)S(1)} collective-permute-done((bf16[256,512]{0,1:T(8,128)(2,1)S(1)}, bf16[256,512]{0,1:T(8,128)(2,1)S(1)}, u32[]{:S(2)}, u32[]{:S(2)}) %collective-permute-start.2) | collective-permute-done | bytes 262176 | tf_op jit(solution)/shard_map/ppermute | solution.py:16
  56.2 3.9 %collective-permute-done.3 = bf16[256,512]{0,1:T(8,128)(2,1)S(1)} collective-permute-done((bf16[256,512]{0,1:T(8,128)(2,1)S(1)}, bf16[256,512]{0,1:T(8,128)(2,1)S(1)}, u32[]{:S(2)}, u32[]{:S(2)}) %collective-permute-start.3) | collective-permute-done | bytes 262176 | tf_op jit(solution)/shard_map/ppermute | solution.py:16
  60.2 5.9 %fusion = f32[2048,1280]{1,0:T(8,128)S(1)} fusion(bf16[512,2048]{1,0:T(8,128)(2,1)S(1)} %bitcast.96, bf16[512,2048]{1,0:T(8,128)(2,1)S(1)} %bitcast.103, bf16[512,1280]{0,1:T(8,128)(2,1)S(1)} %fusion.20, bf16[512,256]{0,1:T(8,128)(2,1)S(1)} %broadcast_in_dim.19, bf16[512,512]{0,1:T(8,128)(2,1)S(1)} %constant_dynamic-update-slice_fusion, ...), kind=kOutput, calls=%fused_computation.2 | convolution fusion | flops 5395447808 | bytes 17301504 | tf_op jit(solution)/shard_map/dot_general | solution.py:20
  66.1 3.0 %dynamic-slice_bitcast_fusion = f32[8,2,64,1280]{3,2,1,0:T(8,128)} fusion(f32[8,2,2,64,1280]{4,3,2,1,0:T(8,128)S(1)} %bitcast.92, s32[]{:T(128)S(6)} %select_n.222), kind=kLoop, calls=%fused_computation.1 | loop fusion | bytes 10485764 | tf_op jit(solution)/shard_map/jit(dynamic_index_in_dim)/squeeze | solution.py:52
  69.1 2.7 %copy-done.2 = f32[2048,1280]{1,0:T(8,128)} copy-done((f32[2048,1280]{1,0:T(8,128)}, f32[2048,1280]{1,0:T(8,128)S(1)}, u32[]{:S(2)}) %copy-start.2) | copy-done | bytes 10485784
  71.8 2.8 %fusion.19 = f32[2048,512]{1,0:T(8,128)S(1)} fusion(bf16[2048,256]{1,0:T(8,128)(2,1)} %get-tuple-element.8, bf16[2048,256]{1,0:T(8,128)(2,1)} %get-tuple-element.9, bf16[256,256]{0,1:T(8,128)(2,1)S(1)} %get-tuple-element.22, bf16[256,256]{0,1:T(8,128)(2,1)S(1)} %copy-done.6, bf16[256,256]{0,1:T(8,128)(2,1)S(1)} %get-tuple-element.14, ...), kind=kOutput, calls=%fused_computation.28 | convolution fusion | flops 1080033280 | bytes 6815744 | tf_op jit(solution)/shard_map/dot_general | solution.py:26
  74.5 1.2 convolution_add_fusion
  75.8 1.7 fusion.46
  77.7 3.1 %collective-permute-start.7 = (f32[512,128]{1,0:T(8,128)S(1)}, f32[512,128]{1,0:T(8,128)S(1)}, u32[]{:S(2)}, u32[]{:S(2)}) collective-permute-start(f32[512,128]{1,0:T(8,128)S(1)} %dynamic-slice_bitcast_fusion.4), channel_id=1, source_target_pairs={{0,6},{2,0},{4,2},{6,4},{1,7},{3,1},{5,3},{7,5},{8,14},{10,8},{12,... | collective-permute-start | bytes 786440 | tf_op jit(solution)/shard_map/ppermute | solution.py:67
  82.3 4.7 %collective-permute-done.7 = f32[512,128]{1,0:T(8,128)S(1)} collective-permute-done((f32[512,128]{1,0:T(8,128)S(1)}, f32[512,128]{1,0:T(8,128)S(1)}, u32[]{:S(2)}, u32[]{:S(2)}) %collective-permute-start.7) | collective-permute-done | bytes 262176 | tf_op jit(solution)/shard_map/ppermute | solution.py:67
  87.1 3.8 %collective-permute-start.8 = (f32[512,128]{1,0:T(8,128)S(1)}, f32[512,128]{1,0:T(8,128)S(1)}, u32[]{:S(2)}, u32[]{:S(2)}) collective-permute-start(f32[512,128]{1,0:T(8,128)S(1)} %bitcast_add_fusion.18), channel_id=1, source_target_pairs={{0,6},{2,0},{4,2},{6,4},{1,7},{3,1},{5,3},{7,5},{8,14},{10,8},{12,... | collective-permute-start | bytes 786440 | tf_op jit(solution)/shard_map/ppermute | solution.py:67
  91.0 5.0 %bitcast_add_fusion = f32[8,2,64,1280]{3,2,1,0:T(8,128)S(1)} fusion(f32[8,2,64,1280]{3,2,1,0:T(8,128)} %collective-permute-done.11, f32[8,2,2,64,1280]{4,3,2,1,0:T(8,128)} %bitcast.93, s32[]{:T(128)S(6)} %select_n.221), kind=kLoop, calls=%fused_computation | loop fusion | flops 1310720 | bytes 15728644 | tf_op jit(solution)/shard_map/add | solution.py:53
  96.7 1.6 collective-permute-start.12
  98.9 3.3 %collective-permute-start.9 = (f32[512,128]{1,0:T(8,128)S(1)}, f32[512,128]{1,0:T(8,128)S(1)}, u32[]{:S(2)}, u32[]{:S(2)}) collective-permute-start(f32[512,128]{1,0:T(8,128)S(1)} %bitcast_add_fusion.17), channel_id=1, source_target_pairs={{0,6},{2,0},{4,2},{6,4},{1,7},{3,1},{5,3},{7,5},{8,14},{10,8},{12,... | collective-permute-start | bytes 786440 | tf_op jit(solution)/shard_map/ppermute | solution.py:67
  102.2 3.3 %collective-permute-done.12 = f32[2,64,640]{2,1,0:T(8,128)S(1)} collective-permute-done((f32[2,64,640]{2,1,0:T(8,128)S(1)}, f32[2,64,640]{2,1,0:T(8,128)S(1)}, u32[]{:S(2)}, u32[]{:S(2)}) %collective-permute-start.12) | collective-permute-done | bytes 327712 | tf_op jit(solution)/shard_map/ppermute | solution.py:41
  105.6 3.0 %collective-permute-start.13 = (f32[2,64,640]{2,1,0:T(8,128)S(1)}, f32[2,64,640]{2,1,0:T(8,128)S(1)}, u32[]{:S(2)}, u32[]{:S(2)}) collective-permute-start(f32[2,64,640]{2,1,0:T(8,128)S(1)} %bitcast_add_fusion.14), channel_id=1, source_target_pairs={{0,32},{32,64},{64,96},{96,128},{128,160},{160,192},{192,224},{224... | collective-permute-start | bytes 983048 | tf_op jit(solution)/shard_map/ppermute | solution.py:41
  108.9 5.4 %collective-permute-done.13 = f32[2,64,640]{2,1,0:T(8,128)S(1)} collective-permute-done((f32[2,64,640]{2,1,0:T(8,128)S(1)}, f32[2,64,640]{2,1,0:T(8,128)S(1)}, u32[]{:S(2)}, u32[]{:S(2)}) %collective-permute-start.13) | collective-permute-done | bytes 327712 | tf_op jit(solution)/shard_map/ppermute | solution.py:41
  114.3 4.0 %collective-permute-start.14 = (f32[2,64,640]{2,1,0:T(8,128)S(1)}, f32[2,64,640]{2,1,0:T(8,128)S(1)}, u32[]{:S(2)}, u32[]{:S(2)}) collective-permute-start(f32[2,64,640]{2,1,0:T(8,128)S(1)} %bitcast_add_fusion.13), channel_id=1, source_target_pairs={{0,32},{32,64},{64,96},{96,128},{128,160},{160,192},{192,224},{224... | collective-permute-start | bytes 983048 | tf_op jit(solution)/shard_map/ppermute | solution.py:41
  118.5 4.6 %collective-permute-done.14 = f32[2,64,640]{2,1,0:T(8,128)S(1)} collective-permute-done((f32[2,64,640]{2,1,0:T(8,128)S(1)}, f32[2,64,640]{2,1,0:T(8,128)S(1)}, u32[]{:S(2)}, u32[]{:S(2)}) %collective-permute-start.14) | collective-permute-done | bytes 327712 | tf_op jit(solution)/shard_map/ppermute | solution.py:41
  123.2 3.8 %collective-permute-start.15 = (f32[2,64,640]{2,1,0:T(8,128)S(1)}, f32[2,64,640]{2,1,0:T(8,128)S(1)}, u32[]{:S(2)}, u32[]{:S(2)}) collective-permute-start(f32[2,64,640]{2,1,0:T(8,128)S(1)} %bitcast_add_fusion.12), channel_id=1, source_target_pairs={{0,32},{32,64},{64,96},{96,128},{128,160},{160,192},{192,224},{224... | collective-permute-start | bytes 983048 | tf_op jit(solution)/shard_map/ppermute | solution.py:41
  127.1 4.6 %collective-permute-done.15 = f32[2,64,640]{2,1,0:T(8,128)S(1)} collective-permute-done((f32[2,64,640]{2,1,0:T(8,128)S(1)}, f32[2,64,640]{2,1,0:T(8,128)S(1)}, u32[]{:S(2)}, u32[]{:S(2)}) %collective-permute-start.15) | collective-permute-done | bytes 327712 | tf_op jit(solution)/shard_map/ppermute | solution.py:41
  131.7 3.8 %collective-permute-start.16 = (f32[2,64,640]{2,1,0:T(8,128)S(1)}, f32[2,64,640]{2,1,0:T(8,128)S(1)}, u32[]{:S(2)}, u32[]{:S(2)}) collective-permute-start(f32[2,64,640]{2,1,0:T(8,128)S(1)} %bitcast_add_fusion.11), channel_id=1, source_target_pairs={{0,32},{32,64},{64,96},{96,128},{128,160},{160,192},{192,224},{224... | collective-permute-start | bytes 983048 | tf_op jit(solution)/shard_map/ppermute | solution.py:41
  136.0 5.4 %collective-permute-done.16 = f32[2,64,640]{2,1,0:T(8,128)S(1)} collective-permute-done((f32[2,64,640]{2,1,0:T(8,128)S(1)}, f32[2,64,640]{2,1,0:T(8,128)S(1)}, u32[]{:S(2)}, u32[]{:S(2)}) %collective-permute-start.16) | collective-permute-done | bytes 327712 | tf_op jit(solution)/shard_map/ppermute | solution.py:41
  141.4 3.8 %collective-permute-start.17 = (f32[2,64,640]{2,1,0:T(8,128)S(1)}, f32[2,64,640]{2,1,0:T(8,128)S(1)}, u32[]{:S(2)}, u32[]{:S(2)}) collective-permute-start(f32[2,64,640]{2,1,0:T(8,128)S(1)} %bitcast_add_fusion.10), channel_id=1, source_target_pairs={{0,32},{32,64},{64,96},{96,128},{128,160},{160,192},{192,224},{224... | collective-permute-start | bytes 983048 | tf_op jit(solution)/shard_map/ppermute | solution.py:41
  146.0 6.2 %collective-permute-done.17 = f32[2,64,640]{2,1,0:T(8,128)S(1)} collective-permute-done((f32[2,64,640]{2,1,0:T(8,128)S(1)}, f32[2,64,640]{2,1,0:T(8,128)S(1)}, u32[]{:S(2)}, u32[]{:S(2)}) %collective-permute-start.17) | collective-permute-done | bytes 327712 | tf_op jit(solution)/shard_map/ppermute | solution.py:41
  152.3 3.8 %collective-permute-start.18 = (f32[2,64,640]{2,1,0:T(8,128)S(1)}, f32[2,64,640]{2,1,0:T(8,128)S(1)}, u32[]{:S(2)}, u32[]{:S(2)}) collective-permute-start(f32[2,64,640]{2,1,0:T(8,128)S(1)} %bitcast_add_fusion.9), channel_id=1, source_target_pairs={{0,32},{32,64},{64,96},{96,128},{128,160},{160,192},{192,224},{224... | collective-permute-start | bytes 983048 | tf_op jit(solution)/shard_map/ppermute | solution.py:41
  156.1 0.8 collective-permute-done.24
  157.1 3.6 %collective-permute-done.18 = f32[2,64,640]{2,1,0:T(8,128)S(1)} collective-permute-done((f32[2,64,640]{2,1,0:T(8,128)S(1)}, f32[2,64,640]{2,1,0:T(8,128)S(1)}, u32[]{:S(2)}, u32[]{:S(2)}) %collective-permute-start.18) | collective-permute-done | bytes 327712 | tf_op jit(solution)/shard_map/ppermute | solution.py:41
  160.7 4.6 %collective-permute-done.25 = f32[2,64,640]{2,1,0:T(8,128)S(1)} collective-permute-done((f32[2,64,640]{2,1,0:T(8,128)S(1)}, f32[2,64,640]{2,1,0:T(8,128)S(1)}, u32[]{:S(2)}, u32[]{:S(2)}) %collective-permute-start.25) | collective-permute-done | bytes 327712 | tf_op jit(solution)/shard_map/ppermute | solution.py:41
  165.4 2.9 %collective-permute-start.26 = (f32[64,1280]{1,0:T(8,128)S(1)}, f32[64,1280]{1,0:T(8,128)}, u32[]{:S(2)}, u32[]{:S(2)}) collective-permute-start(f32[64,1280]{1,0:T(8,128)S(1)} %fusion.29), channel_id=1, source_target_pairs={{0,16},{16,0},{1,17},{17,1},{2,18},{18,2},{3,19},{19,3},{4,20},{20... | collective-permute-start | bytes 983048 | tf_op jit(solution)/shard_map/ppermute | solution.py:53
  168.4 1.1 pad_maximum_fusion.7
  169.7 1.7 add_convert_fusion
  171.4 2.8 %collective-permute-done.26 = f32[64,1280]{1,0:T(8,128)} collective-permute-done((f32[64,1280]{1,0:T(8,128)S(1)}, f32[64,1280]{1,0:T(8,128)}, u32[]{:S(2)}, u32[]{:S(2)}) %collective-permute-start.26) | collective-permute-done | bytes 327712 | tf_op jit(solution)/shard_map/ppermute | solution.py:53
  174.2 1.0 fusion.32
  (92 shorter events, 7.2 us)
Async XLA Ops:
  7.2 17.7 %copy-start = (bf16[256,2048]{1,0:T(8,128)(2,1)S(1)}, bf16[256,2048]{1,0:T(8,128)(2,1)}, u32[]{:S(2)}) copy-start(bf16[256,2048]{1,0:T(8,128)(2,1)} %param.8) | copy-start | bytes 3145732
  7.2 161.2 %reduce-scatter.2.cloned.1.call-start = ((), (), s32[]{:S(2)}) async-start(), calls=%async_computation.1 | async-start | bytes 2359296 | tf_op jit(solution)/shard_map/reduce_scatter | solution.py:120
  7.2 4.0 %copy-start.9 = (bf16[2,256,2048]{2,1,0:T(8,128)(2,1)S(1)}, bf16[2,256,2048]{2,1,0:T(8,128)(2,1)}, u32[]{:S(2)}) copy-start(bf16[2,256,2048]{2,1,0:T(8,128)(2,1)} %param.5) | copy-start | bytes 6291460
  11.2 10.4 %copy-start.8 = (s32[2]{0:T(128)S(1)}, s32[2]{0:T(128)}, u32[]{:S(2)}) copy-start(s32[2]{0:T(128)} %param.9) | copy-start | bytes 28
  13.6 17.6 %collective-permute-start = (f32[256,512]{0,1:T(8,128)}, f32[256,512]{0,1:T(8,128)}, u32[]{:S(2)}, u32[]{:S(2)}) collective-permute-start(f32[256,512]{0,1:T(8,128)} %get-tuple-element.17), channel_id=1, source_target_pairs={{0,32},{8,40},{16,48},{24,56},{32,64},{40,72},{48,80},{56,88},{64,... | collective-permute-start | bytes 1572872 | tf_op jit(solution)/shard_map/ppermute | solution.py:16
  18.7 22.7 %collective-permute-start.1 = (f32[256,512]{0,1:T(8,128)}, f32[256,512]{0,1:T(8,128)}, u32[]{:S(2)}, u32[]{:S(2)}) collective-permute-start(f32[256,512]{0,1:T(8,128)} %get-tuple-element.18), channel_id=1, source_target_pairs={{0,32},{8,40},{16,48},{24,56},{32,64},{40,72},{48,80},{56,88},{64,... | collective-permute-start | bytes 1572872 | tf_op jit(solution)/shard_map/ppermute | solution.py:16
  23.5 1.4 copy-start.3
  30.0 12.8 %copy-start.7 = (f32[512,256]{0,1:T(8,128)S(1)}, f32[512,256]{0,1:T(8,128)}, u32[]{:S(2)}) copy-start(f32[512,256]{0,1:T(8,128)} %fusion.49) | copy-start | bytes 1572868
  42.8 17.4 %copy-start.4 = (bf16[2,256,2048]{2,1,0:T(8,128)(2,1)S(1)}, bf16[2,256,2048]{2,1,0:T(8,128)(2,1)}, u32[]{:S(2)}) copy-start(bf16[2,256,2048]{2,1,0:T(8,128)(2,1)} %copy-done.3) | copy-start | bytes 6291460
  42.8 17.4 %copy-start.10 = (bf16[2,256,2048]{2,1,0:T(8,128)(2,1)S(1)}, bf16[2,256,2048]{2,1,0:T(8,128)(2,1)}, u32[]{:S(2)}) copy-start(bf16[2,256,2048]{2,1,0:T(8,128)(2,1)} %param.5) | copy-start | bytes 6291460
  43.1 22.9 %copy-start.5 = (bf16[256,256]{0,1:T(8,128)(2,1)}, bf16[256,256]{0,1:T(8,128)(2,1)S(1)}, u32[]{:S(2)}) copy-start(bf16[256,256]{0,1:T(8,128)(2,1)S(1)} %get-tuple-element.23) | copy-start | bytes 393220
  43.2 13.0 %collective-permute-start.2 = (bf16[256,512]{0,1:T(8,128)(2,1)S(1)}, bf16[256,512]{0,1:T(8,128)(2,1)S(1)}, u32[]{:S(2)}, u32[]{:S(2)}) collective-permute-start(bf16[256,512]{0,1:T(8,128)(2,1)S(1)} %pad_maximum_fusion.8), channel_id=1, source_target_pairs={{32,0},{40,8},{48,16},{56,24},{64,32},{72,40},{80,48},{88,56},{96,... | collective-permute-start | bytes 786440 | tf_op jit(solution)/shard_map/ppermute | solution.py:16
  45.4 14.7 %collective-permute-start.3 = (bf16[256,512]{0,1:T(8,128)(2,1)S(1)}, bf16[256,512]{0,1:T(8,128)(2,1)S(1)}, u32[]{:S(2)}, u32[]{:S(2)}) collective-permute-start(bf16[256,512]{0,1:T(8,128)(2,1)S(1)} %pad_maximum_fusion.9), channel_id=1, source_target_pairs={{32,0},{40,8},{48,16},{56,24},{64,32},{72,40},{80,48},{88,56},{96,... | collective-permute-start | bytes 786440 | tf_op jit(solution)/shard_map/ppermute | solution.py:16
  66.1 5.7 %copy-start.2 = (f32[2048,1280]{1,0:T(8,128)}, f32[2048,1280]{1,0:T(8,128)S(1)}, u32[]{:S(2)}) copy-start(f32[2048,1280]{1,0:T(8,128)S(1)} %fusion) | copy-start | bytes 31457284
  66.1 5.7 %copy-start.6 = (bf16[256,256]{0,1:T(8,128)(2,1)S(1)}, bf16[256,256]{0,1:T(8,128)(2,1)}, u32[]{:S(2)}) copy-start(bf16[256,256]{0,1:T(8,128)(2,1)} %copy-done.5) | copy-start | bytes 393220
  71.7 19.2 %collective-permute-start.11 = (f32[8,2,64,1280]{3,2,1,0:T(8,128)}, f32[8,2,64,1280]{3,2,1,0:T(8,128)}, u32[]{:S(2)}, u32[]{:S(2)}) collective-permute-start(f32[8,2,64,1280]{3,2,1,0:T(8,128)} %dynamic-slice_bitcast_fusion), channel_id=1, source_target_pairs={{0,8},{8,0},{1,9},{9,1},{2,10},{10,2},{3,11},{11,3},{4,12},{12,4},... | collective-permute-start | bytes 15728648 | tf_op jit(solution)/shard_map/ppermute | solution.py:53
  77.7 9.3 %collective-permute-start.7 = (f32[512,128]{1,0:T(8,128)S(1)}, f32[512,128]{1,0:T(8,128)S(1)}, u32[]{:S(2)}, u32[]{:S(2)}) collective-permute-start(f32[512,128]{1,0:T(8,128)S(1)} %dynamic-slice_bitcast_fusion.4), channel_id=1, source_target_pairs={{0,6},{2,0},{4,2},{6,4},{1,7},{3,1},{5,3},{7,5},{8,14},{10,8},{12,... | collective-permute-start | bytes 786440 | tf_op jit(solution)/shard_map/ppermute | solution.py:67
  80.8 10.0 %collective-permute-start.4 = (f32[512,128]{1,0:T(8,128)S(1)}, f32[512,128]{1,0:T(8,128)S(1)}, u32[]{:S(2)}, u32[]{:S(2)}) collective-permute-start(f32[512,128]{1,0:T(8,128)S(1)} %dynamic-slice_bitcast_fusion.5), channel_id=1, source_target_pairs={{0,2},{2,4},{4,6},{6,0},{1,3},{3,5},{5,7},{7,1},{8,10},{10,12},{12... | collective-permute-start | bytes 786440 | tf_op jit(solution)/shard_map/ppermute | solution.py:67
  87.1 11.8 %collective-permute-start.8 = (f32[512,128]{1,0:T(8,128)S(1)}, f32[512,128]{1,0:T(8,128)S(1)}, u32[]{:S(2)}, u32[]{:S(2)}) collective-permute-start(f32[512,128]{1,0:T(8,128)S(1)} %bitcast_add_fusion.18), channel_id=1, source_target_pairs={{0,6},{2,0},{4,2},{6,4},{1,7},{3,1},{5,3},{7,5},{8,14},{10,8},{12,... | collective-permute-start | bytes 786440 | tf_op jit(solution)/shard_map/ppermute | solution.py:67
  90.9 17.9 %collective-permute-start.5 = (f32[512,128]{1,0:T(8,128)S(1)}, f32[512,128]{1,0:T(8,128)S(1)}, u32[]{:S(2)}, u32[]{:S(2)}) collective-permute-start(f32[512,128]{1,0:T(8,128)S(1)} %bitcast_add_fusion.21), channel_id=1, source_target_pairs={{0,2},{2,4},{4,6},{6,0},{1,3},{3,5},{5,7},{7,1},{8,10},{10,12},{12... | collective-permute-start | bytes 786440 | tf_op jit(solution)/shard_map/ppermute | solution.py:67
  96.7 8.9 %collective-permute-start.12 = (f32[2,64,640]{2,1,0:T(8,128)S(1)}, f32[2,64,640]{2,1,0:T(8,128)S(1)}, u32[]{:S(2)}, u32[]{:S(2)}) collective-permute-start(f32[2,64,640]{2,1,0:T(8,128)S(1)} %dynamic-slice_bitcast_fusion.2), channel_id=1, source_target_pairs={{0,32},{32,64},{64,96},{96,128},{128,160},{160,192},{192,224},{224... | collective-permute-start | bytes 983048 | tf_op jit(solution)/shard_map/ppermute | solution.py:41
  98.3 10.3 %collective-permute-start.19 = (f32[2,64,640]{2,1,0:T(8,128)S(1)}, f32[2,64,640]{2,1,0:T(8,128)S(1)}, u32[]{:S(2)}, u32[]{:S(2)}) collective-permute-start(f32[2,64,640]{2,1,0:T(8,128)S(1)} %dynamic-slice_bitcast_fusion.1), channel_id=1, source_target_pairs={{0,224},{32,0},{64,32},{96,64},{128,96},{160,128},{192,160},{224,1... | collective-permute-start | bytes 983048 | tf_op jit(solution)/shard_map/ppermute | solution.py:41
  98.9 19.5 %collective-permute-start.9 = (f32[512,128]{1,0:T(8,128)S(1)}, f32[512,128]{1,0:T(8,128)S(1)}, u32[]{:S(2)}, u32[]{:S(2)}) collective-permute-start(f32[512,128]{1,0:T(8,128)S(1)} %bitcast_add_fusion.17), channel_id=1, source_target_pairs={{0,6},{2,0},{4,2},{6,4},{1,7},{3,1},{5,3},{7,5},{8,14},{10,8},{12,... | collective-permute-start | bytes 786440 | tf_op jit(solution)/shard_map/ppermute | solution.py:67
  105.6 8.7 %collective-permute-start.13 = (f32[2,64,640]{2,1,0:T(8,128)S(1)}, f32[2,64,640]{2,1,0:T(8,128)S(1)}, u32[]{:S(2)}, u32[]{:S(2)}) collective-permute-start(f32[2,64,640]{2,1,0:T(8,128)S(1)} %bitcast_add_fusion.14), channel_id=1, source_target_pairs={{0,32},{32,64},{64,96},{96,128},{128,160},{160,192},{192,224},{224... | collective-permute-start | bytes 983048 | tf_op jit(solution)/shard_map/ppermute | solution.py:41
  108.7 9.6 %collective-permute-start.20 = (f32[2,64,640]{2,1,0:T(8,128)S(1)}, f32[2,64,640]{2,1,0:T(8,128)S(1)}, u32[]{:S(2)}, u32[]{:S(2)}) collective-permute-start(f32[2,64,640]{2,1,0:T(8,128)S(1)} %bitcast_add_fusion.7), channel_id=1, source_target_pairs={{0,224},{32,0},{64,32},{96,64},{128,96},{160,128},{192,160},{224,1... | collective-permute-start | bytes 983048 | tf_op jit(solution)/shard_map/ppermute | solution.py:41
  108.8 18.2 %collective-permute-start.6 = (f32[512,128]{1,0:T(8,128)S(1)}, f32[512,128]{1,0:T(8,128)S(1)}, u32[]{:S(2)}, u32[]{:S(2)}) collective-permute-start(f32[512,128]{1,0:T(8,128)S(1)} %bitcast_add_fusion.20), channel_id=1, source_target_pairs={{0,2},{2,4},{4,6},{6,0},{1,3},{3,5},{5,7},{7,1},{8,10},{10,12},{12... | collective-permute-start | bytes 786440 | tf_op jit(solution)/shard_map/ppermute | solution.py:67
  114.3 8.8 %collective-permute-start.14 = (f32[2,64,640]{2,1,0:T(8,128)S(1)}, f32[2,64,640]{2,1,0:T(8,128)S(1)}, u32[]{:S(2)}, u32[]{:S(2)}) collective-permute-start(f32[2,64,640]{2,1,0:T(8,128)S(1)} %bitcast_add_fusion.13), channel_id=1, source_target_pairs={{0,32},{32,64},{64,96},{96,128},{128,160},{160,192},{192,224},{224... | collective-permute-start | bytes 983048 | tf_op jit(solution)/shard_map/ppermute | solution.py:41
  118.4 8.6 %collective-permute-start.21 = (f32[2,64,640]{2,1,0:T(8,128)S(1)}, f32[2,64,640]{2,1,0:T(8,128)S(1)}, u32[]{:S(2)}, u32[]{:S(2)}) collective-permute-start(f32[2,64,640]{2,1,0:T(8,128)S(1)} %bitcast_add_fusion.6), channel_id=1, source_target_pairs={{0,224},{32,0},{64,32},{96,64},{128,96},{160,128},{192,160},{224,1... | collective-permute-start | bytes 983048 | tf_op jit(solution)/shard_map/ppermute | solution.py:41
  123.2 8.5 %collective-permute-start.15 = (f32[2,64,640]{2,1,0:T(8,128)S(1)}, f32[2,64,640]{2,1,0:T(8,128)S(1)}, u32[]{:S(2)}, u32[]{:S(2)}) collective-permute-start(f32[2,64,640]{2,1,0:T(8,128)S(1)} %bitcast_add_fusion.12), channel_id=1, source_target_pairs={{0,32},{32,64},{64,96},{96,128},{128,160},{160,192},{192,224},{224... | collective-permute-start | bytes 983048 | tf_op jit(solution)/shard_map/ppermute | solution.py:41
  127.0 8.8 %collective-permute-start.22 = (f32[2,64,640]{2,1,0:T(8,128)S(1)}, f32[2,64,640]{2,1,0:T(8,128)S(1)}, u32[]{:S(2)}, u32[]{:S(2)}) collective-permute-start(f32[2,64,640]{2,1,0:T(8,128)S(1)} %bitcast_add_fusion.5), channel_id=1, source_target_pairs={{0,224},{32,0},{64,32},{96,64},{128,96},{160,128},{192,160},{224,1... | collective-permute-start | bytes 983048 | tf_op jit(solution)/shard_map/ppermute | solution.py:41
  131.7 9.7 %collective-permute-start.16 = (f32[2,64,640]{2,1,0:T(8,128)S(1)}, f32[2,64,640]{2,1,0:T(8,128)S(1)}, u32[]{:S(2)}, u32[]{:S(2)}) collective-permute-start(f32[2,64,640]{2,1,0:T(8,128)S(1)} %bitcast_add_fusion.11), channel_id=1, source_target_pairs={{0,32},{32,64},{64,96},{96,128},{128,160},{160,192},{192,224},{224... | collective-permute-start | bytes 983048 | tf_op jit(solution)/shard_map/ppermute | solution.py:41
  135.8 10.0 %collective-permute-start.23 = (f32[2,64,640]{2,1,0:T(8,128)S(1)}, f32[2,64,640]{2,1,0:T(8,128)S(1)}, u32[]{:S(2)}, u32[]{:S(2)}) collective-permute-start(f32[2,64,640]{2,1,0:T(8,128)S(1)} %bitcast_add_fusion.4), channel_id=1, source_target_pairs={{0,224},{32,0},{64,32},{96,64},{128,96},{160,128},{192,160},{224,1... | collective-permute-start | bytes 983048 | tf_op jit(solution)/shard_map/ppermute | solution.py:41
  141.4 10.8 %collective-permute-start.17 = (f32[2,64,640]{2,1,0:T(8,128)S(1)}, f32[2,64,640]{2,1,0:T(8,128)S(1)}, u32[]{:S(2)}, u32[]{:S(2)}) collective-permute-start(f32[2,64,640]{2,1,0:T(8,128)S(1)} %bitcast_add_fusion.10), channel_id=1, source_target_pairs={{0,32},{32,64},{64,96},{96,128},{128,160},{160,192},{192,224},{224... | collective-permute-start | bytes 983048 | tf_op jit(solution)/shard_map/ppermute | solution.py:41
  145.8 11.1 %collective-permute-start.24 = (f32[2,64,640]{2,1,0:T(8,128)S(1)}, f32[2,64,640]{2,1,0:T(8,128)S(1)}, u32[]{:S(2)}, u32[]{:S(2)}) collective-permute-start(f32[2,64,640]{2,1,0:T(8,128)S(1)} %bitcast_add_fusion.3), channel_id=1, source_target_pairs={{0,224},{32,0},{64,32},{96,64},{128,96},{160,128},{192,160},{224,1... | collective-permute-start | bytes 983048 | tf_op jit(solution)/shard_map/ppermute | solution.py:41
  145.9 11.1 %collective-permute-start.10 = (f32[256,256]{1,0:T(8,128)S(1)}, f32[256,256]{1,0:T(8,128)S(1)}, u32[]{:S(2)}, u32[]{:S(2)}) collective-permute-start(f32[256,256]{1,0:T(8,128)S(1)} %dynamic-slice_bitcast_fusion.3), channel_id=1, source_target_pairs={{0,1},{1,0},{2,3},{3,2},{4,5},{5,4},{6,7},{7,6},{8,9},{9,8},{10,11... | collective-permute-start | bytes 786440 | tf_op jit(solution)/shard_map/ppermute | solution.py:53
  152.3 8.4 %collective-permute-start.18 = (f32[2,64,640]{2,1,0:T(8,128)S(1)}, f32[2,64,640]{2,1,0:T(8,128)S(1)}, u32[]{:S(2)}, u32[]{:S(2)}) collective-permute-start(f32[2,64,640]{2,1,0:T(8,128)S(1)} %bitcast_add_fusion.9), channel_id=1, source_target_pairs={{0,32},{32,64},{64,96},{96,128},{128,160},{160,192},{192,224},{224... | collective-permute-start | bytes 983048 | tf_op jit(solution)/shard_map/ppermute | solution.py:41
  157.0 8.4 %collective-permute-start.25 = (f32[2,64,640]{2,1,0:T(8,128)S(1)}, f32[2,64,640]{2,1,0:T(8,128)S(1)}, u32[]{:S(2)}, u32[]{:S(2)}) collective-permute-start(f32[2,64,640]{2,1,0:T(8,128)S(1)} %bitcast_add_fusion.2), channel_id=1, source_target_pairs={{0,224},{32,0},{64,32},{96,64},{128,96},{160,128},{192,160},{224,1... | collective-permute-start | bytes 983048 | tf_op jit(solution)/shard_map/ppermute | solution.py:41
  165.4 8.8 %collective-permute-start.26 = (f32[64,1280]{1,0:T(8,128)S(1)}, f32[64,1280]{1,0:T(8,128)}, u32[]{:S(2)}, u32[]{:S(2)}) collective-permute-start(f32[64,1280]{1,0:T(8,128)S(1)} %fusion.29), channel_id=1, source_target_pairs={{0,16},{16,0},{1,17},{17,1},{2,18},{18,2},{3,19},{19,3},{4,20},{20... | collective-permute-start | bytes 983048 | tf_op jit(solution)/shard_map/ppermute | solution.py:53
  168.4 8.5 %copy-start.1 = (bf16[256,2048]{1,0:T(8,128)(2,1)S(1)}, bf16[256,2048]{1,0:T(8,128)(2,1)}, u32[]{:S(2)}) copy-start(bf16[256,2048]{1,0:T(8,128)(2,1)} %param.8) | copy-start | bytes 3145732
Sparse Core Ops, SparseCore 0:
  82.5 53.7 reduce-scatter.1

commit v13 on v12

--- a/solution.py
+++ b/solution.py
@@ -98,8 +98,9 @@
     grad_flat = grad_rows.reshape(rows_n, width)
     dmix = contract_cols(grad_flat, w_out)
     mixed_parts, grad_parts, later_parts = [], [], []
-    for b in range(traj):
-        rows_b = slice(b * window_extent, (b + 1) * window_extent)
+    piece = window_extent // 2
+    for b in range(rows_n // piece):
+        rows_b = slice(b * piece, (b + 1) * piece)
         pre = present[rows_b] + shifted(dilated[rows_b], TIME, receptive_extent)
         tangent = jnp.tanh(pre[:, :blocks])
         sigma = jax.nn.sigmoid(pre[:, blocks:])

time: 186 us -> 186 us (level)
  starting transfers between devices: 50.3 us -> 60.4 us
  waiting for transfers between devices: 71 us -> 61.5 us
    ppermute x4 -> x8, starting transfers between devices: 12.1 us -> 21.8 us  [shifted(): return lax.ppermute(x, axis, pairs)]
    ppermute x4 -> x8, waiting for transfers between devices: 24.1 us -> 14.7 us  [shifted(): return lax.ppermute(x, axis, pairs)]
    unnamed x23 -> x35, local copies, waits for them, and re-layouts: 4.11 us -> 2.92 us
  transfers between devices with their start and end apart: 28 -> 32, of which waited for: 17 -> 19; matrix products, arithmetic and copies ran while one was open for 13% -> 13% of each run, Pallas kernels for 0% -> 0%
where the time goes in v13:
time: 186 us; the launch traced here: 184 us
  waiting for transfers between devices  61.5 us (33%)
  starting transfers between devices  60.4 us (32%)
  other arithmetic  16.2 us (9%)
  matrix products  15.6 us (8%)
  between operations  15.5 us (8%)
  local copies, waits for them, and re-layouts  14.6 us (8%)
    ppermute x14, waiting for transfers between devices, ring_sum(): got = lax.ppermute(acc, axis, pairs)  39.3 us
    ppermute x14, starting transfers between devices, ring_sum(): got = lax.ppermute(acc, axis, pairs)  25 us
    ppermute x8, starting transfers between devices, shifted(): return lax.ppermute(x, axis, pairs)  21.8 us
    ppermute x8, waiting for transfers between devices, shifted(): return lax.ppermute(x, axis, pairs)  14.7 us
    ppermute x6, starting transfers between devices, chan_ring_reduce_scatter(): got = lax.ppermute(acc, 'cy', pairs)  10.4 us
    dot_general x3, matrix products, contract_cols(): lax.dot_general(left, right, (((1,), (1,)), ((), ())), preferred_element_...  6.21 us
    add x3, other arithmetic, swap_sum(): return keep + lax.ppermute(give, axis, [(0, 1), (1, 0)])  5.99 us
    dot_general x1, matrix products, contract_rows(): lax.dot_general(left, right, (((0,), (0,)), ((), ())), preferred_element_...  5.74 us
  transfers between devices with their start and end apart: 32, of which 19 were waited for; matrix products, arithmetic and copies ran while one was open for 13% of the time, Pallas kernels for 0%

profile of v13, /device:TPU:98, one launch (start us, length us, event | category | flops | bytes accessed | tf_op | source)
XLA Modules:
  0.0 183.7 jit_solution(6975092123531663727)
XLA Ops:
  7.2 4.0 %slice_bitcast_fusion.1 = (bf16[2048,256]{1,0:T(8,128)(2,1)S(1)}, bf16[2048,256]{1,0:T(8,128)(2,1)}, bf16[2048,256]{1,0:T(8,128)(2,1)}, bf16[2048,256]{1,0:T(8,128)(2,1)S(1)}) fusion(bf16[2,2,2048,256]{3,2,1,0:T(8,128)(2,1)} %param.7), kind=kLoop, calls=%fused_computation.43 | loop fusion | bytes 8388608 | tf_op jit(solution)/shard_map/squeeze | solution.py:91
  11.2 1.3 convolution_bitcast_fusion
  13.5 5.0 %collective-permute-start = (f32[128,512]{0,1:T(8,128)}, f32[128,512]{0,1:T(8,128)S(1)}, u32[]{:S(2)}, u32[]{:S(2)}) collective-permute-start(f32[128,512]{0,1:T(8,128)} %get-tuple-element.17), channel_id=1, source_target_pairs={{0,32},{8,40},{16,48},{24,56},{32,64},{40,72},{48,80},{56,88},{64,... | collective-permute-start | bytes 786440 | tf_op jit(solution)/shard_map/ppermute | solution.py:16
  18.6 2.9 %collective-permute-start.3 = (f32[128,512]{0,1:T(8,128)}, f32[128,512]{0,1:T(8,128)}, u32[]{:S(2)}, u32[]{:S(2)}) collective-permute-start(f32[128,512]{0,1:T(8,128)} %get-tuple-element.18), channel_id=1, source_target_pairs={{0,32},{8,40},{16,48},{24,56},{32,64},{40,72},{48,80},{56,88},{64,... | collective-permute-start | bytes 786440 | tf_op jit(solution)/shard_map/ppermute | solution.py:16
  21.5 2.9 %collective-permute-start.2 = (f32[128,512]{0,1:T(8,128)}, f32[128,512]{0,1:T(8,128)}, u32[]{:S(2)}, u32[]{:S(2)}) collective-permute-start(f32[128,512]{0,1:T(8,128)} %get-tuple-element.19), channel_id=1, source_target_pairs={{0,32},{8,40},{16,48},{24,56},{32,64},{40,72},{48,80},{56,88},{64,... | collective-permute-start | bytes 786440 | tf_op jit(solution)/shard_map/ppermute | solution.py:16
  24.4 2.9 %collective-permute-start.1 = (f32[128,512]{0,1:T(8,128)}, f32[128,512]{0,1:T(8,128)}, u32[]{:S(2)}, u32[]{:S(2)}) collective-permute-start(f32[128,512]{0,1:T(8,128)} %get-tuple-element.20), channel_id=1, source_target_pairs={{0,32},{8,40},{16,48},{24,56},{32,64},{40,72},{48,80},{56,88},{64,... | collective-permute-start | bytes 786440 | tf_op jit(solution)/shard_map/ppermute | solution.py:16
  27.5 3.3 %broadcast_select_fusion = bf16[2,256,2048]{2,1,0:T(8,128)(2,1)} fusion(bf16[2,256,2048]{2,1,0:T(8,128)(2,1)} %param.6, pred[2,256]{1,0:T(4,128)(4,1)S(1)} %broadcast_compare_fusion), kind=kLoop, calls=%fused_computation.35 | loop fusion | flops 1048576 | bytes 4194816 | tf_op jit(solution)/shard_map/jit(_where)/select_n | solution.py:97
  30.8 2.3 %convolution_bitcast_fusion.1 = f32[512,512]{0,1:T(8,128)} fusion(bf16[512,2048]{1,0:T(8,128)(2,1)S(1)} %bitcast.102, bf16[2048,256]{1,0:T(8,128)(2,1)S(1)} %copy-done.5, bf16[2048,256]{1,0:T(8,128)(2,1)S(1)} %copy-done.7), kind=kOutput, calls=%fused_computation.37 | convolution fusion | flops 1077936128 | bytes 5242880 | tf_op jit(solution)/shard_map/dot_general | solution.py:93
  33.1 2.4 %fusion.75 = f32[512,256]{0,1:T(8,128)S(1)} fusion(bf16[512,2048]{1,0:T(8,128)(2,1)} %bitcast.95, bf16[256,2048]{1,0:T(8,128)(2,1)S(1)} %copy-done), kind=kOutput, calls=%fused_computation.159 | convolution fusion | flops 536870912 | bytes 3670016 | tf_op jit(solution)/shard_map/dot_general | solution.py:26
  36.8 4.5 %collective-permute-done.1 = f32[128,512]{0,1:T(8,128)} collective-permute-done((f32[128,512]{0,1:T(8,128)}, f32[128,512]{0,1:T(8,128)}, u32[]{:S(2)}, u32[]{:S(2)}) %collective-permute-start.1) | collective-permute-done | bytes 262176 | tf_op jit(solution)/shard_map/ppermute | solution.py:16
  41.3 1.2 slice_add_fusion.3
  43.1 2.2 %collective-permute-start.4 = (bf16[128,512]{0,1:T(8,128)(2,1)S(1)}, bf16[128,512]{0,1:T(8,128)(2,1)S(1)}, u32[]{:S(2)}, u32[]{:S(2)}) collective-permute-start(bf16[128,512]{0,1:T(8,128)(2,1)S(1)} %pad_maximum_fusion.8), channel_id=1, source_target_pairs={{32,0},{40,8},{48,16},{56,24},{64,32},{72,40},{80,48},{88,56},{96,... | collective-permute-start | bytes 393224 | tf_op jit(solution)/shard_map/ppermute | solution.py:16
  45.3 1.9 %collective-permute-start.5 = (bf16[128,512]{0,1:T(8,128)(2,1)S(1)}, bf16[128,512]{0,1:T(8,128)(2,1)S(1)}, u32[]{:S(2)}, u32[]{:S(2)}) collective-permute-start(bf16[128,512]{0,1:T(8,128)(2,1)S(1)} %pad_maximum_fusion.9), channel_id=1, source_target_pairs={{32,0},{40,8},{48,16},{56,24},{64,32},{72,40},{80,48},{88,56},{96,... | collective-permute-start | bytes 393224 | tf_op jit(solution)/shard_map/ppermute | solution.py:16
  47.3 1.9 %collective-permute-start.6 = (bf16[128,512]{0,1:T(8,128)(2,1)S(1)}, bf16[128,512]{0,1:T(8,128)(2,1)S(1)}, u32[]{:S(2)}, u32[]{:S(2)}) collective-permute-start(bf16[128,512]{0,1:T(8,128)(2,1)S(1)} %pad_maximum_fusion.10), channel_id=1, source_target_pairs={{32,0},{40,8},{48,16},{56,24},{64,32},{72,40},{80,48},{88,56},{96,... | collective-permute-start | bytes 393224 | tf_op jit(solution)/shard_map/ppermute | solution.py:16
  49.2 1.9 %collective-permute-start.7 = (bf16[128,512]{0,1:T(8,128)(2,1)S(1)}, bf16[128,512]{0,1:T(8,128)(2,1)S(1)}, u32[]{:S(2)}, u32[]{:S(2)}) collective-permute-start(bf16[128,512]{0,1:T(8,128)(2,1)S(1)} %pad_maximum_fusion.11), channel_id=1, source_target_pairs={{32,0},{40,8},{48,16},{56,24},{64,32},{72,40},{80,48},{88,56},{96,... | collective-permute-start | bytes 393224 | tf_op jit(solution)/shard_map/ppermute | solution.py:16
  51.2 1.8 %collective-permute-done.4 = bf16[128,512]{0,1:T(8,128)(2,1)S(1)} collective-permute-done((bf16[128,512]{0,1:T(8,128)(2,1)S(1)}, bf16[128,512]{0,1:T(8,128)(2,1)S(1)}, u32[]{:S(2)}, u32[]{:S(2)}) %collective-permute-start.4) | collective-permute-done | bytes 131104 | tf_op jit(solution)/shard_map/ppermute | solution.py:16
  53.1 2.8 %collective-permute-done.5 = bf16[128,512]{0,1:T(8,128)(2,1)S(1)} collective-permute-done((bf16[128,512]{0,1:T(8,128)(2,1)S(1)}, bf16[128,512]{0,1:T(8,128)(2,1)S(1)}, u32[]{:S(2)}, u32[]{:S(2)}) %collective-permute-start.5) | collective-permute-done | bytes 131104 | tf_op jit(solution)/shard_map/ppermute | solution.py:16
  55.9 2.8 %collective-permute-done.6 = bf16[128,512]{0,1:T(8,128)(2,1)S(1)} collective-permute-done((bf16[128,512]{0,1:T(8,128)(2,1)S(1)}, bf16[128,512]{0,1:T(8,128)(2,1)S(1)}, u32[]{:S(2)}, u32[]{:S(2)}) %collective-permute-start.6) | collective-permute-done | bytes 131104 | tf_op jit(solution)/shard_map/ppermute | solution.py:16
  58.7 1.6 collective-permute-done.7
  60.4 5.7 %fusion = f32[2048,1280]{1,0:T(8,128)S(1)} fusion(bf16[512,2048]{1,0:T(8,128)(2,1)S(1)} %bitcast.96, bf16[512,2048]{1,0:T(8,128)(2,1)S(1)} %bitcast.103, bf16[512,1280]{0,1:T(8,128)(2,1)S(1)} %fusion.32, bf16[512,256]{0,1:T(8,128)(2,1)S(1)} %broadcast_in_dim.19, bf16[512,512]{0,1:T(8,128)(2,1)S(1)} %constant_dynamic-update-slice_fusion, ...), kind=kOutput, calls=%fused_computation.2 | convolution fusion | flops 5405933568 | bytes 17301504 | tf_op jit(solution)/shard_map/dot_general | solution.py:20
  66.2 2.8 %dynamic-slice_bitcast_fusion = f32[8,2,64,1280]{3,2,1,0:T(8,128)} fusion(f32[8,2,2,64,1280]{4,3,2,1,0:T(8,128)S(1)} %bitcast.92, s32[]{:T(128)S(6)} %select_n.222), kind=kLoop, calls=%fused_computation.1 | loop fusion | bytes 10485764 | tf_op jit(solution)/shard_map/jit(dynamic_index_in_dim)/squeeze | solution.py:52
  69.1 2.8 %copy-done.2 = f32[2048,1280]{1,0:T(8,128)} copy-done((f32[2048,1280]{1,0:T(8,128)}, f32[2048,1280]{1,0:T(8,128)S(1)}, u32[]{:S(2)}) %copy-start.2) | copy-done | bytes 10485784
  71.8 2.5 %fusion.29 = f32[2048,512]{1,0:T(8,128)S(1)} fusion(bf16[2048,256]{1,0:T(8,128)(2,1)S(1)} %copy-done.6, bf16[2048,256]{1,0:T(8,128)(2,1)} %get-tuple-element.9, bf16[128,256]{0,1:T(8,128)(2,1)S(1)} %get-tuple-element.29, bf16[128,256]{0,1:T(8,128)(2,1)S(1)} %get-tuple-element.30, bf16[128,256]{0,1:T(8,128)(2,1)S(1)} %get-tuple-element.31, ...), kind=kOutput, calls=%fused_computation.38 | convolution fusion | flops 1082130432 | bytes 6815744 | tf_op jit(solution)/shard_map/dot_general | solution.py:26
  74.4 1.3 convolution_add_fusion
  75.6 1.7 fusion.72
  77.5 3.1 %collective-permute-start.11 = (f32[512,128]{1,0:T(8,128)S(1)}, f32[512,128]{1,0:T(8,128)S(1)}, u32[]{:S(2)}, u32[]{:S(2)}) collective-permute-start(f32[512,128]{1,0:T(8,128)S(1)} %dynamic-slice_bitcast_fusion.4), channel_id=1, source_target_pairs={{0,6},{2,0},{4,2},{6,4},{1,7},{3,1},{5,3},{7,5},{8,14},{10,8},{12,... | collective-permute-start | bytes 786440 | tf_op jit(solution)/shard_map/ppermute | solution.py:67
  82.2 4.7 %collective-permute-done.11 = f32[512,128]{1,0:T(8,128)S(1)} collective-permute-done((f32[512,128]{1,0:T(8,128)S(1)}, f32[512,128]{1,0:T(8,128)S(1)}, u32[]{:S(2)}, u32[]{:S(2)}) %collective-permute-start.11) | collective-permute-done | bytes 262176 | tf_op jit(solution)/shard_map/ppermute | solution.py:67
  86.9 3.8 %collective-permute-start.12 = (f32[512,128]{1,0:T(8,128)S(1)}, f32[512,128]{1,0:T(8,128)S(1)}, u32[]{:S(2)}, u32[]{:S(2)}) collective-permute-start(f32[512,128]{1,0:T(8,128)S(1)} %bitcast_add_fusion.18), channel_id=1, source_target_pairs={{0,6},{2,0},{4,2},{6,4},{1,7},{3,1},{5,3},{7,5},{8,14},{10,8},{12,... | collective-permute-start | bytes 786440 | tf_op jit(solution)/shard_map/ppermute | solution.py:67
  90.8 4.9 %bitcast_add_fusion = f32[8,2,64,1280]{3,2,1,0:T(8,128)S(1)} fusion(f32[8,2,64,1280]{3,2,1,0:T(8,128)} %collective-permute-done.15, f32[8,2,2,64,1280]{4,3,2,1,0:T(8,128)} %bitcast.93, s32[]{:T(128)S(6)} %select_n.221), kind=kLoop, calls=%fused_computation | loop fusion | flops 1310720 | bytes 15728644 | tf_op jit(solution)/shard_map/add | solution.py:53
  96.5 1.9 %collective-permute-start.16 = (f32[2,64,640]{2,1,0:T(8,128)S(1)}, f32[2,64,640]{2,1,0:T(8,128)S(1)}, u32[]{:S(2)}, u32[]{:S(2)}) collective-permute-start(f32[2,64,640]{2,1,0:T(8,128)S(1)} %dynamic-slice_bitcast_fusion.2), channel_id=1, source_target_pairs={{0,32},{32,64},{64,96},{96,128},{128,160},{160,192},{192,224},{224... | collective-permute-start | bytes 983048 | tf_op jit(solution)/shard_map/ppermute | solution.py:41
  98.7 3.3 %collective-permute-start.13 = (f32[512,128]{1,0:T(8,128)S(1)}, f32[512,128]{1,0:T(8,128)S(1)}, u32[]{:S(2)}, u32[]{:S(2)}) collective-permute-start(f32[512,128]{1,0:T(8,128)S(1)} %bitcast_add_fusion.17), channel_id=1, source_target_pairs={{0,6},{2,0},{4,2},{6,4},{1,7},{3,1},{5,3},{7,5},{8,14},{10,8},{12,... | collective-permute-start | bytes 786440 | tf_op jit(solution)/shard_map/ppermute | solution.py:67
  102.0 3.3 %collective-permute-done.16 = f32[2,64,640]{2,1,0:T(8,128)S(1)} collective-permute-done((f32[2,64,640]{2,1,0:T(8,128)S(1)}, f32[2,64,640]{2,1,0:T(8,128)S(1)}, u32[]{:S(2)}, u32[]{:S(2)}) %collective-permute-start.16) | collective-permute-done | bytes 327712 | tf_op jit(solution)/shard_map/ppermute | solution.py:41
  105.4 3.3 %collective-permute-start.17 = (f32[2,64,640]{2,1,0:T(8,128)S(1)}, f32[2,64,640]{2,1,0:T(8,128)S(1)}, u32[]{:S(2)}, u32[]{:S(2)}) collective-permute-start(f32[2,64,640]{2,1,0:T(8,128)S(1)} %bitcast_add_fusion.14), channel_id=1, source_target_pairs={{0,32},{32,64},{64,96},{96,128},{128,160},{160,192},{192,224},{224... | collective-permute-start | bytes 983048 | tf_op jit(solution)/shard_map/ppermute | solution.py:41
  109.0 5.4 %collective-permute-done.17 = f32[2,64,640]{2,1,0:T(8,128)S(1)} collective-permute-done((f32[2,64,640]{2,1,0:T(8,128)S(1)}, f32[2,64,640]{2,1,0:T(8,128)S(1)}, u32[]{:S(2)}, u32[]{:S(2)}) %collective-permute-start.17) | collective-permute-done | bytes 327712 | tf_op jit(solution)/shard_map/ppermute | solution.py:41
  114.4 4.0 %collective-permute-start.18 = (f32[2,64,640]{2,1,0:T(8,128)S(1)}, f32[2,64,640]{2,1,0:T(8,128)S(1)}, u32[]{:S(2)}, u32[]{:S(2)}) collective-permute-start(f32[2,64,640]{2,1,0:T(8,128)S(1)} %bitcast_add_fusion.13), channel_id=1, source_target_pairs={{0,32},{32,64},{64,96},{96,128},{128,160},{160,192},{192,224},{224... | collective-permute-start | bytes 983048 | tf_op jit(solution)/shard_map/ppermute | solution.py:41
  118.5 4.6 %collective-permute-done.18 = f32[2,64,640]{2,1,0:T(8,128)S(1)} collective-permute-done((f32[2,64,640]{2,1,0:T(8,128)S(1)}, f32[2,64,640]{2,1,0:T(8,128)S(1)}, u32[]{:S(2)}, u32[]{:S(2)}) %collective-permute-start.18) | collective-permute-done | bytes 327712 | tf_op jit(solution)/shard_map/ppermute | solution.py:41
  123.2 3.8 %collective-permute-start.19 = (f32[2,64,640]{2,1,0:T(8,128)S(1)}, f32[2,64,640]{2,1,0:T(8,128)S(1)}, u32[]{:S(2)}, u32[]{:S(2)}) collective-permute-start(f32[2,64,640]{2,1,0:T(8,128)S(1)} %bitcast_add_fusion.12), channel_id=1, source_target_pairs={{0,32},{32,64},{64,96},{96,128},{128,160},{160,192},{192,224},{224... | collective-permute-start | bytes 983048 | tf_op jit(solution)/shard_map/ppermute | solution.py:41
  127.1 4.6 %collective-permute-done.19 = f32[2,64,640]{2,1,0:T(8,128)S(1)} collective-permute-done((f32[2,64,640]{2,1,0:T(8,128)S(1)}, f32[2,64,640]{2,1,0:T(8,128)S(1)}, u32[]{:S(2)}, u32[]{:S(2)}) %collective-permute-start.19) | collective-permute-done | bytes 327712 | tf_op jit(solution)/shard_map/ppermute | solution.py:41
  131.8 3.8 %collective-permute-start.20 = (f32[2,64,640]{2,1,0:T(8,128)S(1)}, f32[2,64,640]{2,1,0:T(8,128)S(1)}, u32[]{:S(2)}, u32[]{:S(2)}) collective-permute-start(f32[2,64,640]{2,1,0:T(8,128)S(1)} %bitcast_add_fusion.11), channel_id=1, source_target_pairs={{0,32},{32,64},{64,96},{96,128},{128,160},{160,192},{192,224},{224... | collective-permute-start | bytes 983048 | tf_op jit(solution)/shard_map/ppermute | solution.py:41
  136.0 5.4 %collective-permute-done.20 = f32[2,64,640]{2,1,0:T(8,128)S(1)} collective-permute-done((f32[2,64,640]{2,1,0:T(8,128)S(1)}, f32[2,64,640]{2,1,0:T(8,128)S(1)}, u32[]{:S(2)}, u32[]{:S(2)}) %collective-permute-start.20) | collective-permute-done | bytes 327712 | tf_op jit(solution)/shard_map/ppermute | solution.py:41
  141.5 3.8 %collective-permute-start.21 = (f32[2,64,640]{2,1,0:T(8,128)S(1)}, f32[2,64,640]{2,1,0:T(8,128)S(1)}, u32[]{:S(2)}, u32[]{:S(2)}) collective-permute-start(f32[2,64,640]{2,1,0:T(8,128)S(1)} %bitcast_add_fusion.10), channel_id=1, source_target_pairs={{0,32},{32,64},{64,96},{96,128},{128,160},{160,192},{192,224},{224... | collective-permute-start | bytes 983048 | tf_op jit(solution)/shard_map/ppermute | solution.py:41
  146.2 6.1 %collective-permute-done.21 = f32[2,64,640]{2,1,0:T(8,128)S(1)} collective-permute-done((f32[2,64,640]{2,1,0:T(8,128)S(1)}, f32[2,64,640]{2,1,0:T(8,128)S(1)}, u32[]{:S(2)}, u32[]{:S(2)}) %collective-permute-start.21) | collective-permute-done | bytes 327712 | tf_op jit(solution)/shard_map/ppermute | solution.py:41
  152.4 3.8 %collective-permute-start.22 = (f32[2,64,640]{2,1,0:T(8,128)S(1)}, f32[2,64,640]{2,1,0:T(8,128)S(1)}, u32[]{:S(2)}, u32[]{:S(2)}) collective-permute-start(f32[2,64,640]{2,1,0:T(8,128)S(1)} %bitcast_add_fusion.9), channel_id=1, source_target_pairs={{0,32},{32,64},{64,96},{96,128},{128,160},{160,192},{192,224},{224... | collective-permute-start | bytes 983048 | tf_op jit(solution)/shard_map/ppermute | solution.py:41
  157.2 3.6 %collective-permute-done.22 = f32[2,64,640]{2,1,0:T(8,128)S(1)} collective-permute-done((f32[2,64,640]{2,1,0:T(8,128)S(1)}, f32[2,64,640]{2,1,0:T(8,128)S(1)}, u32[]{:S(2)}, u32[]{:S(2)}) %collective-permute-start.22) | collective-permute-done | bytes 327712 | tf_op jit(solution)/shard_map/ppermute | solution.py:41
  160.8 4.6 %collective-permute-done.29 = f32[2,64,640]{2,1,0:T(8,128)S(1)} collective-permute-done((f32[2,64,640]{2,1,0:T(8,128)S(1)}, f32[2,64,640]{2,1,0:T(8,128)S(1)}, u32[]{:S(2)}, u32[]{:S(2)}) %collective-permute-start.29) | collective-permute-done | bytes 327712 | tf_op jit(solution)/shard_map/ppermute | solution.py:41
  165.5 3.0 %collective-permute-start.30 = (f32[64,1280]{1,0:T(8,128)S(1)}, f32[64,1280]{1,0:T(8,128)}, u32[]{:S(2)}, u32[]{:S(2)}) collective-permute-start(f32[64,1280]{1,0:T(8,128)S(1)} %fusion.49), channel_id=1, source_target_pairs={{0,16},{16,0},{1,17},{17,1},{2,18},{18,2},{3,19},{19,3},{4,20},{20... | collective-permute-start | bytes 983048 | tf_op jit(solution)/shard_map/ppermute | solution.py:53
  169.7 1.7 add_convert_fusion
  171.5 2.8 %collective-permute-done.30 = f32[64,1280]{1,0:T(8,128)} collective-permute-done((f32[64,1280]{1,0:T(8,128)S(1)}, f32[64,1280]{1,0:T(8,128)}, u32[]{:S(2)}, u32[]{:S(2)}) %collective-permute-start.30) | collective-permute-done | bytes 327712 | tf_op jit(solution)/shard_map/ppermute | solution.py:53
  (117 shorter events, 12.5 us)
Async XLA Ops:
  7.2 26.0 %copy-start = (bf16[256,2048]{1,0:T(8,128)(2,1)S(1)}, bf16[256,2048]{1,0:T(8,128)(2,1)}, u32[]{:S(2)}) copy-start(bf16[256,2048]{1,0:T(8,128)(2,1)} %param.8) | copy-start | bytes 3145732
  7.2 161.2 %reduce-scatter.2.cloned.1.call-start = ((), (), s32[]{:S(2)}) async-start(), calls=%async_computation.1 | async-start | bytes 2359296 | tf_op jit(solution)/shard_map/reduce_scatter | solution.py:121
  7.2 4.0 %copy-start.13 = (bf16[2,256,2048]{2,1,0:T(8,128)(2,1)S(1)}, bf16[2,256,2048]{2,1,0:T(8,128)(2,1)}, u32[]{:S(2)}) copy-start(bf16[2,256,2048]{2,1,0:T(8,128)(2,1)} %param.5) | copy-start | bytes 6291460
  11.2 16.2 %copy-start.12 = (s32[2]{0:T(128)S(1)}, s32[2]{0:T(128)}, u32[]{:S(2)}) copy-start(s32[2]{0:T(128)} %param.9) | copy-start | bytes 28
  13.5 22.0 %collective-permute-start = (f32[128,512]{0,1:T(8,128)}, f32[128,512]{0,1:T(8,128)S(1)}, u32[]{:S(2)}, u32[]{:S(2)}) collective-permute-start(f32[128,512]{0,1:T(8,128)} %get-tuple-element.17), channel_id=1, source_target_pairs={{0,32},{8,40},{16,48},{24,56},{32,64},{40,72},{48,80},{56,88},{64,... | collective-permute-start | bytes 786440 | tf_op jit(solution)/shard_map/ppermute | solution.py:16
  18.6 17.0 %collective-permute-start.3 = (f32[128,512]{0,1:T(8,128)}, f32[128,512]{0,1:T(8,128)}, u32[]{:S(2)}, u32[]{:S(2)}) collective-permute-start(f32[128,512]{0,1:T(8,128)} %get-tuple-element.18), channel_id=1, source_target_pairs={{0,32},{8,40},{16,48},{24,56},{32,64},{40,72},{48,80},{56,88},{64,... | collective-permute-start | bytes 786440 | tf_op jit(solution)/shard_map/ppermute | solution.py:16
  21.5 15.3 %collective-permute-start.2 = (f32[128,512]{0,1:T(8,128)}, f32[128,512]{0,1:T(8,128)}, u32[]{:S(2)}, u32[]{:S(2)}) collective-permute-start(f32[128,512]{0,1:T(8,128)} %get-tuple-element.19), channel_id=1, source_target_pairs={{0,32},{8,40},{16,48},{24,56},{32,64},{40,72},{48,80},{56,88},{64,... | collective-permute-start | bytes 786440 | tf_op jit(solution)/shard_map/ppermute | solution.py:16
  24.4 16.8 %collective-permute-start.1 = (f32[128,512]{0,1:T(8,128)}, f32[128,512]{0,1:T(8,128)}, u32[]{:S(2)}, u32[]{:S(2)}) collective-permute-start(f32[128,512]{0,1:T(8,128)} %get-tuple-element.20), channel_id=1, source_target_pairs={{0,32},{8,40},{16,48},{24,56},{32,64},{40,72},{48,80},{56,88},{64,... | collective-permute-start | bytes 786440 | tf_op jit(solution)/shard_map/ppermute | solution.py:16
  27.4 3.4 %copy-start.5 = (bf16[2048,256]{1,0:T(8,128)(2,1)S(1)}, bf16[2048,256]{1,0:T(8,128)(2,1)}, u32[]{:S(2)}) copy-start(bf16[2048,256]{1,0:T(8,128)(2,1)} %get-tuple-element.8) | copy-start | bytes 3145732
  27.4 3.4 %copy-start.7 = (bf16[2048,256]{1,0:T(8,128)(2,1)S(1)}, bf16[2048,256]{1,0:T(8,128)(2,1)}, u32[]{:S(2)}) copy-start(bf16[2048,256]{1,0:T(8,128)(2,1)} %get-tuple-element.9) | copy-start | bytes 3145732
  27.4 3.4 %copy-start.14 = (bf16[2,256,2048]{2,1,0:T(8,128)(2,1)S(1)}, bf16[2,256,2048]{2,1,0:T(8,128)(2,1)}, u32[]{:S(2)}) copy-start(bf16[2,256,2048]{2,1,0:T(8,128)(2,1)} %param.5) | copy-start | bytes 6291460
  33.1 8.1 %copy-start.4 = (f32[512,512]{0,1:T(8,128)S(1)}, f32[512,512]{0,1:T(8,128)}, u32[]{:S(2)}) copy-start(f32[512,512]{0,1:T(8,128)} %convolution_bitcast_fusion.1) | copy-start | bytes 3145732
  42.9 17.5 %copy-start.3 = (bf16[2,256,2048]{2,1,0:T(8,128)(2,1)S(1)}, bf16[2,256,2048]{2,1,0:T(8,128)(2,1)}, u32[]{:S(2)}) copy-start(bf16[2,256,2048]{2,1,0:T(8,128)(2,1)} %broadcast_select_fusion) | copy-start | bytes 6291460
  42.9 17.5 %copy-start.15 = (bf16[2,256,2048]{2,1,0:T(8,128)(2,1)S(1)}, bf16[2,256,2048]{2,1,0:T(8,128)(2,1)}, u32[]{:S(2)}) copy-start(bf16[2,256,2048]{2,1,0:T(8,128)(2,1)} %param.5) | copy-start | bytes 6291460
  43.1 23.1 %copy-start.10 = (bf16[128,256]{0,1:T(8,128)(2,1)}, bf16[128,256]{0,1:T(8,128)(2,1)S(1)}, u32[]{:S(2)}) copy-start(bf16[128,256]{0,1:T(8,128)(2,1)S(1)} %get-tuple-element.23) | copy-start | bytes 196612
  43.1 23.1 %copy-start.11 = (bf16[128,256]{0,1:T(8,128)(2,1)}, bf16[128,256]{0,1:T(8,128)(2,1)S(1)}, u32[]{:S(2)}) copy-start(bf16[128,256]{0,1:T(8,128)(2,1)S(1)} %get-tuple-element.24) | copy-start | bytes 196612
  43.1 10.0 %collective-permute-start.4 = (bf16[128,512]{0,1:T(8,128)(2,1)S(1)}, bf16[128,512]{0,1:T(8,128)(2,1)S(1)}, u32[]{:S(2)}, u32[]{:S(2)}) collective-permute-start(bf16[128,512]{0,1:T(8,128)(2,1)S(1)} %pad_maximum_fusion.8), channel_id=1, source_target_pairs={{32,0},{40,8},{48,16},{56,24},{64,32},{72,40},{80,48},{88,56},{96,... | collective-permute-start | bytes 393224 | tf_op jit(solution)/shard_map/ppermute | solution.py:16
  45.3 10.6 %collective-permute-start.5 = (bf16[128,512]{0,1:T(8,128)(2,1)S(1)}, bf16[128,512]{0,1:T(8,128)(2,1)S(1)}, u32[]{:S(2)}, u32[]{:S(2)}) collective-permute-start(bf16[128,512]{0,1:T(8,128)(2,1)S(1)} %pad_maximum_fusion.9), channel_id=1, source_target_pairs={{32,0},{40,8},{48,16},{56,24},{64,32},{72,40},{80,48},{88,56},{96,... | collective-permute-start | bytes 393224 | tf_op jit(solution)/shard_map/ppermute | solution.py:16
  47.3 11.4 %collective-permute-start.6 = (bf16[128,512]{0,1:T(8,128)(2,1)S(1)}, bf16[128,512]{0,1:T(8,128)(2,1)S(1)}, u32[]{:S(2)}, u32[]{:S(2)}) collective-permute-start(bf16[128,512]{0,1:T(8,128)(2,1)S(1)} %pad_maximum_fusion.10), channel_id=1, source_target_pairs={{32,0},{40,8},{48,16},{56,24},{64,32},{72,40},{80,48},{88,56},{96,... | collective-permute-start | bytes 393224 | tf_op jit(solution)/shard_map/ppermute | solution.py:16
  49.2 11.1 %collective-permute-start.7 = (bf16[128,512]{0,1:T(8,128)(2,1)S(1)}, bf16[128,512]{0,1:T(8,128)(2,1)S(1)}, u32[]{:S(2)}, u32[]{:S(2)}) collective-permute-start(bf16[128,512]{0,1:T(8,128)(2,1)S(1)} %pad_maximum_fusion.11), channel_id=1, source_target_pairs={{32,0},{40,8},{48,16},{56,24},{64,32},{72,40},{80,48},{88,56},{96,... | collective-permute-start | bytes 393224 | tf_op jit(solution)/shard_map/ppermute | solution.py:16
  60.4 5.8 %copy-start.8 = (bf16[512,512]{0,1:T(8,128)(2,1)}, bf16[512,512]{0,1:T(8,128)(2,1)S(1)}, u32[]{:S(2)}) copy-start(bf16[512,512]{0,1:T(8,128)(2,1)S(1)} %constant_dynamic-update-slice_fusion) | copy-start | bytes 1572868
  66.2 5.6 %copy-start.2 = (f32[2048,1280]{1,0:T(8,128)}, f32[2048,1280]{1,0:T(8,128)S(1)}, u32[]{:S(2)}) copy-start(f32[2048,1280]{1,0:T(8,128)S(1)} %fusion) | copy-start | bytes 31457284
  66.2 5.6 %copy-start.6 = (bf16[2048,256]{1,0:T(8,128)(2,1)S(1)}, bf16[2048,256]{1,0:T(8,128)(2,1)}, u32[]{:S(2)}) copy-start(bf16[2048,256]{1,0:T(8,128)(2,1)} %get-tuple-element.8) | copy-start | bytes 3145732
  71.8 19.0 %collective-permute-start.15 = (f32[8,2,64,1280]{3,2,1,0:T(8,128)}, f32[8,2,64,1280]{3,2,1,0:T(8,128)}, u32[]{:S(2)}, u32[]{:S(2)}) collective-permute-start(f32[8,2,64,1280]{3,2,1,0:T(8,128)} %dynamic-slice_bitcast_fusion), channel_id=1, source_target_pairs={{0,8},{8,0},{1,9},{9,1},{2,10},{10,2},{3,11},{11,3},{4,12},{12,4},... | collective-permute-start | bytes 15728648 | tf_op jit(solution)/shard_map/ppermute | solution.py:53
  71.8 2.5 %copy-start.9 = (bf16[512,512]{0,1:T(8,128)(2,1)S(1)}, bf16[512,512]{0,1:T(8,128)(2,1)}, u32[]{:S(2)}) copy-start(bf16[512,512]{0,1:T(8,128)(2,1)} %copy-done.8) | copy-start | bytes 1572868
  77.5 9.3 %collective-permute-start.11 = (f32[512,128]{1,0:T(8,128)S(1)}, f32[512,128]{1,0:T(8,128)S(1)}, u32[]{:S(2)}, u32[]{:S(2)}) collective-permute-start(f32[512,128]{1,0:T(8,128)S(1)} %dynamic-slice_bitcast_fusion.4), channel_id=1, source_target_pairs={{0,6},{2,0},{4,2},{6,4},{1,7},{3,1},{5,3},{7,5},{8,14},{10,8},{12,... | collective-permute-start | bytes 786440 | tf_op jit(solution)/shard_map/ppermute | solution.py:67
  80.7 10.0 %collective-permute-start.8 = (f32[512,128]{1,0:T(8,128)S(1)}, f32[512,128]{1,0:T(8,128)S(1)}, u32[]{:S(2)}, u32[]{:S(2)}) collective-permute-start(f32[512,128]{1,0:T(8,128)S(1)} %dynamic-slice_bitcast_fusion.5), channel_id=1, source_target_pairs={{0,2},{2,4},{4,6},{6,0},{1,3},{3,5},{5,7},{7,1},{8,10},{10,12},{12... | collective-permute-start | bytes 786440 | tf_op jit(solution)/shard_map/ppermute | solution.py:67
  86.9 11.8 %collective-permute-start.12 = (f32[512,128]{1,0:T(8,128)S(1)}, f32[512,128]{1,0:T(8,128)S(1)}, u32[]{:S(2)}, u32[]{:S(2)}) collective-permute-start(f32[512,128]{1,0:T(8,128)S(1)} %bitcast_add_fusion.18), channel_id=1, source_target_pairs={{0,6},{2,0},{4,2},{6,4},{1,7},{3,1},{5,3},{7,5},{8,14},{10,8},{12,... | collective-permute-start | bytes 786440 | tf_op jit(solution)/shard_map/ppermute | solution.py:67
  90.7 18.1 %collective-permute-start.9 = (f32[512,128]{1,0:T(8,128)S(1)}, f32[512,128]{1,0:T(8,128)S(1)}, u32[]{:S(2)}, u32[]{:S(2)}) collective-permute-start(f32[512,128]{1,0:T(8,128)S(1)} %bitcast_add_fusion.21), channel_id=1, source_target_pairs={{0,2},{2,4},{4,6},{6,0},{1,3},{3,5},{5,7},{7,1},{8,10},{10,12},{12... | collective-permute-start | bytes 786440 | tf_op jit(solution)/shard_map/ppermute | solution.py:67
  96.5 8.9 %collective-permute-start.16 = (f32[2,64,640]{2,1,0:T(8,128)S(1)}, f32[2,64,640]{2,1,0:T(8,128)S(1)}, u32[]{:S(2)}, u32[]{:S(2)}) collective-permute-start(f32[2,64,640]{2,1,0:T(8,128)S(1)} %dynamic-slice_bitcast_fusion.2), channel_id=1, source_target_pairs={{0,32},{32,64},{64,96},{96,128},{128,160},{160,192},{192,224},{224... | collective-permute-start | bytes 983048 | tf_op jit(solution)/shard_map/ppermute | solution.py:41
  98.4 10.3 %collective-permute-start.23 = (f32[2,64,640]{2,1,0:T(8,128)S(1)}, f32[2,64,640]{2,1,0:T(8,128)S(1)}, u32[]{:S(2)}, u32[]{:S(2)}) collective-permute-start(f32[2,64,640]{2,1,0:T(8,128)S(1)} %dynamic-slice_bitcast_fusion.1), channel_id=1, source_target_pairs={{0,224},{32,0},{64,32},{96,64},{128,96},{160,128},{192,160},{224,1... | collective-permute-start | bytes 983048 | tf_op jit(solution)/shard_map/ppermute | solution.py:41
  98.7 19.8 %collective-permute-start.13 = (f32[512,128]{1,0:T(8,128)S(1)}, f32[512,128]{1,0:T(8,128)S(1)}, u32[]{:S(2)}, u32[]{:S(2)}) collective-permute-start(f32[512,128]{1,0:T(8,128)S(1)} %bitcast_add_fusion.17), channel_id=1, source_target_pairs={{0,6},{2,0},{4,2},{6,4},{1,7},{3,1},{5,3},{7,5},{8,14},{10,8},{12,... | collective-permute-start | bytes 786440 | tf_op jit(solution)/shard_map/ppermute | solution.py:67
  105.4 8.9 %collective-permute-start.17 = (f32[2,64,640]{2,1,0:T(8,128)S(1)}, f32[2,64,640]{2,1,0:T(8,128)S(1)}, u32[]{:S(2)}, u32[]{:S(2)}) collective-permute-start(f32[2,64,640]{2,1,0:T(8,128)S(1)} %bitcast_add_fusion.14), channel_id=1, source_target_pairs={{0,32},{32,64},{64,96},{96,128},{128,160},{160,192},{192,224},{224... | collective-permute-start | bytes 983048 | tf_op jit(solution)/shard_map/ppermute | solution.py:41
  108.7 9.6 %collective-permute-start.24 = (f32[2,64,640]{2,1,0:T(8,128)S(1)}, f32[2,64,640]{2,1,0:T(8,128)S(1)}, u32[]{:S(2)}, u32[]{:S(2)}) collective-permute-start(f32[2,64,640]{2,1,0:T(8,128)S(1)} %bitcast_add_fusion.7), channel_id=1, source_target_pairs={{0,224},{32,0},{64,32},{96,64},{128,96},{160,128},{192,160},{224,1... | collective-permute-start | bytes 983048 | tf_op jit(solution)/shard_map/ppermute | solution.py:41
  108.9 18.2 %collective-permute-start.10 = (f32[512,128]{1,0:T(8,128)S(1)}, f32[512,128]{1,0:T(8,128)S(1)}, u32[]{:S(2)}, u32[]{:S(2)}) collective-permute-start(f32[512,128]{1,0:T(8,128)S(1)} %bitcast_add_fusion.20), channel_id=1, source_target_pairs={{0,2},{2,4},{4,6},{6,0},{1,3},{3,5},{5,7},{7,1},{8,10},{10,12},{12... | collective-permute-start | bytes 786440 | tf_op jit(solution)/shard_map/ppermute | solution.py:67
  114.4 8.8 %collective-permute-start.18 = (f32[2,64,640]{2,1,0:T(8,128)S(1)}, f32[2,64,640]{2,1,0:T(8,128)S(1)}, u32[]{:S(2)}, u32[]{:S(2)}) collective-permute-start(f32[2,64,640]{2,1,0:T(8,128)S(1)} %bitcast_add_fusion.13), channel_id=1, source_target_pairs={{0,32},{32,64},{64,96},{96,128},{128,160},{160,192},{192,224},{224... | collective-permute-start | bytes 983048 | tf_op jit(solution)/shard_map/ppermute | solution.py:41
  118.4 8.6 %collective-permute-start.25 = (f32[2,64,640]{2,1,0:T(8,128)S(1)}, f32[2,64,640]{2,1,0:T(8,128)S(1)}, u32[]{:S(2)}, u32[]{:S(2)}) collective-permute-start(f32[2,64,640]{2,1,0:T(8,128)S(1)} %bitcast_add_fusion.6), channel_id=1, source_target_pairs={{0,224},{32,0},{64,32},{96,64},{128,96},{160,128},{192,160},{224,1... | collective-permute-start | bytes 983048 | tf_op jit(solution)/shard_map/ppermute | solution.py:41
  123.2 8.5 %collective-permute-start.19 = (f32[2,64,640]{2,1,0:T(8,128)S(1)}, f32[2,64,640]{2,1,0:T(8,128)S(1)}, u32[]{:S(2)}, u32[]{:S(2)}) collective-permute-start(f32[2,64,640]{2,1,0:T(8,128)S(1)} %bitcast_add_fusion.12), channel_id=1, source_target_pairs={{0,32},{32,64},{64,96},{96,128},{128,160},{160,192},{192,224},{224... | collective-permute-start | bytes 983048 | tf_op jit(solution)/shard_map/ppermute | solution.py:41
  127.0 8.8 %collective-permute-start.26 = (f32[2,64,640]{2,1,0:T(8,128)S(1)}, f32[2,64,640]{2,1,0:T(8,128)S(1)}, u32[]{:S(2)}, u32[]{:S(2)}) collective-permute-start(f32[2,64,640]{2,1,0:T(8,128)S(1)} %bitcast_add_fusion.5), channel_id=1, source_target_pairs={{0,224},{32,0},{64,32},{96,64},{128,96},{160,128},{192,160},{224,1... | collective-permute-start | bytes 983048 | tf_op jit(solution)/shard_map/ppermute | solution.py:41
  131.8 9.7 %collective-permute-start.20 = (f32[2,64,640]{2,1,0:T(8,128)S(1)}, f32[2,64,640]{2,1,0:T(8,128)S(1)}, u32[]{:S(2)}, u32[]{:S(2)}) collective-permute-start(f32[2,64,640]{2,1,0:T(8,128)S(1)} %bitcast_add_fusion.11), channel_id=1, source_target_pairs={{0,32},{32,64},{64,96},{96,128},{128,160},{160,192},{192,224},{224... | collective-permute-start | bytes 983048 | tf_op jit(solution)/shard_map/ppermute | solution.py:41
  135.9 10.0 %collective-permute-start.27 = (f32[2,64,640]{2,1,0:T(8,128)S(1)}, f32[2,64,640]{2,1,0:T(8,128)S(1)}, u32[]{:S(2)}, u32[]{:S(2)}) collective-permute-start(f32[2,64,640]{2,1,0:T(8,128)S(1)} %bitcast_add_fusion.4), channel_id=1, source_target_pairs={{0,224},{32,0},{64,32},{96,64},{128,96},{160,128},{192,160},{224,1... | collective-permute-start | bytes 983048 | tf_op jit(solution)/shard_map/ppermute | solution.py:41
  141.5 10.8 %collective-permute-start.21 = (f32[2,64,640]{2,1,0:T(8,128)S(1)}, f32[2,64,640]{2,1,0:T(8,128)S(1)}, u32[]{:S(2)}, u32[]{:S(2)}) collective-permute-start(f32[2,64,640]{2,1,0:T(8,128)S(1)} %bitcast_add_fusion.10), channel_id=1, source_target_pairs={{0,32},{32,64},{64,96},{96,128},{128,160},{160,192},{192,224},{224... | collective-permute-start | bytes 983048 | tf_op jit(solution)/shard_map/ppermute | solution.py:41
  145.9 11.1 %collective-permute-start.28 = (f32[2,64,640]{2,1,0:T(8,128)S(1)}, f32[2,64,640]{2,1,0:T(8,128)S(1)}, u32[]{:S(2)}, u32[]{:S(2)}) collective-permute-start(f32[2,64,640]{2,1,0:T(8,128)S(1)} %bitcast_add_fusion.3), channel_id=1, source_target_pairs={{0,224},{32,0},{64,32},{96,64},{128,96},{160,128},{192,160},{224,1... | collective-permute-start | bytes 983048 | tf_op jit(solution)/shard_map/ppermute | solution.py:41
  146.0 11.1 %collective-permute-start.14 = (f32[256,256]{1,0:T(8,128)S(1)}, f32[256,256]{1,0:T(8,128)S(1)}, u32[]{:S(2)}, u32[]{:S(2)}) collective-permute-start(f32[256,256]{1,0:T(8,128)S(1)} %dynamic-slice_bitcast_fusion.3), channel_id=1, source_target_pairs={{0,1},{1,0},{2,3},{3,2},{4,5},{5,4},{6,7},{7,6},{8,9},{9,8},{10,11... | collective-permute-start | bytes 786440 | tf_op jit(solution)/shard_map/ppermute | solution.py:53
  152.4 8.4 %collective-permute-start.22 = (f32[2,64,640]{2,1,0:T(8,128)S(1)}, f32[2,64,640]{2,1,0:T(8,128)S(1)}, u32[]{:S(2)}, u32[]{:S(2)}) collective-permute-start(f32[2,64,640]{2,1,0:T(8,128)S(1)} %bitcast_add_fusion.9), channel_id=1, source_target_pairs={{0,32},{32,64},{64,96},{96,128},{128,160},{160,192},{192,224},{224... | collective-permute-start | bytes 983048 | tf_op jit(solution)/shard_map/ppermute | solution.py:41
  157.0 8.4 %collective-permute-start.29 = (f32[2,64,640]{2,1,0:T(8,128)S(1)}, f32[2,64,640]{2,1,0:T(8,128)S(1)}, u32[]{:S(2)}, u32[]{:S(2)}) collective-permute-start(f32[2,64,640]{2,1,0:T(8,128)S(1)} %bitcast_add_fusion.2), channel_id=1, source_target_pairs={{0,224},{32,0},{64,32},{96,64},{128,96},{160,128},{192,160},{224,1... | collective-permute-start | bytes 983048 | tf_op jit(solution)/shard_map/ppermute | solution.py:41
  165.5 8.8 %collective-permute-start.30 = (f32[64,1280]{1,0:T(8,128)S(1)}, f32[64,1280]{1,0:T(8,128)}, u32[]{:S(2)}, u32[]{:S(2)}) collective-permute-start(f32[64,1280]{1,0:T(8,128)S(1)} %fusion.49), channel_id=1, source_target_pairs={{0,16},{16,0},{1,17},{17,1},{2,18},{18,2},{3,19},{19,3},{4,20},{20... | collective-permute-start | bytes 983048 | tf_op jit(solution)/shard_map/ppermute | solution.py:53
  168.4 8.5 %copy-start.1 = (bf16[256,2048]{1,0:T(8,128)(2,1)S(1)}, bf16[256,2048]{1,0:T(8,128)(2,1)}, u32[]{:S(2)}) copy-start(bf16[256,2048]{1,0:T(8,128)(2,1)} %param.8) | copy-start | bytes 3145732
Sparse Core Ops, SparseCore 0:
  82.3 54.0 reduce-scatter.1

commit v14 on v12

--- a/solution.py
+++ b/solution.py
@@ -31,10 +31,9 @@
 def ring_sum(chunks, axis):
     peers = lax.axis_size(axis)
     at = lax.axis_index(axis)
-    half = chunks.shape[-1] // 2
     sums = []
-    for step, cols in ((1, slice(0, half)), (-1, slice(half, None))):
-        own = chunks[..., cols]
+    for step, half in ((1, 0), (-1, 1)):
+        own = chunks[:, half]
         pairs = [(i, (i + step) % peers) for i in range(peers)]
         acc = lax.dynamic_index_in_dim(own, (at - step) % peers, 0, keepdims=False)
         for s in range(peers - 1):
@@ -43,7 +42,7 @@
                 own, (at - step * (s + 2)) % peers, 0, keepdims=False
             )
         sums.append(acc)
-    return jnp.concatenate(sums, axis=-1)
+    return jnp.stack(sums)
 
 
 def swap_sum(parts, axis):

time: 186 us -> 205 us (1.10)
  waiting for transfers between devices: 71 us -> 98.9 us
  starting transfers between devices: 50.3 us -> 43 us
    ppermute x14, waiting for transfers between devices: 39.4 us -> 53.8 us  [ring_sum(): got = lax.ppermute(acc, axis, pairs)]
    ppermute x6, waiting for transfers between devices: 4.72 us -> 17.8 us  [chan_ring_reduce_scatter(): got = lax.ppermute(acc, 'cy', pairs)]
    ppermute x14, starting transfers between devices: 24.8 us -> 16.9 us  [ring_sum(): got = lax.ppermute(acc, axis, pairs)]
  transfers between devices with their start and end apart: 28 -> 28, of which waited for: 17 -> 22; matrix products, arithmetic and copies ran while one was open for 13% -> 11% of each run, Pallas kernels for 0% -> 0%
where the time goes in v14:
time: 205 us; the launch traced here: 204 us
  waiting for transfers between devices  98.9 us (48%)
  starting transfers between devices  43 us (21%)
  matrix products  16.3 us (8%)
  local copies, waits for them, and re-layouts  15.8 us (8%)
  between operations  15.3 us (7%)
  other arithmetic  14.6 us (7%)
    ppermute x14, waiting for transfers between devices, ring_sum(): got = lax.ppermute(acc, axis, pairs)  53.8 us
    ppermute x4, waiting for transfers between devices, shifted(): return lax.ppermute(x, axis, pairs)  24.1 us
    ppermute x6, waiting for transfers between devices, chan_ring_reduce_scatter(): got = lax.ppermute(acc, 'cy', pairs)  17.8 us
    ppermute x14, starting transfers between devices, ring_sum(): got = lax.ppermute(acc, axis, pairs)  16.9 us
    ppermute x4, starting transfers between devices, shifted(): return lax.ppermute(x, axis, pairs)  12.1 us
    ppermute x6, starting transfers between devices, chan_ring_reduce_scatter(): got = lax.ppermute(acc, 'cy', pairs)  10.9 us
    dot_general x1, matrix products, contract_rows(): lax.dot_general(left, right, (((0,), (0,)), ((), ())), preferred_element_...  5.88 us
    add x3, other arithmetic, swap_sum(): return keep + lax.ppermute(give, axis, [(0, 1), (1, 0)])  5.85 us
  transfers between devices with their start and end apart: 28, of which 22 were waited for; matrix products, arithmetic and copies ran while one was open for 11% of the time, Pallas kernels for 0%

profile of v14, /device:TPU:98, one launch (start us, length us, event | category | flops | bytes accessed | tf_op | source)
XLA Modules:
  0.0 203.9 jit_solution(2575677341740678628)
XLA Ops:
  7.2 4.0 %slice_bitcast_fusion.1 = (bf16[2048,256]{1,0:T(8,128)(2,1)S(1)}, bf16[2048,256]{1,0:T(8,128)(2,1)}, bf16[2048,256]{1,0:T(8,128)(2,1)}, bf16[2048,256]{1,0:T(8,128)(2,1)S(1)}) fusion(bf16[2,2,2048,256]{3,2,1,0:T(8,128)(2,1)} %param.7), kind=kLoop, calls=%fused_computation.31 | loop fusion | bytes 8388608 | tf_op jit(solution)/shard_map/squeeze | solution.py:90
  11.2 1.3 convolution_bitcast_fusion
  13.6 5.0 %collective-permute-start = (f32[256,512]{0,1:T(8,128)}, f32[256,512]{0,1:T(8,128)}, u32[]{:S(2)}, u32[]{:S(2)}) collective-permute-start(f32[256,512]{0,1:T(8,128)} %get-tuple-element.17), channel_id=1, source_target_pairs={{0,32},{8,40},{16,48},{24,56},{32,64},{40,72},{48,80},{56,88},{64,... | collective-permute-start | bytes 1572872 | tf_op jit(solution)/shard_map/ppermute | solution.py:16
  18.7 2.9 %collective-permute-start.1 = (f32[256,512]{0,1:T(8,128)}, f32[256,512]{0,1:T(8,128)}, u32[]{:S(2)}, u32[]{:S(2)}) collective-permute-start(f32[256,512]{0,1:T(8,128)} %get-tuple-element.18), channel_id=1, source_target_pairs={{0,32},{8,40},{16,48},{24,56},{32,64},{40,72},{48,80},{56,88},{64,... | collective-permute-start | bytes 1572872 | tf_op jit(solution)/shard_map/ppermute | solution.py:16
  21.7 1.8 broadcast_select_fusion
  23.5 1.4 copy-done.3
  24.9 1.5 fusion.51
  26.4 3.5 %convolution_bitcast_fusion.1 = f32[512,512]{0,1:T(8,128)S(1)} fusion(bf16[512,2048]{1,0:T(8,128)(2,1)} %bitcast.109, bf16[2048,256]{1,0:T(8,128)(2,1)} %get-tuple-element.8, bf16[2048,256]{1,0:T(8,128)(2,1)} %get-tuple-element.9), kind=kOutput, calls=%fused_computation.27 | convolution fusion | flops 1077936128 | bytes 5242880 | tf_op jit(solution)/shard_map/dot_general | solution.py:92
  30.0 1.3 collective-permute-done
  31.3 10.1 %collective-permute-done.1 = f32[256,512]{0,1:T(8,128)} collective-permute-done((f32[256,512]{0,1:T(8,128)}, f32[256,512]{0,1:T(8,128)}, u32[]{:S(2)}, u32[]{:S(2)}) %collective-permute-start.1) | collective-permute-done | bytes 524320 | tf_op jit(solution)/shard_map/ppermute | solution.py:16
  41.4 1.4 slice_add_fusion.1
  43.2 2.2 %collective-permute-start.2 = (bf16[256,512]{0,1:T(8,128)(2,1)S(1)}, bf16[256,512]{0,1:T(8,128)(2,1)S(1)}, u32[]{:S(2)}, u32[]{:S(2)}) collective-permute-start(bf16[256,512]{0,1:T(8,128)(2,1)S(1)} %pad_maximum_fusion.8), channel_id=1, source_target_pairs={{32,0},{40,8},{48,16},{56,24},{64,32},{72,40},{80,48},{88,56},{96,... | collective-permute-start | bytes 786440 | tf_op jit(solution)/shard_map/ppermute | solution.py:16
  45.4 1.9 collective-permute-start.3
  47.4 8.8 %collective-permute-done.2 = bf16[256,512]{0,1:T(8,128)(2,1)S(1)} collective-permute-done((bf16[256,512]{0,1:T(8,128)(2,1)S(1)}, bf16[256,512]{0,1:T(8,128)(2,1)S(1)}, u32[]{:S(2)}, u32[]{:S(2)}) %collective-permute-start.2) | collective-permute-done | bytes 262176 | tf_op jit(solution)/shard_map/ppermute | solution.py:16
  56.2 3.9 %collective-permute-done.3 = bf16[256,512]{0,1:T(8,128)(2,1)S(1)} collective-permute-done((bf16[256,512]{0,1:T(8,128)(2,1)S(1)}, bf16[256,512]{0,1:T(8,128)(2,1)S(1)}, u32[]{:S(2)}, u32[]{:S(2)}) %collective-permute-start.3) | collective-permute-done | bytes 262176 | tf_op jit(solution)/shard_map/ppermute | solution.py:16
  60.2 5.9 %fusion = f32[2048,1280]{1,0:T(8,128)S(1)} fusion(bf16[512,2048]{1,0:T(8,128)(2,1)S(1)} %bitcast.104, bf16[512,2048]{1,0:T(8,128)(2,1)S(1)} %bitcast.111, bf16[512,1280]{0,1:T(8,128)(2,1)S(1)} %fusion.20, bf16[512,256]{0,1:T(8,128)(2,1)S(1)} %broadcast_in_dim.19, bf16[512,512]{0,1:T(8,128)(2,1)S(1)} %constant_dynamic-update-slice_fusion, ...), kind=kOutput, calls=%fused_computation.2 | convolution fusion | flops 5395447808 | bytes 17301504 | tf_op jit(solution)/shard_map/dot_general | solution.py:20
  66.1 3.0 %dynamic-slice_bitcast_fusion = f32[8,2,64,1280]{3,2,1,0:T(8,128)} fusion(f32[8,2,2,64,1280]{4,3,2,1,0:T(8,128)S(1)} %bitcast.100, s32[]{:T(128)S(6)} %select_n.222), kind=kLoop, calls=%fused_computation.1 | loop fusion | bytes 10485764 | tf_op jit(solution)/shard_map/jit(dynamic_index_in_dim)/squeeze | solution.py:51
  69.1 2.7 %copy-done.2 = f32[2048,1280]{1,0:T(8,128)} copy-done((f32[2048,1280]{1,0:T(8,128)}, f32[2048,1280]{1,0:T(8,128)S(1)}, u32[]{:S(2)}) %copy-start.2) | copy-done | bytes 10485784
  71.8 2.8 %fusion.19 = f32[2048,512]{1,0:T(8,128)S(1)} fusion(bf16[2048,256]{1,0:T(8,128)(2,1)} %get-tuple-element.8, bf16[2048,256]{1,0:T(8,128)(2,1)} %get-tuple-element.9, bf16[256,256]{0,1:T(8,128)(2,1)S(1)} %get-tuple-element.22, bf16[256,256]{0,1:T(8,128)(2,1)S(1)} %copy-done.6, bf16[256,256]{0,1:T(8,128)(2,1)S(1)} %get-tuple-element.14, ...), kind=kOutput, calls=%fused_computation.28 | convolution fusion | flops 1080033280 | bytes 6815744 | tf_op jit(solution)/shard_map/dot_general | solution.py:26
  75.8 1.7 fusion.48
  77.7 3.1 %collective-permute-start.7 = (f32[512,128]{1,0:T(8,128)S(1)}, f32[512,128]{1,0:T(8,128)S(1)}, u32[]{:S(2)}, u32[]{:S(2)}) collective-permute-start(f32[512,128]{1,0:T(8,128)S(1)} %dynamic-slice_bitcast_fusion.4), channel_id=1, source_target_pairs={{0,6},{2,0},{4,2},{6,4},{1,7},{3,1},{5,3},{7,5},{8,14},{10,8},{12,... | collective-permute-start | bytes 786440 | tf_op jit(solution)/shard_map/ppermute | solution.py:66
  81.0 6.1 %collective-permute-done.7 = f32[512,128]{1,0:T(8,128)S(1)} collective-permute-done((f32[512,128]{1,0:T(8,128)S(1)}, f32[512,128]{1,0:T(8,128)S(1)}, u32[]{:S(2)}, u32[]{:S(2)}) %collective-permute-start.7) | collective-permute-done | bytes 262176 | tf_op jit(solution)/shard_map/ppermute | solution.py:66
  87.1 3.8 %collective-permute-start.8 = (f32[512,128]{1,0:T(8,128)S(1)}, f32[512,128]{1,0:T(8,128)S(1)}, u32[]{:S(2)}, u32[]{:S(2)}) collective-permute-start(f32[512,128]{1,0:T(8,128)S(1)} %bitcast_add_fusion.18), channel_id=1, source_target_pairs={{0,6},{2,0},{4,2},{6,4},{1,7},{3,1},{5,3},{7,5},{8,14},{10,8},{12,... | collective-permute-start | bytes 786440 | tf_op jit(solution)/shard_map/ppermute | solution.py:66
  91.0 5.2 %collective-permute-done.8 = f32[512,128]{1,0:T(8,128)S(1)} collective-permute-done((f32[512,128]{1,0:T(8,128)S(1)}, f32[512,128]{1,0:T(8,128)S(1)}, u32[]{:S(2)}, u32[]{:S(2)}) %collective-permute-start.8) | collective-permute-done | bytes 262176 | tf_op jit(solution)/shard_map/ppermute | solution.py:66
  96.3 3.8 %collective-permute-start.9 = (f32[512,128]{1,0:T(8,128)S(1)}, f32[512,128]{1,0:T(8,128)S(1)}, u32[]{:S(2)}, u32[]{:S(2)}) collective-permute-start(f32[512,128]{1,0:T(8,128)S(1)} %bitcast_add_fusion.17), channel_id=1, source_target_pairs={{0,6},{2,0},{4,2},{6,4},{1,7},{3,1},{5,3},{7,5},{8,14},{10,8},{12,... | collective-permute-start | bytes 786440 | tf_op jit(solution)/shard_map/ppermute | solution.py:66
  101.5 3.0 %collective-permute-done.9 = f32[512,128]{1,0:T(8,128)S(1)} collective-permute-done((f32[512,128]{1,0:T(8,128)S(1)}, f32[512,128]{1,0:T(8,128)S(1)}, u32[]{:S(2)}, u32[]{:S(2)}) %collective-permute-start.9) | collective-permute-done | bytes 262176 | tf_op jit(solution)/shard_map/ppermute | solution.py:66
  104.6 3.5 %collective-permute-done.6 = f32[512,128]{1,0:T(8,128)S(1)} collective-permute-done((f32[512,128]{1,0:T(8,128)S(1)}, f32[512,128]{1,0:T(8,128)S(1)}, u32[]{:S(2)}, u32[]{:S(2)}) %collective-permute-start.6) | collective-permute-done | bytes 262176 | tf_op jit(solution)/shard_map/ppermute | solution.py:66
  108.8 4.8 %bitcast_add_fusion = f32[8,2,64,1280]{3,2,1,0:T(8,128)S(1)} fusion(f32[8,2,64,1280]{3,2,1,0:T(8,128)} %collective-permute-done.11, f32[8,2,2,64,1280]{4,3,2,1,0:T(8,128)} %bitcast.101, s32[]{:T(128)S(6)} %select_n.221), kind=kLoop, calls=%fused_computation | loop fusion | flops 1310720 | bytes 15728644 | tf_op jit(solution)/shard_map/add | solution.py:52
  114.0 1.9 collective-permute-start.12
  116.3 6.0 %collective-permute-done.12 = f32[64,1280]{1,0:T(8,128)S(1)} collective-permute-done((f32[64,1280]{1,0:T(8,128)S(1)}, f32[64,1280]{1,0:T(8,128)S(1)}, u32[]{:S(2)}, u32[]{:S(2)}) %collective-permute-start.12) | collective-permute-done | bytes 327712 | tf_op jit(solution)/shard_map/ppermute | solution.py:40
  122.3 2.0 collective-permute-start.13
  124.7 6.5 %collective-permute-done.13 = f32[64,1280]{1,0:T(8,128)S(1)} collective-permute-done((f32[64,1280]{1,0:T(8,128)S(1)}, f32[64,1280]{1,0:T(8,128)S(1)}, u32[]{:S(2)}, u32[]{:S(2)}) %collective-permute-start.13) | collective-permute-done | bytes 327712 | tf_op jit(solution)/shard_map/ppermute | solution.py:40
  131.3 1.8 collective-permute-start.14
  133.8 7.3 %collective-permute-done.14 = f32[64,1280]{1,0:T(8,128)S(1)} collective-permute-done((f32[64,1280]{1,0:T(8,128)S(1)}, f32[64,1280]{1,0:T(8,128)S(1)}, u32[]{:S(2)}, u32[]{:S(2)}) %collective-permute-start.14) | collective-permute-done | bytes 327712 | tf_op jit(solution)/shard_map/ppermute | solution.py:40
  141.1 1.7 collective-permute-start.15
  143.8 7.9 %collective-permute-done.15 = f32[64,1280]{1,0:T(8,128)S(1)} collective-permute-done((f32[64,1280]{1,0:T(8,128)S(1)}, f32[64,1280]{1,0:T(8,128)S(1)}, u32[]{:S(2)}, u32[]{:S(2)}) %collective-permute-start.15) | collective-permute-done | bytes 327712 | tf_op jit(solution)/shard_map/ppermute | solution.py:40
  151.7 1.7 collective-permute-start.16
  153.4 1.4 collective-permute-done.22
  155.0 6.8 %collective-permute-done.16 = f32[64,1280]{1,0:T(8,128)S(1)} collective-permute-done((f32[64,1280]{1,0:T(8,128)S(1)}, f32[64,1280]{1,0:T(8,128)S(1)}, u32[]{:S(2)}, u32[]{:S(2)}) %collective-permute-start.16) | collective-permute-done | bytes 327712 | tf_op jit(solution)/shard_map/ppermute | solution.py:40
  161.8 3.1 %collective-permute-start.17 = (f32[64,1280]{1,0:T(8,128)S(1)}, f32[64,1280]{1,0:T(8,128)S(1)}, u32[]{:S(2)}, u32[]{:S(2)}) collective-permute-start(f32[64,1280]{1,0:T(8,128)S(1)} %bitcast_add_fusion.10), channel_id=1, source_target_pairs={{0,32},{32,64},{64,96},{96,128},{128,160},{160,192},{192,224},{224... | collective-permute-start | bytes 983048 | tf_op jit(solution)/shard_map/ppermute | solution.py:40
  164.9 1.5 collective-permute-done.23
  166.5 5.8 %collective-permute-done.17 = f32[64,1280]{1,0:T(8,128)S(1)} collective-permute-done((f32[64,1280]{1,0:T(8,128)S(1)}, f32[64,1280]{1,0:T(8,128)S(1)}, u32[]{:S(2)}, u32[]{:S(2)}) %collective-permute-start.17) | collective-permute-done | bytes 327712 | tf_op jit(solution)/shard_map/ppermute | solution.py:40
  172.3 3.8 %collective-permute-start.18 = (f32[64,1280]{1,0:T(8,128)S(1)}, f32[64,1280]{1,0:T(8,128)S(1)}, u32[]{:S(2)}, u32[]{:S(2)}) collective-permute-start(f32[64,1280]{1,0:T(8,128)S(1)} %bitcast_add_fusion.9), channel_id=1, source_target_pairs={{0,32},{32,64},{64,96},{96,128},{128,160},{160,192},{192,224},{224... | collective-permute-start | bytes 983048 | tf_op jit(solution)/shard_map/ppermute | solution.py:40
  177.2 3.5 %collective-permute-done.18 = f32[64,1280]{1,0:T(8,128)S(1)} collective-permute-done((f32[64,1280]{1,0:T(8,128)S(1)}, f32[64,1280]{1,0:T(8,128)S(1)}, u32[]{:S(2)}, u32[]{:S(2)}) %collective-permute-start.18) | collective-permute-done | bytes 327712 | tf_op jit(solution)/shard_map/ppermute | solution.py:40
  180.7 4.7 %collective-permute-done.25 = f32[64,1280]{1,0:T(8,128)S(1)} collective-permute-done((f32[64,1280]{1,0:T(8,128)S(1)}, f32[64,1280]{1,0:T(8,128)S(1)}, u32[]{:S(2)}, u32[]{:S(2)}) %collective-permute-start.25) | collective-permute-done | bytes 327712 | tf_op jit(solution)/shard_map/ppermute | solution.py:40
  185.6 2.5 %collective-permute-start.26 = (f32[64,1280]{1,0:T(8,128)S(1)}, f32[64,1280]{1,0:T(8,128)}, u32[]{:S(2)}, u32[]{:S(2)}) collective-permute-start(f32[64,1280]{1,0:T(8,128)S(1)} %fusion.29), channel_id=1, source_target_pairs={{0,16},{16,0},{1,17},{17,1},{2,18},{18,2},{3,19},{19,3},{4,20},{20... | collective-permute-start | bytes 983048 | tf_op jit(solution)/shard_map/ppermute | solution.py:52
  189.4 1.7 add_convert_fusion
  191.1 3.2 %collective-permute-done.26 = f32[64,1280]{1,0:T(8,128)} collective-permute-done((f32[64,1280]{1,0:T(8,128)S(1)}, f32[64,1280]{1,0:T(8,128)}, u32[]{:S(2)}, u32[]{:S(2)}) %collective-permute-start.26) | collective-permute-done | bytes 327712 | tf_op jit(solution)/shard_map/ppermute | solution.py:52
  (92 shorter events, 13.6 us)
Async XLA Ops:
  7.2 17.7 %copy-start = (bf16[256,2048]{1,0:T(8,128)(2,1)S(1)}, bf16[256,2048]{1,0:T(8,128)(2,1)}, u32[]{:S(2)}) copy-start(bf16[256,2048]{1,0:T(8,128)(2,1)} %param.8) | copy-start | bytes 3145732
  7.2 180.9 %reduce-scatter.2.cloned.1.call-start = ((), (), s32[]{:S(2)}) async-start(), calls=%async_computation.1 | async-start | bytes 2359296 | tf_op jit(solution)/shard_map/reduce_scatter | solution.py:119
  7.2 4.0 %copy-start.9 = (bf16[2,256,2048]{2,1,0:T(8,128)(2,1)S(1)}, bf16[2,256,2048]{2,1,0:T(8,128)(2,1)}, u32[]{:S(2)}) copy-start(bf16[2,256,2048]{2,1,0:T(8,128)(2,1)} %param.5) | copy-start | bytes 6291460
  11.2 10.4 %copy-start.8 = (s32[2]{0:T(128)S(1)}, s32[2]{0:T(128)}, u32[]{:S(2)}) copy-start(s32[2]{0:T(128)} %param.9) | copy-start | bytes 28
  13.6 17.6 %collective-permute-start = (f32[256,512]{0,1:T(8,128)}, f32[256,512]{0,1:T(8,128)}, u32[]{:S(2)}, u32[]{:S(2)}) collective-permute-start(f32[256,512]{0,1:T(8,128)} %get-tuple-element.17), channel_id=1, source_target_pairs={{0,32},{8,40},{16,48},{24,56},{32,64},{40,72},{48,80},{56,88},{64,... | collective-permute-start | bytes 1572872 | tf_op jit(solution)/shard_map/ppermute | solution.py:16
  18.7 22.7 %collective-permute-start.1 = (f32[256,512]{0,1:T(8,128)}, f32[256,512]{0,1:T(8,128)}, u32[]{:S(2)}, u32[]{:S(2)}) collective-permute-start(f32[256,512]{0,1:T(8,128)} %get-tuple-element.18), channel_id=1, source_target_pairs={{0,32},{8,40},{16,48},{24,56},{32,64},{40,72},{48,80},{56,88},{64,... | collective-permute-start | bytes 1572872 | tf_op jit(solution)/shard_map/ppermute | solution.py:16
  23.5 1.4 copy-start.3
  30.0 12.8 %copy-start.7 = (f32[512,256]{0,1:T(8,128)S(1)}, f32[512,256]{0,1:T(8,128)}, u32[]{:S(2)}) copy-start(f32[512,256]{0,1:T(8,128)} %fusion.51) | copy-start | bytes 1572868
  42.8 17.4 %copy-start.4 = (bf16[2,256,2048]{2,1,0:T(8,128)(2,1)S(1)}, bf16[2,256,2048]{2,1,0:T(8,128)(2,1)}, u32[]{:S(2)}) copy-start(bf16[2,256,2048]{2,1,0:T(8,128)(2,1)} %copy-done.3) | copy-start | bytes 6291460
  42.8 17.4 %copy-start.10 = (bf16[2,256,2048]{2,1,0:T(8,128)(2,1)S(1)}, bf16[2,256,2048]{2,1,0:T(8,128)(2,1)}, u32[]{:S(2)}) copy-start(bf16[2,256,2048]{2,1,0:T(8,128)(2,1)} %param.5) | copy-start | bytes 6291460
  43.1 22.9 %copy-start.5 = (bf16[256,256]{0,1:T(8,128)(2,1)}, bf16[256,256]{0,1:T(8,128)(2,1)S(1)}, u32[]{:S(2)}) copy-start(bf16[256,256]{0,1:T(8,128)(2,1)S(1)} %get-tuple-element.23) | copy-start | bytes 393220
  43.2 13.0 %collective-permute-start.2 = (bf16[256,512]{0,1:T(8,128)(2,1)S(1)}, bf16[256,512]{0,1:T(8,128)(2,1)S(1)}, u32[]{:S(2)}, u32[]{:S(2)}) collective-permute-start(bf16[256,512]{0,1:T(8,128)(2,1)S(1)} %pad_maximum_fusion.8), channel_id=1, source_target_pairs={{32,0},{40,8},{48,16},{56,24},{64,32},{72,40},{80,48},{88,56},{96,... | collective-permute-start | bytes 786440 | tf_op jit(solution)/shard_map/ppermute | solution.py:16
  45.4 14.7 %collective-permute-start.3 = (bf16[256,512]{0,1:T(8,128)(2,1)S(1)}, bf16[256,512]{0,1:T(8,128)(2,1)S(1)}, u32[]{:S(2)}, u32[]{:S(2)}) collective-permute-start(bf16[256,512]{0,1:T(8,128)(2,1)S(1)} %pad_maximum_fusion.9), channel_id=1, source_target_pairs={{32,0},{40,8},{48,16},{56,24},{64,32},{72,40},{80,48},{88,56},{96,... | collective-permute-start | bytes 786440 | tf_op jit(solution)/shard_map/ppermute | solution.py:16
  66.1 5.7 %copy-start.2 = (f32[2048,1280]{1,0:T(8,128)}, f32[2048,1280]{1,0:T(8,128)S(1)}, u32[]{:S(2)}) copy-start(f32[2048,1280]{1,0:T(8,128)S(1)} %fusion) | copy-start | bytes 31457284
  66.1 5.7 %copy-start.6 = (bf16[256,256]{0,1:T(8,128)(2,1)S(1)}, bf16[256,256]{0,1:T(8,128)(2,1)}, u32[]{:S(2)}) copy-start(bf16[256,256]{0,1:T(8,128)(2,1)} %copy-done.5) | copy-start | bytes 393220
  71.7 37.1 %collective-permute-start.11 = (f32[8,2,64,1280]{3,2,1,0:T(8,128)}, f32[8,2,64,1280]{3,2,1,0:T(8,128)}, u32[]{:S(2)}, u32[]{:S(2)}) collective-permute-start(f32[8,2,64,1280]{3,2,1,0:T(8,128)} %dynamic-slice_bitcast_fusion), channel_id=1, source_target_pairs={{0,8},{8,0},{1,9},{9,1},{2,10},{10,2},{3,11},{11,3},{4,12},{12,4},... | collective-permute-start | bytes 15728648 | tf_op jit(solution)/shard_map/ppermute | solution.py:52
  77.7 9.3 %collective-permute-start.7 = (f32[512,128]{1,0:T(8,128)S(1)}, f32[512,128]{1,0:T(8,128)S(1)}, u32[]{:S(2)}, u32[]{:S(2)}) collective-permute-start(f32[512,128]{1,0:T(8,128)S(1)} %dynamic-slice_bitcast_fusion.4), channel_id=1, source_target_pairs={{0,6},{2,0},{4,2},{6,4},{1,7},{3,1},{5,3},{7,5},{8,14},{10,8},{12,... | collective-permute-start | bytes 786440 | tf_op jit(solution)/shard_map/ppermute | solution.py:66
  80.8 10.0 %collective-permute-start.4 = (f32[512,128]{1,0:T(8,128)S(1)}, f32[512,128]{1,0:T(8,128)S(1)}, u32[]{:S(2)}, u32[]{:S(2)}) collective-permute-start(f32[512,128]{1,0:T(8,128)S(1)} %dynamic-slice_bitcast_fusion.5), channel_id=1, source_target_pairs={{0,2},{2,4},{4,6},{6,0},{1,3},{3,5},{5,7},{7,1},{8,10},{10,12},{12... | collective-permute-start | bytes 786440 | tf_op jit(solution)/shard_map/ppermute | solution.py:66
  87.1 9.1 %collective-permute-start.8 = (f32[512,128]{1,0:T(8,128)S(1)}, f32[512,128]{1,0:T(8,128)S(1)}, u32[]{:S(2)}, u32[]{:S(2)}) collective-permute-start(f32[512,128]{1,0:T(8,128)S(1)} %bitcast_add_fusion.18), channel_id=1, source_target_pairs={{0,6},{2,0},{4,2},{6,4},{1,7},{3,1},{5,3},{7,5},{8,14},{10,8},{12,... | collective-permute-start | bytes 786440 | tf_op jit(solution)/shard_map/ppermute | solution.py:66
  90.9 9.1 %collective-permute-start.5 = (f32[512,128]{1,0:T(8,128)S(1)}, f32[512,128]{1,0:T(8,128)S(1)}, u32[]{:S(2)}, u32[]{:S(2)}) collective-permute-start(f32[512,128]{1,0:T(8,128)S(1)} %bitcast_add_fusion.21), channel_id=1, source_target_pairs={{0,2},{2,4},{4,6},{6,0},{1,3},{3,5},{5,7},{7,1},{8,10},{10,12},{12... | collective-permute-start | bytes 786440 | tf_op jit(solution)/shard_map/ppermute | solution.py:66
  96.3 8.3 %collective-permute-start.9 = (f32[512,128]{1,0:T(8,128)S(1)}, f32[512,128]{1,0:T(8,128)S(1)}, u32[]{:S(2)}, u32[]{:S(2)}) collective-permute-start(f32[512,128]{1,0:T(8,128)S(1)} %bitcast_add_fusion.17), channel_id=1, source_target_pairs={{0,6},{2,0},{4,2},{6,4},{1,7},{3,1},{5,3},{7,5},{8,14},{10,8},{12,... | collective-permute-start | bytes 786440 | tf_op jit(solution)/shard_map/ppermute | solution.py:66
  100.1 8.0 %collective-permute-start.6 = (f32[512,128]{1,0:T(8,128)S(1)}, f32[512,128]{1,0:T(8,128)S(1)}, u32[]{:S(2)}, u32[]{:S(2)}) collective-permute-start(f32[512,128]{1,0:T(8,128)S(1)} %bitcast_add_fusion.20), channel_id=1, source_target_pairs={{0,2},{2,4},{4,6},{6,0},{1,3},{3,5},{5,7},{7,1},{8,10},{10,12},{12... | collective-permute-start | bytes 786440 | tf_op jit(solution)/shard_map/ppermute | solution.py:66
  108.2 7.7 %collective-permute-start.10 = (f32[256,256]{1,0:T(8,128)S(1)}, f32[256,256]{1,0:T(8,128)S(1)}, u32[]{:S(2)}, u32[]{:S(2)}) collective-permute-start(f32[256,256]{1,0:T(8,128)S(1)} %dynamic-slice_bitcast_fusion.3), channel_id=1, source_target_pairs={{0,1},{1,0},{2,3},{3,2},{4,5},{5,4},{6,7},{7,6},{8,9},{9,8},{10,11... | collective-permute-start | bytes 786440 | tf_op jit(solution)/shard_map/ppermute | solution.py:52
  114.0 8.2 %collective-permute-start.12 = (f32[64,1280]{1,0:T(8,128)S(1)}, f32[64,1280]{1,0:T(8,128)S(1)}, u32[]{:S(2)}, u32[]{:S(2)}) collective-permute-start(f32[64,1280]{1,0:T(8,128)S(1)} %dynamic-slice_bitcast_fusion.2), channel_id=1, source_target_pairs={{0,32},{32,64},{64,96},{96,128},{128,160},{160,192},{192,224},{224... | collective-permute-start | bytes 983048 | tf_op jit(solution)/shard_map/ppermute | solution.py:40
  116.0 8.4 %collective-permute-start.19 = (f32[64,1280]{1,0:T(8,128)S(1)}, f32[64,1280]{1,0:T(8,128)S(1)}, u32[]{:S(2)}, u32[]{:S(2)}) collective-permute-start(f32[64,1280]{1,0:T(8,128)S(1)} %dynamic-slice_bitcast_fusion.1), channel_id=1, source_target_pairs={{0,224},{32,0},{64,32},{96,64},{128,96},{160,128},{192,160},{224,1... | collective-permute-start | bytes 983048 | tf_op jit(solution)/shard_map/ppermute | solution.py:40
  122.3 9.0 %collective-permute-start.13 = (f32[64,1280]{1,0:T(8,128)S(1)}, f32[64,1280]{1,0:T(8,128)S(1)}, u32[]{:S(2)}, u32[]{:S(2)}) collective-permute-start(f32[64,1280]{1,0:T(8,128)S(1)} %bitcast_add_fusion.14), channel_id=1, source_target_pairs={{0,32},{32,64},{64,96},{96,128},{128,160},{160,192},{192,224},{224... | collective-permute-start | bytes 983048 | tf_op jit(solution)/shard_map/ppermute | solution.py:40
  124.4 9.3 %collective-permute-start.20 = (f32[64,1280]{1,0:T(8,128)S(1)}, f32[64,1280]{1,0:T(8,128)S(1)}, u32[]{:S(2)}, u32[]{:S(2)}) collective-permute-start(f32[64,1280]{1,0:T(8,128)S(1)} %bitcast_add_fusion.7), channel_id=1, source_target_pairs={{0,224},{32,0},{64,32},{96,64},{128,96},{160,128},{192,160},{224,1... | collective-permute-start | bytes 983048 | tf_op jit(solution)/shard_map/ppermute | solution.py:40
  131.3 9.8 %collective-permute-start.14 = (f32[64,1280]{1,0:T(8,128)S(1)}, f32[64,1280]{1,0:T(8,128)S(1)}, u32[]{:S(2)}, u32[]{:S(2)}) collective-permute-start(f32[64,1280]{1,0:T(8,128)S(1)} %bitcast_add_fusion.13), channel_id=1, source_target_pairs={{0,32},{32,64},{64,96},{96,128},{128,160},{160,192},{192,224},{224... | collective-permute-start | bytes 983048 | tf_op jit(solution)/shard_map/ppermute | solution.py:40
  133.7 10.0 %collective-permute-start.21 = (f32[64,1280]{1,0:T(8,128)S(1)}, f32[64,1280]{1,0:T(8,128)S(1)}, u32[]{:S(2)}, u32[]{:S(2)}) collective-permute-start(f32[64,1280]{1,0:T(8,128)S(1)} %bitcast_add_fusion.6), channel_id=1, source_target_pairs={{0,224},{32,0},{64,32},{96,64},{128,96},{160,128},{192,160},{224,1... | collective-permute-start | bytes 983048 | tf_op jit(solution)/shard_map/ppermute | solution.py:40
  141.1 10.6 %collective-permute-start.15 = (f32[64,1280]{1,0:T(8,128)S(1)}, f32[64,1280]{1,0:T(8,128)S(1)}, u32[]{:S(2)}, u32[]{:S(2)}) collective-permute-start(f32[64,1280]{1,0:T(8,128)S(1)} %bitcast_add_fusion.12), channel_id=1, source_target_pairs={{0,32},{32,64},{64,96},{96,128},{128,160},{160,192},{192,224},{224... | collective-permute-start | bytes 983048 | tf_op jit(solution)/shard_map/ppermute | solution.py:40
  143.7 11.1 %collective-permute-start.22 = (f32[64,1280]{1,0:T(8,128)S(1)}, f32[64,1280]{1,0:T(8,128)S(1)}, u32[]{:S(2)}, u32[]{:S(2)}) collective-permute-start(f32[64,1280]{1,0:T(8,128)S(1)} %bitcast_add_fusion.5), channel_id=1, source_target_pairs={{0,224},{32,0},{64,32},{96,64},{128,96},{160,128},{192,160},{224,1... | collective-permute-start | bytes 983048 | tf_op jit(solution)/shard_map/ppermute | solution.py:40
  151.7 10.0 %collective-permute-start.16 = (f32[64,1280]{1,0:T(8,128)S(1)}, f32[64,1280]{1,0:T(8,128)S(1)}, u32[]{:S(2)}, u32[]{:S(2)}) collective-permute-start(f32[64,1280]{1,0:T(8,128)S(1)} %bitcast_add_fusion.11), channel_id=1, source_target_pairs={{0,32},{32,64},{64,96},{96,128},{128,160},{160,192},{192,224},{224... | collective-permute-start | bytes 983048 | tf_op jit(solution)/shard_map/ppermute | solution.py:40
  154.9 11.5 %collective-permute-start.23 = (f32[64,1280]{1,0:T(8,128)S(1)}, f32[64,1280]{1,0:T(8,128)S(1)}, u32[]{:S(2)}, u32[]{:S(2)}) collective-permute-start(f32[64,1280]{1,0:T(8,128)S(1)} %bitcast_add_fusion.4), channel_id=1, source_target_pairs={{0,224},{32,0},{64,32},{96,64},{128,96},{160,128},{192,160},{224,1... | collective-permute-start | bytes 983048 | tf_op jit(solution)/shard_map/ppermute | solution.py:40
  161.8 10.5 %collective-permute-start.17 = (f32[64,1280]{1,0:T(8,128)S(1)}, f32[64,1280]{1,0:T(8,128)S(1)}, u32[]{:S(2)}, u32[]{:S(2)}) collective-permute-start(f32[64,1280]{1,0:T(8,128)S(1)} %bitcast_add_fusion.10), channel_id=1, source_target_pairs={{0,32},{32,64},{64,96},{96,128},{128,160},{160,192},{192,224},{224... | collective-permute-start | bytes 983048 | tf_op jit(solution)/shard_map/ppermute | solution.py:40
  166.4 10.6 %collective-permute-start.24 = (f32[64,1280]{1,0:T(8,128)S(1)}, f32[64,1280]{1,0:T(8,128)S(1)}, u32[]{:S(2)}, u32[]{:S(2)}) collective-permute-start(f32[64,1280]{1,0:T(8,128)S(1)} %bitcast_add_fusion.3), channel_id=1, source_target_pairs={{0,224},{32,0},{64,32},{96,64},{128,96},{160,128},{192,160},{224,1... | collective-permute-start | bytes 983048 | tf_op jit(solution)/shard_map/ppermute | solution.py:40
  172.3 8.4 %collective-permute-start.18 = (f32[64,1280]{1,0:T(8,128)S(1)}, f32[64,1280]{1,0:T(8,128)S(1)}, u32[]{:S(2)}, u32[]{:S(2)}) collective-permute-start(f32[64,1280]{1,0:T(8,128)S(1)} %bitcast_add_fusion.9), channel_id=1, source_target_pairs={{0,32},{32,64},{64,96},{96,128},{128,160},{160,192},{192,224},{224... | collective-permute-start | bytes 983048 | tf_op jit(solution)/shard_map/ppermute | solution.py:40
  177.1 8.4 %collective-permute-start.25 = (f32[64,1280]{1,0:T(8,128)S(1)}, f32[64,1280]{1,0:T(8,128)S(1)}, u32[]{:S(2)}, u32[]{:S(2)}) collective-permute-start(f32[64,1280]{1,0:T(8,128)S(1)} %bitcast_add_fusion.2), channel_id=1, source_target_pairs={{0,224},{32,0},{64,32},{96,64},{128,96},{160,128},{192,160},{224,1... | collective-permute-start | bytes 983048 | tf_op jit(solution)/shard_map/ppermute | solution.py:40
  185.6 8.8 %collective-permute-start.26 = (f32[64,1280]{1,0:T(8,128)S(1)}, f32[64,1280]{1,0:T(8,128)}, u32[]{:S(2)}, u32[]{:S(2)}) collective-permute-start(f32[64,1280]{1,0:T(8,128)S(1)} %fusion.29), channel_id=1, source_target_pairs={{0,16},{16,0},{1,17},{17,1},{2,18},{18,2},{3,19},{19,3},{4,20},{20... | collective-permute-start | bytes 983048 | tf_op jit(solution)/shard_map/ppermute | solution.py:52
  188.1 8.9 %copy-start.1 = (bf16[256,2048]{1,0:T(8,128)(2,1)S(1)}, bf16[256,2048]{1,0:T(8,128)(2,1)}, u32[]{:S(2)}) copy-start(bf16[256,2048]{1,0:T(8,128)(2,1)} %param.8) | copy-start | bytes 3145732
Sparse Core Ops, SparseCore 0:
  101.7 53.8 reduce-scatter.1

commit v15 on v12

--- a/solution.py
+++ b/solution.py
@@ -114,7 +114,7 @@
     branch_grads = jnp.concatenate(grad_parts, axis=0)
     later = jnp.concatenate(later_parts, axis=0)
     partial_value = contract_cols(w_now, branch_grads) + contract_cols(w_dil, later)
-    cut = partial_value.shape[1] // 2
+    cut = partial_value.shape[1] * 3 // 4
     summed = jnp.concatenate(
         [
             lax.psum_scatter(partial_value[:, :cut], CHAN, scatter_dimension=0, tiled=True),

time: 186 us -> 189 us (1.016); the launches traced: 184 us -> 189 us
  local copies, waits for them, and re-layouts: 16.1 us -> 19.8 us
  waiting for transfers between devices: 71 us -> 74.3 us
    slice x1, local copies, waits for them, and re-layouts: 1.74 us -> 3.71 us  [local(): partial_value[:, :cut]]
    unnamed x23 -> x25, local copies, waits for them, and re-layouts: 4.11 us -> 5.63 us
  transfers between devices with their start and end apart: 28 -> 28, of which waited for: 17 -> 18; matrix products, arithmetic and copies ran while one was open for 13% -> 14% of each run, Pallas kernels for 0% -> 0%
where the time goes in v15:
time: 189 us
  waiting for transfers between devices  74.3 us (39%)
  starting transfers between devices  49.1 us (26%)
  local copies, waits for them, and re-layouts  19.8 us (10%)
  matrix products  16.4 us (9%)
  between operations  15.3 us (8%)
  other arithmetic  13.9 us (7%)
    ppermute x14, waiting for transfers between devices, ring_sum(): got = lax.ppermute(acc, axis, pairs)  40.8 us
    ppermute x14, starting transfers between devices, ring_sum(): got = lax.ppermute(acc, axis, pairs)  24.4 us
    ppermute x4, waiting for transfers between devices, shifted(): return lax.ppermute(x, axis, pairs)  24 us
    ppermute x4, starting transfers between devices, shifted(): return lax.ppermute(x, axis, pairs)  12.1 us
    ppermute x6, starting transfers between devices, chan_ring_reduce_scatter(): got = lax.ppermute(acc, 'cy', pairs)  10.4 us
    dot_general x1, matrix products, contract_rows(): lax.dot_general(left, right, (((0,), (0,)), ((), ())), preferred_element_...  5.87 us
    ppermute x6, waiting for transfers between devices, chan_ring_reduce_scatter(): got = lax.ppermute(acc, 'cy', pairs)  5.81 us
    dot_general x3, matrix products, contract_cols(): lax.dot_general(left, right, (((1,), (1,)), ((), ())), preferred_element_...  5.73 us
  transfers between devices with their start and end apart: 28, of which 18 were waited for; matrix products, arithmetic and copies ran while one was open for 14% of the time, Pallas kernels for 0%

profile of v15, /device:TPU:98, one launch (start us, length us, event | category | flops | bytes accessed | tf_op | source)
XLA Modules:
  0.0 188.9 jit_solution(14403470926764672861)
XLA Ops:
  7.2 4.0 %slice_bitcast_fusion.1 = (bf16[2048,256]{1,0:T(8,128)(2,1)S(1)}, bf16[2048,256]{1,0:T(8,128)(2,1)}, bf16[2048,256]{1,0:T(8,128)(2,1)}, bf16[2048,256]{1,0:T(8,128)(2,1)S(1)}) fusion(bf16[2,2,2048,256]{3,2,1,0:T(8,128)(2,1)} %param.7), kind=kLoop, calls=%fused_computation.31 | loop fusion | bytes 8388608 | tf_op jit(solution)/shard_map/squeeze | solution.py:91
  11.2 1.3 convolution_bitcast_fusion
  13.6 5.0 %collective-permute-start = (f32[256,512]{0,1:T(8,128)}, f32[256,512]{0,1:T(8,128)}, u32[]{:S(2)}, u32[]{:S(2)}) collective-permute-start(f32[256,512]{0,1:T(8,128)} %get-tuple-element.15), channel_id=1, source_target_pairs={{0,32},{8,40},{16,48},{24,56},{32,64},{40,72},{48,80},{56,88},{64,... | collective-permute-start | bytes 1572872 | tf_op jit(solution)/shard_map/ppermute | solution.py:16
  18.6 2.9 %collective-permute-start.1 = (f32[256,512]{0,1:T(8,128)}, f32[256,512]{0,1:T(8,128)}, u32[]{:S(2)}, u32[]{:S(2)}) collective-permute-start(f32[256,512]{0,1:T(8,128)} %get-tuple-element.16), channel_id=1, source_target_pairs={{0,32},{8,40},{16,48},{24,56},{32,64},{40,72},{48,80},{56,88},{64,... | collective-permute-start | bytes 1572872 | tf_op jit(solution)/shard_map/ppermute | solution.py:16
  21.7 1.8 broadcast_select_fusion
  23.5 1.3 copy-done.4
  24.8 1.6 fusion.48
  26.4 3.5 %convolution_bitcast_fusion.1 = f32[512,512]{0,1:T(8,128)S(1)} fusion(bf16[512,2048]{1,0:T(8,128)(2,1)} %bitcast.101, bf16[2048,256]{1,0:T(8,128)(2,1)} %get-tuple-element.6, bf16[2048,256]{1,0:T(8,128)(2,1)} %get-tuple-element.7), kind=kOutput, calls=%fused_computation.27 | convolution fusion | flops 1077936128 | bytes 5242880 | tf_op jit(solution)/shard_map/dot_general | solution.py:93
  29.9 1.3 collective-permute-done
  31.2 10.1 %collective-permute-done.1 = f32[256,512]{0,1:T(8,128)} collective-permute-done((f32[256,512]{0,1:T(8,128)}, f32[256,512]{0,1:T(8,128)}, u32[]{:S(2)}, u32[]{:S(2)}) %collective-permute-start.1) | collective-permute-done | bytes 524320 | tf_op jit(solution)/shard_map/ppermute | solution.py:16
  41.3 1.4 slice_add_fusion.1
  43.1 2.2 %collective-permute-start.2 = (bf16[256,512]{0,1:T(8,128)(2,1)S(1)}, bf16[256,512]{0,1:T(8,128)(2,1)S(1)}, u32[]{:S(2)}, u32[]{:S(2)}) collective-permute-start(bf16[256,512]{0,1:T(8,128)(2,1)S(1)} %pad_maximum_fusion.7), channel_id=1, source_target_pairs={{32,0},{40,8},{48,16},{56,24},{64,32},{72,40},{80,48},{88,56},{96,... | collective-permute-start | bytes 786440 | tf_op jit(solution)/shard_map/ppermute | solution.py:16
  45.3 1.9 %collective-permute-start.3 = (bf16[256,512]{0,1:T(8,128)(2,1)S(1)}, bf16[256,512]{0,1:T(8,128)(2,1)S(1)}, u32[]{:S(2)}, u32[]{:S(2)}) collective-permute-start(bf16[256,512]{0,1:T(8,128)(2,1)S(1)} %pad_maximum_fusion.8), channel_id=1, source_target_pairs={{32,0},{40,8},{48,16},{56,24},{64,32},{72,40},{80,48},{88,56},{96,... | collective-permute-start | bytes 786440 | tf_op jit(solution)/shard_map/ppermute | solution.py:16
  47.4 8.8 %collective-permute-done.2 = bf16[256,512]{0,1:T(8,128)(2,1)S(1)} collective-permute-done((bf16[256,512]{0,1:T(8,128)(2,1)S(1)}, bf16[256,512]{0,1:T(8,128)(2,1)S(1)}, u32[]{:S(2)}, u32[]{:S(2)}) %collective-permute-start.2) | collective-permute-done | bytes 262176 | tf_op jit(solution)/shard_map/ppermute | solution.py:16
  56.2 3.9 %collective-permute-done.3 = bf16[256,512]{0,1:T(8,128)(2,1)S(1)} collective-permute-done((bf16[256,512]{0,1:T(8,128)(2,1)S(1)}, bf16[256,512]{0,1:T(8,128)(2,1)S(1)}, u32[]{:S(2)}, u32[]{:S(2)}) %collective-permute-start.3) | collective-permute-done | bytes 262176 | tf_op jit(solution)/shard_map/ppermute | solution.py:16
  60.1 5.9 %fusion = f32[2048,1280]{1,0:T(8,128)S(1)} fusion(bf16[512,2048]{1,0:T(8,128)(2,1)S(1)} %bitcast.96, bf16[512,2048]{1,0:T(8,128)(2,1)S(1)} %bitcast.103, bf16[512,1280]{0,1:T(8,128)(2,1)S(1)} %fusion.20, bf16[512,256]{0,1:T(8,128)(2,1)S(1)} %broadcast_in_dim.19, bf16[512,512]{0,1:T(8,128)(2,1)S(1)} %constant_dynamic-update-slice_fusion, ...), kind=kOutput, calls=%fused_computation.2 | convolution fusion | flops 5395447808 | bytes 17301504 | tf_op jit(solution)/shard_map/dot_general | solution.py:20
  66.0 3.0 %dynamic-slice_bitcast_fusion = f32[8,2,64,1280]{3,2,1,0:T(8,128)} fusion(f32[8,2,2,64,1280]{4,3,2,1,0:T(8,128)S(1)} %bitcast.92, s32[]{:T(128)S(6)} %select_n.222), kind=kLoop, calls=%fused_computation.1 | loop fusion | bytes 10485764 | tf_op jit(solution)/shard_map/jit(dynamic_index_in_dim)/squeeze | solution.py:52
  69.0 2.7 %copy-done.3 = f32[2048,1280]{1,0:T(8,128)} copy-done((f32[2048,1280]{1,0:T(8,128)}, f32[2048,1280]{1,0:T(8,128)S(1)}, u32[]{:S(2)}) %copy-start.3) | copy-done | bytes 10485784
  72.3 2.9 %fusion.19 = f32[2048,512]{1,0:T(8,128)S(1)} fusion(bf16[2048,256]{1,0:T(8,128)(2,1)} %get-tuple-element.6, bf16[2048,256]{1,0:T(8,128)(2,1)} %get-tuple-element.7, bf16[256,256]{0,1:T(8,128)(2,1)S(1)} %get-tuple-element.20, bf16[256,256]{0,1:T(8,128)(2,1)S(1)} %copy-done.7, bf16[256,256]{0,1:T(8,128)(2,1)S(1)} %get-tuple-element.12, ...), kind=kOutput, calls=%fused_computation.28 | convolution fusion | flops 1080033280 | bytes 6815744 | tf_op jit(solution)/shard_map/dot_general | solution.py:26
  75.1 1.3 convolution_add_fusion
  76.9 1.5 copy-done.2
  78.5 3.1 %collective-permute-start.7 = (f32[512,64]{1,0:T(8,128)S(1)}, f32[512,64]{1,0:T(8,128)S(1)}, u32[]{:S(2)}, u32[]{:S(2)}) collective-permute-start(f32[512,64]{1,0:T(8,128)S(1)} %dynamic-slice_bitcast_fusion.3), channel_id=1, source_target_pairs={{0,6},{2,0},{4,2},{6,4},{1,7},{3,1},{5,3},{7,5},{8,14},{10,8},{12,... | collective-permute-start | bytes 393224 | tf_op jit(solution)/shard_map/ppermute | solution.py:67
  82.4 3.7 %slice.98 = f32[2048,384]{1,0:T(8,128)} slice(f32[2048,512]{1,0:T(8,128)} %copy-done.2), slice={[0:2048], [0:384]} | slice | bytes 6291456 | tf_op jit(solution)/shard_map/slice | solution.py:120
  86.3 1.6 collective-permute-done.7
  87.9 3.8 %collective-permute-start.8 = (f32[512,64]{1,0:T(8,128)S(1)}, f32[512,64]{1,0:T(8,128)S(1)}, u32[]{:S(2)}, u32[]{:S(2)}) collective-permute-start(f32[512,64]{1,0:T(8,128)S(1)} %bitcast_add_fusion.17), channel_id=1, source_target_pairs={{0,6},{2,0},{4,2},{6,4},{1,7},{3,1},{5,3},{7,5},{8,14},{10,8},{12,... | collective-permute-start | bytes 393224 | tf_op jit(solution)/shard_map/ppermute | solution.py:67
  91.6 4.2 %collective-permute-done.4 = f32[512,64]{1,0:T(8,128)S(1)} collective-permute-done((f32[512,64]{1,0:T(8,128)S(1)}, f32[512,64]{1,0:T(8,128)S(1)}, u32[]{:S(2)}, u32[]{:S(2)}) %collective-permute-start.4) | collective-permute-done | bytes 131104 | tf_op jit(solution)/shard_map/ppermute | solution.py:67
  96.0 5.1 %bitcast_add_fusion = f32[8,2,64,1280]{3,2,1,0:T(8,128)S(1)} fusion(f32[8,2,64,1280]{3,2,1,0:T(8,128)} %collective-permute-done.11, f32[8,2,2,64,1280]{4,3,2,1,0:T(8,128)} %bitcast.93, s32[]{:T(128)S(6)} %select_n.221), kind=kLoop, calls=%fused_computation | loop fusion | flops 1310720 | bytes 15728644 | tf_op jit(solution)/shard_map/add | solution.py:53
  101.8 1.8 collective-permute-start.12
  104.1 3.3 %collective-permute-start.9 = (f32[512,64]{1,0:T(8,128)S(1)}, f32[512,64]{1,0:T(8,128)S(1)}, u32[]{:S(2)}, u32[]{:S(2)}) collective-permute-start(f32[512,64]{1,0:T(8,128)S(1)} %bitcast_add_fusion.16), channel_id=1, source_target_pairs={{0,6},{2,0},{4,2},{6,4},{1,7},{3,1},{5,3},{7,5},{8,14},{10,8},{12,... | collective-permute-start | bytes 393224 | tf_op jit(solution)/shard_map/ppermute | solution.py:67
  107.3 3.5 %collective-permute-done.12 = f32[2,64,640]{2,1,0:T(8,128)S(1)} collective-permute-done((f32[2,64,640]{2,1,0:T(8,128)S(1)}, f32[2,64,640]{2,1,0:T(8,128)S(1)}, u32[]{:S(2)}, u32[]{:S(2)}) %collective-permute-start.12) | collective-permute-done | bytes 327712 | tf_op jit(solution)/shard_map/ppermute | solution.py:41
  110.9 2.7 %collective-permute-start.13 = (f32[2,64,640]{2,1,0:T(8,128)S(1)}, f32[2,64,640]{2,1,0:T(8,128)S(1)}, u32[]{:S(2)}, u32[]{:S(2)}) collective-permute-start(f32[2,64,640]{2,1,0:T(8,128)S(1)} %bitcast_add_fusion.14), channel_id=1, source_target_pairs={{0,32},{32,64},{64,96},{96,128},{128,160},{160,192},{192,224},{224... | collective-permute-start | bytes 983048 | tf_op jit(solution)/shard_map/ppermute | solution.py:41
  113.9 5.2 %collective-permute-done.13 = f32[2,64,640]{2,1,0:T(8,128)S(1)} collective-permute-done((f32[2,64,640]{2,1,0:T(8,128)S(1)}, f32[2,64,640]{2,1,0:T(8,128)S(1)}, u32[]{:S(2)}, u32[]{:S(2)}) %collective-permute-start.13) | collective-permute-done | bytes 327712 | tf_op jit(solution)/shard_map/ppermute | solution.py:41
  119.1 3.9 %collective-permute-start.14 = (f32[2,64,640]{2,1,0:T(8,128)S(1)}, f32[2,64,640]{2,1,0:T(8,128)S(1)}, u32[]{:S(2)}, u32[]{:S(2)}) collective-permute-start(f32[2,64,640]{2,1,0:T(8,128)S(1)} %bitcast_add_fusion.13), channel_id=1, source_target_pairs={{0,32},{32,64},{64,96},{96,128},{128,160},{160,192},{192,224},{224... | collective-permute-start | bytes 983048 | tf_op jit(solution)/shard_map/ppermute | solution.py:41
  123.2 4.4 %collective-permute-done.14 = f32[2,64,640]{2,1,0:T(8,128)S(1)} collective-permute-done((f32[2,64,640]{2,1,0:T(8,128)S(1)}, f32[2,64,640]{2,1,0:T(8,128)S(1)}, u32[]{:S(2)}, u32[]{:S(2)}) %collective-permute-start.14) | collective-permute-done | bytes 327712 | tf_op jit(solution)/shard_map/ppermute | solution.py:41
  127.7 3.8 %collective-permute-start.15 = (f32[2,64,640]{2,1,0:T(8,128)S(1)}, f32[2,64,640]{2,1,0:T(8,128)S(1)}, u32[]{:S(2)}, u32[]{:S(2)}) collective-permute-start(f32[2,64,640]{2,1,0:T(8,128)S(1)} %bitcast_add_fusion.12), channel_id=1, source_target_pairs={{0,32},{32,64},{64,96},{96,128},{128,160},{160,192},{192,224},{224... | collective-permute-start | bytes 983048 | tf_op jit(solution)/shard_map/ppermute | solution.py:41
  131.6 5.1 %collective-permute-done.15 = f32[2,64,640]{2,1,0:T(8,128)S(1)} collective-permute-done((f32[2,64,640]{2,1,0:T(8,128)S(1)}, f32[2,64,640]{2,1,0:T(8,128)S(1)}, u32[]{:S(2)}, u32[]{:S(2)}) %collective-permute-start.15) | collective-permute-done | bytes 327712 | tf_op jit(solution)/shard_map/ppermute | solution.py:41
  136.8 3.8 %collective-permute-start.16 = (f32[2,64,640]{2,1,0:T(8,128)S(1)}, f32[2,64,640]{2,1,0:T(8,128)S(1)}, u32[]{:S(2)}, u32[]{:S(2)}) collective-permute-start(f32[2,64,640]{2,1,0:T(8,128)S(1)} %bitcast_add_fusion.11), channel_id=1, source_target_pairs={{0,32},{32,64},{64,96},{96,128},{128,160},{160,192},{192,224},{224... | collective-permute-start | bytes 983048 | tf_op jit(solution)/shard_map/ppermute | solution.py:41
  141.2 5.7 %collective-permute-done.16 = f32[2,64,640]{2,1,0:T(8,128)S(1)} collective-permute-done((f32[2,64,640]{2,1,0:T(8,128)S(1)}, f32[2,64,640]{2,1,0:T(8,128)S(1)}, u32[]{:S(2)}, u32[]{:S(2)}) %collective-permute-start.16) | collective-permute-done | bytes 327712 | tf_op jit(solution)/shard_map/ppermute | solution.py:41
  146.9 3.8 %collective-permute-start.17 = (f32[2,64,640]{2,1,0:T(8,128)S(1)}, f32[2,64,640]{2,1,0:T(8,128)S(1)}, u32[]{:S(2)}, u32[]{:S(2)}) collective-permute-start(f32[2,64,640]{2,1,0:T(8,128)S(1)} %bitcast_add_fusion.10), channel_id=1, source_target_pairs={{0,32},{32,64},{64,96},{96,128},{128,160},{160,192},{192,224},{224... | collective-permute-start | bytes 983048 | tf_op jit(solution)/shard_map/ppermute | solution.py:41
  151.7 6.2 %collective-permute-done.17 = f32[2,64,640]{2,1,0:T(8,128)S(1)} collective-permute-done((f32[2,64,640]{2,1,0:T(8,128)S(1)}, f32[2,64,640]{2,1,0:T(8,128)S(1)}, u32[]{:S(2)}, u32[]{:S(2)}) %collective-permute-start.17) | collective-permute-done | bytes 327712 | tf_op jit(solution)/shard_map/ppermute | solution.py:41
  157.9 3.8 %collective-permute-start.18 = (f32[2,64,640]{2,1,0:T(8,128)S(1)}, f32[2,64,640]{2,1,0:T(8,128)S(1)}, u32[]{:S(2)}, u32[]{:S(2)}) collective-permute-start(f32[2,64,640]{2,1,0:T(8,128)S(1)} %bitcast_add_fusion.9), channel_id=1, source_target_pairs={{0,32},{32,64},{64,96},{96,128},{128,160},{160,192},{192,224},{224... | collective-permute-start | bytes 983048 | tf_op jit(solution)/shard_map/ppermute | solution.py:41
  161.7 1.5 collective-permute-done.24
  163.3 3.0 %collective-permute-done.18 = f32[2,64,640]{2,1,0:T(8,128)S(1)} collective-permute-done((f32[2,64,640]{2,1,0:T(8,128)S(1)}, f32[2,64,640]{2,1,0:T(8,128)S(1)}, u32[]{:S(2)}, u32[]{:S(2)}) %collective-permute-start.18) | collective-permute-done | bytes 327712 | tf_op jit(solution)/shard_map/ppermute | solution.py:41
  166.4 5.2 %collective-permute-done.25 = f32[2,64,640]{2,1,0:T(8,128)S(1)} collective-permute-done((f32[2,64,640]{2,1,0:T(8,128)S(1)}, f32[2,64,640]{2,1,0:T(8,128)S(1)}, u32[]{:S(2)}, u32[]{:S(2)}) %collective-permute-start.25) | collective-permute-done | bytes 327712 | tf_op jit(solution)/shard_map/ppermute | solution.py:41
  171.7 2.0 %collective-permute-start.26 = (f32[64,1280]{1,0:T(8,128)S(1)}, f32[64,1280]{1,0:T(8,128)S(1)}, u32[]{:S(2)}, u32[]{:S(2)}) collective-permute-start(f32[64,1280]{1,0:T(8,128)S(1)} %fusion.29), channel_id=1, source_target_pairs={{0,16},{16,0},{1,17},{17,1},{2,18},{18,2},{3,19},{19,3},{4,20},{20... | collective-permute-start | bytes 983048 | tf_op jit(solution)/shard_map/ppermute | solution.py:53
  173.7 1.1 pad_maximum_fusion.6
  175.0 1.7 add_convert_fusion
  176.7 3.6 %collective-permute-done.26 = f32[64,1280]{1,0:T(8,128)S(1)} collective-permute-done((f32[64,1280]{1,0:T(8,128)S(1)}, f32[64,1280]{1,0:T(8,128)S(1)}, u32[]{:S(2)}, u32[]{:S(2)}) %collective-permute-start.26) | collective-permute-done | bytes 327712 | tf_op jit(solution)/shard_map/ppermute | solution.py:53
  (95 shorter events, 8.7 us)
Async XLA Ops:
  7.2 17.7 %copy-start = (bf16[256,2048]{1,0:T(8,128)(2,1)S(1)}, bf16[256,2048]{1,0:T(8,128)(2,1)}, u32[]{:S(2)}) copy-start(bf16[256,2048]{1,0:T(8,128)(2,1)} %param.8) | copy-start | bytes 3145732
  7.2 166.5 %reduce-scatter.2.cloned.1.call-start = ((), (), s32[]{:S(2)}) async-start(), calls=%async_computation.1 | async-start | bytes 3538944 | tf_op jit(solution)/shard_map/reduce_scatter | solution.py:120
  7.2 4.0 %copy-start.10 = (bf16[2,256,2048]{2,1,0:T(8,128)(2,1)S(1)}, bf16[2,256,2048]{2,1,0:T(8,128)(2,1)}, u32[]{:S(2)}) copy-start(bf16[2,256,2048]{2,1,0:T(8,128)(2,1)} %param.5) | copy-start | bytes 6291460
  11.2 10.4 %copy-start.9 = (s32[2]{0:T(128)S(1)}, s32[2]{0:T(128)}, u32[]{:S(2)}) copy-start(s32[2]{0:T(128)} %param.9) | copy-start | bytes 28
  13.6 17.6 %collective-permute-start = (f32[256,512]{0,1:T(8,128)}, f32[256,512]{0,1:T(8,128)}, u32[]{:S(2)}, u32[]{:S(2)}) collective-permute-start(f32[256,512]{0,1:T(8,128)} %get-tuple-element.15), channel_id=1, source_target_pairs={{0,32},{8,40},{16,48},{24,56},{32,64},{40,72},{48,80},{56,88},{64,... | collective-permute-start | bytes 1572872 | tf_op jit(solution)/shard_map/ppermute | solution.py:16
  18.6 22.7 %collective-permute-start.1 = (f32[256,512]{0,1:T(8,128)}, f32[256,512]{0,1:T(8,128)}, u32[]{:S(2)}, u32[]{:S(2)}) collective-permute-start(f32[256,512]{0,1:T(8,128)} %get-tuple-element.16), channel_id=1, source_target_pairs={{0,32},{8,40},{16,48},{24,56},{32,64},{40,72},{48,80},{56,88},{64,... | collective-permute-start | bytes 1572872 | tf_op jit(solution)/shard_map/ppermute | solution.py:16
  23.5 1.4 copy-start.4
  29.9 12.8 %copy-start.8 = (f32[512,256]{0,1:T(8,128)S(1)}, f32[512,256]{0,1:T(8,128)}, u32[]{:S(2)}) copy-start(f32[512,256]{0,1:T(8,128)} %fusion.48) | copy-start | bytes 1572868
  42.7 17.4 %copy-start.5 = (bf16[2,256,2048]{2,1,0:T(8,128)(2,1)S(1)}, bf16[2,256,2048]{2,1,0:T(8,128)(2,1)}, u32[]{:S(2)}) copy-start(bf16[2,256,2048]{2,1,0:T(8,128)(2,1)} %copy-done.4) | copy-start | bytes 6291460
  42.7 17.4 %copy-start.11 = (bf16[2,256,2048]{2,1,0:T(8,128)(2,1)S(1)}, bf16[2,256,2048]{2,1,0:T(8,128)(2,1)}, u32[]{:S(2)}) copy-start(bf16[2,256,2048]{2,1,0:T(8,128)(2,1)} %param.5) | copy-start | bytes 6291460
  43.1 22.9 %copy-start.6 = (bf16[256,256]{0,1:T(8,128)(2,1)}, bf16[256,256]{0,1:T(8,128)(2,1)S(1)}, u32[]{:S(2)}) copy-start(bf16[256,256]{0,1:T(8,128)(2,1)S(1)} %get-tuple-element.21) | copy-start | bytes 393220
  43.1 13.0 %collective-permute-start.2 = (bf16[256,512]{0,1:T(8,128)(2,1)S(1)}, bf16[256,512]{0,1:T(8,128)(2,1)S(1)}, u32[]{:S(2)}, u32[]{:S(2)}) collective-permute-start(bf16[256,512]{0,1:T(8,128)(2,1)S(1)} %pad_maximum_fusion.7), channel_id=1, source_target_pairs={{32,0},{40,8},{48,16},{56,24},{64,32},{72,40},{80,48},{88,56},{96,... | collective-permute-start | bytes 786440 | tf_op jit(solution)/shard_map/ppermute | solution.py:16
  45.3 14.7 %collective-permute-start.3 = (bf16[256,512]{0,1:T(8,128)(2,1)S(1)}, bf16[256,512]{0,1:T(8,128)(2,1)S(1)}, u32[]{:S(2)}, u32[]{:S(2)}) collective-permute-start(bf16[256,512]{0,1:T(8,128)(2,1)S(1)} %pad_maximum_fusion.8), channel_id=1, source_target_pairs={{32,0},{40,8},{48,16},{56,24},{64,32},{72,40},{80,48},{88,56},{96,... | collective-permute-start | bytes 786440 | tf_op jit(solution)/shard_map/ppermute | solution.py:16
  66.0 5.7 %copy-start.3 = (f32[2048,1280]{1,0:T(8,128)}, f32[2048,1280]{1,0:T(8,128)S(1)}, u32[]{:S(2)}) copy-start(f32[2048,1280]{1,0:T(8,128)S(1)} %fusion) | copy-start | bytes 31457284
  66.0 6.3 %copy-start.7 = (bf16[256,256]{0,1:T(8,128)(2,1)S(1)}, bf16[256,256]{0,1:T(8,128)(2,1)}, u32[]{:S(2)}) copy-start(bf16[256,256]{0,1:T(8,128)(2,1)} %copy-done.6) | copy-start | bytes 393220
  71.7 24.3 %collective-permute-start.11 = (f32[8,2,64,1280]{3,2,1,0:T(8,128)}, f32[8,2,64,1280]{3,2,1,0:T(8,128)}, u32[]{:S(2)}, u32[]{:S(2)}) collective-permute-start(f32[8,2,64,1280]{3,2,1,0:T(8,128)} %dynamic-slice_bitcast_fusion), channel_id=1, source_target_pairs={{0,8},{8,0},{1,9},{9,1},{2,10},{10,2},{3,11},{11,3},{4,12},{12,4},... | collective-permute-start | bytes 15728648 | tf_op jit(solution)/shard_map/ppermute | solution.py:53
  76.4 2.0 %copy-start.2 = (f32[2048,512]{1,0:T(8,128)}, f32[2048,512]{1,0:T(8,128)S(1)}, u32[]{:S(2)}) copy-start(f32[2048,512]{1,0:T(8,128)S(1)} %convolution_add_fusion) | copy-start | bytes 12582916
  78.5 9.3 %collective-permute-start.7 = (f32[512,64]{1,0:T(8,128)S(1)}, f32[512,64]{1,0:T(8,128)S(1)}, u32[]{:S(2)}, u32[]{:S(2)}) collective-permute-start(f32[512,64]{1,0:T(8,128)S(1)} %dynamic-slice_bitcast_fusion.3), channel_id=1, source_target_pairs={{0,6},{2,0},{4,2},{6,4},{1,7},{3,1},{5,3},{7,5},{8,14},{10,8},{12,... | collective-permute-start | bytes 393224 | tf_op jit(solution)/shard_map/ppermute | solution.py:67
  86.1 9.7 %collective-permute-start.4 = (f32[512,64]{1,0:T(8,128)S(1)}, f32[512,64]{1,0:T(8,128)S(1)}, u32[]{:S(2)}, u32[]{:S(2)}) collective-permute-start(f32[512,64]{1,0:T(8,128)S(1)} %dynamic-slice_bitcast_fusion.4), channel_id=1, source_target_pairs={{0,2},{2,4},{4,6},{6,0},{1,3},{3,5},{5,7},{7,1},{8,10},{10,12},{12... | collective-permute-start | bytes 393224 | tf_op jit(solution)/shard_map/ppermute | solution.py:67
  87.9 16.1 %collective-permute-start.8 = (f32[512,64]{1,0:T(8,128)S(1)}, f32[512,64]{1,0:T(8,128)S(1)}, u32[]{:S(2)}, u32[]{:S(2)}) collective-permute-start(f32[512,64]{1,0:T(8,128)S(1)} %bitcast_add_fusion.17), channel_id=1, source_target_pairs={{0,6},{2,0},{4,2},{6,4},{1,7},{3,1},{5,3},{7,5},{8,14},{10,8},{12,... | collective-permute-start | bytes 393224 | tf_op jit(solution)/shard_map/ppermute | solution.py:67
  95.9 17.9 %collective-permute-start.5 = (f32[512,64]{1,0:T(8,128)S(1)}, f32[512,64]{1,0:T(8,128)S(1)}, u32[]{:S(2)}, u32[]{:S(2)}) collective-permute-start(f32[512,64]{1,0:T(8,128)S(1)} %bitcast_add_fusion.20), channel_id=1, source_target_pairs={{0,2},{2,4},{4,6},{6,0},{1,3},{3,5},{5,7},{7,1},{8,10},{10,12},{12... | collective-permute-start | bytes 393224 | tf_op jit(solution)/shard_map/ppermute | solution.py:67
  101.8 9.0 %collective-permute-start.12 = (f32[2,64,640]{2,1,0:T(8,128)S(1)}, f32[2,64,640]{2,1,0:T(8,128)S(1)}, u32[]{:S(2)}, u32[]{:S(2)}) collective-permute-start(f32[2,64,640]{2,1,0:T(8,128)S(1)} %dynamic-slice_bitcast_fusion.2), channel_id=1, source_target_pairs={{0,32},{32,64},{64,96},{96,128},{128,160},{160,192},{192,224},{224... | collective-permute-start | bytes 983048 | tf_op jit(solution)/shard_map/ppermute | solution.py:41
  103.6 10.0 %collective-permute-start.19 = (f32[2,64,640]{2,1,0:T(8,128)S(1)}, f32[2,64,640]{2,1,0:T(8,128)S(1)}, u32[]{:S(2)}, u32[]{:S(2)}) collective-permute-start(f32[2,64,640]{2,1,0:T(8,128)S(1)} %dynamic-slice_bitcast_fusion.1), channel_id=1, source_target_pairs={{0,224},{32,0},{64,32},{96,64},{128,96},{160,128},{192,160},{224,1... | collective-permute-start | bytes 983048 | tf_op jit(solution)/shard_map/ppermute | solution.py:41
  104.1 19.1 %collective-permute-start.9 = (f32[512,64]{1,0:T(8,128)S(1)}, f32[512,64]{1,0:T(8,128)S(1)}, u32[]{:S(2)}, u32[]{:S(2)}) collective-permute-start(f32[512,64]{1,0:T(8,128)S(1)} %bitcast_add_fusion.16), channel_id=1, source_target_pairs={{0,6},{2,0},{4,2},{6,4},{1,7},{3,1},{5,3},{7,5},{8,14},{10,8},{12,... | collective-permute-start | bytes 393224 | tf_op jit(solution)/shard_map/ppermute | solution.py:67
  110.9 8.2 %collective-permute-start.13 = (f32[2,64,640]{2,1,0:T(8,128)S(1)}, f32[2,64,640]{2,1,0:T(8,128)S(1)}, u32[]{:S(2)}, u32[]{:S(2)}) collective-permute-start(f32[2,64,640]{2,1,0:T(8,128)S(1)} %bitcast_add_fusion.14), channel_id=1, source_target_pairs={{0,32},{32,64},{64,96},{96,128},{128,160},{160,192},{192,224},{224... | collective-permute-start | bytes 983048 | tf_op jit(solution)/shard_map/ppermute | solution.py:41
  113.7 9.4 %collective-permute-start.20 = (f32[2,64,640]{2,1,0:T(8,128)S(1)}, f32[2,64,640]{2,1,0:T(8,128)S(1)}, u32[]{:S(2)}, u32[]{:S(2)}) collective-permute-start(f32[2,64,640]{2,1,0:T(8,128)S(1)} %bitcast_add_fusion.7), channel_id=1, source_target_pairs={{0,224},{32,0},{64,32},{96,64},{128,96},{160,128},{192,160},{224,1... | collective-permute-start | bytes 983048 | tf_op jit(solution)/shard_map/ppermute | solution.py:41
  113.8 17.8 %collective-permute-start.6 = (f32[512,64]{1,0:T(8,128)S(1)}, f32[512,64]{1,0:T(8,128)S(1)}, u32[]{:S(2)}, u32[]{:S(2)}) collective-permute-start(f32[512,64]{1,0:T(8,128)S(1)} %bitcast_add_fusion.19), channel_id=1, source_target_pairs={{0,2},{2,4},{4,6},{6,0},{1,3},{3,5},{5,7},{7,1},{8,10},{10,12},{12... | collective-permute-start | bytes 393224 | tf_op jit(solution)/shard_map/ppermute | solution.py:67
  119.1 8.5 %collective-permute-start.14 = (f32[2,64,640]{2,1,0:T(8,128)S(1)}, f32[2,64,640]{2,1,0:T(8,128)S(1)}, u32[]{:S(2)}, u32[]{:S(2)}) collective-permute-start(f32[2,64,640]{2,1,0:T(8,128)S(1)} %bitcast_add_fusion.13), channel_id=1, source_target_pairs={{0,32},{32,64},{64,96},{96,128},{128,160},{160,192},{192,224},{224... | collective-permute-start | bytes 983048 | tf_op jit(solution)/shard_map/ppermute | solution.py:41
  123.1 8.4 %collective-permute-start.21 = (f32[2,64,640]{2,1,0:T(8,128)S(1)}, f32[2,64,640]{2,1,0:T(8,128)S(1)}, u32[]{:S(2)}, u32[]{:S(2)}) collective-permute-start(f32[2,64,640]{2,1,0:T(8,128)S(1)} %bitcast_add_fusion.6), channel_id=1, source_target_pairs={{0,224},{32,0},{64,32},{96,64},{128,96},{160,128},{192,160},{224,1... | collective-permute-start | bytes 983048 | tf_op jit(solution)/shard_map/ppermute | solution.py:41
  127.7 9.1 %collective-permute-start.15 = (f32[2,64,640]{2,1,0:T(8,128)S(1)}, f32[2,64,640]{2,1,0:T(8,128)S(1)}, u32[]{:S(2)}, u32[]{:S(2)}) collective-permute-start(f32[2,64,640]{2,1,0:T(8,128)S(1)} %bitcast_add_fusion.12), channel_id=1, source_target_pairs={{0,32},{32,64},{64,96},{96,128},{128,160},{160,192},{192,224},{224... | collective-permute-start | bytes 983048 | tf_op jit(solution)/shard_map/ppermute | solution.py:41
  131.5 9.4 %collective-permute-start.22 = (f32[2,64,640]{2,1,0:T(8,128)S(1)}, f32[2,64,640]{2,1,0:T(8,128)S(1)}, u32[]{:S(2)}, u32[]{:S(2)}) collective-permute-start(f32[2,64,640]{2,1,0:T(8,128)S(1)} %bitcast_add_fusion.5), channel_id=1, source_target_pairs={{0,224},{32,0},{64,32},{96,64},{128,96},{160,128},{192,160},{224,1... | collective-permute-start | bytes 983048 | tf_op jit(solution)/shard_map/ppermute | solution.py:41
  136.8 10.1 %collective-permute-start.16 = (f32[2,64,640]{2,1,0:T(8,128)S(1)}, f32[2,64,640]{2,1,0:T(8,128)S(1)}, u32[]{:S(2)}, u32[]{:S(2)}) collective-permute-start(f32[2,64,640]{2,1,0:T(8,128)S(1)} %bitcast_add_fusion.11), channel_id=1, source_target_pairs={{0,32},{32,64},{64,96},{96,128},{128,160},{160,192},{192,224},{224... | collective-permute-start | bytes 983048 | tf_op jit(solution)/shard_map/ppermute | solution.py:41
  140.9 10.5 %collective-permute-start.23 = (f32[2,64,640]{2,1,0:T(8,128)S(1)}, f32[2,64,640]{2,1,0:T(8,128)S(1)}, u32[]{:S(2)}, u32[]{:S(2)}) collective-permute-start(f32[2,64,640]{2,1,0:T(8,128)S(1)} %bitcast_add_fusion.4), channel_id=1, source_target_pairs={{0,224},{32,0},{64,32},{96,64},{128,96},{160,128},{192,160},{224,1... | collective-permute-start | bytes 983048 | tf_op jit(solution)/shard_map/ppermute | solution.py:41
  146.9 11.0 %collective-permute-start.17 = (f32[2,64,640]{2,1,0:T(8,128)S(1)}, f32[2,64,640]{2,1,0:T(8,128)S(1)}, u32[]{:S(2)}, u32[]{:S(2)}) collective-permute-start(f32[2,64,640]{2,1,0:T(8,128)S(1)} %bitcast_add_fusion.10), channel_id=1, source_target_pairs={{0,32},{32,64},{64,96},{96,128},{128,160},{160,192},{192,224},{224... | collective-permute-start | bytes 983048 | tf_op jit(solution)/shard_map/ppermute | solution.py:41
  151.5 11.7 %collective-permute-start.24 = (f32[2,64,640]{2,1,0:T(8,128)S(1)}, f32[2,64,640]{2,1,0:T(8,128)S(1)}, u32[]{:S(2)}, u32[]{:S(2)}) collective-permute-start(f32[2,64,640]{2,1,0:T(8,128)S(1)} %bitcast_add_fusion.3), channel_id=1, source_target_pairs={{0,224},{32,0},{64,32},{96,64},{128,96},{160,128},{192,160},{224,1... | collective-permute-start | bytes 983048 | tf_op jit(solution)/shard_map/ppermute | solution.py:41
  151.6 11.7 %collective-permute-start.10 = (f32[256,128]{1,0:T(8,128)S(1)}, f32[256,128]{1,0:T(8,128)S(1)}, u32[]{:S(2)}, u32[]{:S(2)}) collective-permute-start(f32[256,128]{1,0:T(8,128)S(1)} %dynamic-slice_bitcast_fusion.5), channel_id=1, source_target_pairs={{0,1},{1,0},{2,3},{3,2},{4,5},{5,4},{6,7},{7,6},{8,9},{9,8},{10,11... | collective-permute-start | bytes 393224 | tf_op jit(solution)/shard_map/ppermute | solution.py:53
  157.9 8.4 %collective-permute-start.18 = (f32[2,64,640]{2,1,0:T(8,128)S(1)}, f32[2,64,640]{2,1,0:T(8,128)S(1)}, u32[]{:S(2)}, u32[]{:S(2)}) collective-permute-start(f32[2,64,640]{2,1,0:T(8,128)S(1)} %bitcast_add_fusion.9), channel_id=1, source_target_pairs={{0,32},{32,64},{64,96},{96,128},{128,160},{160,192},{192,224},{224... | collective-permute-start | bytes 983048 | tf_op jit(solution)/shard_map/ppermute | solution.py:41
  163.2 8.4 %collective-permute-start.25 = (f32[2,64,640]{2,1,0:T(8,128)S(1)}, f32[2,64,640]{2,1,0:T(8,128)S(1)}, u32[]{:S(2)}, u32[]{:S(2)}) collective-permute-start(f32[2,64,640]{2,1,0:T(8,128)S(1)} %bitcast_add_fusion.2), channel_id=1, source_target_pairs={{0,224},{32,0},{64,32},{96,64},{128,96},{160,128},{192,160},{224,1... | collective-permute-start | bytes 983048 | tf_op jit(solution)/shard_map/ppermute | solution.py:41
  171.7 8.7 %collective-permute-start.26 = (f32[64,1280]{1,0:T(8,128)S(1)}, f32[64,1280]{1,0:T(8,128)S(1)}, u32[]{:S(2)}, u32[]{:S(2)}) collective-permute-start(f32[64,1280]{1,0:T(8,128)S(1)} %fusion.29), channel_id=1, source_target_pairs={{0,16},{16,0},{1,17},{17,1},{2,18},{18,2},{3,19},{19,3},{4,20},{20... | collective-permute-start | bytes 983048 | tf_op jit(solution)/shard_map/ppermute | solution.py:53
  173.7 8.3 %copy-start.1 = (bf16[256,2048]{1,0:T(8,128)(2,1)S(1)}, bf16[256,2048]{1,0:T(8,128)(2,1)}, u32[]{:S(2)}) copy-start(bf16[256,2048]{1,0:T(8,128)(2,1)} %param.8) | copy-start | bytes 3145732
Sparse Core Ops, SparseCore 0:
  86.4 76.3 reduce-scatter.1

commit v16 on v15

--- a/solution.py
+++ b/solution.py
@@ -114,7 +114,7 @@
     branch_grads = jnp.concatenate(grad_parts, axis=0)
     later = jnp.concatenate(later_parts, axis=0)
     partial_value = contract_cols(w_now, branch_grads) + contract_cols(w_dil, later)
-    cut = partial_value.shape[1] * 3 // 4
+    cut = partial_value.shape[1] // 4
     summed = jnp.concatenate(
         [
             lax.psum_scatter(partial_value[:, :cut], CHAN, scatter_dimension=0, tiled=True),

time: 189 us -> 200 us (1.058)
  waiting for transfers between devices: 74.3 us -> 85.2 us
  starting transfers between devices: 49.1 us -> 44.8 us
  local copies, waits for them, and re-layouts: 19.8 us -> 22 us
  other arithmetic: 13.9 us -> 15.9 us
    ppermute x6, waiting for transfers between devices: 5.81 us -> 18.8 us  [chan_ring_reduce_scatter(): got = lax.ppermute(acc, 'cy', pairs)]
    ppermute x14, starting transfers between devices: 24.4 us -> 19.8 us  [ring_sum(): got = lax.ppermute(acc, axis, pairs)]
    ppermute x14, waiting for transfers between devices: 40.8 us -> 38.5 us  [ring_sum(): got = lax.ppermute(acc, axis, pairs)]
    unnamed x25 -> x29, local copies, waits for them, and re-layouts: 5.63 us -> 7.12 us
  transfers between devices with their start and end apart: 28 -> 28, of which waited for: 18 -> 19; matrix products, arithmetic and copies ran while one was open for 14% -> 14% of each run, Pallas kernels for 0% -> 0%
where the time goes in v16:
time: 200 us
  waiting for transfers between devices  85.2 us (43%)
  starting transfers between devices  44.8 us (22%)
  local copies, waits for them, and re-layouts  22 us (11%)
  matrix products  16.4 us (8%)
  other arithmetic  15.9 us (8%)
  between operations  15.4 us (8%)
    ppermute x14, waiting for transfers between devices, ring_sum(): got = lax.ppermute(acc, axis, pairs)  38.5 us
    ppermute x4, waiting for transfers between devices, shifted(): return lax.ppermute(x, axis, pairs)  24.1 us
    ppermute x14, starting transfers between devices, ring_sum(): got = lax.ppermute(acc, axis, pairs)  19.8 us
    ppermute x6, waiting for transfers between devices, chan_ring_reduce_scatter(): got = lax.ppermute(acc, 'cy', pairs)  18.8 us
    ppermute x4, starting transfers between devices, shifted(): return lax.ppermute(x, axis, pairs)  12.1 us
    ppermute x6, starting transfers between devices, chan_ring_reduce_scatter(): got = lax.ppermute(acc, 'cy', pairs)  10.8 us
    unnamed x29, local copies, waits for them, and re-layouts  7.12 us
    dot_general x1, matrix products, contract_rows(): lax.dot_general(left, right, (((0,), (0,)), ((), ())), preferred_element_...  5.87 us
  transfers between devices with their start and end apart: 28, of which 19 were waited for; matrix products, arithmetic and copies ran while one was open for 14% of the time, Pallas kernels for 0%

profile of v16, /device:TPU:98, one launch (start us, length us, event | category | flops | bytes accessed | tf_op | source)
XLA Modules:
  0.0 199.7 jit_solution(18050973074501434835)
XLA Ops:
  7.2 4.0 %slice_bitcast_fusion.1 = (bf16[2048,256]{1,0:T(8,128)(2,1)S(1)}, bf16[2048,256]{1,0:T(8,128)(2,1)}, bf16[2048,256]{1,0:T(8,128)(2,1)}, bf16[2048,256]{1,0:T(8,128)(2,1)S(1)}) fusion(bf16[2,2,2048,256]{3,2,1,0:T(8,128)(2,1)} %param.7), kind=kLoop, calls=%fused_computation.31 | loop fusion | bytes 8388608 | tf_op jit(solution)/shard_map/squeeze | solution.py:91
  11.2 1.3 convolution_bitcast_fusion
  13.6 5.0 %collective-permute-start = (f32[256,512]{0,1:T(8,128)}, f32[256,512]{0,1:T(8,128)}, u32[]{:S(2)}, u32[]{:S(2)}) collective-permute-start(f32[256,512]{0,1:T(8,128)} %get-tuple-element.15), channel_id=1, source_target_pairs={{0,32},{8,40},{16,48},{24,56},{32,64},{40,72},{48,80},{56,88},{64,... | collective-permute-start | bytes 1572872 | tf_op jit(solution)/shard_map/ppermute | solution.py:16
  18.6 2.9 %collective-permute-start.1 = (f32[256,512]{0,1:T(8,128)}, f32[256,512]{0,1:T(8,128)}, u32[]{:S(2)}, u32[]{:S(2)}) collective-permute-start(f32[256,512]{0,1:T(8,128)} %get-tuple-element.16), channel_id=1, source_target_pairs={{0,32},{8,40},{16,48},{24,56},{32,64},{40,72},{48,80},{56,88},{64,... | collective-permute-start | bytes 1572872 | tf_op jit(solution)/shard_map/ppermute | solution.py:16
  21.7 1.8 broadcast_select_fusion
  23.5 1.3 copy-done.6
  24.8 1.5 fusion.48
  26.4 3.5 %convolution_bitcast_fusion.1 = f32[512,512]{0,1:T(8,128)S(1)} fusion(bf16[512,2048]{1,0:T(8,128)(2,1)} %bitcast.101, bf16[2048,256]{1,0:T(8,128)(2,1)} %get-tuple-element.6, bf16[2048,256]{1,0:T(8,128)(2,1)} %get-tuple-element.7), kind=kOutput, calls=%fused_computation.27 | convolution fusion | flops 1077936128 | bytes 5242880 | tf_op jit(solution)/shard_map/dot_general | solution.py:93
  29.9 1.3 collective-permute-done
  31.2 10.1 %collective-permute-done.1 = f32[256,512]{0,1:T(8,128)} collective-permute-done((f32[256,512]{0,1:T(8,128)}, f32[256,512]{0,1:T(8,128)}, u32[]{:S(2)}, u32[]{:S(2)}) %collective-permute-start.1) | collective-permute-done | bytes 524320 | tf_op jit(solution)/shard_map/ppermute | solution.py:16
  41.3 1.4 slice_add_fusion.1
  43.1 2.2 %collective-permute-start.2 = (bf16[256,512]{0,1:T(8,128)(2,1)S(1)}, bf16[256,512]{0,1:T(8,128)(2,1)S(1)}, u32[]{:S(2)}, u32[]{:S(2)}) collective-permute-start(bf16[256,512]{0,1:T(8,128)(2,1)S(1)} %pad_maximum_fusion.8), channel_id=1, source_target_pairs={{32,0},{40,8},{48,16},{56,24},{64,32},{72,40},{80,48},{88,56},{96,... | collective-permute-start | bytes 786440 | tf_op jit(solution)/shard_map/ppermute | solution.py:16
  45.3 1.9 collective-permute-start.3
  47.4 8.8 %collective-permute-done.2 = bf16[256,512]{0,1:T(8,128)(2,1)S(1)} collective-permute-done((bf16[256,512]{0,1:T(8,128)(2,1)S(1)}, bf16[256,512]{0,1:T(8,128)(2,1)S(1)}, u32[]{:S(2)}, u32[]{:S(2)}) %collective-permute-start.2) | collective-permute-done | bytes 262176 | tf_op jit(solution)/shard_map/ppermute | solution.py:16
  56.2 3.9 %collective-permute-done.3 = bf16[256,512]{0,1:T(8,128)(2,1)S(1)} collective-permute-done((bf16[256,512]{0,1:T(8,128)(2,1)S(1)}, bf16[256,512]{0,1:T(8,128)(2,1)S(1)}, u32[]{:S(2)}, u32[]{:S(2)}) %collective-permute-start.3) | collective-permute-done | bytes 262176 | tf_op jit(solution)/shard_map/ppermute | solution.py:16
  60.1 5.9 %fusion = f32[2048,1280]{1,0:T(8,128)S(1)} fusion(bf16[512,2048]{1,0:T(8,128)(2,1)S(1)} %bitcast.98, bf16[512,2048]{1,0:T(8,128)(2,1)S(1)} %bitcast.103, bf16[512,1280]{0,1:T(8,128)(2,1)S(1)} %fusion.20, bf16[512,256]{0,1:T(8,128)(2,1)S(1)} %broadcast_in_dim.19, bf16[512,512]{0,1:T(8,128)(2,1)S(1)} %constant_dynamic-update-slice_fusion, ...), kind=kOutput, calls=%fused_computation.2 | convolution fusion | flops 5395447808 | bytes 17301504 | tf_op jit(solution)/shard_map/dot_general | solution.py:20
  66.0 3.0 %dynamic-slice_bitcast_fusion = f32[8,2,64,1280]{3,2,1,0:T(8,128)} fusion(f32[8,2,2,64,1280]{4,3,2,1,0:T(8,128)S(1)} %bitcast.93, s32[]{:T(128)S(6)} %select_n.222), kind=kLoop, calls=%fused_computation.1 | loop fusion | bytes 10485764 | tf_op jit(solution)/shard_map/jit(dynamic_index_in_dim)/squeeze | solution.py:52
  69.0 2.7 %copy-done.3 = f32[2048,1280]{1,0:T(8,128)} copy-done((f32[2048,1280]{1,0:T(8,128)}, f32[2048,1280]{1,0:T(8,128)S(1)}, u32[]{:S(2)}) %copy-start.3) | copy-done | bytes 10485784
  71.7 2.9 %fusion.19 = f32[2048,512]{1,0:T(8,128)S(1)} fusion(bf16[2048,256]{1,0:T(8,128)(2,1)} %get-tuple-element.6, bf16[2048,256]{1,0:T(8,128)(2,1)} %get-tuple-element.7, bf16[256,256]{0,1:T(8,128)(2,1)S(1)} %get-tuple-element.20, bf16[256,256]{0,1:T(8,128)(2,1)S(1)} %copy-done.9, bf16[256,256]{0,1:T(8,128)(2,1)S(1)} %get-tuple-element.12, ...), kind=kOutput, calls=%fused_computation.28 | convolution fusion | flops 1080033280 | bytes 6815744 | tf_op jit(solution)/shard_map/dot_general | solution.py:26
  74.5 1.3 convolution_add_fusion
  76.2 1.7 copy-done.2
  78.6 1.4 copy-done.4
  80.8 3.0 %collective-permute-start.7 = (f32[512,192]{1,0:T(8,128)}, f32[512,192]{1,0:T(8,128)S(1)}, u32[]{:S(2)}, u32[]{:S(2)}) collective-permute-start(f32[512,192]{1,0:T(8,128)} %dynamic-slice_bitcast_fusion.1), channel_id=1, source_target_pairs={{0,6},{2,0},{4,2},{6,4},{1,7},{3,1},{5,3},{7,5},{8,14},{10,8},{12,... | collective-permute-start | bytes 1179656 | tf_op jit(solution)/shard_map/ppermute | solution.py:67
  86.0 2.3 %slice.98 = f32[2048,128]{1,0:T(8,128)} slice(f32[2048,512]{1,0:T(8,128)} %copy-done.2), slice={[0:2048], [0:128]} | slice | bytes 2097152 | tf_op jit(solution)/shard_map/slice | solution.py:120
  88.3 7.6 %collective-permute-done.7 = f32[512,192]{1,0:T(8,128)S(1)} collective-permute-done((f32[512,192]{1,0:T(8,128)}, f32[512,192]{1,0:T(8,128)S(1)}, u32[]{:S(2)}, u32[]{:S(2)}) %collective-permute-start.7) | collective-permute-done | bytes 393248 | tf_op jit(solution)/shard_map/ppermute | solution.py:67
  96.0 1.1 bitcast_add_fusion.3
  97.1 3.7 %collective-permute-start.8 = (f32[512,192]{1,0:T(8,128)S(1)}, f32[512,192]{1,0:T(8,128)S(1)}, u32[]{:S(2)}, u32[]{:S(2)}) collective-permute-start(f32[512,192]{1,0:T(8,128)S(1)} %bitcast_add_fusion.3), channel_id=1, source_target_pairs={{0,6},{2,0},{4,2},{6,4},{1,7},{3,1},{5,3},{7,5},{8,14},{10,8},{12,... | collective-permute-start | bytes 1179656 | tf_op jit(solution)/shard_map/ppermute | solution.py:67
  100.9 4.8 %bitcast_add_fusion = f32[8,2,64,1280]{3,2,1,0:T(8,128)S(1)} fusion(f32[8,2,64,1280]{3,2,1,0:T(8,128)} %collective-permute-done.11, f32[8,2,2,64,1280]{4,3,2,1,0:T(8,128)} %bitcast.94, s32[]{:T(128)S(6)} %select_n.221), kind=kLoop, calls=%fused_computation | loop fusion | flops 1310720 | bytes 15728644 | tf_op jit(solution)/shard_map/add | solution.py:53
  106.5 1.8 collective-permute-start.12
  108.7 9.3 %collective-permute-done.8 = f32[512,192]{1,0:T(8,128)S(1)} collective-permute-done((f32[512,192]{1,0:T(8,128)S(1)}, f32[512,192]{1,0:T(8,128)S(1)}, u32[]{:S(2)}, u32[]{:S(2)}) %collective-permute-start.8) | collective-permute-done | bytes 393248 | tf_op jit(solution)/shard_map/ppermute | solution.py:67
  118.0 3.7 %collective-permute-start.9 = (f32[512,192]{1,0:T(8,128)S(1)}, f32[512,192]{1,0:T(8,128)S(1)}, u32[]{:S(2)}, u32[]{:S(2)}) collective-permute-start(f32[512,192]{1,0:T(8,128)S(1)} %bitcast_add_fusion.2), channel_id=1, source_target_pairs={{0,6},{2,0},{4,2},{6,4},{1,7},{3,1},{5,3},{7,5},{8,14},{10,8},{12,... | collective-permute-start | bytes 1179656 | tf_op jit(solution)/shard_map/ppermute | solution.py:67
  121.8 1.3 collective-permute-start.13
  124.4 5.7 %collective-permute-done.13 = f32[2,64,640]{2,1,0:T(8,128)S(1)} collective-permute-done((f32[2,64,640]{2,1,0:T(8,128)S(1)}, f32[2,64,640]{2,1,0:T(8,128)S(1)}, u32[]{:S(2)}, u32[]{:S(2)}) %collective-permute-start.13) | collective-permute-done | bytes 327712 | tf_op jit(solution)/shard_map/ppermute | solution.py:41
  130.1 1.8 collective-permute-start.14
  132.4 1.9 collective-permute-done.9
  134.4 3.6 %collective-permute-done.14 = f32[2,64,640]{2,1,0:T(8,128)S(1)} collective-permute-done((f32[2,64,640]{2,1,0:T(8,128)S(1)}, f32[2,64,640]{2,1,0:T(8,128)S(1)}, u32[]{:S(2)}, u32[]{:S(2)}) %collective-permute-start.14) | collective-permute-done | bytes 327712 | tf_op jit(solution)/shard_map/ppermute | solution.py:41
  138.0 2.3 %collective-permute-start.15 = (f32[2,64,640]{2,1,0:T(8,128)S(1)}, f32[2,64,640]{2,1,0:T(8,128)S(1)}, u32[]{:S(2)}, u32[]{:S(2)}) collective-permute-start(f32[2,64,640]{2,1,0:T(8,128)S(1)} %bitcast_add_fusion.19), channel_id=1, source_target_pairs={{0,32},{32,64},{64,96},{96,128},{128,160},{160,192},{192,224},{224... | collective-permute-start | bytes 983048 | tf_op jit(solution)/shard_map/ppermute | solution.py:41
  140.7 5.9 %collective-permute-done.15 = f32[2,64,640]{2,1,0:T(8,128)S(1)} collective-permute-done((f32[2,64,640]{2,1,0:T(8,128)S(1)}, f32[2,64,640]{2,1,0:T(8,128)S(1)}, u32[]{:S(2)}, u32[]{:S(2)}) %collective-permute-start.15) | collective-permute-done | bytes 327712 | tf_op jit(solution)/shard_map/ppermute | solution.py:41
  146.6 3.1 %collective-permute-start.16 = (f32[2,64,640]{2,1,0:T(8,128)S(1)}, f32[2,64,640]{2,1,0:T(8,128)S(1)}, u32[]{:S(2)}, u32[]{:S(2)}) collective-permute-start(f32[2,64,640]{2,1,0:T(8,128)S(1)} %bitcast_add_fusion.18), channel_id=1, source_target_pairs={{0,32},{32,64},{64,96},{96,128},{128,160},{160,192},{192,224},{224... | collective-permute-start | bytes 983048 | tf_op jit(solution)/shard_map/ppermute | solution.py:41
  150.6 6.0 %collective-permute-done.16 = f32[2,64,640]{2,1,0:T(8,128)S(1)} collective-permute-done((f32[2,64,640]{2,1,0:T(8,128)S(1)}, f32[2,64,640]{2,1,0:T(8,128)S(1)}, u32[]{:S(2)}, u32[]{:S(2)}) %collective-permute-start.16) | collective-permute-done | bytes 327712 | tf_op jit(solution)/shard_map/ppermute | solution.py:41
  156.6 3.8 %collective-permute-start.17 = (f32[2,64,640]{2,1,0:T(8,128)S(1)}, f32[2,64,640]{2,1,0:T(8,128)S(1)}, u32[]{:S(2)}, u32[]{:S(2)}) collective-permute-start(f32[2,64,640]{2,1,0:T(8,128)S(1)} %bitcast_add_fusion.17), channel_id=1, source_target_pairs={{0,32},{32,64},{64,96},{96,128},{128,160},{160,192},{192,224},{224... | collective-permute-start | bytes 983048 | tf_op jit(solution)/shard_map/ppermute | solution.py:41
  161.4 6.9 %collective-permute-done.17 = f32[2,64,640]{2,1,0:T(8,128)S(1)} collective-permute-done((f32[2,64,640]{2,1,0:T(8,128)S(1)}, f32[2,64,640]{2,1,0:T(8,128)S(1)}, u32[]{:S(2)}, u32[]{:S(2)}) %collective-permute-start.17) | collective-permute-done | bytes 327712 | tf_op jit(solution)/shard_map/ppermute | solution.py:41
  168.4 3.8 %collective-permute-start.18 = (f32[2,64,640]{2,1,0:T(8,128)S(1)}, f32[2,64,640]{2,1,0:T(8,128)S(1)}, u32[]{:S(2)}, u32[]{:S(2)}) collective-permute-start(f32[2,64,640]{2,1,0:T(8,128)S(1)} %bitcast_add_fusion.16), channel_id=1, source_target_pairs={{0,32},{32,64},{64,96},{96,128},{128,160},{160,192},{192,224},{224... | collective-permute-start | bytes 983048 | tf_op jit(solution)/shard_map/ppermute | solution.py:41
  173.1 3.6 %collective-permute-done.18 = f32[2,64,640]{2,1,0:T(8,128)S(1)} collective-permute-done((f32[2,64,640]{2,1,0:T(8,128)S(1)}, f32[2,64,640]{2,1,0:T(8,128)S(1)}, u32[]{:S(2)}, u32[]{:S(2)}) %collective-permute-start.18) | collective-permute-done | bytes 327712 | tf_op jit(solution)/shard_map/ppermute | solution.py:41
  176.8 4.5 %collective-permute-done.25 = f32[2,64,640]{2,1,0:T(8,128)S(1)} collective-permute-done((f32[2,64,640]{2,1,0:T(8,128)S(1)}, f32[2,64,640]{2,1,0:T(8,128)S(1)}, u32[]{:S(2)}, u32[]{:S(2)}) %collective-permute-start.25) | collective-permute-done | bytes 327712 | tf_op jit(solution)/shard_map/ppermute | solution.py:41
  181.4 2.0 collective-permute-start.26
  184.7 1.7 add_convert_fusion
  186.4 3.8 %collective-permute-done.26 = f32[64,1280]{1,0:T(8,128)} collective-permute-done((f32[64,1280]{1,0:T(8,128)S(1)}, f32[64,1280]{1,0:T(8,128)}, u32[]{:S(2)}, u32[]{:S(2)}) %collective-permute-start.26) | collective-permute-done | bytes 327712 | tf_op jit(solution)/shard_map/ppermute | solution.py:53
  (99 shorter events, 15.6 us)
Async XLA Ops:
  7.2 17.6 %copy-start = (bf16[256,2048]{1,0:T(8,128)(2,1)S(1)}, bf16[256,2048]{1,0:T(8,128)(2,1)}, u32[]{:S(2)}) copy-start(bf16[256,2048]{1,0:T(8,128)(2,1)} %param.8) | copy-start | bytes 3145732
  7.2 176.2 %reduce-scatter.2.cloned.1.call-start = ((), (), s32[]{:S(2)}) async-start(), calls=%async_computation.1 | async-start | bytes 1179648 | tf_op jit(solution)/shard_map/reduce_scatter | solution.py:120
  7.2 4.0 %copy-start.12 = (bf16[2,256,2048]{2,1,0:T(8,128)(2,1)S(1)}, bf16[2,256,2048]{2,1,0:T(8,128)(2,1)}, u32[]{:S(2)}) copy-start(bf16[2,256,2048]{2,1,0:T(8,128)(2,1)} %param.5) | copy-start | bytes 6291460
  11.2 10.4 %copy-start.11 = (s32[2]{0:T(128)S(1)}, s32[2]{0:T(128)}, u32[]{:S(2)}) copy-start(s32[2]{0:T(128)} %param.9) | copy-start | bytes 28
  13.6 17.6 %collective-permute-start = (f32[256,512]{0,1:T(8,128)}, f32[256,512]{0,1:T(8,128)}, u32[]{:S(2)}, u32[]{:S(2)}) collective-permute-start(f32[256,512]{0,1:T(8,128)} %get-tuple-element.15), channel_id=1, source_target_pairs={{0,32},{8,40},{16,48},{24,56},{32,64},{40,72},{48,80},{56,88},{64,... | collective-permute-start | bytes 1572872 | tf_op jit(solution)/shard_map/ppermute | solution.py:16
  18.6 22.7 %collective-permute-start.1 = (f32[256,512]{0,1:T(8,128)}, f32[256,512]{0,1:T(8,128)}, u32[]{:S(2)}, u32[]{:S(2)}) collective-permute-start(f32[256,512]{0,1:T(8,128)} %get-tuple-element.16), channel_id=1, source_target_pairs={{0,32},{8,40},{16,48},{24,56},{32,64},{40,72},{48,80},{56,88},{64,... | collective-permute-start | bytes 1572872 | tf_op jit(solution)/shard_map/ppermute | solution.py:16
  23.5 1.3 copy-start.6
  29.9 12.8 %copy-start.10 = (f32[512,256]{0,1:T(8,128)S(1)}, f32[512,256]{0,1:T(8,128)}, u32[]{:S(2)}) copy-start(f32[512,256]{0,1:T(8,128)} %fusion.48) | copy-start | bytes 1572868
  42.7 17.4 %copy-start.7 = (bf16[2,256,2048]{2,1,0:T(8,128)(2,1)S(1)}, bf16[2,256,2048]{2,1,0:T(8,128)(2,1)}, u32[]{:S(2)}) copy-start(bf16[2,256,2048]{2,1,0:T(8,128)(2,1)} %copy-done.6) | copy-start | bytes 6291460
  42.7 17.4 %copy-start.13 = (bf16[2,256,2048]{2,1,0:T(8,128)(2,1)S(1)}, bf16[2,256,2048]{2,1,0:T(8,128)(2,1)}, u32[]{:S(2)}) copy-start(bf16[2,256,2048]{2,1,0:T(8,128)(2,1)} %param.5) | copy-start | bytes 6291460
  43.1 22.9 %copy-start.8 = (bf16[256,256]{0,1:T(8,128)(2,1)}, bf16[256,256]{0,1:T(8,128)(2,1)S(1)}, u32[]{:S(2)}) copy-start(bf16[256,256]{0,1:T(8,128)(2,1)S(1)} %get-tuple-element.21) | copy-start | bytes 393220
  43.1 13.0 %collective-permute-start.2 = (bf16[256,512]{0,1:T(8,128)(2,1)S(1)}, bf16[256,512]{0,1:T(8,128)(2,1)S(1)}, u32[]{:S(2)}, u32[]{:S(2)}) collective-permute-start(bf16[256,512]{0,1:T(8,128)(2,1)S(1)} %pad_maximum_fusion.8), channel_id=1, source_target_pairs={{32,0},{40,8},{48,16},{56,24},{64,32},{72,40},{80,48},{88,56},{96,... | collective-permute-start | bytes 786440 | tf_op jit(solution)/shard_map/ppermute | solution.py:16
  45.3 14.7 %collective-permute-start.3 = (bf16[256,512]{0,1:T(8,128)(2,1)S(1)}, bf16[256,512]{0,1:T(8,128)(2,1)S(1)}, u32[]{:S(2)}, u32[]{:S(2)}) collective-permute-start(bf16[256,512]{0,1:T(8,128)(2,1)S(1)} %pad_maximum_fusion.9), channel_id=1, source_target_pairs={{32,0},{40,8},{48,16},{56,24},{64,32},{72,40},{80,48},{88,56},{96,... | collective-permute-start | bytes 786440 | tf_op jit(solution)/shard_map/ppermute | solution.py:16
  66.0 5.7 %copy-start.3 = (f32[2048,1280]{1,0:T(8,128)}, f32[2048,1280]{1,0:T(8,128)S(1)}, u32[]{:S(2)}) copy-start(f32[2048,1280]{1,0:T(8,128)S(1)} %fusion) | copy-start | bytes 31457284
  66.0 5.7 %copy-start.9 = (bf16[256,256]{0,1:T(8,128)(2,1)S(1)}, bf16[256,256]{0,1:T(8,128)(2,1)}, u32[]{:S(2)}) copy-start(bf16[256,256]{0,1:T(8,128)(2,1)} %copy-done.8) | copy-start | bytes 393220
  71.7 29.2 %collective-permute-start.11 = (f32[8,2,64,1280]{3,2,1,0:T(8,128)}, f32[8,2,64,1280]{3,2,1,0:T(8,128)}, u32[]{:S(2)}, u32[]{:S(2)}) collective-permute-start(f32[8,2,64,1280]{3,2,1,0:T(8,128)} %dynamic-slice_bitcast_fusion), channel_id=1, source_target_pairs={{0,8},{8,0},{1,9},{9,1},{2,10},{10,2},{3,11},{11,3},{4,12},{12,4},... | collective-permute-start | bytes 15728648 | tf_op jit(solution)/shard_map/ppermute | solution.py:53
  75.8 2.0 %copy-start.2 = (f32[2048,512]{1,0:T(8,128)}, f32[2048,512]{1,0:T(8,128)S(1)}, u32[]{:S(2)}) copy-start(f32[2048,512]{1,0:T(8,128)S(1)} %convolution_add_fusion) | copy-start | bytes 12582916
  78.6 1.4 copy-start.4
  80.8 15.2 %collective-permute-start.7 = (f32[512,192]{1,0:T(8,128)}, f32[512,192]{1,0:T(8,128)S(1)}, u32[]{:S(2)}, u32[]{:S(2)}) collective-permute-start(f32[512,192]{1,0:T(8,128)} %dynamic-slice_bitcast_fusion.1), channel_id=1, source_target_pairs={{0,6},{2,0},{4,2},{6,4},{1,7},{3,1},{5,3},{7,5},{8,14},{10,8},{12,... | collective-permute-start | bytes 1179656 | tf_op jit(solution)/shard_map/ppermute | solution.py:67
  84.6 16.1 %collective-permute-start.4 = (f32[512,192]{1,0:T(8,128)}, f32[512,192]{1,0:T(8,128)S(1)}, u32[]{:S(2)}, u32[]{:S(2)}) collective-permute-start(f32[512,192]{1,0:T(8,128)} %dynamic-slice_bitcast_fusion.2), channel_id=1, source_target_pairs={{0,2},{2,4},{4,6},{6,0},{1,3},{3,5},{5,7},{7,1},{8,10},{10,12},{12... | collective-permute-start | bytes 1179656 | tf_op jit(solution)/shard_map/ppermute | solution.py:67
  97.1 20.8 %collective-permute-start.8 = (f32[512,192]{1,0:T(8,128)S(1)}, f32[512,192]{1,0:T(8,128)S(1)}, u32[]{:S(2)}, u32[]{:S(2)}) collective-permute-start(f32[512,192]{1,0:T(8,128)S(1)} %bitcast_add_fusion.3), channel_id=1, source_target_pairs={{0,6},{2,0},{4,2},{6,4},{1,7},{3,1},{5,3},{7,5},{8,14},{10,8},{12,... | collective-permute-start | bytes 1179656 | tf_op jit(solution)/shard_map/ppermute | solution.py:67
  100.8 23.2 %collective-permute-start.5 = (f32[512,192]{1,0:T(8,128)S(1)}, f32[512,192]{1,0:T(8,128)S(1)}, u32[]{:S(2)}, u32[]{:S(2)}) collective-permute-start(f32[512,192]{1,0:T(8,128)S(1)} %bitcast_add_fusion.6), channel_id=1, source_target_pairs={{0,2},{2,4},{4,6},{6,0},{1,3},{3,5},{5,7},{7,1},{8,10},{10,12},{12... | collective-permute-start | bytes 1179656 | tf_op jit(solution)/shard_map/ppermute | solution.py:67
  105.7 12.2 %copy-start.5 = (f32[4,512,192]{2,1,0:T(8,128)S(1)}, f32[4,512,192]{2,1,0:T(8,128)}, u32[]{:S(2)}) copy-start(f32[4,512,192]{2,1,0:T(8,128)} %copy-done.4) | copy-start | bytes 4718596
  106.5 15.3 %collective-permute-start.12 = (f32[2,64,640]{2,1,0:T(8,128)S(1)}, f32[2,64,640]{2,1,0:T(8,128)S(1)}, u32[]{:S(2)}, u32[]{:S(2)}) collective-permute-start(f32[2,64,640]{2,1,0:T(8,128)S(1)} %dynamic-slice_bitcast_fusion.5), channel_id=1, source_target_pairs={{0,32},{32,64},{64,96},{96,128},{128,160},{160,192},{192,224},{224... | collective-permute-start | bytes 983048 | tf_op jit(solution)/shard_map/ppermute | solution.py:41
  108.3 14.8 %collective-permute-start.19 = (f32[2,64,640]{2,1,0:T(8,128)S(1)}, f32[2,64,640]{2,1,0:T(8,128)S(1)}, u32[]{:S(2)}, u32[]{:S(2)}) collective-permute-start(f32[2,64,640]{2,1,0:T(8,128)S(1)} %dynamic-slice_bitcast_fusion.4), channel_id=1, source_target_pairs={{0,224},{32,0},{64,32},{96,64},{128,96},{160,128},{192,160},{224,1... | collective-permute-start | bytes 983048 | tf_op jit(solution)/shard_map/ppermute | solution.py:41
  118.0 16.3 %collective-permute-start.9 = (f32[512,192]{1,0:T(8,128)S(1)}, f32[512,192]{1,0:T(8,128)S(1)}, u32[]{:S(2)}, u32[]{:S(2)}) collective-permute-start(f32[512,192]{1,0:T(8,128)S(1)} %bitcast_add_fusion.2), channel_id=1, source_target_pairs={{0,6},{2,0},{4,2},{6,4},{1,7},{3,1},{5,3},{7,5},{8,14},{10,8},{12,... | collective-permute-start | bytes 1179656 | tf_op jit(solution)/shard_map/ppermute | solution.py:67
  121.8 8.3 %collective-permute-start.13 = (f32[2,64,640]{2,1,0:T(8,128)S(1)}, f32[2,64,640]{2,1,0:T(8,128)S(1)}, u32[]{:S(2)}, u32[]{:S(2)}) collective-permute-start(f32[2,64,640]{2,1,0:T(8,128)S(1)} %bitcast_add_fusion.21), channel_id=1, source_target_pairs={{0,32},{32,64},{64,96},{96,128},{128,160},{160,192},{192,224},{224... | collective-permute-start | bytes 983048 | tf_op jit(solution)/shard_map/ppermute | solution.py:41
  123.1 8.8 %collective-permute-start.20 = (f32[2,64,640]{2,1,0:T(8,128)S(1)}, f32[2,64,640]{2,1,0:T(8,128)S(1)}, u32[]{:S(2)}, u32[]{:S(2)}) collective-permute-start(f32[2,64,640]{2,1,0:T(8,128)S(1)} %bitcast_add_fusion.14), channel_id=1, source_target_pairs={{0,224},{32,0},{64,32},{96,64},{128,96},{160,128},{192,160},{224,1... | collective-permute-start | bytes 983048 | tf_op jit(solution)/shard_map/ppermute | solution.py:41
  124.1 16.5 %collective-permute-start.6 = (f32[512,192]{1,0:T(8,128)S(1)}, f32[512,192]{1,0:T(8,128)S(1)}, u32[]{:S(2)}, u32[]{:S(2)}) collective-permute-start(f32[512,192]{1,0:T(8,128)S(1)} %bitcast_add_fusion.5), channel_id=1, source_target_pairs={{0,2},{2,4},{4,6},{6,0},{1,3},{3,5},{5,7},{7,1},{8,10},{10,12},{12... | collective-permute-start | bytes 1179656 | tf_op jit(solution)/shard_map/ppermute | solution.py:67
  130.1 7.8 %collective-permute-start.14 = (f32[2,64,640]{2,1,0:T(8,128)S(1)}, f32[2,64,640]{2,1,0:T(8,128)S(1)}, u32[]{:S(2)}, u32[]{:S(2)}) collective-permute-start(f32[2,64,640]{2,1,0:T(8,128)S(1)} %bitcast_add_fusion.20), channel_id=1, source_target_pairs={{0,32},{32,64},{64,96},{96,128},{128,160},{160,192},{192,224},{224... | collective-permute-start | bytes 983048 | tf_op jit(solution)/shard_map/ppermute | solution.py:41
  131.9 8.6 %collective-permute-start.21 = (f32[2,64,640]{2,1,0:T(8,128)S(1)}, f32[2,64,640]{2,1,0:T(8,128)S(1)}, u32[]{:S(2)}, u32[]{:S(2)}) collective-permute-start(f32[2,64,640]{2,1,0:T(8,128)S(1)} %bitcast_add_fusion.13), channel_id=1, source_target_pairs={{0,224},{32,0},{64,32},{96,64},{128,96},{160,128},{192,160},{224,1... | collective-permute-start | bytes 983048 | tf_op jit(solution)/shard_map/ppermute | solution.py:41
  138.0 8.6 %collective-permute-start.15 = (f32[2,64,640]{2,1,0:T(8,128)S(1)}, f32[2,64,640]{2,1,0:T(8,128)S(1)}, u32[]{:S(2)}, u32[]{:S(2)}) collective-permute-start(f32[2,64,640]{2,1,0:T(8,128)S(1)} %bitcast_add_fusion.19), channel_id=1, source_target_pairs={{0,32},{32,64},{64,96},{96,128},{128,160},{160,192},{192,224},{224... | collective-permute-start | bytes 983048 | tf_op jit(solution)/shard_map/ppermute | solution.py:41
  140.5 9.7 %collective-permute-start.22 = (f32[2,64,640]{2,1,0:T(8,128)S(1)}, f32[2,64,640]{2,1,0:T(8,128)S(1)}, u32[]{:S(2)}, u32[]{:S(2)}) collective-permute-start(f32[2,64,640]{2,1,0:T(8,128)S(1)} %bitcast_add_fusion.12), channel_id=1, source_target_pairs={{0,224},{32,0},{64,32},{96,64},{128,96},{160,128},{192,160},{224,1... | collective-permute-start | bytes 983048 | tf_op jit(solution)/shard_map/ppermute | solution.py:41
  146.6 9.9 %collective-permute-start.16 = (f32[2,64,640]{2,1,0:T(8,128)S(1)}, f32[2,64,640]{2,1,0:T(8,128)S(1)}, u32[]{:S(2)}, u32[]{:S(2)}) collective-permute-start(f32[2,64,640]{2,1,0:T(8,128)S(1)} %bitcast_add_fusion.18), channel_id=1, source_target_pairs={{0,32},{32,64},{64,96},{96,128},{128,160},{160,192},{192,224},{224... | collective-permute-start | bytes 983048 | tf_op jit(solution)/shard_map/ppermute | solution.py:41
  150.3 10.8 %collective-permute-start.23 = (f32[2,64,640]{2,1,0:T(8,128)S(1)}, f32[2,64,640]{2,1,0:T(8,128)S(1)}, u32[]{:S(2)}, u32[]{:S(2)}) collective-permute-start(f32[2,64,640]{2,1,0:T(8,128)S(1)} %bitcast_add_fusion.11), channel_id=1, source_target_pairs={{0,224},{32,0},{64,32},{96,64},{128,96},{160,128},{192,160},{224,1... | collective-permute-start | bytes 983048 | tf_op jit(solution)/shard_map/ppermute | solution.py:41
  156.6 11.7 %collective-permute-start.17 = (f32[2,64,640]{2,1,0:T(8,128)S(1)}, f32[2,64,640]{2,1,0:T(8,128)S(1)}, u32[]{:S(2)}, u32[]{:S(2)}) collective-permute-start(f32[2,64,640]{2,1,0:T(8,128)S(1)} %bitcast_add_fusion.17), channel_id=1, source_target_pairs={{0,32},{32,64},{64,96},{96,128},{128,160},{160,192},{192,224},{224... | collective-permute-start | bytes 983048 | tf_op jit(solution)/shard_map/ppermute | solution.py:41
  161.2 11.7 %collective-permute-start.24 = (f32[2,64,640]{2,1,0:T(8,128)S(1)}, f32[2,64,640]{2,1,0:T(8,128)S(1)}, u32[]{:S(2)}, u32[]{:S(2)}) collective-permute-start(f32[2,64,640]{2,1,0:T(8,128)S(1)} %bitcast_add_fusion.10), channel_id=1, source_target_pairs={{0,224},{32,0},{64,32},{96,64},{128,96},{160,128},{192,160},{224,1... | collective-permute-start | bytes 983048 | tf_op jit(solution)/shard_map/ppermute | solution.py:41
  161.3 11.7 %collective-permute-start.10 = (f32[256,384]{1,0:T(8,128)S(1)}, f32[256,384]{1,0:T(8,128)S(1)}, u32[]{:S(2)}, u32[]{:S(2)}) collective-permute-start(f32[256,384]{1,0:T(8,128)S(1)} %dynamic-slice_bitcast_fusion.3), channel_id=1, source_target_pairs={{0,1},{1,0},{2,3},{3,2},{4,5},{5,4},{6,7},{7,6},{8,9},{9,8},{10,11... | collective-permute-start | bytes 1179656 | tf_op jit(solution)/shard_map/ppermute | solution.py:53
  168.4 8.4 %collective-permute-start.18 = (f32[2,64,640]{2,1,0:T(8,128)S(1)}, f32[2,64,640]{2,1,0:T(8,128)S(1)}, u32[]{:S(2)}, u32[]{:S(2)}) collective-permute-start(f32[2,64,640]{2,1,0:T(8,128)S(1)} %bitcast_add_fusion.16), channel_id=1, source_target_pairs={{0,32},{32,64},{64,96},{96,128},{128,160},{160,192},{192,224},{224... | collective-permute-start | bytes 983048 | tf_op jit(solution)/shard_map/ppermute | solution.py:41
  173.0 8.4 %collective-permute-start.25 = (f32[2,64,640]{2,1,0:T(8,128)S(1)}, f32[2,64,640]{2,1,0:T(8,128)S(1)}, u32[]{:S(2)}, u32[]{:S(2)}) collective-permute-start(f32[2,64,640]{2,1,0:T(8,128)S(1)} %bitcast_add_fusion.9), channel_id=1, source_target_pairs={{0,224},{32,0},{64,32},{96,64},{128,96},{160,128},{192,160},{224,1... | collective-permute-start | bytes 983048 | tf_op jit(solution)/shard_map/ppermute | solution.py:41
  181.4 8.8 %collective-permute-start.26 = (f32[64,1280]{1,0:T(8,128)S(1)}, f32[64,1280]{1,0:T(8,128)}, u32[]{:S(2)}, u32[]{:S(2)}) collective-permute-start(f32[64,1280]{1,0:T(8,128)S(1)} %fusion.29), channel_id=1, source_target_pairs={{0,16},{16,0},{1,17},{17,1},{2,18},{18,2},{3,19},{19,3},{4,20},{20... | collective-permute-start | bytes 983048 | tf_op jit(solution)/shard_map/ppermute | solution.py:53
  183.4 9.4 %copy-start.1 = (bf16[256,2048]{1,0:T(8,128)(2,1)S(1)}, bf16[256,2048]{1,0:T(8,128)(2,1)}, u32[]{:S(2)}) copy-start(bf16[256,2048]{1,0:T(8,128)(2,1)} %param.8) | copy-start | bytes 3145732
Sparse Core Ops, SparseCore 0:
  88.5 41.8 reduce-scatter.1
